TPU v7x, 512 devices: a whole 4x4x16 slice. The times are simulated.
512 devices in a mesh: pool: 64 (over y, z), tensor: 8 (over x, core).
Axes of the slice: x: 4, y: 4, z: 16, core: 2. Of those that a mesh axis runs over, the one named last changes fastest.
Arguments:
- queries: bfloat16 [8192, 4096], P(('pool', 'tensor')), may hold values from -6 to 6
- incoming_keys: bfloat16 [8192, 2048], P(('pool', 'tensor')), may hold values from -6 to 6
- incoming_values: bfloat16 [8192, 2048], P(('pool', 'tensor')), may hold values from -6 to 6
- cached_key_pages: bfloat16 [1024, 128, 2048], P('pool', None, 'tensor'), may hold values from -6 to 6
- cached_value_pages: bfloat16 [1024, 128, 2048], P('pool', None, 'tensor'), may hold values from -6 to 6
- page_table: int32 [64, 64], replicated, may hold values from -1 to 1023, as said below
- lengths: int32 [64], replicated, may hold values from 1 to 8192, as said below
Outputs:
- attended: bfloat16 [8192, 4096], P(('pool', 'tensor'))
Inputs may be any that keep to these rules, and one draw needn't show every extreme that they name: Request r has ceil(lengths[r] / 128) pages; for j below that, page_table[r, j] is the slot of its page j, a slot g of pool device g // 16, which is one of r, r + 1, ..., r + 3 counted modulo 64. No slot holds two pages. All other entries are -1. `lengths`: some request has exactly 8192 cached tokens.
All inputs are finite; a program needn't handle non-finite values.
Results may differ from a plain program's by a relative error of at most 0.008.
Values may be sent and summed in bfloat16 or wider, within the bound.
No kernel may reach another device: no remote copies, remote signals or barrier semaphores. Data moves between devices by JAX's collectives and lax.ppermute only.
A program may use at most 64 MiB of HBM per device.

v0:
```python
import jax
import jax.numpy as jnp
from jax import lax
from jax.sharding import PartitionSpec as P

QUERY_HEADS = 16
KEY_VALUE_HEADS = 8
HEAD_SIZE = 256
SPAN = 4


SOFTCAP = 50.0


def shifted(block, axis, distance):
    devices = range(lax.axis_size(axis))
    route = [((i - distance) % len(devices), i) for i in devices]
    return lax.ppermute(block, axis, route)


def capped(scores, visible):
    capped_scores = SOFTCAP * jnp.tanh(scores / SOFTCAP)
    return jnp.where(visible, jnp.exp(capped_scores), 0.0).astype(jnp.bfloat16)


def on_device(
    queries,
    incoming_keys,
    incoming_values,
    cached_key_pages,
    cached_value_pages,
    page_table,
    lengths,
):
    heads_q, keys_new, values_new = (
        lax.all_to_all(queries, "tensor", split_axis=1, concat_axis=0, tiled=True),
        lax.all_to_all(incoming_keys, "tensor", split_axis=1, concat_axis=0, tiled=True),
        lax.all_to_all(incoming_values, "tensor", split_axis=1, concat_axis=0, tiled=True),
    )
    stretch_len = heads_q.shape[0]
    kv_heads = keys_new.shape[1] // HEAD_SIZE
    query_group_width = QUERY_HEADS // KEY_VALUE_HEADS
    head_count = kv_heads * query_group_width
    score_scale = HEAD_SIZE ** (-0.5)
    query_layout_grid = heads_q.reshape(stretch_len, kv_heads, query_group_width, HEAD_SIZE)
    key_own = keys_new.reshape(stretch_len, kv_heads, HEAD_SIZE)
    value_own = values_new.reshape(stretch_len, kv_heads, HEAD_SIZE)
    causal = jnp.arange(stretch_len)[None, :] <= jnp.arange(stretch_len)[:, None]
    own_scores = (
        jnp.einsum("qgah,kgh->gaqk", query_layout_grid, key_own, preferred_element_type=jnp.float32)
        * score_scale
    )
    own_weights = capped(own_scores, causal)
    own_numer = jnp.einsum(
        "gaqk,kgh->qgah", own_weights, value_own, preferred_element_type=jnp.float32
    )
    own_numer = own_numer.reshape(stretch_len, head_count * HEAD_SIZE)
    own_total = jnp.transpose(jnp.sum(own_weights.astype(jnp.float32), axis=-1), (2, 0, 1)).reshape(
        stretch_len, head_count
    )
    received = [heads_q] + [shifted(heads_q, "pool", offset) for offset in range(1, SPAN)]
    stacked = jnp.stack(received)
    pool_size = lax.axis_size("pool")
    holder = lax.axis_index("pool")
    slots_dev = cached_key_pages.shape[0]
    page_len = cached_key_pages.shape[1]
    owners = (holder - jnp.arange(SPAN, dtype=jnp.int32)) % pool_size
    table_rows = jnp.take(page_table, owners, axis=0)
    global_slot = holder * slots_dev + jnp.arange(slots_dev, dtype=jnp.int32)
    matches = table_rows[:, :, None] == global_slot[None, None, :]
    owner_hot = jnp.any(matches, axis=1)
    page_index = jnp.sum(
        jnp.where(matches, jnp.arange(table_rows.shape[1], dtype=jnp.int32)[None, :, None], 0),
        axis=(0, 1),
    )
    distance = jnp.sum(jnp.where(owner_hot, jnp.arange(SPAN, dtype=jnp.int32)[:, None], 0), axis=0)
    alive_slot = jnp.any(owner_hot, axis=0)
    owner_len = jnp.take(lengths, owners)
    slot_len = jnp.sum(jnp.where(owner_hot, owner_len[:, None], 0), axis=0)
    group_pages = 4
    group_count = slots_dev // group_pages

    def compute(running, input_arrays):
        (
            key_page_block,
            value_page_block,
            picks,
            index_block,
            limit_block,
            alive_block,
            hot_block,
        ) = input_arrays
        query_pick = jnp.take(stacked, picks, axis=0).reshape(
            group_pages, stretch_len, kv_heads, query_group_width, HEAD_SIZE
        )
        key_layout_grid = key_page_block.reshape(group_pages, page_len, kv_heads, HEAD_SIZE)
        value_layout_grid = value_page_block.reshape(group_pages, page_len, kv_heads, HEAD_SIZE)
        scores = (
            jnp.einsum(
                "pqgah,pkgh->pgaqk", query_pick, key_layout_grid, preferred_element_type=jnp.float32
            )
            * score_scale
        )
        position = index_block[:, None] * page_len + jnp.arange(page_len, dtype=jnp.int32)[None, :]
        visible = position < limit_block[:, None]
        weights = capped(scores, visible[:, None, None, None, :])
        numerator = jnp.einsum(
            "pgaqk,pkgh->pqgah", weights, value_layout_grid, preferred_element_type=jnp.float32
        )
        numerator = numerator.reshape(group_pages, stretch_len, head_count * HEAD_SIZE)
        totals = jnp.sum(weights.astype(jnp.float32), axis=-1)
        totals = jnp.transpose(totals, (0, 3, 1, 2)).reshape(group_pages, stretch_len, head_count)
        numer_acc, total_acc = running
        numer_acc = numer_acc + jnp.einsum(
            "pd,pqx->dqx", hot_block, numerator, precision=lax.Precision.HIGHEST
        )
        total_acc = total_acc + jnp.einsum(
            "pd,pqx->dqx", hot_block, totals, precision=lax.Precision.HIGHEST
        )
        return (numer_acc, total_acc)

    def one_group(running, input_arrays):
        running = compute(running, input_arrays)
        return (running, None)

    start_offset = (
        jnp.zeros((SPAN, stretch_len, head_count * HEAD_SIZE), jnp.float32),
        jnp.zeros((SPAN, stretch_len, head_count), jnp.float32),
    )
    input_arrays = (
        cached_key_pages.reshape(group_count, group_pages, page_len, kv_heads * HEAD_SIZE),
        cached_value_pages.reshape(group_count, group_pages, page_len, kv_heads * HEAD_SIZE),
        distance.reshape(group_count, group_pages),
        page_index.reshape(group_count, group_pages),
        slot_len.reshape(group_count, group_pages),
        alive_slot.reshape(group_count, group_pages),
        jnp.transpose(owner_hot).astype(jnp.float32).reshape(group_count, group_pages, SPAN),
    )
    (numer_acc, total_acc), _ = lax.scan(one_group, start_offset, input_arrays)
    numerator = numer_acc[0]
    totals = total_acc[0]
    for offset in range(1, SPAN):
        recv_numer, recv_total = shifted((numer_acc[offset], total_acc[offset]), "pool", -offset)
        numerator = numerator + recv_numer
        totals = totals + recv_total
    numerator = numerator + own_numer
    totals = totals + own_total
    attended = numerator.reshape(stretch_len, head_count, HEAD_SIZE) / totals[:, :, None]
    attended = attended.reshape(stretch_len, head_count * HEAD_SIZE).astype(jnp.bfloat16)
    return lax.all_to_all(attended, "tensor", split_axis=0, concat_axis=1, tiled=True)


def solution(mesh):
    placed = (
        P(("pool", "tensor"), None),
        P(("pool", "tensor"), None),
        P(("pool", "tensor"), None),
        P("pool", None, "tensor"),
        P("pool", None, "tensor"),
        P(),
        P(),
    )
    return jax.shard_map(
        on_device,
        mesh=mesh,
        in_specs=placed,
        out_specs=P(("pool", "tensor"), None),
        check_vma=False,
    )
```

profile of v0, /device:TPU:32, one launch (start us, length us, event | category | flops | bytes accessed | tf_op | source)
XLA Modules:
  0.0 141.5 jit_solution(8766257629097754466)
XLA Ops:
  0.0 1.6 %copy.166 = bf16[2,8,8,512]{3,2,0,1:T(8,128)(2,1)} copy(bf16[2,8,8,512]{3,2,1,0:T(8,128)(2,1)} %bitcast.211) | data formatting | bytes 262144 | tf_op jit(solution)/shard_map/all_to_all | solution.py:36
  1.6 4.3 %all-to-all-start = ((bf16[16,8,512]{2,0,1:T(8,128)(2,1)}), bf16[16,8,512]{2,0,1:T(8,128)(2,1)S(1)}, u32[]{:S(2)}, u32[]{:S(2)}) async-start(bf16[16,8,512]{2,0,1:T(8,128)(2,1)} %bitcast.167), calls=%async_computation | async-start | bytes 262144 | tf_op jit(solution)/shard_map/all_to_all | solution.py:36
  8.2 2.3 %copy.120 = bf16[16,128,256]{1,2,0:T(8,128)(2,1)} copy(bf16[16,128,256]{2,1,0:T(8,128)(2,1)} %param.13) | data formatting | bytes 2097152 | tf_op args[4]
  12.0 4.8 %all-to-all-start.1 = ((bf16[16,8,256]{2,0,1:T(8,128)(2,1)}), bf16[16,8,256]{2,0,1:T(8,128)(2,1)S(1)}, u32[]{:S(2)}, u32[]{:S(2)}) async-start(bf16[16,8,256]{2,0,1:T(8,128)(2,1)} %bitcast.169), calls=%async_computation.1 | async-start | bytes 131072 | tf_op jit(solution)/shard_map/all_to_all | solution.py:37
  16.8 5.2 %collective-permute-start.1 = (bf16[128,512]{1,0:T(8,128)(2,1)S(1)}, bf16[128,512]{1,0:T(8,128)(2,1)S(1)}, u32[]{:S(2)}, u32[]{:S(2)}) collective-permute-start(bf16[128,512]{1,0:T(8,128)(2,1)S(1)} %bitcast.203), channel_id=1, source_target_pairs={{496,0},{504,8},{0,16},{8,24},{16,32},{24,40},{32,48},{40,56},{48,... | collective-permute-start | bytes 393224 | tf_op jit(solution)/shard_map/ppermute | solution.py:18
  22.0 7.7 %collective-permute-start.2 = (bf16[128,512]{1,0:T(8,128)(2,1)S(1)}, bf16[128,512]{1,0:T(8,128)(2,1)S(1)}, u32[]{:S(2)}, u32[]{:S(2)}) collective-permute-start(bf16[128,512]{1,0:T(8,128)(2,1)S(1)} %bitcast.204), channel_id=1, source_target_pairs={{488,0},{496,8},{504,16},{0,24},{8,32},{16,40},{24,48},{32,56},{40... | collective-permute-start | bytes 393224 | tf_op jit(solution)/shard_map/ppermute | solution.py:18
  29.7 3.8 %collective-permute-start = (bf16[128,512]{1,0:T(8,128)(2,1)S(1)}, bf16[128,512]{1,0:T(8,128)(2,1)S(1)}, u32[]{:S(2)}, u32[]{:S(2)}) collective-permute-start(bf16[128,512]{1,0:T(8,128)(2,1)S(1)} %bitcast.205), channel_id=1, source_target_pairs={{504,0},{0,8},{8,16},{16,24},{24,32},{32,40},{40,48},{48,56},{56,6... | collective-permute-start | bytes 393224 | tf_op jit(solution)/shard_map/ppermute | solution.py:18
  33.6 4.8 %all-to-all-start.2 = ((bf16[16,8,256]{2,0,1:T(8,128)(2,1)}), bf16[16,8,256]{2,0,1:T(8,128)(2,1)S(1)}, u32[]{:S(2)}, u32[]{:S(2)}) async-start(bf16[16,8,256]{2,0,1:T(8,128)(2,1)} %bitcast.168), calls=%async_computation.2 | async-start | bytes 131072 | tf_op jit(solution)/shard_map/all_to_all | solution.py:38
  39.0 4.6 %collective-permute-done.2 = bf16[128,512]{1,0:T(8,128)(2,1)S(1)} collective-permute-done((bf16[128,512]{1,0:T(8,128)(2,1)S(1)}, bf16[128,512]{1,0:T(8,128)(2,1)S(1)}, u32[]{:S(2)}, u32[]{:S(2)}) %collective-permute-start.2) | collective-permute-done | bytes 131104 | tf_op jit(solution)/shard_map/ppermute | solution.py:18
  45.0 31.1 %while.15 = (s32[]{:T(128)}, f32[4,128,512]{2,0,1:T(4,128)S(1)}, f32[4,128,2]{1,0,2:T(4,128)S(1)}, f32[4,4,4]{2,1,0:T(4,128)S(1)}, bf16[4,4,128,256]{2,3,1,0:T(8...) while((s32[]{:T(128)}, f32[4,128,512]{2,0,1:T(4,128)S(1)}, ...), condition=%wide.region_6.7_spmd.clone, body=%wide.region_4.6_spmd.clone.sunk | while | flops 148425760 | bytes 8939852 | solution.py:139
  45.1 1.6 %gather_fusion = bf16[4,128,512]{2,1,0:T(8,128)(2,1)S(1)} fusion(bf16[4,128,512]{2,1,0:T(8,128)(2,1)} %get-tuple-element.361, s32[1024]{0:T(1024)S(1)} %pad_clamp_fusion.3), kind=kCustom, calls=%fused_computation.clone.clone.1 | custom fusion | bytes 1048592 | tf_op jit(solution)/shard_map/while/body/eval_jaxpr/jit(_take)/gather | solution.py:93
  46.8 1.4 convert_reduce_fusion.3
  50.0 2.6 %convolution_add_fusion.4 = f32[4,128,512]{2,0,1:T(4,128)S(1)} fusion(f32[4,128,512]{2,0,1:T(4,128)S(1)} %copy.174, f32[4,128,512]{2,0,1:T(4,128)S(1)} %get-tuple-element.341, pred[]{:T(512)S(6)} %compare.13, f32[4,4,4]{2,1,0:T(4,128)S(1)} %get-tuple-element.355, s32[]{:T(128)} %get-tuple-element.340), kind=kOutput, calls=%fused_computation.3.clone.1 | convolution fusion | flops 13107200 | bytes 3147781 | tf_op jit(solution)/shard_map/while/body/eval_jaxpr/pd,pqx->dqx/dot_general | solution.py:114
  52.9 1.6 %gather_fusion = bf16[4,128,512]{2,1,0:T(8,128)(2,1)S(1)} fusion(bf16[4,128,512]{2,1,0:T(8,128)(2,1)} %get-tuple-element.361, s32[1024]{0:T(1024)S(1)} %pad_clamp_fusion.3), kind=kCustom, calls=%fused_computation.clone.clone.1 | custom fusion | bytes 1048592 | tf_op jit(solution)/shard_map/while/body/eval_jaxpr/jit(_take)/gather | solution.py:93
  54.6 1.4 convert_reduce_fusion.3
  57.7 2.6 %convolution_add_fusion.4 = f32[4,128,512]{2,0,1:T(4,128)S(1)} fusion(f32[4,128,512]{2,0,1:T(4,128)S(1)} %copy.174, f32[4,128,512]{2,0,1:T(4,128)S(1)} %get-tuple-element.341, pred[]{:T(512)S(6)} %compare.13, f32[4,4,4]{2,1,0:T(4,128)S(1)} %get-tuple-element.355, s32[]{:T(128)} %get-tuple-element.340), kind=kOutput, calls=%fused_computation.3.clone.1 | convolution fusion | flops 13107200 | bytes 3147781 | tf_op jit(solution)/shard_map/while/body/eval_jaxpr/pd,pqx->dqx/dot_general | solution.py:114
  60.7 1.6 %gather_fusion = bf16[4,128,512]{2,1,0:T(8,128)(2,1)S(1)} fusion(bf16[4,128,512]{2,1,0:T(8,128)(2,1)} %get-tuple-element.361, s32[1024]{0:T(1024)S(1)} %pad_clamp_fusion.3), kind=kCustom, calls=%fused_computation.clone.clone.1 | custom fusion | bytes 1048592 | tf_op jit(solution)/shard_map/while/body/eval_jaxpr/jit(_take)/gather | solution.py:93
  62.3 1.4 convert_reduce_fusion.3
  65.5 2.6 %convolution_add_fusion.4 = f32[4,128,512]{2,0,1:T(4,128)S(1)} fusion(f32[4,128,512]{2,0,1:T(4,128)S(1)} %copy.174, f32[4,128,512]{2,0,1:T(4,128)S(1)} %get-tuple-element.341, pred[]{:T(512)S(6)} %compare.13, f32[4,4,4]{2,1,0:T(4,128)S(1)} %get-tuple-element.355, s32[]{:T(128)} %get-tuple-element.340), kind=kOutput, calls=%fused_computation.3.clone.1 | convolution fusion | flops 13107200 | bytes 3147781 | tf_op jit(solution)/shard_map/while/body/eval_jaxpr/pd,pqx->dqx/dot_general | solution.py:114
  68.5 1.6 %gather_fusion = bf16[4,128,512]{2,1,0:T(8,128)(2,1)S(1)} fusion(bf16[4,128,512]{2,1,0:T(8,128)(2,1)} %get-tuple-element.361, s32[1024]{0:T(1024)S(1)} %pad_clamp_fusion.3), kind=kCustom, calls=%fused_computation.clone.clone.1 | custom fusion | bytes 1048592 | tf_op jit(solution)/shard_map/while/body/eval_jaxpr/jit(_take)/gather | solution.py:93
  70.1 1.4 convert_reduce_fusion.3
  73.3 2.6 %convolution_add_fusion.4 = f32[4,128,512]{2,0,1:T(4,128)S(1)} fusion(f32[4,128,512]{2,0,1:T(4,128)S(1)} %copy.174, f32[4,128,512]{2,0,1:T(4,128)S(1)} %get-tuple-element.341, pred[]{:T(512)S(6)} %compare.13, f32[4,4,4]{2,1,0:T(4,128)S(1)} %get-tuple-element.355, s32[]{:T(128)} %get-tuple-element.340), kind=kOutput, calls=%fused_computation.3.clone.1 | convolution fusion | flops 13107200 | bytes 3147781 | tf_op jit(solution)/shard_map/while/body/eval_jaxpr/pd,pqx->dqx/dot_general | solution.py:114
  76.2 7.2 %collective-permute-start.7 = (f32[128,2]{0,1:T(2,128)S(1)}, f32[128,2]{0,1:T(2,128)S(1)}, u32[]{:S(2)}, u32[]{:S(2)}) collective-permute-start(f32[128,2]{0,1:T(2,128)S(1)} %get-tuple-element.255), channel_id=1, source_target_pairs={{16,0},{24,8},{32,16},{40,24},{48,32},{56,40},{64,48},{72,56},{80,... | collective-permute-start | bytes 3080 | tf_op jit(solution)/shard_map/ppermute | solution.py:18
  83.4 6.2 %collective-permute-start.8 = (f32[128,2]{0,1:T(2,128)S(1)}, f32[128,2]{0,1:T(2,128)S(1)}, u32[]{:S(2)}, u32[]{:S(2)}) collective-permute-start(f32[128,2]{0,1:T(2,128)S(1)} %get-tuple-element.256), channel_id=1, source_target_pairs={{24,0},{32,8},{40,16},{48,24},{56,32},{64,40},{72,48},{80,56},{88,... | collective-permute-start | bytes 3080 | tf_op jit(solution)/shard_map/ppermute | solution.py:18
  89.5 2.9 %collective-permute-start.6 = (f32[128,2]{0,1:T(2,128)S(1)}, f32[128,2]{0,1:T(2,128)S(1)}, u32[]{:S(2)}, u32[]{:S(2)}) collective-permute-start(f32[128,2]{0,1:T(2,128)S(1)} %bitcast.220), channel_id=1, source_target_pairs={{8,0},{16,8},{24,16},{32,24},{40,32},{48,40},{56,48},{64,56},{72,6... | collective-permute-start | bytes 3080 | tf_op jit(solution)/shard_map/ppermute | solution.py:18
  92.9 3.0 %collective-permute-start.3 = (f32[128,512]{0,1:T(8,128)S(1)}, f32[128,512]{0,1:T(8,128)S(1)}, u32[]{:S(2)}, u32[]{:S(2)}) collective-permute-start(f32[128,512]{0,1:T(8,128)S(1)} %get-tuple-element.252), channel_id=1, source_target_pairs={{8,0},{16,8},{24,16},{32,24},{40,32},{48,40},{56,48},{64,56},{72,6... | collective-permute-start | bytes 786440 | tf_op jit(solution)/shard_map/ppermute | solution.py:18
  96.0 4.4 %collective-permute-start.4 = (f32[128,512]{0,1:T(8,128)S(1)}, f32[128,512]{0,1:T(8,128)S(1)}, u32[]{:S(2)}, u32[]{:S(2)}) collective-permute-start(f32[128,512]{0,1:T(8,128)S(1)} %get-tuple-element.254), channel_id=1, source_target_pairs={{16,0},{24,8},{32,16},{40,24},{48,32},{56,40},{64,48},{72,56},{80,... | collective-permute-start | bytes 786440 | tf_op jit(solution)/shard_map/ppermute | solution.py:18
  100.5 1.9 %collective-permute-start.5 = (f32[128,512]{0,1:T(8,128)S(1)}, f32[128,512]{0,1:T(8,128)S(1)}, u32[]{:S(2)}, u32[]{:S(2)}) collective-permute-start(f32[128,512]{0,1:T(8,128)S(1)} %get-tuple-element.253), channel_id=1, source_target_pairs={{24,0},{32,8},{40,16},{48,24},{56,32},{64,40},{72,48},{80,56},{88,... | collective-permute-start | bytes 786440 | tf_op jit(solution)/shard_map/ppermute | solution.py:18
  102.8 3.2 %collective-permute-done.3 = f32[128,512]{0,1:T(8,128)S(1)} collective-permute-done((f32[128,512]{0,1:T(8,128)S(1)}, f32[128,512]{0,1:T(8,128)S(1)}, u32[]{:S(2)}, u32[]{:S(2)}) %collective-permute-start.3) | collective-permute-done | bytes 262176 | tf_op jit(solution)/shard_map/ppermute | solution.py:18
  106.0 12.8 %collective-permute-done.4 = f32[128,512]{0,1:T(8,128)S(1)} collective-permute-done((f32[128,512]{0,1:T(8,128)S(1)}, f32[128,512]{0,1:T(8,128)S(1)}, u32[]{:S(2)}, u32[]{:S(2)}) %collective-permute-start.4) | collective-permute-done | bytes 262176 | tf_op jit(solution)/shard_map/ppermute | solution.py:18
  118.7 12.2 %collective-permute-done.5 = f32[128,512]{0,1:T(8,128)S(1)} collective-permute-done((f32[128,512]{0,1:T(8,128)S(1)}, f32[128,512]{0,1:T(8,128)S(1)}, u32[]{:S(2)}, u32[]{:S(2)}) %collective-permute-start.5) | collective-permute-done | bytes 262176 | tf_op jit(solution)/shard_map/ppermute | solution.py:18
  131.2 9.7 %all_to_all.70 = bf16[8,16,512]{2,1,0:T(8,128)(2,1)S(1)} all-to-all(bf16[8,16,512]{2,1,0:T(8,128)(2,1)S(1)} %bitcast.208), channel_id=1, replica_groups=mesh['pool'=64,'tensor'=8] {'tensor'}, dimensions={0} | all-to-all | bytes 262144 | tf_op jit(solution)/shard_map/all_to_all | solution.py:150
  (83 shorter events, 15.7 us)
Async XLA Ops:
  0.0 5.9 %copy-start = (s32[64,64]{1,0:T(8,128)S(1)}, s32[64,64]{1,0:T(8,128)}, u32[]{:S(2)}) copy-start(s32[64,64]{1,0:T(8,128)} %param.14) | copy-start | bytes 49156
  1.6 10.4 %all-to-all-start = ((bf16[16,8,512]{2,0,1:T(8,128)(2,1)}), bf16[16,8,512]{2,0,1:T(8,128)(2,1)S(1)}, u32[]{:S(2)}, u32[]{:S(2)}) async-start(bf16[16,8,512]{2,0,1:T(8,128)(2,1)} %bitcast.167), calls=%async_computation | async-start | bytes 262144 | tf_op jit(solution)/shard_map/all_to_all | solution.py:36
  5.9 0.7 copy-start.1
  8.2 2.3 %copy-start.2 = (bf16[16,2048]{1,0:T(8,128)(2,1)S(1)}, bf16[16,2048]{1,0:T(8,128)(2,1)}, u32[]{:S(2)}) copy-start(bf16[16,2048]{1,0:T(8,128)(2,1)} %param.10) | copy-start | bytes 196612
  10.5 0.9 copy-start.3
  12.0 21.6 %all-to-all-start.1 = ((bf16[16,8,256]{2,0,1:T(8,128)(2,1)}), bf16[16,8,256]{2,0,1:T(8,128)(2,1)S(1)}, u32[]{:S(2)}, u32[]{:S(2)}) async-start(bf16[16,8,256]{2,0,1:T(8,128)(2,1)} %bitcast.169), calls=%async_computation.1 | async-start | bytes 131072 | tf_op jit(solution)/shard_map/all_to_all | solution.py:37
  16.8 22.2 %collective-permute-start.1 = (bf16[128,512]{1,0:T(8,128)(2,1)S(1)}, bf16[128,512]{1,0:T(8,128)(2,1)S(1)}, u32[]{:S(2)}, u32[]{:S(2)}) collective-permute-start(bf16[128,512]{1,0:T(8,128)(2,1)S(1)} %bitcast.203), channel_id=1, source_target_pairs={{496,0},{504,8},{0,16},{8,24},{16,32},{24,40},{32,48},{40,56},{48,... | collective-permute-start | bytes 393224 | tf_op jit(solution)/shard_map/ppermute | solution.py:18
  22.0 21.6 %collective-permute-start.2 = (bf16[128,512]{1,0:T(8,128)(2,1)S(1)}, bf16[128,512]{1,0:T(8,128)(2,1)S(1)}, u32[]{:S(2)}, u32[]{:S(2)}) collective-permute-start(bf16[128,512]{1,0:T(8,128)(2,1)S(1)} %bitcast.204), channel_id=1, source_target_pairs={{488,0},{496,8},{504,16},{0,24},{8,32},{16,40},{24,48},{32,56},{40... | collective-permute-start | bytes 393224 | tf_op jit(solution)/shard_map/ppermute | solution.py:18
  29.7 14.4 %collective-permute-start = (bf16[128,512]{1,0:T(8,128)(2,1)S(1)}, bf16[128,512]{1,0:T(8,128)(2,1)S(1)}, u32[]{:S(2)}, u32[]{:S(2)}) collective-permute-start(bf16[128,512]{1,0:T(8,128)(2,1)S(1)} %bitcast.205), channel_id=1, source_target_pairs={{504,0},{0,8},{8,16},{16,24},{24,32},{32,40},{40,48},{48,56},{56,6... | collective-permute-start | bytes 393224 | tf_op jit(solution)/shard_map/ppermute | solution.py:18
  33.6 68.8 %all-to-all-start.2 = ((bf16[16,8,256]{2,0,1:T(8,128)(2,1)}), bf16[16,8,256]{2,0,1:T(8,128)(2,1)S(1)}, u32[]{:S(2)}, u32[]{:S(2)}) async-start(bf16[16,8,256]{2,0,1:T(8,128)(2,1)} %bitcast.168), calls=%async_computation.2 | async-start | bytes 131072 | tf_op jit(solution)/shard_map/all_to_all | solution.py:38
  76.2 24.3 %collective-permute-start.7 = (f32[128,2]{0,1:T(2,128)S(1)}, f32[128,2]{0,1:T(2,128)S(1)}, u32[]{:S(2)}, u32[]{:S(2)}) collective-permute-start(f32[128,2]{0,1:T(2,128)S(1)} %get-tuple-element.255), channel_id=1, source_target_pairs={{16,0},{24,8},{32,16},{40,24},{48,32},{56,40},{64,48},{72,56},{80,... | collective-permute-start | bytes 3080 | tf_op jit(solution)/shard_map/ppermute | solution.py:18
  83.4 19.4 %collective-permute-start.8 = (f32[128,2]{0,1:T(2,128)S(1)}, f32[128,2]{0,1:T(2,128)S(1)}, u32[]{:S(2)}, u32[]{:S(2)}) collective-permute-start(f32[128,2]{0,1:T(2,128)S(1)} %get-tuple-element.256), channel_id=1, source_target_pairs={{24,0},{32,8},{40,16},{48,24},{56,32},{64,40},{72,48},{80,56},{88,... | collective-permute-start | bytes 3080 | tf_op jit(solution)/shard_map/ppermute | solution.py:18
  89.5 13.2 %collective-permute-start.6 = (f32[128,2]{0,1:T(2,128)S(1)}, f32[128,2]{0,1:T(2,128)S(1)}, u32[]{:S(2)}, u32[]{:S(2)}) collective-permute-start(f32[128,2]{0,1:T(2,128)S(1)} %bitcast.220), channel_id=1, source_target_pairs={{8,0},{16,8},{24,16},{32,24},{40,32},{48,40},{56,48},{64,56},{72,6... | collective-permute-start | bytes 3080 | tf_op jit(solution)/shard_map/ppermute | solution.py:18
  92.9 13.0 %collective-permute-start.3 = (f32[128,512]{0,1:T(8,128)S(1)}, f32[128,512]{0,1:T(8,128)S(1)}, u32[]{:S(2)}, u32[]{:S(2)}) collective-permute-start(f32[128,512]{0,1:T(8,128)S(1)} %get-tuple-element.252), channel_id=1, source_target_pairs={{8,0},{16,8},{24,16},{32,24},{40,32},{48,40},{56,48},{64,56},{72,6... | collective-permute-start | bytes 786440 | tf_op jit(solution)/shard_map/ppermute | solution.py:18
  96.0 22.7 %collective-permute-start.4 = (f32[128,512]{0,1:T(8,128)S(1)}, f32[128,512]{0,1:T(8,128)S(1)}, u32[]{:S(2)}, u32[]{:S(2)}) collective-permute-start(f32[128,512]{0,1:T(8,128)S(1)} %get-tuple-element.254), channel_id=1, source_target_pairs={{16,0},{24,8},{32,16},{40,24},{48,32},{56,40},{64,48},{72,56},{80,... | collective-permute-start | bytes 786440 | tf_op jit(solution)/shard_map/ppermute | solution.py:18
  100.5 30.5 %collective-permute-start.5 = (f32[128,512]{0,1:T(8,128)S(1)}, f32[128,512]{0,1:T(8,128)S(1)}, u32[]{:S(2)}, u32[]{:S(2)}) collective-permute-start(f32[128,512]{0,1:T(8,128)S(1)} %get-tuple-element.253), channel_id=1, source_target_pairs={{24,0},{32,8},{40,16},{48,24},{56,32},{64,40},{72,48},{80,56},{88,... | collective-permute-start | bytes 786440 | tf_op jit(solution)/shard_map/ppermute | solution.py:18
where the time goes:
time: 143 us; the launch traced here: 141 us
  starting transfers between devices  56.3 us (39%)
  waiting for transfers between devices  33.7 us (24%)
  matrix products  22.4 us (16%)
  local copies, waits for them, and re-layouts  16.9 us (12%)
  blocking collectives  9.67 us (7%)
  other arithmetic  2.02 us (1%)
    ppermute x9, starting transfers between devices, shifted(): return lax.ppermute(block, axis, route)  42.4 us
    ppermute x9, waiting for transfers between devices, shifted(): return lax.ppermute(block, axis, route)  33.7 us
    dot_general x4, matrix products, compute(): jnp.einsum('pd,pqx->dqx', hot_block, numerator, precision=lax.Precision.H...  10.6 us
    all_to_all x1, blocking collectives, on_device(): lax.all_to_all(attended, 'tensor', split_axis=0, concat_axis=1, tiled=True)  9.67 us
    gather x4, local copies, waits for them, and re-layouts, compute(): jnp.take(stacked, picks, axis=0)  6.49 us
    dot_general x4, matrix products, compute(): jnp.einsum('pqgah,pkgh->pgaqk', query_pick, key_layout_grid, preferred_el...  5.63 us
    dot_general x4, matrix products, compute(): jnp.einsum('pgaqk,pkgh->pqgah', weights, value_layout_grid, preferred_ele...  4.94 us
    all_to_all x1, starting transfers between devices, on_device(): lax.all_to_all(incoming_values, 'tensor', split_axis=1, concat_axis=0, ti...  4.82 us
  transfers between devices with their start and end apart: 12, of which 6 were waited for; matrix products, arithmetic and copies ran while one was open for 27% of the time, Pallas kernels for 0%

commit v1 on v0

v1 whole, which is shorter than its diff:
```python
import functools

import jax
import jax.numpy as jnp
from jax import lax
from jax.experimental import pallas as pl
from jax.experimental.pallas import tpu as pltpu
from jax.sharding import PartitionSpec as P

QUERY_HEADS = 16
KEY_VALUE_HEADS = 8
HEAD_SIZE = 256
SPAN = 4

SOFTCAP = 50.0
SCORE_SCALE = HEAD_SIZE ** (-0.5)


def shifted(block, axis, distance):
    devices = range(lax.axis_size(axis))
    route = [((i - distance) % len(devices), i) for i in devices]
    return lax.ppermute(block, axis, route)


def _attend_kernel(ds, with_own, meta_ref, *refs):
    nq = len(ds)
    q_refs = refs[:nq]
    kp_ref, vp_ref = refs[nq], refs[nq + 1]
    rest = refs[nq + 2:]
    if with_own:
        kn_ref, vn_ref = rest[0], rest[1]
        rest = rest[2:]
    out_ref = rest[0]
    rows = q_refs[0].shape[0]
    slots, page_len, kv_width = kp_ref.shape
    kv_local = kv_width // HEAD_SIZE
    group = QUERY_HEADS // KEY_VALUE_HEADS
    out_ref[...] = jnp.zeros(out_ref.shape, jnp.float32)
    ones = jnp.ones((8, page_len), jnp.bfloat16)

    def add_block(i, q_ref, k, v, visible):
        for g in range(kv_local):
            kg = k[:, g * HEAD_SIZE:(g + 1) * HEAD_SIZE]
            vg = v[:, g * HEAD_SIZE:(g + 1) * HEAD_SIZE]
            for a in range(group):
                h = g * group + a
                col = h * HEAD_SIZE
                q = q_ref[:, col:col + HEAD_SIZE]
                s = lax.dot_general(
                    q, kg, (((1,), (1,)), ((), ())), preferred_element_type=jnp.float32
                ) * SCORE_SCALE
                w = jnp.where(visible, jnp.exp(SOFTCAP * jnp.tanh(s / SOFTCAP)), 0.0).astype(
                    jnp.bfloat16
                )
                out_ref[i, :rows, col:col + HEAD_SIZE] += jnp.dot(
                    w, vg, preferred_element_type=jnp.float32
                )
                t = lax.dot_general(
                    ones, w, (((1,), (1,)), ((), ())), preferred_element_type=jnp.float32
                )
                out_ref[i, rows:rows + 8, h * rows:(h + 1) * rows] += t

    key_pos = lax.broadcasted_iota(jnp.int32, (rows, page_len), 1)
    if with_own:
        q_pos = lax.broadcasted_iota(jnp.int32, (rows, page_len), 0)
        add_block(ds.index(0), q_refs[ds.index(0)], kn_ref[...], vn_ref[...], key_pos <= q_pos)

    def slot(s, carry):
        d = meta_ref[0, s]
        lim = meta_ref[1, s]
        for i, dd in enumerate(ds):
            @pl.when((d == dd) & (lim > 0))
            def _():
                add_block(i, q_refs[i], kp_ref[s], vp_ref[s], key_pos < lim)

        return carry

    lax.fori_loop(0, slots, slot, 0)


def attend(ds, meta, qs, kp, vp, kn=None, vn=None):
    with_own = kn is not None
    rows, width = qs[0].shape
    slots, page_len, kv_width = kp.shape
    args = [meta, *qs, kp, vp] + ([kn, vn] if with_own else [])
    blocks = slots + (1 if with_own else 0)
    heads = width // HEAD_SIZE
    flops = blocks * heads * rows * page_len * HEAD_SIZE * 4
    cost = pl.CostEstimate(
        flops=flops,
        transcendentals=blocks * heads * rows * page_len * 2,
        bytes_accessed=sum(int(x.size) * x.dtype.itemsize for x in args)
        + len(ds) * (rows + 8) * width * 4,
    )
    return pl.pallas_call(
        functools.partial(_attend_kernel, tuple(ds), with_own),
        out_shape=jax.ShapeDtypeStruct((len(ds), rows + 8, width), jnp.float32),
        in_specs=[pl.BlockSpec(memory_space=pltpu.SMEM)]
        + [pl.BlockSpec(memory_space=pltpu.VMEM)] * (len(args) - 1),
        out_specs=pl.BlockSpec(memory_space=pltpu.VMEM),
        cost_estimate=cost,
    )(*args)


def on_device(
    queries,
    incoming_keys,
    incoming_values,
    cached_key_pages,
    cached_value_pages,
    page_table,
    lengths,
):
    tensor_size = lax.axis_size("tensor")
    n_tok = queries.shape[0]
    q_width = queries.shape[1] // tensor_size
    kv_width = incoming_keys.shape[1] // tensor_size
    packed = jnp.concatenate(
        [
            queries.reshape(n_tok, tensor_size, q_width),
            incoming_keys.reshape(n_tok, tensor_size, kv_width),
            incoming_values.reshape(n_tok, tensor_size, kv_width),
        ],
        axis=2,
    )
    mixed = lax.all_to_all(packed, "tensor", split_axis=1, concat_axis=0, tiled=True)
    rows = mixed.shape[0]
    mixed = mixed.reshape(rows, q_width + 2 * kv_width)
    q_own = mixed[:, :q_width]
    k_new = mixed[:, q_width:q_width + kv_width]
    v_new = mixed[:, q_width + kv_width:]

    received = [q_own] + [shifted(q_own, "pool", offset) for offset in range(1, SPAN)]

    pool_size = lax.axis_size("pool")
    holder = lax.axis_index("pool")
    slots_dev = cached_key_pages.shape[0]
    page_len = cached_key_pages.shape[1]
    owners = (holder - jnp.arange(SPAN, dtype=jnp.int32)) % pool_size
    table_rows = jnp.take(page_table, owners, axis=0)
    global_slot = holder * slots_dev + jnp.arange(slots_dev, dtype=jnp.int32)
    matches = table_rows[:, :, None] == global_slot[None, None, :]
    owner_hot = jnp.any(matches, axis=1)
    page_index = jnp.sum(
        jnp.where(matches, jnp.arange(table_rows.shape[1], dtype=jnp.int32)[None, :, None], 0),
        axis=(0, 1),
    )
    distance = jnp.sum(jnp.where(owner_hot, jnp.arange(SPAN, dtype=jnp.int32)[:, None], 0), axis=0)
    owner_len = jnp.take(lengths, owners)
    slot_len = jnp.sum(jnp.where(owner_hot, owner_len[:, None], 0), axis=0)
    limit = jnp.clip(slot_len - page_index * page_len, 0, page_len)
    meta = jnp.stack([distance, limit]).astype(jnp.int32)

    acc = attend(
        list(range(SPAN)), meta, received, cached_key_pages, cached_value_pages, k_new, v_new
    )
    total = acc[0]
    for offset in range(1, SPAN):
        total = total + shifted(acc[offset], "pool", -offset)
    heads = q_width // HEAD_SIZE
    numerator = total[:rows].reshape(rows, heads, HEAD_SIZE)
    totals = total[rows, : heads * rows].reshape(heads, rows)
    attended = numerator / jnp.transpose(totals)[:, :, None]
    attended = attended.reshape(rows, q_width).astype(jnp.bfloat16)
    return lax.all_to_all(attended, "tensor", split_axis=0, concat_axis=1, tiled=True)


def solution(mesh):
    placed = (
        P(("pool", "tensor"), None),
        P(("pool", "tensor"), None),
        P(("pool", "tensor"), None),
        P("pool", None, "tensor"),
        P("pool", None, "tensor"),
        P(),
        P(),
    )
    return jax.shard_map(
        on_device,
        mesh=mesh,
        in_specs=placed,
        out_specs=P(("pool", "tensor"), None),
        check_vma=False,
    )
```

time: 143 us -> 105 us (0.73)
  the two profiles are of different devices: /device:TPU:32 before, /device:TPU:1 now
where the time goes in v1:
time: 105 us; the launch traced here: 104 us
  waiting for transfers between devices  40.6 us (39%)
  starting transfers between devices  34.5 us (33%)
  blocking collectives  10.1 us (10%)
  Pallas kernels  8.68 us (8%)
  local copies, waits for them, and re-layouts  6.52 us (6%)
  other arithmetic  3.04 us (3%)
    ppermute x6, waiting for transfers between devices, shifted(): return lax.ppermute(block, axis, route)  36.5 us
    ppermute x6, starting transfers between devices, shifted(): return lax.ppermute(block, axis, route)  24.4 us
    all_to_all x1, starting transfers between devices, on_device(): lax.all_to_all(packed, 'tensor', split_axis=1, concat_axis=0, tiled=True)  10.2 us
    all_to_all x1, blocking collectives, on_device(): lax.all_to_all(attended, 'tensor', split_axis=0, concat_axis=1, tiled=True)  10.1 us
    pallas_call x1, Pallas kernels, attend(): pl.pallas_call(functools.partial(_attend_kernel, tuple(ds), with_own), ou...  8.68 us
    all_to_all x1, waiting for transfers between devices, on_device(): lax.all_to_all(packed, 'tensor', split_axis=1, concat_axis=0, tiled=True)  4.06 us
  transfers between devices with their start and end apart: 7, of which 7 were waited for; matrix products, arithmetic and copies ran while one was open for 3% of the time, Pallas kernels for 0%

profile of v1, /device:TPU:1, one launch (start us, length us, event | category | flops | bytes accessed | tf_op | source)
XLA Modules:
  0.0 103.7 jit_solution(2033555615038618462)
XLA Ops:
  0.0 0.9 copy.31
  0.9 0.9 copy_bitcast_fusion.1
  1.8 0.7 pad_maximum_fusion
  2.5 10.2 %all-to-all-start = ((bf16[16,8,1024]{2,0,1:T(8,128)(2,1)}), bf16[16,8,1024]{2,0,1:T(8,128)(2,1)S(1)}, u32[]{:S(2)}, u32[]{:S(2)}) async-start(bf16[16,8,1024]{2,0,1:T(8,128)(2,1)} %pad_maximum_fusion), calls=%async_computation | async-start | bytes 524288 | tf_op jit(solution)/shard_map/all_to_all | solution.py:126
  12.8 0.6 gather_fusion
  13.4 0.2 fusion.4
  13.6 0.2 compare_reduce_fusion
  13.8 0.6 gather_fusion.1
  14.5 0.1 select_reduce_fusion.1
  14.6 0.6 pad_add_fusion.meta_ref
  15.2 4.1 %all-to-all-done = bf16[16,8,1024]{2,0,1:T(8,128)(2,1)S(1)} async-done(((bf16[16,8,1024]{2,0,1:T(8,128)(2,1)}), bf16[16,8,1024]{2,0,1:T(8,128)(2,1)S(1)}, u32[]{:S(2)}, u32[]{:S(2)}) %all-to-all-start) | async-done | bytes 262176 | tf_op jit(solution)/shard_map/all_to_all | solution.py:126
  19.3 1.9 %collective-permute-start.2 = (bf16[128,512]{1,0:T(8,128)(2,1)S(1)}, bf16[128,512]{1,0:T(8,128)(2,1)S(1)}, u32[]{:S(2)}, u32[]{:S(2)}) collective-permute-start(bf16[128,512]{1,0:T(8,128)(2,1)S(1)} %slice.40.refs_0_), channel_id=1, source_target_pairs={{488,0},{496,8},{504,16},{0,24},{8,32},{16,40},{24,48},{32,56},{40... | collective-permute-start | bytes 393224 | tf_op jit(solution)/shard_map/ppermute | solution.py:22
  21.2 6.0 %collective-permute-start.1 = (bf16[128,512]{1,0:T(8,128)(2,1)S(1)}, bf16[128,512]{1,0:T(8,128)(2,1)S(1)}, u32[]{:S(2)}, u32[]{:S(2)}) collective-permute-start(bf16[128,512]{1,0:T(8,128)(2,1)S(1)} %slice.40.refs_0_), channel_id=1, source_target_pairs={{496,0},{504,8},{0,16},{8,24},{16,32},{24,40},{32,48},{40,56},{48,... | collective-permute-start | bytes 393224 | tf_op jit(solution)/shard_map/ppermute | solution.py:22
  27.3 3.5 %collective-permute-start = (bf16[128,512]{1,0:T(8,128)(2,1)S(1)}, bf16[128,512]{1,0:T(8,128)(2,1)S(1)}, u32[]{:S(2)}, u32[]{:S(2)}) collective-permute-start(bf16[128,512]{1,0:T(8,128)(2,1)S(1)} %slice.40.refs_0_), channel_id=1, source_target_pairs={{504,0},{0,8},{8,16},{16,24},{24,32},{32,40},{40,48},{48,56},{56,6... | collective-permute-start | bytes 393224 | tf_op jit(solution)/shard_map/ppermute | solution.py:22
  30.8 0.7 fusion.8
  31.5 0.8 collective-permute-done.2.refs_3_
  32.3 11.0 %collective-permute-done.1.refs_2_ = bf16[128,512]{1,0:T(8,128)(2,1)S(1)} collective-permute-done((bf16[128,512]{1,0:T(8,128)(2,1)S(1)}, bf16[128,512]{1,0:T(8,128)(2,1)S(1)}, u32[]{:S(2)}, u32[]{:S(2)}) %collective-permute-start.1) | collective-permute-done | bytes 131104 | tf_op jit(solution)/shard_map/ppermute | solution.py:22
  43.3 2.7 %collective-permute-done.refs_1_ = bf16[128,512]{1,0:T(8,128)(2,1)S(1)} collective-permute-done((bf16[128,512]{1,0:T(8,128)(2,1)S(1)}, bf16[128,512]{1,0:T(8,128)(2,1)S(1)}, u32[]{:S(2)}, u32[]{:S(2)}) %collective-permute-start) | collective-permute-done | bytes 131104 | tf_op jit(solution)/shard_map/ppermute | solution.py:22
  46.0 0.6 copy-done.5
  46.6 8.7 %shard_map.73 = f32[4,136,512]{2,1,0:T(8,128)} custom-call(s32[2,16]{1,0:T(2,128)} %pad_add_fusion.meta_ref, bf16[128,512]{1,0:T(8,128)(2,1)} %copy-done.2, bf16[128,512]{1,0:T(8,128)(2,1)} %copy-done.5, bf16[128,512]{1,0:T(8,128)(2,1)} %copy-done.4, bf16[128,512]{1,0:T(8,128)(2,1)} %copy-done.3, bf16[16,128,256]{2,1,0:T(8,128)(2,1)} %refs_4_.1, ...), custom_call_target="tpu_custom_call" | custom-call | flops 570425344 | bytes 3866752 | tf_op jit(solution)/shard_map/pallas_call | solution.py:95
  55.3 1.2 %slice_bitcast_fusion.2 = (f32[136,512]{1,0:T(8,128)S(1)}, f32[136,512]{1,0:T(8,128)S(1)}, f32[136,512]{1,0:T(8,128)S(1)}) fusion(f32[4,136,512]{2,1,0:T(8,128)} %shard_map.73), kind=kLoop, calls=%fused_computation.4 | loop fusion | bytes 1671168 | tf_op jit(solution)/shard_map/squeeze | solution.py:159
  56.5 1.9 %collective-permute-start.3 = (f32[136,512]{1,0:T(8,128)S(1)}, f32[136,512]{1,0:T(8,128)S(1)}, u32[]{:S(2)}, u32[]{:S(2)}) collective-permute-start(f32[136,512]{1,0:T(8,128)S(1)} %get-tuple-element.7), channel_id=1, source_target_pairs={{8,0},{16,8},{24,16},{32,24},{40,32},{48,40},{56,48},{64,56},{72,6... | collective-permute-start | bytes 835592 | tf_op jit(solution)/shard_map/ppermute | solution.py:22
  58.4 7.8 %collective-permute-start.5 = (f32[136,512]{1,0:T(8,128)S(1)}, f32[136,512]{1,0:T(8,128)S(1)}, u32[]{:S(2)}, u32[]{:S(2)}) collective-permute-start(f32[136,512]{1,0:T(8,128)S(1)} %get-tuple-element.8), channel_id=1, source_target_pairs={{24,0},{32,8},{40,16},{48,24},{56,32},{64,40},{72,48},{80,56},{88,... | collective-permute-start | bytes 835592 | tf_op jit(solution)/shard_map/ppermute | solution.py:22
  66.2 3.2 %collective-permute-start.4 = (f32[136,512]{1,0:T(8,128)S(1)}, f32[136,512]{1,0:T(8,128)S(1)}, u32[]{:S(2)}, u32[]{:S(2)}) collective-permute-start(f32[136,512]{1,0:T(8,128)S(1)} %get-tuple-element.9), channel_id=1, source_target_pairs={{16,0},{24,8},{32,16},{40,24},{48,32},{56,40},{64,48},{72,56},{80,... | collective-permute-start | bytes 835592 | tf_op jit(solution)/shard_map/ppermute | solution.py:22
  69.4 3.7 %collective-permute-done.3 = f32[136,512]{1,0:T(8,128)S(1)} collective-permute-done((f32[136,512]{1,0:T(8,128)S(1)}, f32[136,512]{1,0:T(8,128)S(1)}, u32[]{:S(2)}, u32[]{:S(2)}) %collective-permute-start.3) | collective-permute-done | bytes 278560 | tf_op jit(solution)/shard_map/ppermute | solution.py:22
  73.1 1.5 %collective-permute-done.5 = f32[136,512]{1,0:T(8,128)S(1)} collective-permute-done((f32[136,512]{1,0:T(8,128)S(1)}, f32[136,512]{1,0:T(8,128)S(1)}, u32[]{:S(2)}, u32[]{:S(2)}) %collective-permute-start.5) | collective-permute-done | bytes 278560 | tf_op jit(solution)/shard_map/ppermute | solution.py:22
  74.5 16.9 %collective-permute-done.4 = f32[136,512]{1,0:T(8,128)S(1)} collective-permute-done((f32[136,512]{1,0:T(8,128)S(1)}, f32[136,512]{1,0:T(8,128)S(1)}, u32[]{:S(2)}, u32[]{:S(2)}) %collective-permute-start.4) | collective-permute-done | bytes 278560 | tf_op jit(solution)/shard_map/ppermute | solution.py:22
  91.4 1.1 %fusion.2 = f32[136,512]{1,0:T(8,128)S(1)} fusion(f32[136,512]{1,0:T(8,128)S(1)} %collective-permute-done.5, f32[136,512]{1,0:T(8,128)S(1)} %collective-permute-done.4, f32[136,512]{1,0:T(8,128)S(1)} %collective-permute-done.3, f32[4,136,512]{2,1,0:T(8,128)} %shard_map.73), kind=kLoop, calls=%fused_computation.8 | loop fusion | flops 208896 | bytes 1392640 | tf_op jit(solution)/shard_map/add | solution.py:159
  92.5 0.1 copy.21
  92.6 0.2 div.11
  92.9 10.1 %all_to_all.34 = bf16[8,16,512]{2,1,0:T(8,128)(2,1)S(1)} all-to-all(bf16[8,16,512]{2,1,0:T(8,128)(2,1)S(1)} %bitcast.47), channel_id=1, replica_groups=mesh['pool'=64,'tensor'=8] {'tensor'}, dimensions={0} | all-to-all | bytes 262144 | tf_op jit(solution)/shard_map/all_to_all | solution.py:165
  103.0 0.7 copy.26
  (22 shorter events, 0.2 us)
Async XLA Ops:
  0.0 12.8 %copy-start = (s32[64,64]{1,0:T(8,128)S(1)}, s32[64,64]{1,0:T(8,128)}, u32[]{:S(2)}) copy-start(s32[64,64]{1,0:T(8,128)} %param.12) | copy-start | bytes 49156
  0.0 13.8 %copy-start.1 = (s32[64]{0:T(128)S(1)}, s32[64]{0:T(128)}, u32[]{:S(2)}) copy-start(s32[64]{0:T(128)} %param.13) | copy-start | bytes 772
  2.5 16.7 %all-to-all-start = ((bf16[16,8,1024]{2,0,1:T(8,128)(2,1)}), bf16[16,8,1024]{2,0,1:T(8,128)(2,1)S(1)}, u32[]{:S(2)}, u32[]{:S(2)}) async-start(bf16[16,8,1024]{2,0,1:T(8,128)(2,1)} %pad_maximum_fusion), calls=%async_computation | async-start | bytes 524288 | tf_op jit(solution)/shard_map/all_to_all | solution.py:126
  19.3 26.7 %copy-start.2 = (bf16[128,512]{1,0:T(8,128)(2,1)}, bf16[128,512]{1,0:T(8,128)(2,1)S(1)}, u32[]{:S(2)}) copy-start(bf16[128,512]{1,0:T(8,128)(2,1)S(1)} %slice.40.refs_0_) | copy-start | bytes 393220
  19.3 13.0 %collective-permute-start.2 = (bf16[128,512]{1,0:T(8,128)(2,1)S(1)}, bf16[128,512]{1,0:T(8,128)(2,1)S(1)}, u32[]{:S(2)}, u32[]{:S(2)}) collective-permute-start(bf16[128,512]{1,0:T(8,128)(2,1)S(1)} %slice.40.refs_0_), channel_id=1, source_target_pairs={{488,0},{496,8},{504,16},{0,24},{8,32},{16,40},{24,48},{32,56},{40... | collective-permute-start | bytes 393224 | tf_op jit(solution)/shard_map/ppermute | solution.py:22
  21.2 22.1 %collective-permute-start.1 = (bf16[128,512]{1,0:T(8,128)(2,1)S(1)}, bf16[128,512]{1,0:T(8,128)(2,1)S(1)}, u32[]{:S(2)}, u32[]{:S(2)}) collective-permute-start(bf16[128,512]{1,0:T(8,128)(2,1)S(1)} %slice.40.refs_0_), channel_id=1, source_target_pairs={{496,0},{504,8},{0,16},{8,24},{16,32},{24,40},{32,48},{40,56},{48,... | collective-permute-start | bytes 393224 | tf_op jit(solution)/shard_map/ppermute | solution.py:22
  27.3 18.7 %collective-permute-start = (bf16[128,512]{1,0:T(8,128)(2,1)S(1)}, bf16[128,512]{1,0:T(8,128)(2,1)S(1)}, u32[]{:S(2)}, u32[]{:S(2)}) collective-permute-start(bf16[128,512]{1,0:T(8,128)(2,1)S(1)} %slice.40.refs_0_), channel_id=1, source_target_pairs={{504,0},{0,8},{8,16},{16,24},{24,32},{32,40},{40,48},{48,56},{56,6... | collective-permute-start | bytes 393224 | tf_op jit(solution)/shard_map/ppermute | solution.py:22
  32.3 13.7 %copy-start.3 = (bf16[128,512]{1,0:T(8,128)(2,1)}, bf16[128,512]{1,0:T(8,128)(2,1)S(1)}, u32[]{:S(2)}) copy-start(bf16[128,512]{1,0:T(8,128)(2,1)S(1)} %collective-permute-done.2.refs_3_) | copy-start | bytes 393220
  43.3 2.7 %copy-start.4 = (bf16[128,512]{1,0:T(8,128)(2,1)}, bf16[128,512]{1,0:T(8,128)(2,1)S(1)}, u32[]{:S(2)}) copy-start(bf16[128,512]{1,0:T(8,128)(2,1)S(1)} %collective-permute-done.1.refs_2_) | copy-start | bytes 393220
  46.0 0.7 copy-start.5
  56.5 16.6 %collective-permute-start.3 = (f32[136,512]{1,0:T(8,128)S(1)}, f32[136,512]{1,0:T(8,128)S(1)}, u32[]{:S(2)}, u32[]{:S(2)}) collective-permute-start(f32[136,512]{1,0:T(8,128)S(1)} %get-tuple-element.7), channel_id=1, source_target_pairs={{8,0},{16,8},{24,16},{32,24},{40,32},{48,40},{56,48},{64,56},{72,6... | collective-permute-start | bytes 835592 | tf_op jit(solution)/shard_map/ppermute | solution.py:22
  58.4 16.1 %collective-permute-start.5 = (f32[136,512]{1,0:T(8,128)S(1)}, f32[136,512]{1,0:T(8,128)S(1)}, u32[]{:S(2)}, u32[]{:S(2)}) collective-permute-start(f32[136,512]{1,0:T(8,128)S(1)} %get-tuple-element.8), channel_id=1, source_target_pairs={{24,0},{32,8},{40,16},{48,24},{56,32},{64,40},{72,48},{80,56},{88,... | collective-permute-start | bytes 835592 | tf_op jit(solution)/shard_map/ppermute | solution.py:22
  66.2 25.2 %collective-permute-start.4 = (f32[136,512]{1,0:T(8,128)S(1)}, f32[136,512]{1,0:T(8,128)S(1)}, u32[]{:S(2)}, u32[]{:S(2)}) collective-permute-start(f32[136,512]{1,0:T(8,128)S(1)} %get-tuple-element.9), channel_id=1, source_target_pairs={{16,0},{24,8},{32,16},{40,24},{48,32},{56,40},{64,48},{72,56},{80,... | collective-permute-start | bytes 835592 | tf_op jit(solution)/shard_map/ppermute | solution.py:22

commit v2 on v1

--- a/solution.py
+++ b/solution.py
@@ -130,7 +130,9 @@
     k_new = mixed[:, q_width:q_width + kv_width]
     v_new = mixed[:, q_width + kv_width:]
 
-    received = [q_own] + [shifted(q_own, "pool", offset) for offset in range(1, SPAN)]
+    received = [q_own]
+    for offset in range(1, SPAN):
+        received.append(shifted(received[-1], "pool", 1))
 
     pool_size = lax.axis_size("pool")
     holder = lax.axis_index("pool")
@@ -151,12 +153,16 @@
     limit = jnp.clip(slot_len - page_index * page_len, 0, page_len)
     meta = jnp.stack([distance, limit]).astype(jnp.int32)
 
-    acc = attend(
-        list(range(SPAN)), meta, received, cached_key_pages, cached_value_pages, k_new, v_new
-    )
-    total = acc[0]
+    parts = [
+        attend([0], meta, received[:1], cached_key_pages, cached_value_pages, k_new, v_new)[0]
+    ]
     for offset in range(1, SPAN):
-        total = total + shifted(acc[offset], "pool", -offset)
+        parts.append(
+            attend([offset], meta, received[offset : offset + 1], cached_key_pages, cached_value_pages)[0]
+        )
+    total = parts[SPAN - 1]
+    for offset in range(SPAN - 2, -1, -1):
+        total = parts[offset] + shifted(total, "pool", -1)
     heads = q_width // HEAD_SIZE
     numerator = total[:rows].reshape(rows, heads, HEAD_SIZE)
     totals = total[rows, : heads * rows].reshape(heads, rows)

time: 105 us -> 99.6 us (0.949)
  waiting for transfers between devices: 40.6 us -> 30.4 us
  Pallas kernels: 8.68 us -> 14.6 us
  starting transfers between devices: 34.5 us -> 30.3 us
  blocking collectives: 10.1 us -> 13.9 us
  local copies, waits for them, and re-layouts: 6.52 us -> 4.5 us
  other arithmetic: 3.04 us -> 4.97 us
    ppermute x6, waiting for transfers between devices: 36.5 us -> 25.3 us  [shifted(): return lax.ppermute(block, axis, route)]
    pallas_call x1 -> x4, Pallas kernels: 8.68 us -> 14.6 us  [attend(): pl.pallas_call(functools.partial(_attend_kernel, tuple(ds), with_own), ou...]
    ppermute x6, starting transfers between devices: 24.4 us -> 20 us  [shifted(): return lax.ppermute(block, axis, route)]
    all_to_all x1, blocking collectives: 10.1 us -> 13.9 us  [on_device(): lax.all_to_all(attended, 'tensor', split_axis=0, concat_axis=1, tiled=True)]
    add x1 -> x3, other arithmetic: 1.05 us -> 3.01 us  [on_device(): total = parts[offset] + shifted(total, 'pool', -1)]
    squeeze x1 -> x0, local copies, waits for them, and re-layouts: 1.18 us -> none  [on_device(): total = total + shifted(acc[offset], 'pool', -offset)]
    all_to_all x1, waiting for transfers between devices: 4.06 us -> 5.17 us  [on_device(): lax.all_to_all(packed, 'tensor', split_axis=1, concat_axis=0, tiled=True)]
  transfers between devices with their start and end apart: 7 -> 7, of which waited for: 7 -> 6; matrix products, arithmetic and copies ran while one was open for 3% -> 3% of each run, Pallas kernels for 0% -> 12%
where the time goes in v2:
time: 99.6 us; the launch traced here: 98.9 us
  waiting for transfers between devices  30.4 us (31%)
  starting transfers between devices  30.3 us (30%)
  Pallas kernels  14.6 us (15%)
  blocking collectives  13.9 us (14%)
  other arithmetic  4.97 us (5%)
  local copies, waits for them, and re-layouts  4.5 us (5%)
    ppermute x6, waiting for transfers between devices, shifted(): return lax.ppermute(block, axis, route)  25.3 us
    ppermute x6, starting transfers between devices, shifted(): return lax.ppermute(block, axis, route)  20 us
    pallas_call x4, Pallas kernels, attend(): pl.pallas_call(functools.partial(_attend_kernel, tuple(ds), with_own), ou...  14.6 us
    all_to_all x1, blocking collectives, on_device(): lax.all_to_all(attended, 'tensor', split_axis=0, concat_axis=1, tiled=True)  13.9 us
    all_to_all x1, starting transfers between devices, on_device(): lax.all_to_all(packed, 'tensor', split_axis=1, concat_axis=0, tiled=True)  10.3 us
    all_to_all x1, waiting for transfers between devices, on_device(): lax.all_to_all(packed, 'tensor', split_axis=1, concat_axis=0, tiled=True)  5.17 us
    add x3, other arithmetic, on_device(): total = parts[offset] + shifted(total, 'pool', -1)  3.01 us
  transfers between devices with their start and end apart: 7, of which 6 were waited for; matrix products, arithmetic and copies ran while one was open for 3% of the time, Pallas kernels for 12%

profile of v2, /device:TPU:1, one launch (start us, length us, event | category | flops | bytes accessed | tf_op | source)
XLA Modules:
  0.0 98.9 jit_solution(6741435456295458713)
XLA Ops:
  0.0 1.0 copy.31
  1.0 0.7 pad_maximum_fusion
  1.7 10.3 %all-to-all-start = ((bf16[16,8,1024]{2,0,1:T(8,128)(2,1)}), bf16[16,8,1024]{2,0,1:T(8,128)(2,1)S(1)}, u32[]{:S(2)}, u32[]{:S(2)}) async-start(bf16[16,8,1024]{2,0,1:T(8,128)(2,1)} %pad_maximum_fusion), calls=%async_computation | async-start | bytes 524288 | tf_op jit(solution)/shard_map/all_to_all | solution.py:126
  12.1 0.6 gather_fusion.1
  12.8 0.6 gather_fusion
  13.4 5.2 %all-to-all-done = bf16[16,8,1024]{2,0,1:T(8,128)(2,1)S(1)} async-done(((bf16[16,8,1024]{2,0,1:T(8,128)(2,1)}), bf16[16,8,1024]{2,0,1:T(8,128)(2,1)S(1)}, u32[]{:S(2)}, u32[]{:S(2)}) %all-to-all-start) | async-done | bytes 262176 | tf_op jit(solution)/shard_map/all_to_all | solution.py:126
  18.6 1.9 %collective-permute-start = (bf16[128,512]{1,0:T(8,128)(2,1)S(1)}, bf16[128,512]{1,0:T(8,128)(2,1)S(1)}, u32[]{:S(2)}, u32[]{:S(2)}) collective-permute-start(bf16[128,512]{1,0:T(8,128)(2,1)S(1)} %slice.24.refs_0_), channel_id=1, source_target_pairs={{504,0},{0,8},{8,16},{16,24},{24,32},{32,40},{40,48},{48,56},{56,6... | collective-permute-start | bytes 393224 | tf_op jit(solution)/shard_map/ppermute | solution.py:22
  20.5 0.2 compare_reduce_fusion
  20.7 9.8 %collective-permute-done.refs_0_ = bf16[128,512]{1,0:T(8,128)(2,1)S(1)} collective-permute-done((bf16[128,512]{1,0:T(8,128)(2,1)S(1)}, bf16[128,512]{1,0:T(8,128)(2,1)S(1)}, u32[]{:S(2)}, u32[]{:S(2)}) %collective-permute-start) | collective-permute-done | bytes 131104 | tf_op jit(solution)/shard_map/ppermute | solution.py:22
  30.6 1.9 %collective-permute-start.1 = (bf16[128,512]{1,0:T(8,128)(2,1)S(1)}, bf16[128,512]{1,0:T(8,128)(2,1)S(1)}, u32[]{:S(2)}, u32[]{:S(2)}) collective-permute-start(bf16[128,512]{1,0:T(8,128)(2,1)S(1)} %collective-permute-done.refs_0_), channel_id=1, source_target_pairs={{504,0},{0,8},{8,16},{16,24},{24,32},{32,40},{40,48},{48,56},{56,6... | collective-permute-start | bytes 393224 | tf_op jit(solution)/shard_map/ppermute | solution.py:22
  32.6 0.2 fusion.1
  32.8 6.8 %collective-permute-done.1.refs_0_ = bf16[128,512]{1,0:T(8,128)(2,1)S(1)} collective-permute-done((bf16[128,512]{1,0:T(8,128)(2,1)S(1)}, bf16[128,512]{1,0:T(8,128)(2,1)S(1)}, u32[]{:S(2)}, u32[]{:S(2)}) %collective-permute-start.1) | collective-permute-done | bytes 131104 | tf_op jit(solution)/shard_map/ppermute | solution.py:22
  39.6 1.9 %collective-permute-start.2 = (bf16[128,512]{1,0:T(8,128)(2,1)S(1)}, bf16[128,512]{1,0:T(8,128)(2,1)S(1)}, u32[]{:S(2)}, u32[]{:S(2)}) collective-permute-start(bf16[128,512]{1,0:T(8,128)(2,1)S(1)} %collective-permute-done.1.refs_0_), channel_id=1, source_target_pairs={{504,0},{0,8},{8,16},{16,24},{24,32},{32,40},{40,48},{48,56},{56,6... | collective-permute-start | bytes 393224 | tf_op jit(solution)/shard_map/ppermute | solution.py:22
  41.5 0.6 pad_add_fusion.meta_ref
  42.1 6.5 %collective-permute-done.2.refs_0_ = bf16[128,512]{1,0:T(8,128)(2,1)S(1)} collective-permute-done((bf16[128,512]{1,0:T(8,128)(2,1)S(1)}, bf16[128,512]{1,0:T(8,128)(2,1)S(1)}, u32[]{:S(2)}, u32[]{:S(2)}) %collective-permute-start.2) | collective-permute-done | bytes 131104 | tf_op jit(solution)/shard_map/ppermute | solution.py:22
  48.6 0.7 copy-done.5
  49.3 2.9 %shard_map.76 = f32[1,136,512]{2,1,0:T(8,128)} custom-call(s32[2,16]{1,0:T(2,128)} %pad_add_fusion.meta_ref, bf16[128,512]{1,0:T(8,128)(2,1)} %copy-done.5, bf16[16,128,256]{2,1,0:T(8,128)(2,1)} %refs_1_.7, bf16[16,128,256]{2,1,0:T(8,128)(2,1)} %refs_2_.7), custom_call_target="tpu_custom_call" | custom-call | flops 536870912 | bytes 2506880 | tf_op jit(solution)/shard_map/pallas_call | solution.py:95
  52.2 1.9 %collective-permute-start.3 = (f32[136,512]{1,0:T(8,128)}, f32[136,512]{1,0:T(8,128)S(1)}, u32[]{:S(2)}, u32[]{:S(2)}) collective-permute-start(f32[136,512]{1,0:T(8,128)} %bitcast.43), channel_id=1, source_target_pairs={{8,0},{16,8},{24,16},{32,24},{40,32},{48,40},{56,48},{64,56},{72,6... | collective-permute-start | bytes 835592 | tf_op jit(solution)/shard_map/ppermute | solution.py:22
  54.1 3.7 %shard_map.75 = f32[1,136,512]{2,1,0:T(8,128)} custom-call(s32[2,16]{1,0:T(2,128)} %pad_add_fusion.meta_ref, bf16[128,512]{1,0:T(8,128)(2,1)} %copy-done.4, bf16[16,128,256]{2,1,0:T(8,128)(2,1)} %refs_1_.7, bf16[16,128,256]{2,1,0:T(8,128)(2,1)} %refs_2_.7), custom_call_target="tpu_custom_call" | custom-call | flops 536870912 | bytes 2506880 | tf_op jit(solution)/shard_map/pallas_call | solution.py:95
  57.8 1.9 %collective-permute-done.3 = f32[136,512]{1,0:T(8,128)S(1)} collective-permute-done((f32[136,512]{1,0:T(8,128)}, f32[136,512]{1,0:T(8,128)S(1)}, u32[]{:S(2)}, u32[]{:S(2)}) %collective-permute-start.3) | collective-permute-done | bytes 278560 | tf_op jit(solution)/shard_map/ppermute | solution.py:22
  59.7 1.0 %bitcast_add_fusion = f32[136,512]{1,0:T(8,128)S(1)} fusion(f32[136,512]{1,0:T(8,128)S(1)} %collective-permute-done.3, f32[1,136,512]{2,1,0:T(8,128)} %shard_map.75), kind=kLoop, calls=%fused_computation.2 | loop fusion | flops 69632 | bytes 835584 | tf_op jit(solution)/shard_map/add | solution.py:165
  60.7 5.2 %collective-permute-start.4 = (f32[136,512]{1,0:T(8,128)S(1)}, f32[136,512]{1,0:T(8,128)S(1)}, u32[]{:S(2)}, u32[]{:S(2)}) collective-permute-start(f32[136,512]{1,0:T(8,128)S(1)} %bitcast_add_fusion), channel_id=1, source_target_pairs={{8,0},{16,8},{24,16},{32,24},{40,32},{48,40},{56,48},{64,56},{72,6... | collective-permute-start | bytes 835592 | tf_op jit(solution)/shard_map/ppermute | solution.py:22
  66.0 3.3 %shard_map.74 = f32[1,136,512]{2,1,0:T(8,128)} custom-call(s32[2,16]{1,0:T(2,128)} %pad_add_fusion.meta_ref, bf16[128,512]{1,0:T(8,128)(2,1)} %copy-done.3, bf16[16,128,256]{2,1,0:T(8,128)(2,1)} %refs_1_.7, bf16[16,128,256]{2,1,0:T(8,128)(2,1)} %refs_2_.7), custom_call_target="tpu_custom_call" | custom-call | flops 536870912 | bytes 2506880 | tf_op jit(solution)/shard_map/pallas_call | solution.py:95
  69.2 0.2 collective-permute-done.4
  69.4 1.0 %bitcast_add_fusion.1 = f32[136,512]{1,0:T(8,128)S(1)} fusion(f32[136,512]{1,0:T(8,128)S(1)} %collective-permute-done.4, f32[1,136,512]{2,1,0:T(8,128)} %shard_map.74), kind=kLoop, calls=%fused_computation.3 | loop fusion | flops 69632 | bytes 835584 | tf_op jit(solution)/shard_map/add | solution.py:165
  70.4 7.1 %collective-permute-start.5 = (f32[136,512]{1,0:T(8,128)S(1)}, f32[136,512]{1,0:T(8,128)S(1)}, u32[]{:S(2)}, u32[]{:S(2)}) collective-permute-start(f32[136,512]{1,0:T(8,128)S(1)} %bitcast_add_fusion.1), channel_id=1, source_target_pairs={{8,0},{16,8},{24,16},{32,24},{40,32},{48,40},{56,48},{64,56},{72,6... | collective-permute-start | bytes 835592 | tf_op jit(solution)/shard_map/ppermute | solution.py:22
  77.6 0.7 fusion.5
  78.2 4.7 %shard_map.73 = f32[1,136,512]{2,1,0:T(8,128)} custom-call(s32[2,16]{1,0:T(2,128)} %pad_add_fusion.meta_ref, bf16[128,512]{1,0:T(8,128)(2,1)} %copy-done.2, bf16[16,128,256]{2,1,0:T(8,128)(2,1)} %refs_1_.7, bf16[16,128,256]{2,1,0:T(8,128)(2,1)} %refs_2_.7, bf16[128,256]{1,0:T(8,128)(2,1)} %get-tuple-element.8.refs_3_, bf16[128,256]{1,0:T(8,128)(2,1)} %get-tuple-element.7.refs_4_), custom_call_target="tpu_custom_call" | custom-call | flops 570425344 | bytes 2637952 | tf_op jit(solution)/shard_map/pallas_call | solution.py:95
  83.0 1.0 %bitcast_add_fusion.2 = f32[136,512]{1,0:T(8,128)S(1)} fusion(f32[136,512]{1,0:T(8,128)S(1)} %collective-permute-done.5, f32[1,136,512]{2,1,0:T(8,128)} %shard_map.73), kind=kLoop, calls=%fused_computation.4 | loop fusion | flops 69632 | bytes 835584 | tf_op jit(solution)/shard_map/add | solution.py:165
  84.1 0.2 div.11
  84.4 13.9 %all_to_all.34 = bf16[8,16,512]{2,1,0:T(8,128)(2,1)S(1)} all-to-all(bf16[8,16,512]{2,1,0:T(8,128)(2,1)S(1)} %bitcast.40), channel_id=1, replica_groups=mesh['pool'=64,'tensor'=8] {'tensor'}, dimensions={0} | all-to-all | bytes 262144 | tf_op jit(solution)/shard_map/all_to_all | solution.py:171
  98.3 0.7 copy.26
  (30 shorter events, 0.5 us)
Async XLA Ops:
  0.0 12.8 %copy-start = (s32[64,64]{1,0:T(8,128)S(1)}, s32[64,64]{1,0:T(8,128)}, u32[]{:S(2)}) copy-start(s32[64,64]{1,0:T(8,128)} %param.12) | copy-start | bytes 49156
  0.0 1.0 copy-start.6
  0.0 1.0 copy-start.7
  1.7 10.3 %copy-start.1 = (s32[64]{0:T(128)S(1)}, s32[64]{0:T(128)}, u32[]{:S(2)}) copy-start(s32[64]{0:T(128)} %param.13) | copy-start | bytes 772
  1.7 16.8 %all-to-all-start = ((bf16[16,8,1024]{2,0,1:T(8,128)(2,1)}), bf16[16,8,1024]{2,0,1:T(8,128)(2,1)S(1)}, u32[]{:S(2)}, u32[]{:S(2)}) async-start(bf16[16,8,1024]{2,0,1:T(8,128)(2,1)} %pad_maximum_fusion), calls=%async_computation | async-start | bytes 524288 | tf_op jit(solution)/shard_map/all_to_all | solution.py:126
  18.6 33.6 %copy-start.2 = (bf16[128,512]{1,0:T(8,128)(2,1)}, bf16[128,512]{1,0:T(8,128)(2,1)S(1)}, u32[]{:S(2)}) copy-start(bf16[128,512]{1,0:T(8,128)(2,1)S(1)} %slice.24.refs_0_) | copy-start | bytes 393220
  18.6 12.0 %collective-permute-start = (bf16[128,512]{1,0:T(8,128)(2,1)S(1)}, bf16[128,512]{1,0:T(8,128)(2,1)S(1)}, u32[]{:S(2)}, u32[]{:S(2)}) collective-permute-start(bf16[128,512]{1,0:T(8,128)(2,1)S(1)} %slice.24.refs_0_), channel_id=1, source_target_pairs={{504,0},{0,8},{8,16},{16,24},{24,32},{32,40},{40,48},{48,56},{56,6... | collective-permute-start | bytes 393224 | tf_op jit(solution)/shard_map/ppermute | solution.py:22
  30.6 21.6 %copy-start.3 = (bf16[128,512]{1,0:T(8,128)(2,1)}, bf16[128,512]{1,0:T(8,128)(2,1)S(1)}, u32[]{:S(2)}) copy-start(bf16[128,512]{1,0:T(8,128)(2,1)S(1)} %collective-permute-done.refs_0_) | copy-start | bytes 393220
  30.6 9.0 %collective-permute-start.1 = (bf16[128,512]{1,0:T(8,128)(2,1)S(1)}, bf16[128,512]{1,0:T(8,128)(2,1)S(1)}, u32[]{:S(2)}, u32[]{:S(2)}) collective-permute-start(bf16[128,512]{1,0:T(8,128)(2,1)S(1)} %collective-permute-done.refs_0_), channel_id=1, source_target_pairs={{504,0},{0,8},{8,16},{16,24},{24,32},{32,40},{40,48},{48,56},{56,6... | collective-permute-start | bytes 393224 | tf_op jit(solution)/shard_map/ppermute | solution.py:22
  39.6 12.6 %copy-start.4 = (bf16[128,512]{1,0:T(8,128)(2,1)}, bf16[128,512]{1,0:T(8,128)(2,1)S(1)}, u32[]{:S(2)}) copy-start(bf16[128,512]{1,0:T(8,128)(2,1)S(1)} %collective-permute-done.1.refs_0_) | copy-start | bytes 393220
  39.6 9.0 %collective-permute-start.2 = (bf16[128,512]{1,0:T(8,128)(2,1)S(1)}, bf16[128,512]{1,0:T(8,128)(2,1)S(1)}, u32[]{:S(2)}, u32[]{:S(2)}) collective-permute-start(bf16[128,512]{1,0:T(8,128)(2,1)S(1)} %collective-permute-done.1.refs_0_), channel_id=1, source_target_pairs={{504,0},{0,8},{8,16},{16,24},{24,32},{32,40},{40,48},{48,56},{56,6... | collective-permute-start | bytes 393224 | tf_op jit(solution)/shard_map/ppermute | solution.py:22
  48.6 0.7 copy-start.5
  52.2 7.5 %collective-permute-start.3 = (f32[136,512]{1,0:T(8,128)}, f32[136,512]{1,0:T(8,128)S(1)}, u32[]{:S(2)}, u32[]{:S(2)}) collective-permute-start(f32[136,512]{1,0:T(8,128)} %bitcast.43), channel_id=1, source_target_pairs={{8,0},{16,8},{24,16},{32,24},{40,32},{48,40},{56,48},{64,56},{72,6... | collective-permute-start | bytes 835592 | tf_op jit(solution)/shard_map/ppermute | solution.py:22
  60.7 8.7 %collective-permute-start.4 = (f32[136,512]{1,0:T(8,128)S(1)}, f32[136,512]{1,0:T(8,128)S(1)}, u32[]{:S(2)}, u32[]{:S(2)}) collective-permute-start(f32[136,512]{1,0:T(8,128)S(1)} %bitcast_add_fusion), channel_id=1, source_target_pairs={{8,0},{16,8},{24,16},{32,24},{40,32},{48,40},{56,48},{64,56},{72,6... | collective-permute-start | bytes 835592 | tf_op jit(solution)/shard_map/ppermute | solution.py:22
  70.4 12.5 %collective-permute-start.5 = (f32[136,512]{1,0:T(8,128)S(1)}, f32[136,512]{1,0:T(8,128)S(1)}, u32[]{:S(2)}, u32[]{:S(2)}) collective-permute-start(f32[136,512]{1,0:T(8,128)S(1)} %bitcast_add_fusion.1), channel_id=1, source_target_pairs={{8,0},{16,8},{24,16},{32,24},{40,32},{48,40},{56,48},{64,56},{72,6... | collective-permute-start | bytes 835592 | tf_op jit(solution)/shard_map/ppermute | solution.py:22

commit v3 on v2

--- a/solution.py
+++ b/solution.py
@@ -130,10 +130,6 @@
     k_new = mixed[:, q_width:q_width + kv_width]
     v_new = mixed[:, q_width + kv_width:]
 
-    received = [q_own]
-    for offset in range(1, SPAN):
-        received.append(shifted(received[-1], "pool", 1))
-
     pool_size = lax.axis_size("pool")
     holder = lax.axis_index("pool")
     slots_dev = cached_key_pages.shape[0]
@@ -153,13 +149,14 @@
     limit = jnp.clip(slot_len - page_index * page_len, 0, page_len)
     meta = jnp.stack([distance, limit]).astype(jnp.int32)
 
-    parts = [
-        attend([0], meta, received[:1], cached_key_pages, cached_value_pages, k_new, v_new)[0]
-    ]
-    for offset in range(1, SPAN):
-        parts.append(
-            attend([offset], meta, received[offset : offset + 1], cached_key_pages, cached_value_pages)[0]
-        )
+    held = q_own
+    parts = []
+    for offset in range(SPAN):
+        own = (k_new, v_new) if offset == 0 else ()
+        part = attend([offset], meta, [held], cached_key_pages, cached_value_pages, *own)[0]
+        if offset < SPAN - 1:
+            held, part = lax.optimization_barrier((shifted(held, "pool", 1), part))
+        parts.append(part)
     total = parts[SPAN - 1]
     for offset in range(SPAN - 2, -1, -1):
         total = parts[offset] + shifted(total, "pool", -1)

time: 99.6 us -> 96.5 us (0.969)
  other arithmetic: 4.97 us -> 2.14 us
  waiting for transfers between devices: 30.4 us -> 28.3 us
  Pallas kernels: 14.6 us -> 16.5 us
  starting transfers between devices: 30.3 us -> 31.5 us
  blocking collectives: 13.9 us -> 12.8 us
    add x3, other arithmetic: 3.01 us -> 0.12 us  [on_device(): total = parts[offset] + shifted(total, 'pool', -1)]
    pallas_call x4, Pallas kernels: 14.6 us -> 16.5 us  [attend(): pl.pallas_call(functools.partial(_attend_kernel, tuple(ds), with_own), ou...]
    ppermute x6, starting transfers between devices: 20 us -> 21.3 us  [shifted(): return lax.ppermute(block, axis, route)]
    all_to_all x1, waiting for transfers between devices: 5.17 us -> 4.04 us  [on_device(): lax.all_to_all(packed, 'tensor', split_axis=1, concat_axis=0, tiled=True)]
    all_to_all x1, blocking collectives: 13.9 us -> 12.8 us  [on_device(): lax.all_to_all(attended, 'tensor', split_axis=0, concat_axis=1, tiled=True)]
    ppermute x6, waiting for transfers between devices: 25.3 us -> 24.2 us  [shifted(): return lax.ppermute(block, axis, route)]
  transfers between devices with their start and end apart: 7 -> 7, of which waited for: 6 -> 7; matrix products, arithmetic and copies ran while one was open for 3% -> 3% of each run, Pallas kernels for 12% -> 14%
where the time goes in v3:
time: 96.5 us; the launch traced here: 96 us
  starting transfers between devices  31.5 us (33%)
  waiting for transfers between devices  28.3 us (29%)
  Pallas kernels  16.5 us (17%)
  blocking collectives  12.8 us (13%)
  local copies, waits for them, and re-layouts  4.52 us (5%)
  other arithmetic  2.14 us (2%)
    ppermute x6, waiting for transfers between devices, shifted(): return lax.ppermute(block, axis, route)  24.2 us
    ppermute x6, starting transfers between devices, shifted(): return lax.ppermute(block, axis, route)  21.3 us
    pallas_call x4, Pallas kernels, attend(): pl.pallas_call(functools.partial(_attend_kernel, tuple(ds), with_own), ou...  16.5 us
    all_to_all x1, blocking collectives, on_device(): lax.all_to_all(attended, 'tensor', split_axis=0, concat_axis=1, tiled=True)  12.8 us
    all_to_all x1, starting transfers between devices, on_device(): lax.all_to_all(packed, 'tensor', split_axis=1, concat_axis=0, tiled=True)  10.2 us
    all_to_all x1, waiting for transfers between devices, on_device(): lax.all_to_all(packed, 'tensor', split_axis=1, concat_axis=0, tiled=True)  4.04 us
  transfers between devices with their start and end apart: 7, of which 7 were waited for; matrix products, arithmetic and copies ran while one was open for 3% of the time, Pallas kernels for 14%

profile of v3, /device:TPU:1, one launch (start us, length us, event | category | flops | bytes accessed | tf_op | source)
XLA Modules:
  0.0 96.0 jit_solution(11865508894295956064)
XLA Ops:
  0.0 1.0 copy.31
  1.0 0.7 pad_maximum_fusion
  1.7 10.2 %all-to-all-start = ((bf16[16,8,1024]{2,0,1:T(8,128)(2,1)}), bf16[16,8,1024]{2,0,1:T(8,128)(2,1)S(1)}, u32[]{:S(2)}, u32[]{:S(2)}) async-start(bf16[16,8,1024]{2,0,1:T(8,128)(2,1)} %pad_maximum_fusion), calls=%async_computation | async-start | bytes 524288 | tf_op jit(solution)/shard_map/all_to_all | solution.py:126
  12.0 0.6 gather_fusion
  12.6 0.2 fusion.1
  12.8 0.2 compare_reduce_fusion
  13.1 0.6 gather_fusion.1
  13.7 0.1 select_reduce_fusion.1
  13.8 0.6 pad_add_fusion.meta_ref
  14.4 4.0 %all-to-all-done = bf16[16,8,1024]{2,0,1:T(8,128)(2,1)S(1)} async-done(((bf16[16,8,1024]{2,0,1:T(8,128)(2,1)}), bf16[16,8,1024]{2,0,1:T(8,128)(2,1)S(1)}, u32[]{:S(2)}, u32[]{:S(2)}) %all-to-all-start) | async-done | bytes 262176 | tf_op jit(solution)/shard_map/all_to_all | solution.py:126
  18.5 1.9 %collective-permute-start = (bf16[128,512]{1,0:T(8,128)(2,1)S(1)}, bf16[128,512]{1,0:T(8,128)(2,1)S(1)}, u32[]{:S(2)}, u32[]{:S(2)}) collective-permute-start(bf16[128,512]{1,0:T(8,128)(2,1)S(1)} %slice.24.refs_0_), channel_id=1, source_target_pairs={{504,0},{0,8},{8,16},{16,24},{24,32},{32,40},{40,48},{48,56},{56,6... | collective-permute-start | bytes 393224 | tf_op jit(solution)/shard_map/ppermute | solution.py:22
  20.4 0.7 fusion.5
  21.1 2.9 %shard_map.73 = f32[1,136,512]{2,1,0:T(8,128)} custom-call(s32[2,16]{1,0:T(2,128)} %pad_add_fusion.meta_ref, bf16[128,512]{1,0:T(8,128)(2,1)} %copy-done.5, bf16[16,128,256]{2,1,0:T(8,128)(2,1)} %refs_1_.7, bf16[16,128,256]{2,1,0:T(8,128)(2,1)} %refs_2_.7, bf16[128,256]{1,0:T(8,128)(2,1)} %get-tuple-element.20.refs_3_, ...), custom_call_target="tpu_custom_call" | custom-call | flops 570425344 | bytes 2637952 | tf_op jit(solution)/shard_map/pallas_call | solution.py:95
  24.0 6.4 %collective-permute-done.refs_0_ = bf16[128,512]{1,0:T(8,128)(2,1)S(1)} collective-permute-done((bf16[128,512]{1,0:T(8,128)(2,1)S(1)}, bf16[128,512]{1,0:T(8,128)(2,1)S(1)}, u32[]{:S(2)}, u32[]{:S(2)}) %collective-permute-start) | collective-permute-done | bytes 131104 | tf_op jit(solution)/shard_map/ppermute | solution.py:22
  30.4 1.9 %collective-permute-start.1 = (bf16[128,512]{1,0:T(8,128)(2,1)S(1)}, bf16[128,512]{1,0:T(8,128)(2,1)S(1)}, u32[]{:S(2)}, u32[]{:S(2)}) collective-permute-start(bf16[128,512]{1,0:T(8,128)(2,1)S(1)} %collective-permute-done.refs_0_), channel_id=1, source_target_pairs={{504,0},{0,8},{8,16},{16,24},{24,32},{32,40},{40,48},{48,56},{56,6... | collective-permute-start | bytes 393224 | tf_op jit(solution)/shard_map/ppermute | solution.py:22
  32.4 8.3 %shard_map.74 = f32[1,136,512]{2,1,0:T(8,128)} custom-call(s32[2,16]{1,0:T(2,128)} %pad_add_fusion.meta_ref, bf16[128,512]{1,0:T(8,128)(2,1)} %copy-done.6, bf16[16,128,256]{2,1,0:T(8,128)(2,1)} %refs_1_.7, bf16[16,128,256]{2,1,0:T(8,128)(2,1)} %refs_2_.7), custom_call_target="tpu_custom_call" | custom-call | flops 536870912 | bytes 2506880 | tf_op jit(solution)/shard_map/pallas_call | solution.py:95
  40.7 1.0 %collective-permute-done.1.refs_0_ = bf16[128,512]{1,0:T(8,128)(2,1)S(1)} collective-permute-done((bf16[128,512]{1,0:T(8,128)(2,1)S(1)}, bf16[128,512]{1,0:T(8,128)(2,1)S(1)}, u32[]{:S(2)}, u32[]{:S(2)}) %collective-permute-start.1) | collective-permute-done | bytes 131104 | tf_op jit(solution)/shard_map/ppermute | solution.py:22
  41.7 1.9 %collective-permute-start.2 = (bf16[128,512]{1,0:T(8,128)(2,1)S(1)}, bf16[128,512]{1,0:T(8,128)(2,1)S(1)}, u32[]{:S(2)}, u32[]{:S(2)}) collective-permute-start(bf16[128,512]{1,0:T(8,128)(2,1)S(1)} %collective-permute-done.1.refs_0_), channel_id=1, source_target_pairs={{504,0},{0,8},{8,16},{16,24},{24,32},{32,40},{40,48},{48,56},{56,6... | collective-permute-start | bytes 393224 | tf_op jit(solution)/shard_map/ppermute | solution.py:22
  43.6 2.6 %shard_map.75 = f32[1,136,512]{2,1,0:T(8,128)} custom-call(s32[2,16]{1,0:T(2,128)} %pad_add_fusion.meta_ref, bf16[128,512]{1,0:T(8,128)(2,1)} %copy-done.7, bf16[16,128,256]{2,1,0:T(8,128)(2,1)} %refs_1_.7, bf16[16,128,256]{2,1,0:T(8,128)(2,1)} %refs_2_.7), custom_call_target="tpu_custom_call" | custom-call | flops 536870912 | bytes 2506880 | tf_op jit(solution)/shard_map/pallas_call | solution.py:95
  46.2 4.5 %collective-permute-done.2.refs_0_ = bf16[128,512]{1,0:T(8,128)(2,1)S(1)} collective-permute-done((bf16[128,512]{1,0:T(8,128)(2,1)S(1)}, bf16[128,512]{1,0:T(8,128)(2,1)S(1)}, u32[]{:S(2)}, u32[]{:S(2)}) %collective-permute-start.2) | collective-permute-done | bytes 131104 | tf_op jit(solution)/shard_map/ppermute | solution.py:22
  50.7 0.7 copy-done.8
  51.4 2.6 %shard_map.76 = f32[1,136,512]{2,1,0:T(8,128)} custom-call(s32[2,16]{1,0:T(2,128)} %pad_add_fusion.meta_ref, bf16[128,512]{1,0:T(8,128)(2,1)} %copy-done.8, bf16[16,128,256]{2,1,0:T(8,128)(2,1)} %refs_1_.7, bf16[16,128,256]{2,1,0:T(8,128)(2,1)} %refs_2_.7), custom_call_target="tpu_custom_call" | custom-call | flops 536870912 | bytes 2506880 | tf_op jit(solution)/shard_map/pallas_call | solution.py:95
  54.1 2.3 %collective-permute-start.3 = (f32[136,512]{1,0:T(8,128)}, f32[136,512]{1,0:T(8,128)S(1)}, u32[]{:S(2)}, u32[]{:S(2)}) collective-permute-start(f32[136,512]{1,0:T(8,128)} %bitcast.43), channel_id=1, source_target_pairs={{8,0},{16,8},{24,16},{32,24},{40,32},{48,40},{56,48},{64,56},{72,6... | collective-permute-start | bytes 835592 | tf_op jit(solution)/shard_map/ppermute | solution.py:22
  56.4 5.3 %collective-permute-done.3 = f32[136,512]{1,0:T(8,128)S(1)} collective-permute-done((f32[136,512]{1,0:T(8,128)}, f32[136,512]{1,0:T(8,128)S(1)}, u32[]{:S(2)}, u32[]{:S(2)}) %collective-permute-start.3) | collective-permute-done | bytes 278560 | tf_op jit(solution)/shard_map/ppermute | solution.py:22
  61.7 6.1 %collective-permute-start.4 = (f32[136,512]{1,0:T(8,128)S(1)}, f32[136,512]{1,0:T(8,128)S(1)}, u32[]{:S(2)}, u32[]{:S(2)}) collective-permute-start(f32[136,512]{1,0:T(8,128)S(1)} %add.65), channel_id=1, source_target_pairs={{8,0},{16,8},{24,16},{32,24},{40,32},{48,40},{56,48},{64,56},{72,6... | collective-permute-start | bytes 835592 | tf_op jit(solution)/shard_map/ppermute | solution.py:22
  67.9 3.5 %collective-permute-done.4 = f32[136,512]{1,0:T(8,128)S(1)} collective-permute-done((f32[136,512]{1,0:T(8,128)S(1)}, f32[136,512]{1,0:T(8,128)S(1)}, u32[]{:S(2)}, u32[]{:S(2)}) %collective-permute-start.4) | collective-permute-done | bytes 278560 | tf_op jit(solution)/shard_map/ppermute | solution.py:22
  71.4 7.1 %collective-permute-start.5 = (f32[136,512]{1,0:T(8,128)S(1)}, f32[136,512]{1,0:T(8,128)S(1)}, u32[]{:S(2)}, u32[]{:S(2)}) collective-permute-start(f32[136,512]{1,0:T(8,128)S(1)} %add.66), channel_id=1, source_target_pairs={{8,0},{16,8},{24,16},{32,24},{40,32},{48,40},{56,48},{64,56},{72,6... | collective-permute-start | bytes 835592 | tf_op jit(solution)/shard_map/ppermute | solution.py:22
  78.5 3.5 %collective-permute-done.5 = f32[136,512]{1,0:T(8,128)S(1)} collective-permute-done((f32[136,512]{1,0:T(8,128)S(1)}, f32[136,512]{1,0:T(8,128)S(1)}, u32[]{:S(2)}, u32[]{:S(2)}) %collective-permute-start.5) | collective-permute-done | bytes 278560 | tf_op jit(solution)/shard_map/ppermute | solution.py:22
  82.1 0.1 copy.21
  82.2 0.2 div.11
  82.5 12.8 %all_to_all.34 = bf16[8,16,512]{2,1,0:T(8,128)(2,1)S(1)} all-to-all(bf16[8,16,512]{2,1,0:T(8,128)(2,1)S(1)} %bitcast.40), channel_id=1, replica_groups=mesh['pool'=64,'tensor'=8] {'tensor'}, dimensions={0} | all-to-all | bytes 262144 | tf_op jit(solution)/shard_map/all_to_all | solution.py:168
  95.3 0.7 copy.26
  (36 shorter events, 0.4 us)
Async XLA Ops:
  0.0 12.0 %copy-start = (s32[64,64]{1,0:T(8,128)S(1)}, s32[64,64]{1,0:T(8,128)}, u32[]{:S(2)}) copy-start(s32[64,64]{1,0:T(8,128)} %param.12) | copy-start | bytes 49156
  0.0 1.0 %copy-start.9 = (bf16[16,2048]{1,0:T(8,128)(2,1)S(1)}, bf16[16,2048]{1,0:T(8,128)(2,1)}, u32[]{:S(2)}) copy-start(bf16[16,2048]{1,0:T(8,128)(2,1)} %param.9) | copy-start | bytes 196612
  0.0 1.0 %copy-start.10 = (bf16[16,2048]{1,0:T(8,128)(2,1)S(1)}, bf16[16,2048]{1,0:T(8,128)(2,1)}, u32[]{:S(2)}) copy-start(bf16[16,2048]{1,0:T(8,128)(2,1)} %param.8) | copy-start | bytes 196612
  1.7 16.7 %all-to-all-start = ((bf16[16,8,1024]{2,0,1:T(8,128)(2,1)}), bf16[16,8,1024]{2,0,1:T(8,128)(2,1)S(1)}, u32[]{:S(2)}, u32[]{:S(2)}) async-start(bf16[16,8,1024]{2,0,1:T(8,128)(2,1)} %pad_maximum_fusion), calls=%async_computation | async-start | bytes 524288 | tf_op jit(solution)/shard_map/all_to_all | solution.py:126
  12.0 1.0 %copy-start.1 = (s32[64]{0:T(128)S(1)}, s32[64]{0:T(128)}, u32[]{:S(2)}) copy-start(s32[64]{0:T(128)} %param.13) | copy-start | bytes 772
  18.5 2.6 %copy-start.5 = (bf16[128,512]{1,0:T(8,128)(2,1)}, bf16[128,512]{1,0:T(8,128)(2,1)S(1)}, u32[]{:S(2)}) copy-start(bf16[128,512]{1,0:T(8,128)(2,1)S(1)} %slice.24.refs_0_) | copy-start | bytes 393220
  18.5 12.0 %collective-permute-start = (bf16[128,512]{1,0:T(8,128)(2,1)S(1)}, bf16[128,512]{1,0:T(8,128)(2,1)S(1)}, u32[]{:S(2)}, u32[]{:S(2)}) collective-permute-start(bf16[128,512]{1,0:T(8,128)(2,1)S(1)} %slice.24.refs_0_), channel_id=1, source_target_pairs={{504,0},{0,8},{8,16},{16,24},{24,32},{32,40},{40,48},{48,56},{56,6... | collective-permute-start | bytes 393224 | tf_op jit(solution)/shard_map/ppermute | solution.py:22
  30.4 1.9 %copy-start.6 = (bf16[128,512]{1,0:T(8,128)(2,1)}, bf16[128,512]{1,0:T(8,128)(2,1)S(1)}, u32[]{:S(2)}) copy-start(bf16[128,512]{1,0:T(8,128)(2,1)S(1)} %collective-permute-done.refs_0_) | copy-start | bytes 393220
  30.4 11.3 %collective-permute-start.1 = (bf16[128,512]{1,0:T(8,128)(2,1)S(1)}, bf16[128,512]{1,0:T(8,128)(2,1)S(1)}, u32[]{:S(2)}, u32[]{:S(2)}) collective-permute-start(bf16[128,512]{1,0:T(8,128)(2,1)S(1)} %collective-permute-done.refs_0_), channel_id=1, source_target_pairs={{504,0},{0,8},{8,16},{16,24},{24,32},{32,40},{40,48},{48,56},{56,6... | collective-permute-start | bytes 393224 | tf_op jit(solution)/shard_map/ppermute | solution.py:22
  41.7 1.9 %copy-start.7 = (bf16[128,512]{1,0:T(8,128)(2,1)}, bf16[128,512]{1,0:T(8,128)(2,1)S(1)}, u32[]{:S(2)}) copy-start(bf16[128,512]{1,0:T(8,128)(2,1)S(1)} %collective-permute-done.1.refs_0_) | copy-start | bytes 393220
  41.7 9.0 %collective-permute-start.2 = (bf16[128,512]{1,0:T(8,128)(2,1)S(1)}, bf16[128,512]{1,0:T(8,128)(2,1)S(1)}, u32[]{:S(2)}, u32[]{:S(2)}) collective-permute-start(bf16[128,512]{1,0:T(8,128)(2,1)S(1)} %collective-permute-done.1.refs_0_), channel_id=1, source_target_pairs={{504,0},{0,8},{8,16},{16,24},{24,32},{32,40},{40,48},{48,56},{56,6... | collective-permute-start | bytes 393224 | tf_op jit(solution)/shard_map/ppermute | solution.py:22
  50.7 0.7 copy-start.8
  51.4 10.3 %copy-start.4 = (f32[1,136,512]{2,1,0:T(8,128)S(1)}, f32[1,136,512]{2,1,0:T(8,128)}, u32[]{:S(2)}) copy-start(f32[1,136,512]{2,1,0:T(8,128)} %shard_map.75) | copy-start | bytes 835588
  54.0 17.3 %copy-start.3 = (f32[1,136,512]{2,1,0:T(8,128)S(1)}, f32[1,136,512]{2,1,0:T(8,128)}, u32[]{:S(2)}) copy-start(f32[1,136,512]{2,1,0:T(8,128)} %shard_map.74) | copy-start | bytes 835588
  54.1 7.6 %collective-permute-start.3 = (f32[136,512]{1,0:T(8,128)}, f32[136,512]{1,0:T(8,128)S(1)}, u32[]{:S(2)}, u32[]{:S(2)}) collective-permute-start(f32[136,512]{1,0:T(8,128)} %bitcast.43), channel_id=1, source_target_pairs={{8,0},{16,8},{24,16},{32,24},{40,32},{48,40},{56,48},{64,56},{72,6... | collective-permute-start | bytes 835592 | tf_op jit(solution)/shard_map/ppermute | solution.py:22
  61.7 20.3 %copy-start.2 = (f32[1,136,512]{2,1,0:T(8,128)S(1)}, f32[1,136,512]{2,1,0:T(8,128)}, u32[]{:S(2)}) copy-start(f32[1,136,512]{2,1,0:T(8,128)} %shard_map.73) | copy-start | bytes 835588
  61.7 9.6 %collective-permute-start.4 = (f32[136,512]{1,0:T(8,128)S(1)}, f32[136,512]{1,0:T(8,128)S(1)}, u32[]{:S(2)}, u32[]{:S(2)}) collective-permute-start(f32[136,512]{1,0:T(8,128)S(1)} %add.65), channel_id=1, source_target_pairs={{8,0},{16,8},{24,16},{32,24},{40,32},{48,40},{56,48},{64,56},{72,6... | collective-permute-start | bytes 835592 | tf_op jit(solution)/shard_map/ppermute | solution.py:22
  71.4 10.6 %collective-permute-start.5 = (f32[136,512]{1,0:T(8,128)S(1)}, f32[136,512]{1,0:T(8,128)S(1)}, u32[]{:S(2)}, u32[]{:S(2)}) collective-permute-start(f32[136,512]{1,0:T(8,128)S(1)} %add.66), channel_id=1, source_target_pairs={{8,0},{16,8},{24,16},{32,24},{40,32},{48,40},{56,48},{64,56},{72,6... | collective-permute-start | bytes 835592 | tf_op jit(solution)/shard_map/ppermute | solution.py:22

commit v4 on v1

--- a/solution.py
+++ b/solution.py
@@ -130,8 +130,6 @@
     k_new = mixed[:, q_width:q_width + kv_width]
     v_new = mixed[:, q_width + kv_width:]
 
-    received = [q_own] + [shifted(q_own, "pool", offset) for offset in range(1, SPAN)]
-
     pool_size = lax.axis_size("pool")
     holder = lax.axis_index("pool")
     slots_dev = cached_key_pages.shape[0]
@@ -151,12 +149,20 @@
     limit = jnp.clip(slot_len - page_index * page_len, 0, page_len)
     meta = jnp.stack([distance, limit]).astype(jnp.int32)
 
-    acc = attend(
-        list(range(SPAN)), meta, received, cached_key_pages, cached_value_pages, k_new, v_new
-    )
-    total = acc[0]
-    for offset in range(1, SPAN):
-        total = total + shifted(acc[offset], "pool", -offset)
+    received = [shifted(q_own, "pool", offset) for offset in range(1, SPAN)]
+    part_own = attend([0], meta, [q_own], cached_key_pages, cached_value_pages, k_new, v_new)[0]
+    *received, part_own = lax.optimization_barrier((*received, part_own))
+    received = [q_own] + received
+
+    def part(offset):
+        return attend([offset], meta, [received[offset]], cached_key_pages, cached_value_pages)[0]
+
+    total = part(SPAN - 1)
+    for offset in range(SPAN - 2, -1, -1):
+        moved = shifted(total, "pool", -1)
+        here = part(offset) if offset > 0 else part_own
+        moved, here = lax.optimization_barrier((moved, here))
+        total = here + moved
     heads = q_width // HEAD_SIZE
     numerator = total[:rows].reshape(rows, heads, HEAD_SIZE)
     totals = total[rows, : heads * rows].reshape(heads, rows)

time: 105 us -> 95 us (0.905)
  waiting for transfers between devices: 40.6 us -> 23.2 us
  blocking collectives: 10.1 us -> 16.5 us
  Pallas kernels: 8.68 us -> 12.8 us
  local copies, waits for them, and re-layouts: 6.52 us -> 4.49 us
  starting transfers between devices: 34.5 us -> 33.2 us
    ppermute x6, waiting for transfers between devices: 36.5 us -> 19.2 us  [shifted(): return lax.ppermute(block, axis, route)]
    all_to_all x1, blocking collectives: 10.1 us -> 16.5 us  [on_device(): lax.all_to_all(attended, 'tensor', split_axis=0, concat_axis=1, tiled=True)]
    pallas_call x1 -> x4, Pallas kernels: 8.68 us -> 12.8 us  [attend(): pl.pallas_call(functools.partial(_attend_kernel, tuple(ds), with_own), ou...]
    ppermute x6, starting transfers between devices: 24.4 us -> 23 us  [shifted(): return lax.ppermute(block, axis, route)]
    squeeze x1 -> x0, local copies, waits for them, and re-layouts: 1.18 us -> none  [on_device(): total = total + shifted(acc[offset], 'pool', -offset)]
  transfers between devices with their start and end apart: 7 -> 7, of which waited for: 7 -> 6; matrix products, arithmetic and copies ran while one was open for 3% -> 3% of each run, Pallas kernels for 0% -> 10%
where the time goes in v4:
time: 95 us; the launch traced here: 94.4 us
  starting transfers between devices  33.2 us (35%)
  waiting for transfers between devices  23.2 us (24%)
  blocking collectives  16.5 us (17%)
  Pallas kernels  12.8 us (13%)
  local copies, waits for them, and re-layouts  4.49 us (5%)
  other arithmetic  4.05 us (4%)
    ppermute x6, starting transfers between devices, shifted(): return lax.ppermute(block, axis, route)  23 us
    ppermute x6, waiting for transfers between devices, shifted(): return lax.ppermute(block, axis, route)  19.2 us
    all_to_all x1, blocking collectives, on_device(): lax.all_to_all(attended, 'tensor', split_axis=0, concat_axis=1, tiled=True)  16.5 us
    pallas_call x4, Pallas kernels, attend(): pl.pallas_call(functools.partial(_attend_kernel, tuple(ds), with_own), ou...  12.8 us
    all_to_all x1, starting transfers between devices, on_device(): lax.all_to_all(packed, 'tensor', split_axis=1, concat_axis=0, tiled=True)  10.2 us
    all_to_all x1, waiting for transfers between devices, on_device(): lax.all_to_all(packed, 'tensor', split_axis=1, concat_axis=0, tiled=True)  4.05 us
    add x3, other arithmetic, on_device(): total = here + moved  2.07 us
  transfers between devices with their start and end apart: 7, of which 6 were waited for; matrix products, arithmetic and copies ran while one was open for 3% of the time, Pallas kernels for 10%

profile of v4, /device:TPU:1, one launch (start us, length us, event | category | flops | bytes accessed | tf_op | source)
XLA Modules:
  0.0 94.4 jit_solution(10167061388301309449)
XLA Ops:
  0.0 1.0 %copy.31 = bf16[2,8,8,512]{3,2,0,1:T(8,128)(2,1)S(1)} copy(bf16[2,8,8,512]{3,2,1,0:T(8,128)(2,1)} %bitcast.44) | data formatting | bytes 262144 | tf_op jit(solution)/shard_map/reshape | solution.py:120
  1.0 0.7 pad_maximum_fusion
  1.7 10.2 %all-to-all-start = ((bf16[16,8,1024]{2,0,1:T(8,128)(2,1)}), bf16[16,8,1024]{2,0,1:T(8,128)(2,1)S(1)}, u32[]{:S(2)}, u32[]{:S(2)}) async-start(bf16[16,8,1024]{2,0,1:T(8,128)(2,1)} %pad_maximum_fusion), calls=%async_computation | async-start | bytes 524288 | tf_op jit(solution)/shard_map/all_to_all | solution.py:126
  12.0 0.6 gather_fusion
  12.6 0.2 compare_reduce_fusion
  12.8 0.2 fusion.1
  13.0 0.6 gather_fusion.1
  13.8 0.6 pad_add_fusion.meta_ref
  14.4 4.1 %all-to-all-done = bf16[16,8,1024]{2,0,1:T(8,128)(2,1)S(1)} async-done(((bf16[16,8,1024]{2,0,1:T(8,128)(2,1)}), bf16[16,8,1024]{2,0,1:T(8,128)(2,1)S(1)}, u32[]{:S(2)}, u32[]{:S(2)}) %all-to-all-start) | async-done | bytes 262176 | tf_op jit(solution)/shard_map/all_to_all | solution.py:126
  18.5 1.9 %collective-permute-start = (bf16[128,512]{1,0:T(8,128)(2,1)S(1)}, bf16[128,512]{1,0:T(8,128)(2,1)S(1)}, u32[]{:S(2)}, u32[]{:S(2)}) collective-permute-start(bf16[128,512]{1,0:T(8,128)(2,1)S(1)} %slice.24.refs_0_), channel_id=1, source_target_pairs={{504,0},{0,8},{8,16},{16,24},{24,32},{32,40},{40,48},{48,56},{56,6... | collective-permute-start | bytes 393224 | tf_op jit(solution)/shard_map/ppermute | solution.py:22
  20.4 2.1 %collective-permute-start.1 = (bf16[128,512]{1,0:T(8,128)(2,1)S(1)}, bf16[128,512]{1,0:T(8,128)(2,1)S(1)}, u32[]{:S(2)}, u32[]{:S(2)}) collective-permute-start(bf16[128,512]{1,0:T(8,128)(2,1)S(1)} %slice.24.refs_0_), channel_id=1, source_target_pairs={{496,0},{504,8},{0,16},{8,24},{16,32},{24,40},{32,48},{40,56},{48,... | collective-permute-start | bytes 393224 | tf_op jit(solution)/shard_map/ppermute | solution.py:22
  22.5 7.5 %collective-permute-start.2 = (bf16[128,512]{1,0:T(8,128)(2,1)S(1)}, bf16[128,512]{1,0:T(8,128)(2,1)S(1)}, u32[]{:S(2)}, u32[]{:S(2)}) collective-permute-start(bf16[128,512]{1,0:T(8,128)(2,1)S(1)} %slice.24.refs_0_), channel_id=1, source_target_pairs={{488,0},{496,8},{504,16},{0,24},{8,32},{16,40},{24,48},{32,56},{40... | collective-permute-start | bytes 393224 | tf_op jit(solution)/shard_map/ppermute | solution.py:22
  30.0 0.7 fusion.5
  30.6 3.3 %shard_map.73 = f32[1,136,512]{2,1,0:T(8,128)} custom-call(s32[2,16]{1,0:T(2,128)} %pad_add_fusion.meta_ref, bf16[128,512]{1,0:T(8,128)(2,1)} %copy-done.3, bf16[16,128,256]{2,1,0:T(8,128)(2,1)} %refs_1_.7, bf16[16,128,256]{2,1,0:T(8,128)(2,1)} %refs_2_.7, bf16[128,256]{1,0:T(8,128)(2,1)} %get-tuple-element.28.refs_3_, ...), custom_call_target="tpu_custom_call" | custom-call | flops 570425344 | bytes 2637952 | tf_op jit(solution)/shard_map/pallas_call | solution.py:95
  33.9 1.5 %collective-permute-done.1.refs_0_ = bf16[128,512]{1,0:T(8,128)(2,1)S(1)} collective-permute-done((bf16[128,512]{1,0:T(8,128)(2,1)S(1)}, bf16[128,512]{1,0:T(8,128)(2,1)S(1)}, u32[]{:S(2)}, u32[]{:S(2)}) %collective-permute-start.1) | collective-permute-done | bytes 131104 | tf_op jit(solution)/shard_map/ppermute | solution.py:22
  35.4 9.0 %collective-permute-done.2.refs_0_ = bf16[128,512]{1,0:T(8,128)(2,1)S(1)} collective-permute-done((bf16[128,512]{1,0:T(8,128)(2,1)S(1)}, bf16[128,512]{1,0:T(8,128)(2,1)S(1)}, u32[]{:S(2)}, u32[]{:S(2)}) %collective-permute-start.2) | collective-permute-done | bytes 131104 | tf_op jit(solution)/shard_map/ppermute | solution.py:22
  44.4 0.6 copy-done.6
  45.1 2.9 %shard_map.74 = f32[1,136,512]{2,1,0:T(8,128)} custom-call(s32[2,16]{1,0:T(2,128)} %pad_add_fusion.meta_ref, bf16[128,512]{1,0:T(8,128)(2,1)} %copy-done.6, bf16[16,128,256]{2,1,0:T(8,128)(2,1)} %refs_1_.7, bf16[16,128,256]{2,1,0:T(8,128)(2,1)} %refs_2_.7), custom_call_target="tpu_custom_call" | custom-call | flops 536870912 | bytes 2506880 | tf_op jit(solution)/shard_map/pallas_call | solution.py:95
  48.0 1.9 %collective-permute-start.3 = (f32[136,512]{1,0:T(8,128)}, f32[136,512]{1,0:T(8,128)S(1)}, u32[]{:S(2)}, u32[]{:S(2)}) collective-permute-start(f32[136,512]{1,0:T(8,128)} %bitcast.43), channel_id=1, source_target_pairs={{8,0},{16,8},{24,16},{32,24},{40,32},{48,40},{56,48},{64,56},{72,6... | collective-permute-start | bytes 835592 | tf_op jit(solution)/shard_map/ppermute | solution.py:22
  49.9 3.3 %shard_map.75 = f32[1,136,512]{2,1,0:T(8,128)} custom-call(s32[2,16]{1,0:T(2,128)} %pad_add_fusion.meta_ref, bf16[128,512]{1,0:T(8,128)(2,1)} %copy-done.5, bf16[16,128,256]{2,1,0:T(8,128)(2,1)} %refs_1_.7, bf16[16,128,256]{2,1,0:T(8,128)(2,1)} %refs_2_.7), custom_call_target="tpu_custom_call" | custom-call | flops 536870912 | bytes 2506880 | tf_op jit(solution)/shard_map/pallas_call | solution.py:95
  53.2 4.4 %collective-permute-done.3 = f32[136,512]{1,0:T(8,128)S(1)} collective-permute-done((f32[136,512]{1,0:T(8,128)}, f32[136,512]{1,0:T(8,128)S(1)}, u32[]{:S(2)}, u32[]{:S(2)}) %collective-permute-start.3) | collective-permute-done | bytes 278560 | tf_op jit(solution)/shard_map/ppermute | solution.py:22
  57.6 1.0 %add.65 = f32[136,512]{1,0:T(8,128)S(1)} add(f32[136,512]{1,0:T(8,128)} %bitcast.35, f32[136,512]{1,0:T(8,128)S(1)} %collective-permute-done.3) | non-fusion elementwise | flops 69632 | bytes 835584 | tf_op jit(solution)/shard_map/add | solution.py:165
  58.6 3.1 %collective-permute-start.4 = (f32[136,512]{1,0:T(8,128)S(1)}, f32[136,512]{1,0:T(8,128)S(1)}, u32[]{:S(2)}, u32[]{:S(2)}) collective-permute-start(f32[136,512]{1,0:T(8,128)S(1)} %add.65), channel_id=1, source_target_pairs={{8,0},{16,8},{24,16},{32,24},{40,32},{48,40},{56,48},{64,56},{72,6... | collective-permute-start | bytes 835592 | tf_op jit(solution)/shard_map/ppermute | solution.py:22
  61.7 3.3 %shard_map.76 = f32[1,136,512]{2,1,0:T(8,128)} custom-call(s32[2,16]{1,0:T(2,128)} %pad_add_fusion.meta_ref, bf16[128,512]{1,0:T(8,128)(2,1)} %copy-done.4, bf16[16,128,256]{2,1,0:T(8,128)(2,1)} %refs_1_.7, bf16[16,128,256]{2,1,0:T(8,128)(2,1)} %refs_2_.7), custom_call_target="tpu_custom_call" | custom-call | flops 536870912 | bytes 2506880 | tf_op jit(solution)/shard_map/pallas_call | solution.py:95
  65.0 0.8 collective-permute-done.4
  65.9 1.0 %add.66 = f32[136,512]{1,0:T(8,128)S(1)} add(f32[136,512]{1,0:T(8,128)} %bitcast.34, f32[136,512]{1,0:T(8,128)S(1)} %collective-permute-done.4) | non-fusion elementwise | flops 69632 | bytes 835584 | tf_op jit(solution)/shard_map/add | solution.py:165
  66.9 6.5 %collective-permute-start.5 = (f32[136,512]{1,0:T(8,128)S(1)}, f32[136,512]{1,0:T(8,128)S(1)}, u32[]{:S(2)}, u32[]{:S(2)}) collective-permute-start(f32[136,512]{1,0:T(8,128)S(1)} %add.66), channel_id=1, source_target_pairs={{8,0},{16,8},{24,16},{32,24},{40,32},{48,40},{56,48},{64,56},{72,6... | collective-permute-start | bytes 835592 | tf_op jit(solution)/shard_map/ppermute | solution.py:22
  73.4 3.5 %collective-permute-done.5 = f32[136,512]{1,0:T(8,128)S(1)} collective-permute-done((f32[136,512]{1,0:T(8,128)S(1)}, f32[136,512]{1,0:T(8,128)S(1)}, u32[]{:S(2)}, u32[]{:S(2)}) %collective-permute-start.5) | collective-permute-done | bytes 278560 | tf_op jit(solution)/shard_map/ppermute | solution.py:22
  76.9 0.1 copy.21
  77.0 0.2 div.11
  77.3 16.5 %all_to_all.34 = bf16[8,16,512]{2,1,0:T(8,128)(2,1)S(1)} all-to-all(bf16[8,16,512]{2,1,0:T(8,128)(2,1)S(1)} %bitcast.40), channel_id=1, replica_groups=mesh['pool'=64,'tensor'=8] {'tensor'}, dimensions={0} | all-to-all | bytes 262144 | tf_op jit(solution)/shard_map/all_to_all | solution.py:171
  93.8 0.7 copy.26
  (32 shorter events, 0.4 us)
Async XLA Ops:
  0.0 12.0 %copy-start = (s32[64,64]{1,0:T(8,128)S(1)}, s32[64,64]{1,0:T(8,128)}, u32[]{:S(2)}) copy-start(s32[64,64]{1,0:T(8,128)} %param.12) | copy-start | bytes 49156
  0.0 1.0 %copy-start.7 = (bf16[16,2048]{1,0:T(8,128)(2,1)S(1)}, bf16[16,2048]{1,0:T(8,128)(2,1)}, u32[]{:S(2)}) copy-start(bf16[16,2048]{1,0:T(8,128)(2,1)} %param.9) | copy-start | bytes 196612
  0.0 1.0 %copy-start.8 = (bf16[16,2048]{1,0:T(8,128)(2,1)S(1)}, bf16[16,2048]{1,0:T(8,128)(2,1)}, u32[]{:S(2)}) copy-start(bf16[16,2048]{1,0:T(8,128)(2,1)} %param.8) | copy-start | bytes 196612
  1.7 16.7 %all-to-all-start = ((bf16[16,8,1024]{2,0,1:T(8,128)(2,1)}), bf16[16,8,1024]{2,0,1:T(8,128)(2,1)S(1)}, u32[]{:S(2)}, u32[]{:S(2)}) async-start(bf16[16,8,1024]{2,0,1:T(8,128)(2,1)} %pad_maximum_fusion), calls=%async_computation | async-start | bytes 524288 | tf_op jit(solution)/shard_map/all_to_all | solution.py:126
  12.0 1.0 %copy-start.1 = (s32[64]{0:T(128)S(1)}, s32[64]{0:T(128)}, u32[]{:S(2)}) copy-start(s32[64]{0:T(128)} %param.13) | copy-start | bytes 772
  18.4 12.2 %copy-start.3 = (bf16[128,512]{1,0:T(8,128)(2,1)}, bf16[128,512]{1,0:T(8,128)(2,1)S(1)}, u32[]{:S(2)}) copy-start(bf16[128,512]{1,0:T(8,128)(2,1)S(1)} %slice.24.refs_0_) | copy-start | bytes 393220
  18.5 15.5 %collective-permute-start = (bf16[128,512]{1,0:T(8,128)(2,1)S(1)}, bf16[128,512]{1,0:T(8,128)(2,1)S(1)}, u32[]{:S(2)}, u32[]{:S(2)}) collective-permute-start(bf16[128,512]{1,0:T(8,128)(2,1)S(1)} %slice.24.refs_0_), channel_id=1, source_target_pairs={{504,0},{0,8},{8,16},{16,24},{24,32},{32,40},{40,48},{48,56},{56,6... | collective-permute-start | bytes 393224 | tf_op jit(solution)/shard_map/ppermute | solution.py:22
  20.4 15.1 %collective-permute-start.1 = (bf16[128,512]{1,0:T(8,128)(2,1)S(1)}, bf16[128,512]{1,0:T(8,128)(2,1)S(1)}, u32[]{:S(2)}, u32[]{:S(2)}) collective-permute-start(bf16[128,512]{1,0:T(8,128)(2,1)S(1)} %slice.24.refs_0_), channel_id=1, source_target_pairs={{496,0},{504,8},{0,16},{8,24},{16,32},{24,40},{32,48},{40,56},{48,... | collective-permute-start | bytes 393224 | tf_op jit(solution)/shard_map/ppermute | solution.py:22
  22.5 21.9 %collective-permute-start.2 = (bf16[128,512]{1,0:T(8,128)(2,1)S(1)}, bf16[128,512]{1,0:T(8,128)(2,1)S(1)}, u32[]{:S(2)}, u32[]{:S(2)}) collective-permute-start(bf16[128,512]{1,0:T(8,128)(2,1)S(1)} %slice.24.refs_0_), channel_id=1, source_target_pairs={{488,0},{496,8},{504,16},{0,24},{8,32},{16,40},{24,48},{32,56},{40... | collective-permute-start | bytes 393224 | tf_op jit(solution)/shard_map/ppermute | solution.py:22
  33.9 14.1 %copy-start.4 = (bf16[128,512]{1,0:T(8,128)(2,1)}, bf16[128,512]{1,0:T(8,128)(2,1)S(1)}, u32[]{:S(2)}) copy-start(bf16[128,512]{1,0:T(8,128)(2,1)S(1)} %collective-permute-done.refs_0_) | copy-start | bytes 393220
  35.4 12.6 %copy-start.5 = (bf16[128,512]{1,0:T(8,128)(2,1)}, bf16[128,512]{1,0:T(8,128)(2,1)S(1)}, u32[]{:S(2)}) copy-start(bf16[128,512]{1,0:T(8,128)(2,1)S(1)} %collective-permute-done.1.refs_0_) | copy-start | bytes 393220
  44.4 0.6 copy-start.6
  48.0 9.6 %collective-permute-start.3 = (f32[136,512]{1,0:T(8,128)}, f32[136,512]{1,0:T(8,128)S(1)}, u32[]{:S(2)}, u32[]{:S(2)}) collective-permute-start(f32[136,512]{1,0:T(8,128)} %bitcast.43), channel_id=1, source_target_pairs={{8,0},{16,8},{24,16},{32,24},{40,32},{48,40},{56,48},{64,56},{72,6... | collective-permute-start | bytes 835592 | tf_op jit(solution)/shard_map/ppermute | solution.py:22
  58.6 7.3 %collective-permute-start.4 = (f32[136,512]{1,0:T(8,128)S(1)}, f32[136,512]{1,0:T(8,128)S(1)}, u32[]{:S(2)}, u32[]{:S(2)}) collective-permute-start(f32[136,512]{1,0:T(8,128)S(1)} %add.65), channel_id=1, source_target_pairs={{8,0},{16,8},{24,16},{32,24},{40,32},{48,40},{56,48},{64,56},{72,6... | collective-permute-start | bytes 835592 | tf_op jit(solution)/shard_map/ppermute | solution.py:22
  65.9 11.0 %copy-start.2 = (f32[1,136,512]{2,1,0:T(8,128)S(1)}, f32[1,136,512]{2,1,0:T(8,128)}, u32[]{:S(2)}) copy-start(f32[1,136,512]{2,1,0:T(8,128)} %shard_map.73) | copy-start | bytes 835588
  66.9 9.9 %collective-permute-start.5 = (f32[136,512]{1,0:T(8,128)S(1)}, f32[136,512]{1,0:T(8,128)S(1)}, u32[]{:S(2)}, u32[]{:S(2)}) collective-permute-start(f32[136,512]{1,0:T(8,128)S(1)} %add.66), channel_id=1, source_target_pairs={{8,0},{16,8},{24,16},{32,24},{40,32},{48,40},{56,48},{64,56},{72,6... | collective-permute-start | bytes 835592 | tf_op jit(solution)/shard_map/ppermute | solution.py:22

commit v5 on v4

--- a/solution.py
+++ b/solution.py
@@ -22,23 +22,33 @@
     return lax.ppermute(block, axis, route)
 
 
-def _attend_kernel(ds, with_own, meta_ref, *refs):
-    nq = len(ds)
-    q_refs = refs[:nq]
-    kp_ref, vp_ref = refs[nq], refs[nq + 1]
-    rest = refs[nq + 2:]
+def _attend_kernel(dist, with_own, meta_ref, q_ref, kp_hbm, vp_hbm, *refs):
     if with_own:
-        kn_ref, vn_ref = rest[0], rest[1]
-        rest = rest[2:]
-    out_ref = rest[0]
-    rows = q_refs[0].shape[0]
-    slots, page_len, kv_width = kp_ref.shape
+        kn_ref, vn_ref = refs[0], refs[1]
+        refs = refs[2:]
+    out_ref, kbuf, vbuf, sem = refs
+    rows = q_ref.shape[0]
+    page_len, kv_width = kbuf.shape[1], kbuf.shape[2]
     kv_local = kv_width // HEAD_SIZE
     group = QUERY_HEADS // KEY_VALUE_HEADS
+    count = meta_ref[dist, 2, 0]
+
+    def copies(i, b):
+        s = meta_ref[dist, 0, i]
+        return (
+            pltpu.make_async_copy(kp_hbm.at[s], kbuf.at[b], sem.at[0, b]),
+            pltpu.make_async_copy(vp_hbm.at[s], vbuf.at[b], sem.at[1, b]),
+        )
+
+    @pl.when(count > 0)
+    def _():
+        for c in copies(0, 0):
+            c.start()
+
     out_ref[...] = jnp.zeros(out_ref.shape, jnp.float32)
     ones = jnp.ones((8, page_len), jnp.bfloat16)
 
-    def add_block(i, q_ref, k, v, visible):
+    def add_block(k, v, visible):
         for g in range(kv_local):
             kg = k[:, g * HEAD_SIZE:(g + 1) * HEAD_SIZE]
             vg = v[:, g * HEAD_SIZE:(g + 1) * HEAD_SIZE]
@@ -52,52 +62,61 @@
                 w = jnp.where(visible, jnp.exp(SOFTCAP * jnp.tanh(s / SOFTCAP)), 0.0).astype(
                     jnp.bfloat16
                 )
-                out_ref[i, :rows, col:col + HEAD_SIZE] += jnp.dot(
+                out_ref[:rows, col:col + HEAD_SIZE] += jnp.dot(
                     w, vg, preferred_element_type=jnp.float32
                 )
                 t = lax.dot_general(
                     ones, w, (((1,), (1,)), ((), ())), preferred_element_type=jnp.float32
                 )
-                out_ref[i, rows:rows + 8, h * rows:(h + 1) * rows] += t
+                out_ref[rows:rows + 8, h * rows:(h + 1) * rows] += t
 
     key_pos = lax.broadcasted_iota(jnp.int32, (rows, page_len), 1)
     if with_own:
         q_pos = lax.broadcasted_iota(jnp.int32, (rows, page_len), 0)
-        add_block(ds.index(0), q_refs[ds.index(0)], kn_ref[...], vn_ref[...], key_pos <= q_pos)
-
-    def slot(s, carry):
-        d = meta_ref[0, s]
-        lim = meta_ref[1, s]
-        for i, dd in enumerate(ds):
-            @pl.when((d == dd) & (lim > 0))
-            def _():
-                add_block(i, q_refs[i], kp_ref[s], vp_ref[s], key_pos < lim)
-
+        add_block(kn_ref[...], vn_ref[...], key_pos <= q_pos)
+
+    def slot(i, carry):
+        b = i % 2
+
+        @pl.when(i + 1 < count)
+        def _():
+            for c in copies(i + 1, 1 - b):
+                c.start()
+
+        for c in copies(i, b):
+            c.wait()
+        add_block(kbuf[b], vbuf[b], key_pos < meta_ref[dist, 1, i])
         return carry
 
-    lax.fori_loop(0, slots, slot, 0)
-
-
-def attend(ds, meta, qs, kp, vp, kn=None, vn=None):
+    lax.fori_loop(0, count, slot, 0)
+
+
+def attend(dist, meta, q, kp, vp, kn=None, vn=None):
     with_own = kn is not None
-    rows, width = qs[0].shape
+    rows, width = q.shape
     slots, page_len, kv_width = kp.shape
-    args = [meta, *qs, kp, vp] + ([kn, vn] if with_own else [])
-    blocks = slots + (1 if with_own else 0)
+    args = [meta, q, kp, vp] + ([kn, vn] if with_own else [])
+    blocks = slots // SPAN + (1 if with_own else 0)
     heads = width // HEAD_SIZE
-    flops = blocks * heads * rows * page_len * HEAD_SIZE * 4
     cost = pl.CostEstimate(
-        flops=flops,
+        flops=blocks * heads * rows * page_len * HEAD_SIZE * 4,
         transcendentals=blocks * heads * rows * page_len * 2,
-        bytes_accessed=sum(int(x.size) * x.dtype.itemsize for x in args)
-        + len(ds) * (rows + 8) * width * 4,
-    )
+        bytes_accessed=int(q.size) * 2 + blocks * page_len * kv_width * 4
+        + (rows + 8) * width * 4,
+    )
+    vmem = pl.BlockSpec(memory_space=pltpu.VMEM)
+    hbm = pl.BlockSpec(memory_space=pl.ANY)
     return pl.pallas_call(
-        functools.partial(_attend_kernel, tuple(ds), with_own),
-        out_shape=jax.ShapeDtypeStruct((len(ds), rows + 8, width), jnp.float32),
-        in_specs=[pl.BlockSpec(memory_space=pltpu.SMEM)]
-        + [pl.BlockSpec(memory_space=pltpu.VMEM)] * (len(args) - 1),
-        out_specs=pl.BlockSpec(memory_space=pltpu.VMEM),
+        functools.partial(_attend_kernel, dist, with_own),
+        out_shape=jax.ShapeDtypeStruct((rows + 8, width), jnp.float32),
+        in_specs=[pl.BlockSpec(memory_space=pltpu.SMEM), vmem, hbm, hbm]
+        + [vmem] * (2 if with_own else 0),
+        out_specs=vmem,
+        scratch_shapes=[
+            pltpu.VMEM((2, page_len, kv_width), kp.dtype),
+            pltpu.VMEM((2, page_len, kv_width), vp.dtype),
+            pltpu.SemaphoreType.DMA((2, 2)),
+        ],
         cost_estimate=cost,
     )(*args)
 
@@ -147,15 +166,21 @@
     owner_len = jnp.take(lengths, owners)
     slot_len = jnp.sum(jnp.where(owner_hot, owner_len[:, None], 0), axis=0)
     limit = jnp.clip(slot_len - page_index * page_len, 0, page_len)
-    meta = jnp.stack([distance, limit]).astype(jnp.int32)
+    wanted = (distance[None, :] == jnp.arange(SPAN, dtype=jnp.int32)[:, None]) & (limit > 0)
+    rank = jnp.cumsum(wanted.astype(jnp.int32), axis=1) - 1
+    place = wanted[:, :, None] & (rank[:, :, None] == jnp.arange(slots_dev, dtype=jnp.int32))
+    order = jnp.sum(jnp.where(place, jnp.arange(slots_dev, dtype=jnp.int32)[None, :, None], 0), axis=1)
+    order_limit = jnp.sum(jnp.where(place, limit[None, :, None], 0), axis=1)
+    count = jnp.broadcast_to(jnp.sum(wanted.astype(jnp.int32), axis=1, keepdims=True), (SPAN, slots_dev))
+    meta = jnp.stack([order, order_limit, count], axis=1).astype(jnp.int32)
 
     received = [shifted(q_own, "pool", offset) for offset in range(1, SPAN)]
-    part_own = attend([0], meta, [q_own], cached_key_pages, cached_value_pages, k_new, v_new)[0]
+    part_own = attend(0, meta, q_own, cached_key_pages, cached_value_pages, k_new, v_new)
     *received, part_own = lax.optimization_barrier((*received, part_own))
     received = [q_own] + received
 
     def part(offset):
-        return attend([offset], meta, [received[offset]], cached_key_pages, cached_value_pages)[0]
+        return attend(offset, meta, received[offset], cached_key_pages, cached_value_pages)
 
     total = part(SPAN - 1)
     for offset in range(SPAN - 2, -1, -1):

time: 95 us -> 102 us (1.074)
  blocking collectives: 16.5 us -> 11.4 us
  Pallas kernels: 12.8 us -> 17.4 us
  starting transfers between devices: 33.2 us -> 36.6 us
  waiting for transfers between devices: 23.2 us -> 26.5 us
    all_to_all x1, blocking collectives: 16.5 us -> 11.4 us  [on_device(): lax.all_to_all(attended, 'tensor', split_axis=0, concat_axis=1, tiled=True)]
    pallas_call x4, Pallas kernels: 12.8 us -> 17.4 us  [attend(): pl.pallas_call(functools.partial(_attend_kernel, dist, with_own), out_sha...]
    ppermute x6, waiting for transfers between devices: 19.2 us -> 23 us  [shifted(): return lax.ppermute(block, axis, route)]
    ppermute x6, starting transfers between devices: 23 us -> 26.4 us  [shifted(): return lax.ppermute(block, axis, route)]
  transfers between devices with their start and end apart: 7 -> 7, of which waited for: 6 -> 6; matrix products, arithmetic and copies ran while one was open for 3% -> 4% of each run, Pallas kernels for 10% -> 5%
where the time goes in v5:
time: 102 us; the launch traced here: 101 us
  starting transfers between devices  36.6 us (36%)
  waiting for transfers between devices  26.5 us (26%)
  Pallas kernels  17.4 us (17%)
  blocking collectives  11.4 us (11%)
  local copies, waits for them, and re-layouts  4.59 us (4%)
  other arithmetic  4.46 us (4%)
    ppermute x6, starting transfers between devices, shifted(): return lax.ppermute(block, axis, route)  26.4 us
    ppermute x6, waiting for transfers between devices, shifted(): return lax.ppermute(block, axis, route)  23 us
    pallas_call x4, Pallas kernels, attend(): pl.pallas_call(functools.partial(_attend_kernel, dist, with_own), out_sha...  17.4 us
    all_to_all x1, blocking collectives, on_device(): lax.all_to_all(attended, 'tensor', split_axis=0, concat_axis=1, tiled=True)  11.4 us
    all_to_all x1, starting transfers between devices, on_device(): lax.all_to_all(packed, 'tensor', split_axis=1, concat_axis=0, tiled=True)  10.2 us
    all_to_all x1, waiting for transfers between devices, on_device(): lax.all_to_all(packed, 'tensor', split_axis=1, concat_axis=0, tiled=True)  3.52 us
  transfers between devices with their start and end apart: 7, of which 6 were waited for; matrix products, arithmetic and copies ran while one was open for 4% of the time, Pallas kernels for 5%

profile of v5, /device:TPU:1, one launch (start us, length us, event | category | flops | bytes accessed | tf_op | source)
XLA Modules:
  0.0 101.2 jit_solution(7396453262854211987)
XLA Ops:
  0.0 1.0 copy.37
  1.0 0.7 pad_maximum_fusion
  1.7 10.2 %all-to-all-start = ((bf16[16,8,1024]{2,0,1:T(8,128)(2,1)}), bf16[16,8,1024]{2,0,1:T(8,128)(2,1)S(1)}, u32[]{:S(2)}, u32[]{:S(2)}) async-start(bf16[16,8,1024]{2,0,1:T(8,128)(2,1)} %pad_maximum_fusion), calls=%async_computation | async-start | bytes 524288 | tf_op jit(solution)/shard_map/all_to_all | solution.py:145
  12.0 0.6 gather_fusion
  12.6 0.2 compare_reduce_fusion
  12.8 0.2 fusion.1
  13.0 0.6 gather_fusion.1
  13.8 0.2 reduce_window_sum.11
  14.3 0.6 pad_add_fusion.meta_ref
  14.9 3.5 %all-to-all-done = bf16[16,8,1024]{2,0,1:T(8,128)(2,1)S(1)} async-done(((bf16[16,8,1024]{2,0,1:T(8,128)(2,1)}), bf16[16,8,1024]{2,0,1:T(8,128)(2,1)S(1)}, u32[]{:S(2)}, u32[]{:S(2)}) %all-to-all-start) | async-done | bytes 262176 | tf_op jit(solution)/shard_map/all_to_all | solution.py:145
  18.5 1.9 %collective-permute-start = (bf16[128,512]{1,0:T(8,128)(2,1)S(1)}, bf16[128,512]{1,0:T(8,128)(2,1)S(1)}, u32[]{:S(2)}, u32[]{:S(2)}) collective-permute-start(bf16[128,512]{1,0:T(8,128)(2,1)S(1)} %slice.24.q_ref), channel_id=1, source_target_pairs={{504,0},{0,8},{8,16},{16,24},{24,32},{32,40},{40,48},{48,56},{56,6... | collective-permute-start | bytes 393224 | tf_op jit(solution)/shard_map/ppermute | solution.py:22
  20.4 2.1 %collective-permute-start.1 = (bf16[128,512]{1,0:T(8,128)(2,1)S(1)}, bf16[128,512]{1,0:T(8,128)(2,1)S(1)}, u32[]{:S(2)}, u32[]{:S(2)}) collective-permute-start(bf16[128,512]{1,0:T(8,128)(2,1)S(1)} %slice.24.q_ref), channel_id=1, source_target_pairs={{496,0},{504,8},{0,16},{8,24},{16,32},{24,40},{32,48},{40,56},{48,... | collective-permute-start | bytes 393224 | tf_op jit(solution)/shard_map/ppermute | solution.py:22
  22.5 7.5 %collective-permute-start.2 = (bf16[128,512]{1,0:T(8,128)(2,1)S(1)}, bf16[128,512]{1,0:T(8,128)(2,1)S(1)}, u32[]{:S(2)}, u32[]{:S(2)}) collective-permute-start(bf16[128,512]{1,0:T(8,128)(2,1)S(1)} %slice.24.q_ref), channel_id=1, source_target_pairs={{488,0},{496,8},{504,16},{0,24},{8,32},{16,40},{24,48},{32,56},{40... | collective-permute-start | bytes 393224 | tf_op jit(solution)/shard_map/ppermute | solution.py:22
  30.0 0.7 fusion.9
  30.7 2.1 %shard_map.73 = f32[136,512]{1,0:T(8,128)} custom-call(s32[4,3,16]{2,1,0:T(4,128)} %pad_add_fusion.meta_ref, bf16[128,512]{1,0:T(8,128)(2,1)} %copy-done.3, bf16[16,128,256]{2,1,0:T(8,128)(2,1)} %kp_hbm.7, bf16[16,128,256]{2,1,0:T(8,128)(2,1)} %vp_hbm.7, bf16[128,256]{1,0:T(8,128)(2,1)} %get-tuple-element.34.refs_0_, bf16[128,256]{1,0:T(8,128)(2,1)} %get-tuple-element.33.refs_1_), custom_call_target="tpu_custom_call" | custom-call | flops 167772160 | bytes 1064960 | tf_op jit(solution)/shard_map/pallas_call | solution.py:109
  32.7 2.7 %collective-permute-done.1.q_ref = bf16[128,512]{1,0:T(8,128)(2,1)S(1)} collective-permute-done((bf16[128,512]{1,0:T(8,128)(2,1)S(1)}, bf16[128,512]{1,0:T(8,128)(2,1)S(1)}, u32[]{:S(2)}, u32[]{:S(2)}) %collective-permute-start.1) | collective-permute-done | bytes 131104 | tf_op jit(solution)/shard_map/ppermute | solution.py:22
  35.4 9.0 %collective-permute-done.2.q_ref = bf16[128,512]{1,0:T(8,128)(2,1)S(1)} collective-permute-done((bf16[128,512]{1,0:T(8,128)(2,1)S(1)}, bf16[128,512]{1,0:T(8,128)(2,1)S(1)}, u32[]{:S(2)}, u32[]{:S(2)}) %collective-permute-start.2) | collective-permute-done | bytes 131104 | tf_op jit(solution)/shard_map/ppermute | solution.py:22
  44.4 0.6 copy-done.6
  45.1 12.0 %shard_map.74 = f32[136,512]{1,0:T(8,128)} custom-call(s32[4,3,16]{2,1,0:T(4,128)} %pad_add_fusion.meta_ref, bf16[128,512]{1,0:T(8,128)(2,1)} %copy-done.6, bf16[16,128,256]{2,1,0:T(8,128)(2,1)} %kp_hbm.7, bf16[16,128,256]{2,1,0:T(8,128)(2,1)} %vp_hbm.7), custom_call_target="tpu_custom_call" | custom-call | flops 134217728 | bytes 933888 | tf_op jit(solution)/shard_map/pallas_call | solution.py:109
  57.1 1.9 %collective-permute-start.3 = (f32[136,512]{1,0:T(8,128)}, f32[136,512]{1,0:T(8,128)S(1)}, u32[]{:S(2)}, u32[]{:S(2)}) collective-permute-start(f32[136,512]{1,0:T(8,128)} %shard_map.74), channel_id=1, source_target_pairs={{8,0},{16,8},{24,16},{32,24},{40,32},{48,40},{56,48},{64,56},{72,6... | collective-permute-start | bytes 835592 | tf_op jit(solution)/shard_map/ppermute | solution.py:22
  59.1 1.7 %shard_map.75 = f32[136,512]{1,0:T(8,128)} custom-call(s32[4,3,16]{2,1,0:T(4,128)} %pad_add_fusion.meta_ref, bf16[128,512]{1,0:T(8,128)(2,1)} %copy-done.5, bf16[16,128,256]{2,1,0:T(8,128)(2,1)} %kp_hbm.7, bf16[16,128,256]{2,1,0:T(8,128)(2,1)} %vp_hbm.7), custom_call_target="tpu_custom_call" | custom-call | flops 134217728 | bytes 933888 | tf_op jit(solution)/shard_map/pallas_call | solution.py:109
  60.8 5.4 %collective-permute-done.3 = f32[136,512]{1,0:T(8,128)S(1)} collective-permute-done((f32[136,512]{1,0:T(8,128)}, f32[136,512]{1,0:T(8,128)S(1)}, u32[]{:S(2)}, u32[]{:S(2)}) %collective-permute-start.3) | collective-permute-done | bytes 278560 | tf_op jit(solution)/shard_map/ppermute | solution.py:22
  66.2 1.0 add.70
  67.2 5.5 %collective-permute-start.4 = (f32[136,512]{1,0:T(8,128)S(1)}, f32[136,512]{1,0:T(8,128)S(1)}, u32[]{:S(2)}, u32[]{:S(2)}) collective-permute-start(f32[136,512]{1,0:T(8,128)S(1)} %add.70), channel_id=1, source_target_pairs={{8,0},{16,8},{24,16},{32,24},{40,32},{48,40},{56,48},{64,56},{72,6... | collective-permute-start | bytes 835592 | tf_op jit(solution)/shard_map/ppermute | solution.py:22
  72.7 1.7 %shard_map.76 = f32[136,512]{1,0:T(8,128)} custom-call(s32[4,3,16]{2,1,0:T(4,128)} %pad_add_fusion.meta_ref, bf16[128,512]{1,0:T(8,128)(2,1)} %copy-done.4, bf16[16,128,256]{2,1,0:T(8,128)(2,1)} %kp_hbm.7, bf16[16,128,256]{2,1,0:T(8,128)(2,1)} %vp_hbm.7), custom_call_target="tpu_custom_call" | custom-call | flops 134217728 | bytes 933888 | tf_op jit(solution)/shard_map/pallas_call | solution.py:109
  74.4 2.4 %collective-permute-done.4 = f32[136,512]{1,0:T(8,128)S(1)} collective-permute-done((f32[136,512]{1,0:T(8,128)S(1)}, f32[136,512]{1,0:T(8,128)S(1)}, u32[]{:S(2)}, u32[]{:S(2)}) %collective-permute-start.4) | collective-permute-done | bytes 278560 | tf_op jit(solution)/shard_map/ppermute | solution.py:22
  76.8 1.0 add.71
  77.8 7.4 %collective-permute-start.5 = (f32[136,512]{1,0:T(8,128)S(1)}, f32[136,512]{1,0:T(8,128)S(1)}, u32[]{:S(2)}, u32[]{:S(2)}) collective-permute-start(f32[136,512]{1,0:T(8,128)S(1)} %add.71), channel_id=1, source_target_pairs={{8,0},{16,8},{24,16},{32,24},{40,32},{48,40},{56,48},{64,56},{72,6... | collective-permute-start | bytes 835592 | tf_op jit(solution)/shard_map/ppermute | solution.py:22
  85.2 3.5 %collective-permute-done.5 = f32[136,512]{1,0:T(8,128)S(1)} collective-permute-done((f32[136,512]{1,0:T(8,128)S(1)}, f32[136,512]{1,0:T(8,128)S(1)}, u32[]{:S(2)}, u32[]{:S(2)}) %collective-permute-start.5) | collective-permute-done | bytes 278560 | tf_op jit(solution)/shard_map/ppermute | solution.py:22
  88.9 0.2 div.11
  89.2 11.4 %all_to_all.34 = bf16[8,16,512]{2,1,0:T(8,128)(2,1)S(1)} all-to-all(bf16[8,16,512]{2,1,0:T(8,128)(2,1)S(1)} %bitcast.36), channel_id=1, replica_groups=mesh['pool'=64,'tensor'=8] {'tensor'}, dimensions={0} | all-to-all | bytes 262144 | tf_op jit(solution)/shard_map/all_to_all | solution.py:196
  100.5 0.7 copy.32
  (38 shorter events, 0.8 us)
Async XLA Ops:
  0.0 12.0 %copy-start = (s32[64,64]{1,0:T(8,128)S(1)}, s32[64,64]{1,0:T(8,128)}, u32[]{:S(2)}) copy-start(s32[64,64]{1,0:T(8,128)} %param.12) | copy-start | bytes 49156
  0.0 1.0 copy-start.7
  0.0 1.0 copy-start.8
  1.7 16.7 %all-to-all-start = ((bf16[16,8,1024]{2,0,1:T(8,128)(2,1)}), bf16[16,8,1024]{2,0,1:T(8,128)(2,1)S(1)}, u32[]{:S(2)}, u32[]{:S(2)}) async-start(bf16[16,8,1024]{2,0,1:T(8,128)(2,1)} %pad_maximum_fusion), calls=%async_computation | async-start | bytes 524288 | tf_op jit(solution)/shard_map/all_to_all | solution.py:145
  12.0 1.0 %copy-start.1 = (s32[64]{0:T(128)S(1)}, s32[64]{0:T(128)}, u32[]{:S(2)}) copy-start(s32[64]{0:T(128)} %param.13) | copy-start | bytes 772
  18.4 12.2 %copy-start.3 = (bf16[128,512]{1,0:T(8,128)(2,1)}, bf16[128,512]{1,0:T(8,128)(2,1)S(1)}, u32[]{:S(2)}) copy-start(bf16[128,512]{1,0:T(8,128)(2,1)S(1)} %slice.24.q_ref) | copy-start | bytes 393220
  18.5 14.3 %collective-permute-start = (bf16[128,512]{1,0:T(8,128)(2,1)S(1)}, bf16[128,512]{1,0:T(8,128)(2,1)S(1)}, u32[]{:S(2)}, u32[]{:S(2)}) collective-permute-start(bf16[128,512]{1,0:T(8,128)(2,1)S(1)} %slice.24.q_ref), channel_id=1, source_target_pairs={{504,0},{0,8},{8,16},{16,24},{24,32},{32,40},{40,48},{48,56},{56,6... | collective-permute-start | bytes 393224 | tf_op jit(solution)/shard_map/ppermute | solution.py:22
  20.4 15.1 %collective-permute-start.1 = (bf16[128,512]{1,0:T(8,128)(2,1)S(1)}, bf16[128,512]{1,0:T(8,128)(2,1)S(1)}, u32[]{:S(2)}, u32[]{:S(2)}) collective-permute-start(bf16[128,512]{1,0:T(8,128)(2,1)S(1)} %slice.24.q_ref), channel_id=1, source_target_pairs={{496,0},{504,8},{0,16},{8,24},{16,32},{24,40},{32,48},{40,56},{48,... | collective-permute-start | bytes 393224 | tf_op jit(solution)/shard_map/ppermute | solution.py:22
  22.5 21.9 %collective-permute-start.2 = (bf16[128,512]{1,0:T(8,128)(2,1)S(1)}, bf16[128,512]{1,0:T(8,128)(2,1)S(1)}, u32[]{:S(2)}, u32[]{:S(2)}) collective-permute-start(bf16[128,512]{1,0:T(8,128)(2,1)S(1)} %slice.24.q_ref), channel_id=1, source_target_pairs={{488,0},{496,8},{504,16},{0,24},{8,32},{16,40},{24,48},{32,56},{40... | collective-permute-start | bytes 393224 | tf_op jit(solution)/shard_map/ppermute | solution.py:22
  32.7 24.4 %copy-start.4 = (bf16[128,512]{1,0:T(8,128)(2,1)}, bf16[128,512]{1,0:T(8,128)(2,1)S(1)}, u32[]{:S(2)}) copy-start(bf16[128,512]{1,0:T(8,128)(2,1)S(1)} %collective-permute-done.q_ref) | copy-start | bytes 393220
  35.4 21.7 %copy-start.5 = (bf16[128,512]{1,0:T(8,128)(2,1)}, bf16[128,512]{1,0:T(8,128)(2,1)S(1)}, u32[]{:S(2)}) copy-start(bf16[128,512]{1,0:T(8,128)(2,1)S(1)} %collective-permute-done.1.q_ref) | copy-start | bytes 393220
  44.4 0.7 copy-start.6
  57.1 9.0 %collective-permute-start.3 = (f32[136,512]{1,0:T(8,128)}, f32[136,512]{1,0:T(8,128)S(1)}, u32[]{:S(2)}, u32[]{:S(2)}) collective-permute-start(f32[136,512]{1,0:T(8,128)} %shard_map.74), channel_id=1, source_target_pairs={{8,0},{16,8},{24,16},{32,24},{40,32},{48,40},{56,48},{64,56},{72,6... | collective-permute-start | bytes 835592 | tf_op jit(solution)/shard_map/ppermute | solution.py:22
  67.2 9.6 %collective-permute-start.4 = (f32[136,512]{1,0:T(8,128)S(1)}, f32[136,512]{1,0:T(8,128)S(1)}, u32[]{:S(2)}, u32[]{:S(2)}) collective-permute-start(f32[136,512]{1,0:T(8,128)S(1)} %add.70), channel_id=1, source_target_pairs={{8,0},{16,8},{24,16},{32,24},{40,32},{48,40},{56,48},{64,56},{72,6... | collective-permute-start | bytes 835592 | tf_op jit(solution)/shard_map/ppermute | solution.py:22
  74.4 14.3 %copy-start.2 = (f32[136,512]{1,0:T(8,128)S(1)}, f32[136,512]{1,0:T(8,128)}, u32[]{:S(2)}) copy-start(f32[136,512]{1,0:T(8,128)} %shard_map.73) | copy-start | bytes 835588
  77.8 10.9 %collective-permute-start.5 = (f32[136,512]{1,0:T(8,128)S(1)}, f32[136,512]{1,0:T(8,128)S(1)}, u32[]{:S(2)}, u32[]{:S(2)}) collective-permute-start(f32[136,512]{1,0:T(8,128)S(1)} %add.71), channel_id=1, source_target_pairs={{8,0},{16,8},{24,16},{32,24},{40,32},{48,40},{56,48},{64,56},{72,6... | collective-permute-start | bytes 835592 | tf_op jit(solution)/shard_map/ppermute | solution.py:22

commit v6 on v5

--- a/solution.py
+++ b/solution.py
@@ -33,59 +33,60 @@
     group = QUERY_HEADS // KEY_VALUE_HEADS
     count = meta_ref[dist, 2, 0]
 
-    def copies(i, b):
+    def copies(i):
         s = meta_ref[dist, 0, i]
         return (
-            pltpu.make_async_copy(kp_hbm.at[s], kbuf.at[b], sem.at[0, b]),
-            pltpu.make_async_copy(vp_hbm.at[s], vbuf.at[b], sem.at[1, b]),
+            pltpu.make_async_copy(kp_hbm.at[s], kbuf.at[i], sem.at[0, i]),
+            pltpu.make_async_copy(vp_hbm.at[s], vbuf.at[i], sem.at[1, i]),
         )
 
-    @pl.when(count > 0)
-    def _():
-        for c in copies(0, 0):
+    def request(i, carry):
+        for c in copies(i):
             c.start()
+        return carry
+
+    lax.fori_loop(0, count, request, 0)
 
     out_ref[...] = jnp.zeros(out_ref.shape, jnp.float32)
     ones = jnp.ones((8, page_len), jnp.bfloat16)
+
+    stacked = [
+        jnp.concatenate(
+            [q_ref[:, (g * group + a) * HEAD_SIZE:(g * group + a + 1) * HEAD_SIZE] for a in range(group)],
+            axis=0,
+        )
+        for g in range(kv_local)
+    ]
 
     def add_block(k, v, visible):
         for g in range(kv_local):
             kg = k[:, g * HEAD_SIZE:(g + 1) * HEAD_SIZE]
             vg = v[:, g * HEAD_SIZE:(g + 1) * HEAD_SIZE]
+            s = lax.dot_general(
+                stacked[g], kg, (((1,), (1,)), ((), ())), preferred_element_type=jnp.float32
+            ) * SCORE_SCALE
+            w = jnp.where(visible, jnp.exp(SOFTCAP * jnp.tanh(s / SOFTCAP)), 0.0).astype(
+                jnp.bfloat16
+            )
+            pv = jnp.dot(w, vg, preferred_element_type=jnp.float32)
+            t = lax.dot_general(
+                ones, w, (((1,), (1,)), ((), ())), preferred_element_type=jnp.float32
+            )
             for a in range(group):
                 h = g * group + a
                 col = h * HEAD_SIZE
-                q = q_ref[:, col:col + HEAD_SIZE]
-                s = lax.dot_general(
-                    q, kg, (((1,), (1,)), ((), ())), preferred_element_type=jnp.float32
-                ) * SCORE_SCALE
-                w = jnp.where(visible, jnp.exp(SOFTCAP * jnp.tanh(s / SOFTCAP)), 0.0).astype(
-                    jnp.bfloat16
-                )
-                out_ref[:rows, col:col + HEAD_SIZE] += jnp.dot(
-                    w, vg, preferred_element_type=jnp.float32
-                )
-                t = lax.dot_general(
-                    ones, w, (((1,), (1,)), ((), ())), preferred_element_type=jnp.float32
-                )
-                out_ref[rows:rows + 8, h * rows:(h + 1) * rows] += t
-
-    key_pos = lax.broadcasted_iota(jnp.int32, (rows, page_len), 1)
+                out_ref[:rows, col:col + HEAD_SIZE] += pv[a * rows:(a + 1) * rows]
+            out_ref[rows:rows + 8, g * group * rows:(g + 1) * group * rows] += t
+
+    key_pos = lax.broadcasted_iota(jnp.int32, (group * rows, page_len), 1)
     if with_own:
-        q_pos = lax.broadcasted_iota(jnp.int32, (rows, page_len), 0)
+        q_pos = lax.broadcasted_iota(jnp.int32, (group * rows, page_len), 0) % rows
         add_block(kn_ref[...], vn_ref[...], key_pos <= q_pos)
 
     def slot(i, carry):
-        b = i % 2
-
-        @pl.when(i + 1 < count)
-        def _():
-            for c in copies(i + 1, 1 - b):
-                c.start()
-
-        for c in copies(i, b):
+        for c in copies(i):
             c.wait()
-        add_block(kbuf[b], vbuf[b], key_pos < meta_ref[dist, 1, i])
+        add_block(kbuf[i], vbuf[i], key_pos < meta_ref[dist, 1, i])
         return carry
 
     lax.fori_loop(0, count, slot, 0)
@@ -113,9 +114,9 @@
         + [vmem] * (2 if with_own else 0),
         out_specs=vmem,
         scratch_shapes=[
-            pltpu.VMEM((2, page_len, kv_width), kp.dtype),
-            pltpu.VMEM((2, page_len, kv_width), vp.dtype),
-            pltpu.SemaphoreType.DMA((2, 2)),
+            pltpu.VMEM((slots, page_len, kv_width), kp.dtype),
+            pltpu.VMEM((slots, page_len, kv_width), vp.dtype),
+            pltpu.SemaphoreType.DMA((2, slots)),
         ],
         cost_estimate=cost,
     )(*args)

time: 102 us -> 94.5 us (0.926)
  starting transfers between devices: 36.6 us -> 31.2 us
  waiting for transfers between devices: 26.5 us -> 21.9 us
  blocking collectives: 11.4 us -> 15 us
  Pallas kernels: 17.4 us -> 16.1 us
    ppermute x6, starting transfers between devices: 26.4 us -> 21 us  [shifted(): return lax.ppermute(block, axis, route)]
    ppermute x6, waiting for transfers between devices: 23 us -> 18.3 us  [shifted(): return lax.ppermute(block, axis, route)]
    all_to_all x1, blocking collectives: 11.4 us -> 15 us  [on_device(): lax.all_to_all(attended, 'tensor', split_axis=0, concat_axis=1, tiled=True)]
    pallas_call x4, Pallas kernels: 17.4 us -> 16.1 us  [attend(): pl.pallas_call(functools.partial(_attend_kernel, dist, with_own), out_sha...]
  transfers between devices with their start and end apart: 7 -> 7, of which waited for: 6 -> 5; matrix products, arithmetic and copies ran while one was open for 4% -> 4% of each run, Pallas kernels for 5% -> 13%
where the time goes in v6:
time: 94.5 us; the launch traced here: 93.6 us
  starting transfers between devices  31.2 us (33%)
  waiting for transfers between devices  21.9 us (23%)
  Pallas kernels  16.1 us (17%)
  blocking collectives  15 us (16%)
  local copies, waits for them, and re-layouts  4.6 us (5%)
  other arithmetic  4.46 us (5%)
    ppermute x6, starting transfers between devices, shifted(): return lax.ppermute(block, axis, route)  21 us
    ppermute x6, waiting for transfers between devices, shifted(): return lax.ppermute(block, axis, route)  18.3 us
    pallas_call x4, Pallas kernels, attend(): pl.pallas_call(functools.partial(_attend_kernel, dist, with_own), out_sha...  16.1 us
    all_to_all x1, blocking collectives, on_device(): lax.all_to_all(attended, 'tensor', split_axis=0, concat_axis=1, tiled=True)  15 us
    all_to_all x1, starting transfers between devices, on_device(): lax.all_to_all(packed, 'tensor', split_axis=1, concat_axis=0, tiled=True)  10.2 us
    all_to_all x1, waiting for transfers between devices, on_device(): lax.all_to_all(packed, 'tensor', split_axis=1, concat_axis=0, tiled=True)  3.52 us
    add x3, other arithmetic, on_device(): total = here + moved  2.02 us
  transfers between devices with their start and end apart: 7, of which 5 were waited for; matrix products, arithmetic and copies ran while one was open for 4% of the time, Pallas kernels for 13%

profile of v6, /device:TPU:1, one launch (start us, length us, event | category | flops | bytes accessed | tf_op | source)
XLA Modules:
  0.0 93.6 jit_solution(2920120695965201409)
XLA Ops:
  0.0 1.0 %copy.37 = bf16[2,8,8,512]{3,2,0,1:T(8,128)(2,1)S(1)} copy(bf16[2,8,8,512]{3,2,1,0:T(8,128)(2,1)} %bitcast.39) | data formatting | bytes 262144 | tf_op jit(solution)/shard_map/reshape | solution.py:140
  1.0 0.7 pad_maximum_fusion
  1.7 10.2 %all-to-all-start = ((bf16[16,8,1024]{2,0,1:T(8,128)(2,1)}), bf16[16,8,1024]{2,0,1:T(8,128)(2,1)S(1)}, u32[]{:S(2)}, u32[]{:S(2)}) async-start(bf16[16,8,1024]{2,0,1:T(8,128)(2,1)} %pad_maximum_fusion), calls=%async_computation | async-start | bytes 524288 | tf_op jit(solution)/shard_map/all_to_all | solution.py:146
  12.0 0.6 gather_fusion
  12.6 0.2 compare_reduce_fusion
  12.8 0.2 fusion.1
  13.0 0.6 gather_fusion.1
  13.8 0.2 reduce_window_sum.11
  14.0 0.1 convert_reduce_fusion
  14.3 0.6 pad_add_fusion.meta_ref
  14.9 3.5 %all-to-all-done = bf16[16,8,1024]{2,0,1:T(8,128)(2,1)S(1)} async-done(((bf16[16,8,1024]{2,0,1:T(8,128)(2,1)}), bf16[16,8,1024]{2,0,1:T(8,128)(2,1)S(1)}, u32[]{:S(2)}, u32[]{:S(2)}) %all-to-all-start) | async-done | bytes 262176 | tf_op jit(solution)/shard_map/all_to_all | solution.py:146
  18.5 1.9 %collective-permute-start = (bf16[128,512]{1,0:T(8,128)(2,1)S(1)}, bf16[128,512]{1,0:T(8,128)(2,1)S(1)}, u32[]{:S(2)}, u32[]{:S(2)}) collective-permute-start(bf16[128,512]{1,0:T(8,128)(2,1)S(1)} %slice.24.q_ref), channel_id=1, source_target_pairs={{504,0},{0,8},{8,16},{16,24},{24,32},{32,40},{40,48},{48,56},{56,6... | collective-permute-start | bytes 393224 | tf_op jit(solution)/shard_map/ppermute | solution.py:22
  20.4 2.1 %collective-permute-start.1 = (bf16[128,512]{1,0:T(8,128)(2,1)S(1)}, bf16[128,512]{1,0:T(8,128)(2,1)S(1)}, u32[]{:S(2)}, u32[]{:S(2)}) collective-permute-start(bf16[128,512]{1,0:T(8,128)(2,1)S(1)} %slice.24.q_ref), channel_id=1, source_target_pairs={{496,0},{504,8},{0,16},{8,24},{16,32},{24,40},{32,48},{40,56},{48,... | collective-permute-start | bytes 393224 | tf_op jit(solution)/shard_map/ppermute | solution.py:22
  22.5 7.5 %collective-permute-start.2 = (bf16[128,512]{1,0:T(8,128)(2,1)S(1)}, bf16[128,512]{1,0:T(8,128)(2,1)S(1)}, u32[]{:S(2)}, u32[]{:S(2)}) collective-permute-start(bf16[128,512]{1,0:T(8,128)(2,1)S(1)} %slice.24.q_ref), channel_id=1, source_target_pairs={{488,0},{496,8},{504,16},{0,24},{8,32},{16,40},{24,48},{32,56},{40... | collective-permute-start | bytes 393224 | tf_op jit(solution)/shard_map/ppermute | solution.py:22
  30.0 0.7 fusion.9
  30.7 4.9 %shard_map.73 = f32[136,512]{1,0:T(8,128)} custom-call(s32[4,3,16]{2,1,0:T(4,128)} %pad_add_fusion.meta_ref, bf16[128,512]{1,0:T(8,128)(2,1)} %copy-done.3, bf16[16,128,256]{2,1,0:T(8,128)(2,1)} %kp_hbm.7, bf16[16,128,256]{2,1,0:T(8,128)(2,1)} %vp_hbm.7, bf16[128,256]{1,0:T(8,128)(2,1)} %get-tuple-element.34.refs_0_, bf16[128,256]{1,0:T(8,128)(2,1)} %get-tuple-element.33.refs_1_), custom_call_target="tpu_custom_call" | custom-call | flops 167772160 | bytes 1064960 | tf_op jit(solution)/shard_map/pallas_call | solution.py:110
  35.7 8.8 %collective-permute-done.2.q_ref = bf16[128,512]{1,0:T(8,128)(2,1)S(1)} collective-permute-done((bf16[128,512]{1,0:T(8,128)(2,1)S(1)}, bf16[128,512]{1,0:T(8,128)(2,1)S(1)}, u32[]{:S(2)}, u32[]{:S(2)}) %collective-permute-start.2) | collective-permute-done | bytes 131104 | tf_op jit(solution)/shard_map/ppermute | solution.py:22
  44.4 0.6 copy-done.6
  45.1 3.5 %shard_map.74 = f32[136,512]{1,0:T(8,128)} custom-call(s32[4,3,16]{2,1,0:T(4,128)} %pad_add_fusion.meta_ref, bf16[128,512]{1,0:T(8,128)(2,1)} %copy-done.6, bf16[16,128,256]{2,1,0:T(8,128)(2,1)} %kp_hbm.7, bf16[16,128,256]{2,1,0:T(8,128)(2,1)} %vp_hbm.7), custom_call_target="tpu_custom_call" | custom-call | flops 134217728 | bytes 933888 | tf_op jit(solution)/shard_map/pallas_call | solution.py:110
  48.6 1.9 %collective-permute-start.3 = (f32[136,512]{1,0:T(8,128)}, f32[136,512]{1,0:T(8,128)S(1)}, u32[]{:S(2)}, u32[]{:S(2)}) collective-permute-start(f32[136,512]{1,0:T(8,128)} %shard_map.74), channel_id=1, source_target_pairs={{8,0},{16,8},{24,16},{32,24},{40,32},{48,40},{56,48},{64,56},{72,6... | collective-permute-start | bytes 835592 | tf_op jit(solution)/shard_map/ppermute | solution.py:22
  50.5 3.8 %shard_map.75 = f32[136,512]{1,0:T(8,128)} custom-call(s32[4,3,16]{2,1,0:T(4,128)} %pad_add_fusion.meta_ref, bf16[128,512]{1,0:T(8,128)(2,1)} %copy-done.5, bf16[16,128,256]{2,1,0:T(8,128)(2,1)} %kp_hbm.7, bf16[16,128,256]{2,1,0:T(8,128)(2,1)} %vp_hbm.7), custom_call_target="tpu_custom_call" | custom-call | flops 134217728 | bytes 933888 | tf_op jit(solution)/shard_map/pallas_call | solution.py:110
  54.4 4.5 %collective-permute-done.3 = f32[136,512]{1,0:T(8,128)S(1)} collective-permute-done((f32[136,512]{1,0:T(8,128)}, f32[136,512]{1,0:T(8,128)S(1)}, u32[]{:S(2)}, u32[]{:S(2)}) %collective-permute-start.3) | collective-permute-done | bytes 278560 | tf_op jit(solution)/shard_map/ppermute | solution.py:22
  58.9 1.0 %add.70 = f32[136,512]{1,0:T(8,128)S(1)} add(f32[136,512]{1,0:T(8,128)} %shard_map.75, f32[136,512]{1,0:T(8,128)S(1)} %collective-permute-done.3) | non-fusion elementwise | flops 69632 | bytes 835584 | tf_op jit(solution)/shard_map/add | solution.py:191
  59.9 2.4 %collective-permute-start.4 = (f32[136,512]{1,0:T(8,128)S(1)}, f32[136,512]{1,0:T(8,128)S(1)}, u32[]{:S(2)}, u32[]{:S(2)}) collective-permute-start(f32[136,512]{1,0:T(8,128)S(1)} %add.70), channel_id=1, source_target_pairs={{8,0},{16,8},{24,16},{32,24},{40,32},{48,40},{56,48},{64,56},{72,6... | collective-permute-start | bytes 835592 | tf_op jit(solution)/shard_map/ppermute | solution.py:22
  62.3 3.8 %shard_map.76 = f32[136,512]{1,0:T(8,128)} custom-call(s32[4,3,16]{2,1,0:T(4,128)} %pad_add_fusion.meta_ref, bf16[128,512]{1,0:T(8,128)(2,1)} %copy-done.4, bf16[16,128,256]{2,1,0:T(8,128)(2,1)} %kp_hbm.7, bf16[16,128,256]{2,1,0:T(8,128)(2,1)} %vp_hbm.7), custom_call_target="tpu_custom_call" | custom-call | flops 134217728 | bytes 933888 | tf_op jit(solution)/shard_map/pallas_call | solution.py:110
  66.2 1.6 %collective-permute-done.4 = f32[136,512]{1,0:T(8,128)S(1)} collective-permute-done((f32[136,512]{1,0:T(8,128)S(1)}, f32[136,512]{1,0:T(8,128)S(1)}, u32[]{:S(2)}, u32[]{:S(2)}) %collective-permute-start.4) | collective-permute-done | bytes 278560 | tf_op jit(solution)/shard_map/ppermute | solution.py:22
  67.8 1.0 %add.71 = f32[136,512]{1,0:T(8,128)S(1)} add(f32[136,512]{1,0:T(8,128)} %shard_map.76, f32[136,512]{1,0:T(8,128)S(1)} %collective-permute-done.4) | non-fusion elementwise | flops 69632 | bytes 835584 | tf_op jit(solution)/shard_map/add | solution.py:191
  68.8 5.2 %collective-permute-start.5 = (f32[136,512]{1,0:T(8,128)S(1)}, f32[136,512]{1,0:T(8,128)S(1)}, u32[]{:S(2)}, u32[]{:S(2)}) collective-permute-start(f32[136,512]{1,0:T(8,128)S(1)} %add.71), channel_id=1, source_target_pairs={{8,0},{16,8},{24,16},{32,24},{40,32},{48,40},{56,48},{64,56},{72,6... | collective-permute-start | bytes 835592 | tf_op jit(solution)/shard_map/ppermute | solution.py:22
  73.9 3.5 %collective-permute-done.5 = f32[136,512]{1,0:T(8,128)S(1)} collective-permute-done((f32[136,512]{1,0:T(8,128)S(1)}, f32[136,512]{1,0:T(8,128)S(1)}, u32[]{:S(2)}, u32[]{:S(2)}) %collective-permute-start.5) | collective-permute-done | bytes 278560 | tf_op jit(solution)/shard_map/ppermute | solution.py:22
  77.6 0.2 div.11
  77.9 15.0 %all_to_all.34 = bf16[8,16,512]{2,1,0:T(8,128)(2,1)S(1)} all-to-all(bf16[8,16,512]{2,1,0:T(8,128)(2,1)S(1)} %bitcast.36), channel_id=1, replica_groups=mesh['pool'=64,'tensor'=8] {'tensor'}, dimensions={0} | all-to-all | bytes 262144 | tf_op jit(solution)/shard_map/all_to_all | solution.py:197
  92.9 0.7 copy.32
  (38 shorter events, 0.7 us)
Async XLA Ops:
  0.0 12.0 %copy-start = (s32[64,64]{1,0:T(8,128)S(1)}, s32[64,64]{1,0:T(8,128)}, u32[]{:S(2)}) copy-start(s32[64,64]{1,0:T(8,128)} %param.12) | copy-start | bytes 49156
  0.0 1.0 %copy-start.7 = (bf16[16,2048]{1,0:T(8,128)(2,1)S(1)}, bf16[16,2048]{1,0:T(8,128)(2,1)}, u32[]{:S(2)}) copy-start(bf16[16,2048]{1,0:T(8,128)(2,1)} %param.9) | copy-start | bytes 196612
  0.0 1.0 %copy-start.8 = (bf16[16,2048]{1,0:T(8,128)(2,1)S(1)}, bf16[16,2048]{1,0:T(8,128)(2,1)}, u32[]{:S(2)}) copy-start(bf16[16,2048]{1,0:T(8,128)(2,1)} %param.8) | copy-start | bytes 196612
  1.7 16.7 %all-to-all-start = ((bf16[16,8,1024]{2,0,1:T(8,128)(2,1)}), bf16[16,8,1024]{2,0,1:T(8,128)(2,1)S(1)}, u32[]{:S(2)}, u32[]{:S(2)}) async-start(bf16[16,8,1024]{2,0,1:T(8,128)(2,1)} %pad_maximum_fusion), calls=%async_computation | async-start | bytes 524288 | tf_op jit(solution)/shard_map/all_to_all | solution.py:146
  12.0 1.0 %copy-start.1 = (s32[64]{0:T(128)S(1)}, s32[64]{0:T(128)}, u32[]{:S(2)}) copy-start(s32[64]{0:T(128)} %param.13) | copy-start | bytes 772
  18.4 12.2 %copy-start.3 = (bf16[128,512]{1,0:T(8,128)(2,1)}, bf16[128,512]{1,0:T(8,128)(2,1)S(1)}, u32[]{:S(2)}) copy-start(bf16[128,512]{1,0:T(8,128)(2,1)S(1)} %slice.24.q_ref) | copy-start | bytes 393220
  18.5 17.2 %collective-permute-start = (bf16[128,512]{1,0:T(8,128)(2,1)S(1)}, bf16[128,512]{1,0:T(8,128)(2,1)S(1)}, u32[]{:S(2)}, u32[]{:S(2)}) collective-permute-start(bf16[128,512]{1,0:T(8,128)(2,1)S(1)} %slice.24.q_ref), channel_id=1, source_target_pairs={{504,0},{0,8},{8,16},{16,24},{24,32},{32,40},{40,48},{48,56},{56,6... | collective-permute-start | bytes 393224 | tf_op jit(solution)/shard_map/ppermute | solution.py:22
  20.4 15.2 %collective-permute-start.1 = (bf16[128,512]{1,0:T(8,128)(2,1)S(1)}, bf16[128,512]{1,0:T(8,128)(2,1)S(1)}, u32[]{:S(2)}, u32[]{:S(2)}) collective-permute-start(bf16[128,512]{1,0:T(8,128)(2,1)S(1)} %slice.24.q_ref), channel_id=1, source_target_pairs={{496,0},{504,8},{0,16},{8,24},{16,32},{24,40},{32,48},{40,56},{48,... | collective-permute-start | bytes 393224 | tf_op jit(solution)/shard_map/ppermute | solution.py:22
  22.5 21.9 %collective-permute-start.2 = (bf16[128,512]{1,0:T(8,128)(2,1)S(1)}, bf16[128,512]{1,0:T(8,128)(2,1)S(1)}, u32[]{:S(2)}, u32[]{:S(2)}) collective-permute-start(bf16[128,512]{1,0:T(8,128)(2,1)S(1)} %slice.24.q_ref), channel_id=1, source_target_pairs={{488,0},{496,8},{504,16},{0,24},{8,32},{16,40},{24,48},{32,56},{40... | collective-permute-start | bytes 393224 | tf_op jit(solution)/shard_map/ppermute | solution.py:22
  35.6 12.9 %copy-start.4 = (bf16[128,512]{1,0:T(8,128)(2,1)}, bf16[128,512]{1,0:T(8,128)(2,1)S(1)}, u32[]{:S(2)}) copy-start(bf16[128,512]{1,0:T(8,128)(2,1)S(1)} %collective-permute-done.q_ref) | copy-start | bytes 393220
  35.6 12.9 %copy-start.5 = (bf16[128,512]{1,0:T(8,128)(2,1)}, bf16[128,512]{1,0:T(8,128)(2,1)S(1)}, u32[]{:S(2)}) copy-start(bf16[128,512]{1,0:T(8,128)(2,1)S(1)} %collective-permute-done.1.q_ref) | copy-start | bytes 393220
  44.4 0.7 copy-start.6
  48.6 10.3 %collective-permute-start.3 = (f32[136,512]{1,0:T(8,128)}, f32[136,512]{1,0:T(8,128)S(1)}, u32[]{:S(2)}, u32[]{:S(2)}) collective-permute-start(f32[136,512]{1,0:T(8,128)} %shard_map.74), channel_id=1, source_target_pairs={{8,0},{16,8},{24,16},{32,24},{40,32},{48,40},{56,48},{64,56},{72,6... | collective-permute-start | bytes 835592 | tf_op jit(solution)/shard_map/ppermute | solution.py:22
  59.9 7.9 %collective-permute-start.4 = (f32[136,512]{1,0:T(8,128)S(1)}, f32[136,512]{1,0:T(8,128)S(1)}, u32[]{:S(2)}, u32[]{:S(2)}) collective-permute-start(f32[136,512]{1,0:T(8,128)S(1)} %add.70), channel_id=1, source_target_pairs={{8,0},{16,8},{24,16},{32,24},{40,32},{48,40},{56,48},{64,56},{72,6... | collective-permute-start | bytes 835592 | tf_op jit(solution)/shard_map/ppermute | solution.py:22
  66.2 11.2 %copy-start.2 = (f32[136,512]{1,0:T(8,128)S(1)}, f32[136,512]{1,0:T(8,128)}, u32[]{:S(2)}) copy-start(f32[136,512]{1,0:T(8,128)} %shard_map.73) | copy-start | bytes 835588
  68.8 8.6 %collective-permute-start.5 = (f32[136,512]{1,0:T(8,128)S(1)}, f32[136,512]{1,0:T(8,128)S(1)}, u32[]{:S(2)}, u32[]{:S(2)}) collective-permute-start(f32[136,512]{1,0:T(8,128)S(1)} %add.71), channel_id=1, source_target_pairs={{8,0},{16,8},{24,16},{32,24},{40,32},{48,40},{56,48},{64,56},{72,6... | collective-permute-start | bytes 835592 | tf_op jit(solution)/shard_map/ppermute | solution.py:22

commit v7 on v6

--- a/solution.py
+++ b/solution.py
@@ -22,19 +22,22 @@
     return lax.ppermute(block, axis, route)
 
 
-def _attend_kernel(dist, with_own, meta_ref, q_ref, kp_hbm, vp_hbm, *refs):
+def _attend_kernel(group_index, n_dist, with_own, meta_ref, *refs):
+    q_refs = refs[:n_dist]
+    kp_hbm, vp_hbm = refs[n_dist], refs[n_dist + 1]
+    refs = refs[n_dist + 2:]
     if with_own:
         kn_ref, vn_ref = refs[0], refs[1]
         refs = refs[2:]
-    out_ref, kbuf, vbuf, sem = refs
-    rows = q_ref.shape[0]
+    out_ref, stacked, kbuf, vbuf, sem = refs
+    rows = q_refs[0].shape[0]
     page_len, kv_width = kbuf.shape[1], kbuf.shape[2]
     kv_local = kv_width // HEAD_SIZE
     group = QUERY_HEADS // KEY_VALUE_HEADS
-    count = meta_ref[dist, 2, 0]
+    count = meta_ref[group_index, 3, 0]
 
     def copies(i):
-        s = meta_ref[dist, 0, i]
+        s = meta_ref[group_index, 0, i]
         return (
             pltpu.make_async_copy(kp_hbm.at[s], kbuf.at[i], sem.at[0, i]),
             pltpu.make_async_copy(vp_hbm.at[s], vbuf.at[i], sem.at[1, i]),
@@ -47,23 +50,20 @@
 
     lax.fori_loop(0, count, request, 0)
 
+    for j in range(n_dist):
+        for g in range(kv_local):
+            for a in range(group):
+                col = (g * group + a) * HEAD_SIZE
+                stacked[j, g, a * rows:(a + 1) * rows, :] = q_refs[j][:, col:col + HEAD_SIZE]
     out_ref[...] = jnp.zeros(out_ref.shape, jnp.float32)
     ones = jnp.ones((8, page_len), jnp.bfloat16)
 
-    stacked = [
-        jnp.concatenate(
-            [q_ref[:, (g * group + a) * HEAD_SIZE:(g * group + a + 1) * HEAD_SIZE] for a in range(group)],
-            axis=0,
-        )
-        for g in range(kv_local)
-    ]
-
-    def add_block(k, v, visible):
+    def add_block(j, k, v, visible):
         for g in range(kv_local):
             kg = k[:, g * HEAD_SIZE:(g + 1) * HEAD_SIZE]
             vg = v[:, g * HEAD_SIZE:(g + 1) * HEAD_SIZE]
             s = lax.dot_general(
-                stacked[g], kg, (((1,), (1,)), ((), ())), preferred_element_type=jnp.float32
+                stacked[j, g], kg, (((1,), (1,)), ((), ())), preferred_element_type=jnp.float32
             ) * SCORE_SCALE
             w = jnp.where(visible, jnp.exp(SOFTCAP * jnp.tanh(s / SOFTCAP)), 0.0).astype(
                 jnp.bfloat16
@@ -73,47 +73,52 @@
                 ones, w, (((1,), (1,)), ((), ())), preferred_element_type=jnp.float32
             )
             for a in range(group):
-                h = g * group + a
-                col = h * HEAD_SIZE
-                out_ref[:rows, col:col + HEAD_SIZE] += pv[a * rows:(a + 1) * rows]
-            out_ref[rows:rows + 8, g * group * rows:(g + 1) * group * rows] += t
+                col = (g * group + a) * HEAD_SIZE
+                out_ref[j, :rows, col:col + HEAD_SIZE] += pv[a * rows:(a + 1) * rows]
+            out_ref[j, rows:rows + 8, g * group * rows:(g + 1) * group * rows] += t
 
     key_pos = lax.broadcasted_iota(jnp.int32, (group * rows, page_len), 1)
     if with_own:
         q_pos = lax.broadcasted_iota(jnp.int32, (group * rows, page_len), 0) % rows
-        add_block(kn_ref[...], vn_ref[...], key_pos <= q_pos)
+        add_block(0, kn_ref[...], vn_ref[...], key_pos <= q_pos)
 
     def slot(i, carry):
         for c in copies(i):
             c.wait()
-        add_block(kbuf[i], vbuf[i], key_pos < meta_ref[dist, 1, i])
+        add_block(
+            meta_ref[group_index, 2, i], kbuf[i], vbuf[i], key_pos < meta_ref[group_index, 1, i]
+        )
         return carry
 
     lax.fori_loop(0, count, slot, 0)
 
 
-def attend(dist, meta, q, kp, vp, kn=None, vn=None):
+def attend(group_index, meta, qs, kp, vp, kn=None, vn=None):
     with_own = kn is not None
-    rows, width = q.shape
+    n_dist = len(qs)
+    rows, width = qs[0].shape
     slots, page_len, kv_width = kp.shape
-    args = [meta, q, kp, vp] + ([kn, vn] if with_own else [])
-    blocks = slots // SPAN + (1 if with_own else 0)
+    args = [meta, *qs, kp, vp] + ([kn, vn] if with_own else [])
+    blocks = n_dist * slots // SPAN + (1 if with_own else 0)
     heads = width // HEAD_SIZE
     cost = pl.CostEstimate(
         flops=blocks * heads * rows * page_len * HEAD_SIZE * 4,
         transcendentals=blocks * heads * rows * page_len * 2,
-        bytes_accessed=int(q.size) * 2 + blocks * page_len * kv_width * 4
-        + (rows + 8) * width * 4,
+        bytes_accessed=n_dist * int(qs[0].size) * 2 + blocks * page_len * kv_width * 4
+        + n_dist * (rows + 8) * width * 4,
     )
     vmem = pl.BlockSpec(memory_space=pltpu.VMEM)
     hbm = pl.BlockSpec(memory_space=pl.ANY)
+    group = QUERY_HEADS // KEY_VALUE_HEADS
+    kv_local = kv_width // HEAD_SIZE
     return pl.pallas_call(
-        functools.partial(_attend_kernel, dist, with_own),
-        out_shape=jax.ShapeDtypeStruct((rows + 8, width), jnp.float32),
-        in_specs=[pl.BlockSpec(memory_space=pltpu.SMEM), vmem, hbm, hbm]
+        functools.partial(_attend_kernel, group_index, n_dist, with_own),
+        out_shape=jax.ShapeDtypeStruct((n_dist, rows + 8, width), jnp.float32),
+        in_specs=[pl.BlockSpec(memory_space=pltpu.SMEM)] + [vmem] * n_dist + [hbm, hbm]
         + [vmem] * (2 if with_own else 0),
         out_specs=vmem,
         scratch_shapes=[
+            pltpu.VMEM((n_dist, kv_local, group * rows, HEAD_SIZE), qs[0].dtype),
             pltpu.VMEM((slots, page_len, kv_width), kp.dtype),
             pltpu.VMEM((slots, page_len, kv_width), vp.dtype),
             pltpu.SemaphoreType.DMA((2, slots)),
@@ -167,28 +172,30 @@
     owner_len = jnp.take(lengths, owners)
     slot_len = jnp.sum(jnp.where(owner_hot, owner_len[:, None], 0), axis=0)
     limit = jnp.clip(slot_len - page_index * page_len, 0, page_len)
-    wanted = (distance[None, :] == jnp.arange(SPAN, dtype=jnp.int32)[:, None]) & (limit > 0)
-    rank = jnp.cumsum(wanted.astype(jnp.int32), axis=1) - 1
-    place = wanted[:, :, None] & (rank[:, :, None] == jnp.arange(slots_dev, dtype=jnp.int32))
-    order = jnp.sum(jnp.where(place, jnp.arange(slots_dev, dtype=jnp.int32)[None, :, None], 0), axis=1)
-    order_limit = jnp.sum(jnp.where(place, limit[None, :, None], 0), axis=1)
-    count = jnp.broadcast_to(jnp.sum(wanted.astype(jnp.int32), axis=1, keepdims=True), (SPAN, slots_dev))
-    meta = jnp.stack([order, order_limit, count], axis=1).astype(jnp.int32)
+    groups = [(0,), tuple(range(1, SPAN))]
+    slot_ids = jnp.arange(slots_dev, dtype=jnp.int32)
+    rows_of = []
+    for dists in groups:
+        wanted = (distance >= dists[0]) & (distance <= dists[-1]) & (limit > 0)
+        rank = jnp.cumsum(wanted.astype(jnp.int32)) - 1
+        place = wanted[:, None] & (rank[:, None] == slot_ids[None, :])
+        pick = lambda values: jnp.sum(jnp.where(place, values[:, None], 0), axis=0)
+        rows_of.append(jnp.stack([
+            pick(slot_ids),
+            pick(limit),
+            pick(distance - dists[0]),
+            jnp.broadcast_to(jnp.sum(wanted.astype(jnp.int32)), (slots_dev,)),
+        ]))
+    meta = jnp.stack(rows_of).astype(jnp.int32)
 
     received = [shifted(q_own, "pool", offset) for offset in range(1, SPAN)]
-    part_own = attend(0, meta, q_own, cached_key_pages, cached_value_pages, k_new, v_new)
+    part_own = attend(0, meta, [q_own], cached_key_pages, cached_value_pages, k_new, v_new)[0]
     *received, part_own = lax.optimization_barrier((*received, part_own))
-    received = [q_own] + received
-
-    def part(offset):
-        return attend(offset, meta, received[offset], cached_key_pages, cached_value_pages)
-
-    total = part(SPAN - 1)
+    parts = [part_own] + list(attend(1, meta, received, cached_key_pages, cached_value_pages))
+
+    total = parts[SPAN - 1]
     for offset in range(SPAN - 2, -1, -1):
-        moved = shifted(total, "pool", -1)
-        here = part(offset) if offset > 0 else part_own
-        moved, here = lax.optimization_barrier((moved, here))
-        total = here + moved
+        total = parts[offset] + shifted(total, "pool", -1)
     heads = q_width // HEAD_SIZE
     numerator = total[:rows].reshape(rows, heads, HEAD_SIZE)
     totals = total[rows, : heads * rows].reshape(heads, rows)

time: 94.5 us -> 100 us (1.058)
  starting transfers between devices: 31.2 us -> 38.6 us
  Pallas kernels: 16.1 us -> 11.6 us
  local copies, waits for them, and re-layouts: 4.6 us -> 7.05 us
  blocking collectives: 15 us -> 12.7 us
  waiting for transfers between devices: 21.9 us -> 23.5 us
  other arithmetic: 4.46 us -> 5.79 us
    ppermute x6, starting transfers between devices: 21 us -> 28.5 us  [shifted(): return lax.ppermute(block, axis, route)]
    pallas_call x4 -> x2, Pallas kernels: 16.1 us -> 11.6 us  [attend(): pl.pallas_call(functools.partial(_attend_kernel, group_index, n_dist, wit...]
    ppermute x6, waiting for transfers between devices: 18.3 us -> 22.8 us  [shifted(): return lax.ppermute(block, axis, route)]
    all_to_all x1, waiting for transfers between devices: 3.52 us -> 0.7 us  [on_device(): lax.all_to_all(packed, 'tensor', split_axis=1, concat_axis=0, tiled=True)]
    all_to_all x1, blocking collectives: 15 us -> 12.7 us  [on_device(): lax.all_to_all(attended, 'tensor', split_axis=0, concat_axis=1, tiled=True)]
    another operation x1 -> x3, local copies, waits for them, and re-layouts: 0.07 us -> 2.39 us  [the longest x2 1.41 us: on_device(): jnp.stack([pick(slot_ids), pick(limit), pick(distance - dists[0]), jnp.br...]
    reduce_sum x2 -> x3, other arithmetic: 0.22 us -> 1.44 us  [the longest x2 1.33 us: on_device(): jnp.sum(wanted.astype(jnp.int32))]
  transfers between devices with their start and end apart: 7 -> 7, of which waited for: 5 -> 6; matrix products, arithmetic and copies ran while one was open for 4% -> 6% of each run, Pallas kernels for 13% -> 5%
where the time goes in v7:
time: 100 us; the launch traced here: 99.5 us
  starting transfers between devices  38.6 us (39%)
  waiting for transfers between devices  23.5 us (24%)
  blocking collectives  12.7 us (13%)
  Pallas kernels  11.6 us (12%)
  local copies, waits for them, and re-layouts  7.05 us (7%)
  other arithmetic  5.79 us (6%)
    ppermute x6, starting transfers between devices, shifted(): return lax.ppermute(block, axis, route)  28.5 us
    ppermute x6, waiting for transfers between devices, shifted(): return lax.ppermute(block, axis, route)  22.8 us
    all_to_all x1, blocking collectives, on_device(): lax.all_to_all(attended, 'tensor', split_axis=0, concat_axis=1, tiled=True)  12.7 us
    pallas_call x2, Pallas kernels, attend(): pl.pallas_call(functools.partial(_attend_kernel, group_index, n_dist, wit...  11.6 us
    all_to_all x1, starting transfers between devices, on_device(): lax.all_to_all(packed, 'tensor', split_axis=1, concat_axis=0, tiled=True)  10.2 us
    add x3, other arithmetic, on_device(): total = parts[offset] + shifted(total, 'pool', -1)  2.04 us
  transfers between devices with their start and end apart: 7, of which 6 were waited for; matrix products, arithmetic and copies ran while one was open for 6% of the time, Pallas kernels for 5%

profile of v7, /device:TPU:1, one launch (start us, length us, event | category | flops | bytes accessed | tf_op | source)
XLA Modules:
  0.0 99.5 jit_solution(15475168898970640727)
XLA Ops:
  0.0 1.0 copy.37
  1.0 0.7 pad_maximum_fusion
  1.7 10.2 %all-to-all-start = ((bf16[16,8,1024]{2,0,1:T(8,128)(2,1)}), bf16[16,8,1024]{2,0,1:T(8,128)(2,1)S(1)}, u32[]{:S(2)}, u32[]{:S(2)}) async-start(bf16[16,8,1024]{2,0,1:T(8,128)(2,1)} %pad_maximum_fusion), calls=%async_computation | async-start | bytes 524288 | tf_op jit(solution)/shard_map/all_to_all | solution.py:151
  12.0 0.6 gather_fusion
  12.8 0.2 compare_reduce_fusion
  13.0 0.6 gather_fusion.1
  13.8 0.6 convert_reduce_fusion.1
  14.4 0.7 convert_reduce_fusion
  15.1 0.7 pad.9.clone
  15.8 0.7 pad.5.clone
  17.1 0.6 pad_add_fusion.meta_ref
  17.7 0.7 all-to-all-done
  18.5 1.9 %collective-permute-start.2 = (bf16[128,512]{1,0:T(8,128)(2,1)S(1)}, bf16[128,512]{1,0:T(8,128)(2,1)S(1)}, u32[]{:S(2)}, u32[]{:S(2)}) collective-permute-start(bf16[128,512]{1,0:T(8,128)(2,1)S(1)} %slice.24.refs_0_), channel_id=1, source_target_pairs={{488,0},{496,8},{504,16},{0,24},{8,32},{16,40},{24,48},{32,56},{40... | collective-permute-start | bytes 393224 | tf_op jit(solution)/shard_map/ppermute | solution.py:22
  20.4 6.0 %collective-permute-start.1 = (bf16[128,512]{1,0:T(8,128)(2,1)S(1)}, bf16[128,512]{1,0:T(8,128)(2,1)S(1)}, u32[]{:S(2)}, u32[]{:S(2)}) collective-permute-start(bf16[128,512]{1,0:T(8,128)(2,1)S(1)} %slice.24.refs_0_), channel_id=1, source_target_pairs={{496,0},{504,8},{0,16},{8,24},{16,32},{24,40},{32,48},{40,56},{48,... | collective-permute-start | bytes 393224 | tf_op jit(solution)/shard_map/ppermute | solution.py:22
  26.4 3.5 %collective-permute-start = (bf16[128,512]{1,0:T(8,128)(2,1)S(1)}, bf16[128,512]{1,0:T(8,128)(2,1)S(1)}, u32[]{:S(2)}, u32[]{:S(2)}) collective-permute-start(bf16[128,512]{1,0:T(8,128)(2,1)S(1)} %slice.24.refs_0_), channel_id=1, source_target_pairs={{504,0},{0,8},{8,16},{16,24},{24,32},{32,40},{40,48},{48,56},{56,6... | collective-permute-start | bytes 393224 | tf_op jit(solution)/shard_map/ppermute | solution.py:22
  30.0 0.6 fusion.9
  30.6 5.3 %shard_map.73 = f32[1,136,512]{2,1,0:T(8,128)} custom-call(s32[2,4,16]{2,1,0:T(4,128)} %pad_add_fusion.meta_ref, bf16[128,512]{1,0:T(8,128)(2,1)} %copy-done.3, bf16[16,128,256]{2,1,0:T(8,128)(2,1)} %refs_3_.1, bf16[16,128,256]{2,1,0:T(8,128)(2,1)} %refs_4_.1, bf16[128,256]{1,0:T(8,128)(2,1)} %get-tuple-element.27.refs_3_, ...), custom_call_target="tpu_custom_call" | custom-call | flops 167772160 | bytes 1064960 | tf_op jit(solution)/shard_map/pallas_call | solution.py:114
  36.0 6.5 %collective-permute-done.1.refs_1_ = bf16[128,512]{1,0:T(8,128)(2,1)S(1)} collective-permute-done((bf16[128,512]{1,0:T(8,128)(2,1)S(1)}, bf16[128,512]{1,0:T(8,128)(2,1)S(1)}, u32[]{:S(2)}, u32[]{:S(2)}) %collective-permute-start.1) | collective-permute-done | bytes 131104 | tf_op jit(solution)/shard_map/ppermute | solution.py:22
  42.5 2.7 %collective-permute-done.refs_0_ = bf16[128,512]{1,0:T(8,128)(2,1)S(1)} collective-permute-done((bf16[128,512]{1,0:T(8,128)(2,1)S(1)}, bf16[128,512]{1,0:T(8,128)(2,1)S(1)}, u32[]{:S(2)}, u32[]{:S(2)}) %collective-permute-start) | collective-permute-done | bytes 131104 | tf_op jit(solution)/shard_map/ppermute | solution.py:22
  45.2 0.6 copy-done.6
  45.8 6.3 %shard_map.74 = f32[3,136,512]{2,1,0:T(8,128)} custom-call(s32[2,4,16]{2,1,0:T(4,128)} %pad_add_fusion.meta_ref, bf16[128,512]{1,0:T(8,128)(2,1)} %copy-done.6, bf16[128,512]{1,0:T(8,128)(2,1)} %copy-done.5, bf16[128,512]{1,0:T(8,128)(2,1)} %copy-done.4, bf16[16,128,256]{2,1,0:T(8,128)(2,1)} %refs_3_.1, bf16[16,128,256]{2,1,0:T(8,128)(2,1)} %refs_4_.1), custom_call_target="tpu_custom_call" | custom-call | flops 402653184 | bytes 2801664 | tf_op jit(solution)/shard_map/pallas_call | solution.py:114
  52.1 1.0 slice_bitcast_fusion
  53.1 3.0 %collective-permute-start.3 = (f32[136,512]{1,0:T(8,128)S(1)}, f32[136,512]{1,0:T(8,128)S(1)}, u32[]{:S(2)}, u32[]{:S(2)}) collective-permute-start(f32[136,512]{1,0:T(8,128)S(1)} %slice_bitcast_fusion), channel_id=1, source_target_pairs={{8,0},{16,8},{24,16},{32,24},{40,32},{48,40},{56,48},{64,56},{72,6... | collective-permute-start | bytes 835592 | tf_op jit(solution)/shard_map/ppermute | solution.py:22
  56.1 6.0 %collective-permute-done.3 = f32[136,512]{1,0:T(8,128)S(1)} collective-permute-done((f32[136,512]{1,0:T(8,128)S(1)}, f32[136,512]{1,0:T(8,128)S(1)}, u32[]{:S(2)}, u32[]{:S(2)}) %collective-permute-start.3) | collective-permute-done | bytes 278560 | tf_op jit(solution)/shard_map/ppermute | solution.py:22
  62.2 1.0 %fusion = f32[136,512]{1,0:T(8,128)S(1)} fusion(f32[136,512]{1,0:T(8,128)S(1)} %collective-permute-done.3, f32[3,136,512]{2,1,0:T(8,128)} %shard_map.74), kind=kLoop, calls=%fused_computation.4 | loop fusion | flops 69632 | bytes 835584 | tf_op jit(solution)/shard_map/add | solution.py:198
  63.2 6.5 %collective-permute-start.4 = (f32[136,512]{1,0:T(8,128)S(1)}, f32[136,512]{1,0:T(8,128)S(1)}, u32[]{:S(2)}, u32[]{:S(2)}) collective-permute-start(f32[136,512]{1,0:T(8,128)S(1)} %fusion), channel_id=1, source_target_pairs={{8,0},{16,8},{24,16},{32,24},{40,32},{48,40},{56,48},{64,56},{72,6... | collective-permute-start | bytes 835592 | tf_op jit(solution)/shard_map/ppermute | solution.py:22
  69.7 4.1 %collective-permute-done.4 = f32[136,512]{1,0:T(8,128)S(1)} collective-permute-done((f32[136,512]{1,0:T(8,128)S(1)}, f32[136,512]{1,0:T(8,128)S(1)}, u32[]{:S(2)}, u32[]{:S(2)}) %collective-permute-start.4) | collective-permute-done | bytes 278560 | tf_op jit(solution)/shard_map/ppermute | solution.py:22
  73.7 1.0 %fusion.1 = f32[136,512]{1,0:T(8,128)S(1)} fusion(f32[136,512]{1,0:T(8,128)S(1)} %collective-permute-done.4, f32[3,136,512]{2,1,0:T(8,128)} %shard_map.74), kind=kLoop, calls=%fused_computation.6 | loop fusion | flops 69632 | bytes 835584 | tf_op jit(solution)/shard_map/add | solution.py:198
  74.7 7.4 %collective-permute-start.5 = (f32[136,512]{1,0:T(8,128)S(1)}, f32[136,512]{1,0:T(8,128)S(1)}, u32[]{:S(2)}, u32[]{:S(2)}) collective-permute-start(f32[136,512]{1,0:T(8,128)S(1)} %fusion.1), channel_id=1, source_target_pairs={{8,0},{16,8},{24,16},{32,24},{40,32},{48,40},{56,48},{64,56},{72,6... | collective-permute-start | bytes 835592 | tf_op jit(solution)/shard_map/ppermute | solution.py:22
  82.2 3.5 %collective-permute-done.5 = f32[136,512]{1,0:T(8,128)S(1)} collective-permute-done((f32[136,512]{1,0:T(8,128)S(1)}, f32[136,512]{1,0:T(8,128)S(1)}, u32[]{:S(2)}, u32[]{:S(2)}) %collective-permute-start.5) | collective-permute-done | bytes 278560 | tf_op jit(solution)/shard_map/ppermute | solution.py:22
  86.1 12.7 %all_to_all.34 = bf16[8,16,512]{2,1,0:T(8,128)(2,1)S(1)} all-to-all(bf16[8,16,512]{2,1,0:T(8,128)(2,1)S(1)} %bitcast.58), channel_id=1, replica_groups=mesh['pool'=64,'tensor'=8] {'tensor'}, dimensions={0} | all-to-all | bytes 262144 | tf_op jit(solution)/shard_map/all_to_all | solution.py:204
  98.8 0.7 copy.32
  (44 shorter events, 1.5 us)
Async XLA Ops:
  0.0 12.0 %copy-start = (s32[64,64]{1,0:T(8,128)S(1)}, s32[64,64]{1,0:T(8,128)}, u32[]{:S(2)}) copy-start(s32[64,64]{1,0:T(8,128)} %param.12) | copy-start | bytes 49156
  0.0 1.0 copy-start.7
  0.0 1.0 copy-start.8
  1.7 16.7 %all-to-all-start = ((bf16[16,8,1024]{2,0,1:T(8,128)(2,1)}), bf16[16,8,1024]{2,0,1:T(8,128)(2,1)S(1)}, u32[]{:S(2)}, u32[]{:S(2)}) async-start(bf16[16,8,1024]{2,0,1:T(8,128)(2,1)} %pad_maximum_fusion), calls=%async_computation | async-start | bytes 524288 | tf_op jit(solution)/shard_map/all_to_all | solution.py:151
  12.0 1.0 %copy-start.1 = (s32[64]{0:T(128)S(1)}, s32[64]{0:T(128)}, u32[]{:S(2)}) copy-start(s32[64]{0:T(128)} %param.13) | copy-start | bytes 772
  18.4 12.2 %copy-start.3 = (bf16[128,512]{1,0:T(8,128)(2,1)}, bf16[128,512]{1,0:T(8,128)(2,1)S(1)}, u32[]{:S(2)}) copy-start(bf16[128,512]{1,0:T(8,128)(2,1)S(1)} %slice.24.refs_0_) | copy-start | bytes 393220
  18.5 17.5 %collective-permute-start.2 = (bf16[128,512]{1,0:T(8,128)(2,1)S(1)}, bf16[128,512]{1,0:T(8,128)(2,1)S(1)}, u32[]{:S(2)}, u32[]{:S(2)}) collective-permute-start(bf16[128,512]{1,0:T(8,128)(2,1)S(1)} %slice.24.refs_0_), channel_id=1, source_target_pairs={{488,0},{496,8},{504,16},{0,24},{8,32},{16,40},{24,48},{32,56},{40... | collective-permute-start | bytes 393224 | tf_op jit(solution)/shard_map/ppermute | solution.py:22
  20.4 22.1 %collective-permute-start.1 = (bf16[128,512]{1,0:T(8,128)(2,1)S(1)}, bf16[128,512]{1,0:T(8,128)(2,1)S(1)}, u32[]{:S(2)}, u32[]{:S(2)}) collective-permute-start(bf16[128,512]{1,0:T(8,128)(2,1)S(1)} %slice.24.refs_0_), channel_id=1, source_target_pairs={{496,0},{504,8},{0,16},{8,24},{16,32},{24,40},{32,48},{40,56},{48,... | collective-permute-start | bytes 393224 | tf_op jit(solution)/shard_map/ppermute | solution.py:22
  26.4 18.7 %collective-permute-start = (bf16[128,512]{1,0:T(8,128)(2,1)S(1)}, bf16[128,512]{1,0:T(8,128)(2,1)S(1)}, u32[]{:S(2)}, u32[]{:S(2)}) collective-permute-start(bf16[128,512]{1,0:T(8,128)(2,1)S(1)} %slice.24.refs_0_), channel_id=1, source_target_pairs={{504,0},{0,8},{8,16},{16,24},{24,32},{32,40},{40,48},{48,56},{56,6... | collective-permute-start | bytes 393224 | tf_op jit(solution)/shard_map/ppermute | solution.py:22
  36.0 9.2 %copy-start.4 = (bf16[128,512]{1,0:T(8,128)(2,1)}, bf16[128,512]{1,0:T(8,128)(2,1)S(1)}, u32[]{:S(2)}) copy-start(bf16[128,512]{1,0:T(8,128)(2,1)S(1)} %collective-permute-done.2.refs_2_) | copy-start | bytes 393220
  42.5 2.7 %copy-start.5 = (bf16[128,512]{1,0:T(8,128)(2,1)}, bf16[128,512]{1,0:T(8,128)(2,1)S(1)}, u32[]{:S(2)}) copy-start(bf16[128,512]{1,0:T(8,128)(2,1)S(1)} %collective-permute-done.1.refs_1_) | copy-start | bytes 393220
  45.1 0.7 copy-start.6
  53.1 9.1 %collective-permute-start.3 = (f32[136,512]{1,0:T(8,128)S(1)}, f32[136,512]{1,0:T(8,128)S(1)}, u32[]{:S(2)}, u32[]{:S(2)}) collective-permute-start(f32[136,512]{1,0:T(8,128)S(1)} %slice_bitcast_fusion), channel_id=1, source_target_pairs={{8,0},{16,8},{24,16},{32,24},{40,32},{48,40},{56,48},{64,56},{72,6... | collective-permute-start | bytes 835592 | tf_op jit(solution)/shard_map/ppermute | solution.py:22
  63.2 22.5 %copy-start.2 = (f32[1,136,512]{2,1,0:T(8,128)S(1)}, f32[1,136,512]{2,1,0:T(8,128)}, u32[]{:S(2)}) copy-start(f32[1,136,512]{2,1,0:T(8,128)} %shard_map.73) | copy-start | bytes 835588
  63.2 10.5 %collective-permute-start.4 = (f32[136,512]{1,0:T(8,128)S(1)}, f32[136,512]{1,0:T(8,128)S(1)}, u32[]{:S(2)}, u32[]{:S(2)}) collective-permute-start(f32[136,512]{1,0:T(8,128)S(1)} %fusion), channel_id=1, source_target_pairs={{8,0},{16,8},{24,16},{32,24},{40,32},{48,40},{56,48},{64,56},{72,6... | collective-permute-start | bytes 835592 | tf_op jit(solution)/shard_map/ppermute | solution.py:22
  74.7 10.9 %collective-permute-start.5 = (f32[136,512]{1,0:T(8,128)S(1)}, f32[136,512]{1,0:T(8,128)S(1)}, u32[]{:S(2)}, u32[]{:S(2)}) collective-permute-start(f32[136,512]{1,0:T(8,128)S(1)} %fusion.1), channel_id=1, source_target_pairs={{8,0},{16,8},{24,16},{32,24},{40,32},{48,40},{56,48},{64,56},{72,6... | collective-permute-start | bytes 835592 | tf_op jit(solution)/shard_map/ppermute | solution.py:22

commit v8 on v6

--- a/solution.py
+++ b/solution.py
@@ -183,12 +183,14 @@
     def part(offset):
         return attend(offset, meta, received[offset], cached_key_pages, cached_value_pages)
 
-    total = part(SPAN - 1)
+    half = q_width // 2
+    totals = [part(SPAN - 1)[:, :half], part(SPAN - 1)[:, half:]]
     for offset in range(SPAN - 2, -1, -1):
-        moved = shifted(total, "pool", -1)
+        moved = [shifted(piece, "pool", -1) for piece in totals]
         here = part(offset) if offset > 0 else part_own
-        moved, here = lax.optimization_barrier((moved, here))
-        total = here + moved
+        *moved, here = lax.optimization_barrier((*moved, here))
+        totals = [here[:, :half] + moved[0], here[:, half:] + moved[1]]
+    total = jnp.concatenate(totals, axis=1)
     heads = q_width // HEAD_SIZE
     numerator = total[:rows].reshape(rows, heads, HEAD_SIZE)
     totals = total[rows, : heads * rows].reshape(heads, rows)

time: 94.5 us -> 99.5 us (1.053)
  starting transfers between devices: 31.2 us -> 43.4 us
  blocking collectives: 15 us -> 11 us
  waiting for transfers between devices: 21.9 us -> 19.3 us
  Pallas kernels: 16.1 us -> 15.1 us
    ppermute x6 -> x9, starting transfers between devices: 21 us -> 33.3 us  [shifted(): return lax.ppermute(block, axis, route)]
    all_to_all x1, blocking collectives: 15 us -> 11 us  [on_device(): lax.all_to_all(attended, 'tensor', split_axis=0, concat_axis=1, tiled=True)]
    ppermute x6 -> x9, waiting for transfers between devices: 18.3 us -> 15.8 us  [shifted(): return lax.ppermute(block, axis, route)]
    slice x0 -> x1, local copies, waits for them, and re-layouts: none -> 1 us  [on_device(): totals = [part(SPAN - 1)[:, :half], part(SPAN - 1)[:, half:]]]
  transfers between devices with their start and end apart: 7 -> 10, of which waited for: 5 -> 7; matrix products, arithmetic and copies ran while one was open for 4% -> 4% of each run, Pallas kernels for 13% -> 11%
where the time goes in v8:
time: 99.5 us; the launch traced here: 98.7 us
  starting transfers between devices  43.4 us (44%)
  waiting for transfers between devices  19.3 us (19%)
  Pallas kernels  15.1 us (15%)
  blocking collectives  11 us (11%)
  local copies, waits for them, and re-layouts  4.94 us (5%)
  other arithmetic  4.55 us (5%)
    ppermute x9, starting transfers between devices, shifted(): return lax.ppermute(block, axis, route)  33.3 us
    ppermute x9, waiting for transfers between devices, shifted(): return lax.ppermute(block, axis, route)  15.8 us
    pallas_call x4, Pallas kernels, attend(): pl.pallas_call(functools.partial(_attend_kernel, dist, with_own), out_sha...  15.1 us
    all_to_all x1, blocking collectives, on_device(): lax.all_to_all(attended, 'tensor', split_axis=0, concat_axis=1, tiled=True)  11 us
    all_to_all x1, starting transfers between devices, on_device(): lax.all_to_all(packed, 'tensor', split_axis=1, concat_axis=0, tiled=True)  10.2 us
    all_to_all x1, waiting for transfers between devices, on_device(): lax.all_to_all(packed, 'tensor', split_axis=1, concat_axis=0, tiled=True)  3.52 us
    add x3, other arithmetic, on_device(): totals = [here[:, :half] + moved[0], here[:, half:] + moved[1]]  2.09 us
  transfers between devices with their start and end apart: 10, of which 7 were waited for; matrix products, arithmetic and copies ran while one was open for 4% of the time, Pallas kernels for 11%

profile of v8, /device:TPU:1, one launch (start us, length us, event | category | flops | bytes accessed | tf_op | source)
XLA Modules:
  0.0 98.7 jit_solution(9718192768665377228)
XLA Ops:
  0.0 1.0 copy.37
  1.0 0.7 pad_maximum_fusion.1
  1.7 10.2 %all-to-all-start = ((bf16[16,8,1024]{2,0,1:T(8,128)(2,1)}), bf16[16,8,1024]{2,0,1:T(8,128)(2,1)S(1)}, u32[]{:S(2)}, u32[]{:S(2)}) async-start(bf16[16,8,1024]{2,0,1:T(8,128)(2,1)} %pad_maximum_fusion.1), calls=%async_computation | async-start | bytes 524288 | tf_op jit(solution)/shard_map/all_to_all | solution.py:146
  12.0 0.6 gather_fusion
  12.8 0.2 compare_reduce_fusion
  13.0 0.6 gather_fusion.1
  14.3 0.6 pad_add_fusion.meta_ref
  14.9 3.5 %all-to-all-done = bf16[16,8,1024]{2,0,1:T(8,128)(2,1)S(1)} async-done(((bf16[16,8,1024]{2,0,1:T(8,128)(2,1)}), bf16[16,8,1024]{2,0,1:T(8,128)(2,1)S(1)}, u32[]{:S(2)}, u32[]{:S(2)}) %all-to-all-start) | async-done | bytes 262176 | tf_op jit(solution)/shard_map/all_to_all | solution.py:146
  18.5 1.9 %collective-permute-start.2 = (bf16[128,512]{1,0:T(8,128)(2,1)S(1)}, bf16[128,512]{1,0:T(8,128)(2,1)S(1)}, u32[]{:S(2)}, u32[]{:S(2)}) collective-permute-start(bf16[128,512]{1,0:T(8,128)(2,1)S(1)} %slice.56.q_ref), channel_id=1, source_target_pairs={{488,0},{496,8},{504,16},{0,24},{8,32},{16,40},{24,48},{32,56},{40... | collective-permute-start | bytes 393224 | tf_op jit(solution)/shard_map/ppermute | solution.py:22
  20.4 6.0 %collective-permute-start.1 = (bf16[128,512]{1,0:T(8,128)(2,1)S(1)}, bf16[128,512]{1,0:T(8,128)(2,1)S(1)}, u32[]{:S(2)}, u32[]{:S(2)}) collective-permute-start(bf16[128,512]{1,0:T(8,128)(2,1)S(1)} %slice.56.q_ref), channel_id=1, source_target_pairs={{496,0},{504,8},{0,16},{8,24},{16,32},{24,40},{32,48},{40,56},{48,... | collective-permute-start | bytes 393224 | tf_op jit(solution)/shard_map/ppermute | solution.py:22
  26.4 3.5 %collective-permute-start = (bf16[128,512]{1,0:T(8,128)(2,1)S(1)}, bf16[128,512]{1,0:T(8,128)(2,1)S(1)}, u32[]{:S(2)}, u32[]{:S(2)}) collective-permute-start(bf16[128,512]{1,0:T(8,128)(2,1)S(1)} %slice.56.q_ref), channel_id=1, source_target_pairs={{504,0},{0,8},{8,16},{16,24},{24,32},{32,40},{40,48},{48,56},{56,6... | collective-permute-start | bytes 393224 | tf_op jit(solution)/shard_map/ppermute | solution.py:22
  30.0 0.7 fusion.11
  30.7 4.6 %shard_map.73 = f32[136,512]{1,0:T(8,128)} custom-call(s32[4,3,16]{2,1,0:T(4,128)} %pad_add_fusion.meta_ref, bf16[128,512]{1,0:T(8,128)(2,1)} %copy-done.3, bf16[16,128,256]{2,1,0:T(8,128)(2,1)} %kp_hbm.7, bf16[16,128,256]{2,1,0:T(8,128)(2,1)} %vp_hbm.7, bf16[128,256]{1,0:T(8,128)(2,1)} %get-tuple-element.48.refs_0_, bf16[128,256]{1,0:T(8,128)(2,1)} %get-tuple-element.47.refs_1_), custom_call_target="tpu_custom_call" | custom-call | flops 167772160 | bytes 1064960 | tf_op jit(solution)/shard_map/pallas_call | solution.py:110
  35.3 7.2 %collective-permute-done.1.q_ref = bf16[128,512]{1,0:T(8,128)(2,1)S(1)} collective-permute-done((bf16[128,512]{1,0:T(8,128)(2,1)S(1)}, bf16[128,512]{1,0:T(8,128)(2,1)S(1)}, u32[]{:S(2)}, u32[]{:S(2)}) %collective-permute-start.1) | collective-permute-done | bytes 131104 | tf_op jit(solution)/shard_map/ppermute | solution.py:22
  42.5 2.7 %collective-permute-done.q_ref = bf16[128,512]{1,0:T(8,128)(2,1)S(1)} collective-permute-done((bf16[128,512]{1,0:T(8,128)(2,1)S(1)}, bf16[128,512]{1,0:T(8,128)(2,1)S(1)}, u32[]{:S(2)}, u32[]{:S(2)}) %collective-permute-start) | collective-permute-done | bytes 131104 | tf_op jit(solution)/shard_map/ppermute | solution.py:22
  45.2 4.3 %shard_map.74 = f32[136,512]{1,0:T(8,128)} custom-call(s32[4,3,16]{2,1,0:T(4,128)} %pad_add_fusion.meta_ref, bf16[128,512]{1,0:T(8,128)(2,1)} %copy-done.6, bf16[16,128,256]{2,1,0:T(8,128)(2,1)} %kp_hbm.7, bf16[16,128,256]{2,1,0:T(8,128)(2,1)} %vp_hbm.7), custom_call_target="tpu_custom_call" | custom-call | flops 134217728 | bytes 933888 | tf_op jit(solution)/shard_map/pallas_call | solution.py:110
  49.4 1.0 %fusion.10 = (f32[136,256]{1,0:T(8,128)S(1)}, f32[136,256]{1,0:T(8,128)S(1)}) fusion(f32[136,512]{1,0:T(8,128)} %shard_map.74), kind=kLoop, calls=%fused_computation.48 | loop fusion | bytes 557056 | tf_op jit(solution)/shard_map/slice | solution.py:187
  50.4 2.7 %collective-permute-start.4 = (f32[136,256]{1,0:T(8,128)S(1)}, f32[136,256]{1,0:T(8,128)S(1)}, u32[]{:S(2)}, u32[]{:S(2)}) collective-permute-start(f32[136,256]{1,0:T(8,128)S(1)} %get-tuple-element.45), channel_id=1, source_target_pairs={{8,0},{16,8},{24,16},{32,24},{40,32},{48,40},{56,48},{64,56},{72,6... | collective-permute-start | bytes 417800 | tf_op jit(solution)/shard_map/ppermute | solution.py:22
  53.1 1.9 %collective-permute-start.3 = (f32[136,256]{1,0:T(8,128)S(1)}, f32[136,256]{1,0:T(8,128)S(1)}, u32[]{:S(2)}, u32[]{:S(2)}) collective-permute-start(f32[136,256]{1,0:T(8,128)S(1)} %get-tuple-element.46), channel_id=1, source_target_pairs={{8,0},{16,8},{24,16},{32,24},{40,32},{48,40},{56,48},{64,56},{72,6... | collective-permute-start | bytes 417800 | tf_op jit(solution)/shard_map/ppermute | solution.py:22
  55.1 3.1 %shard_map.75 = f32[136,512]{1,0:T(8,128)} custom-call(s32[4,3,16]{2,1,0:T(4,128)} %pad_add_fusion.meta_ref, bf16[128,512]{1,0:T(8,128)(2,1)} %copy-done.5, bf16[16,128,256]{2,1,0:T(8,128)(2,1)} %kp_hbm.7, bf16[16,128,256]{2,1,0:T(8,128)(2,1)} %vp_hbm.7), custom_call_target="tpu_custom_call" | custom-call | flops 134217728 | bytes 933888 | tf_op jit(solution)/shard_map/pallas_call | solution.py:110
  58.2 1.3 %collective-permute-done.3 = f32[136,256]{1,0:T(8,128)S(1)} collective-permute-done((f32[136,256]{1,0:T(8,128)S(1)}, f32[136,256]{1,0:T(8,128)S(1)}, u32[]{:S(2)}, u32[]{:S(2)}) %collective-permute-start.3) | collective-permute-done | bytes 139296 | tf_op jit(solution)/shard_map/ppermute | solution.py:22
  59.5 1.0 %slice_add_fusion.4 = (f32[136,256]{1,0:T(8,128)S(1)}, f32[136,256]{1,0:T(8,128)S(1)}) fusion(f32[136,256]{1,0:T(8,128)S(1)} %collective-permute-done.4, f32[136,512]{1,0:T(8,128)} %shard_map.75, f32[136,256]{1,0:T(8,128)S(1)} %collective-permute-done.3), kind=kLoop, calls=%fused_computation.10 | loop fusion | flops 69632 | bytes 835584 | tf_op jit(solution)/shard_map/add | solution.py:192
  60.6 6.3 %collective-permute-start.6 = (f32[136,256]{1,0:T(8,128)S(1)}, f32[136,256]{1,0:T(8,128)S(1)}, u32[]{:S(2)}, u32[]{:S(2)}) collective-permute-start(f32[136,256]{1,0:T(8,128)S(1)} %get-tuple-element.43), channel_id=1, source_target_pairs={{8,0},{16,8},{24,16},{32,24},{40,32},{48,40},{56,48},{64,56},{72,6... | collective-permute-start | bytes 417800 | tf_op jit(solution)/shard_map/ppermute | solution.py:22
  66.9 1.9 %collective-permute-start.5 = (f32[136,256]{1,0:T(8,128)S(1)}, f32[136,256]{1,0:T(8,128)S(1)}, u32[]{:S(2)}, u32[]{:S(2)}) collective-permute-start(f32[136,256]{1,0:T(8,128)S(1)} %get-tuple-element.44), channel_id=1, source_target_pairs={{8,0},{16,8},{24,16},{32,24},{40,32},{48,40},{56,48},{64,56},{72,6... | collective-permute-start | bytes 417800 | tf_op jit(solution)/shard_map/ppermute | solution.py:22
  68.9 3.1 %shard_map.76 = f32[136,512]{1,0:T(8,128)} custom-call(s32[4,3,16]{2,1,0:T(4,128)} %pad_add_fusion.meta_ref, bf16[128,512]{1,0:T(8,128)(2,1)} %copy-done.4, bf16[16,128,256]{2,1,0:T(8,128)(2,1)} %kp_hbm.7, bf16[16,128,256]{2,1,0:T(8,128)(2,1)} %vp_hbm.7), custom_call_target="tpu_custom_call" | custom-call | flops 134217728 | bytes 933888 | tf_op jit(solution)/shard_map/pallas_call | solution.py:110
  72.0 0.7 collective-permute-done.5
  72.7 1.0 %slice_add_fusion.2 = (f32[136,256]{1,0:T(8,128)S(1)}, f32[136,256]{1,0:T(8,128)S(1)}) fusion(f32[136,256]{1,0:T(8,128)S(1)} %collective-permute-done.6, f32[136,512]{1,0:T(8,128)} %shard_map.76, f32[136,256]{1,0:T(8,128)S(1)} %collective-permute-done.5), kind=kLoop, calls=%fused_computation.8 | loop fusion | flops 69632 | bytes 835584 | tf_op jit(solution)/shard_map/add | solution.py:192
  73.8 7.0 %collective-permute-start.8 = (f32[136,256]{1,0:T(8,128)S(1)}, f32[136,256]{1,0:T(8,128)S(1)}, u32[]{:S(2)}, u32[]{:S(2)}) collective-permute-start(f32[136,256]{1,0:T(8,128)S(1)} %get-tuple-element.41), channel_id=1, source_target_pairs={{8,0},{16,8},{24,16},{32,24},{40,32},{48,40},{56,48},{64,56},{72,6... | collective-permute-start | bytes 417800 | tf_op jit(solution)/shard_map/ppermute | solution.py:22
  80.7 1.9 %collective-permute-start.7 = (f32[136,256]{1,0:T(8,128)S(1)}, f32[136,256]{1,0:T(8,128)S(1)}, u32[]{:S(2)}, u32[]{:S(2)}) collective-permute-start(f32[136,256]{1,0:T(8,128)S(1)} %get-tuple-element.42), channel_id=1, source_target_pairs={{8,0},{16,8},{24,16},{32,24},{40,32},{48,40},{56,48},{64,56},{72,6... | collective-permute-start | bytes 417800 | tf_op jit(solution)/shard_map/ppermute | solution.py:22
  82.7 3.8 %collective-permute-done.7 = f32[136,256]{1,0:T(8,128)S(1)} collective-permute-done((f32[136,256]{1,0:T(8,128)S(1)}, f32[136,256]{1,0:T(8,128)S(1)}, u32[]{:S(2)}, u32[]{:S(2)}) %collective-permute-start.7) | collective-permute-done | bytes 139296 | tf_op jit(solution)/shard_map/ppermute | solution.py:22
  87.0 11.0 %all_to_all.34 = bf16[8,16,512]{2,1,0:T(8,128)(2,1)S(1)} all-to-all(bf16[8,16,512]{2,1,0:T(8,128)(2,1)S(1)} %bitcast.38), channel_id=1, replica_groups=mesh['pool'=64,'tensor'=8] {'tensor'}, dimensions={0} | all-to-all | bytes 262144 | tf_op jit(solution)/shard_map/all_to_all | solution.py:199
  98.0 0.7 copy.32
  (45 shorter events, 1.5 us)
Async XLA Ops:
  0.0 12.0 %copy-start = (s32[64,64]{1,0:T(8,128)S(1)}, s32[64,64]{1,0:T(8,128)}, u32[]{:S(2)}) copy-start(s32[64,64]{1,0:T(8,128)} %param.12) | copy-start | bytes 49156
  0.0 1.0 copy-start.7
  0.0 1.0 copy-start.8
  1.7 16.7 %all-to-all-start = ((bf16[16,8,1024]{2,0,1:T(8,128)(2,1)}), bf16[16,8,1024]{2,0,1:T(8,128)(2,1)S(1)}, u32[]{:S(2)}, u32[]{:S(2)}) async-start(bf16[16,8,1024]{2,0,1:T(8,128)(2,1)} %pad_maximum_fusion.1), calls=%async_computation | async-start | bytes 524288 | tf_op jit(solution)/shard_map/all_to_all | solution.py:146
  12.0 1.0 %copy-start.1 = (s32[64]{0:T(128)S(1)}, s32[64]{0:T(128)}, u32[]{:S(2)}) copy-start(s32[64]{0:T(128)} %param.13) | copy-start | bytes 772
  18.5 12.2 %copy-start.3 = (bf16[128,512]{1,0:T(8,128)(2,1)}, bf16[128,512]{1,0:T(8,128)(2,1)S(1)}, u32[]{:S(2)}) copy-start(bf16[128,512]{1,0:T(8,128)(2,1)S(1)} %slice.56.q_ref) | copy-start | bytes 393220
  18.5 16.8 %collective-permute-start.2 = (bf16[128,512]{1,0:T(8,128)(2,1)S(1)}, bf16[128,512]{1,0:T(8,128)(2,1)S(1)}, u32[]{:S(2)}, u32[]{:S(2)}) collective-permute-start(bf16[128,512]{1,0:T(8,128)(2,1)S(1)} %slice.56.q_ref), channel_id=1, source_target_pairs={{488,0},{496,8},{504,16},{0,24},{8,32},{16,40},{24,48},{32,56},{40... | collective-permute-start | bytes 393224 | tf_op jit(solution)/shard_map/ppermute | solution.py:22
  20.4 22.1 %collective-permute-start.1 = (bf16[128,512]{1,0:T(8,128)(2,1)S(1)}, bf16[128,512]{1,0:T(8,128)(2,1)S(1)}, u32[]{:S(2)}, u32[]{:S(2)}) collective-permute-start(bf16[128,512]{1,0:T(8,128)(2,1)S(1)} %slice.56.q_ref), channel_id=1, source_target_pairs={{496,0},{504,8},{0,16},{8,24},{16,32},{24,40},{32,48},{40,56},{48,... | collective-permute-start | bytes 393224 | tf_op jit(solution)/shard_map/ppermute | solution.py:22
  26.4 18.7 %collective-permute-start = (bf16[128,512]{1,0:T(8,128)(2,1)S(1)}, bf16[128,512]{1,0:T(8,128)(2,1)S(1)}, u32[]{:S(2)}, u32[]{:S(2)}) collective-permute-start(bf16[128,512]{1,0:T(8,128)(2,1)S(1)} %slice.56.q_ref), channel_id=1, source_target_pairs={{504,0},{0,8},{8,16},{16,24},{24,32},{32,40},{40,48},{48,56},{56,6... | collective-permute-start | bytes 393224 | tf_op jit(solution)/shard_map/ppermute | solution.py:22
  35.3 9.9 %copy-start.6 = (bf16[128,512]{1,0:T(8,128)(2,1)}, bf16[128,512]{1,0:T(8,128)(2,1)S(1)}, u32[]{:S(2)}) copy-start(bf16[128,512]{1,0:T(8,128)(2,1)S(1)} %collective-permute-done.2.q_ref) | copy-start | bytes 393220
  42.5 7.0 %copy-start.5 = (bf16[128,512]{1,0:T(8,128)(2,1)}, bf16[128,512]{1,0:T(8,128)(2,1)S(1)}, u32[]{:S(2)}) copy-start(bf16[128,512]{1,0:T(8,128)(2,1)S(1)} %collective-permute-done.1.q_ref) | copy-start | bytes 393220
  45.2 4.3 %copy-start.4 = (bf16[128,512]{1,0:T(8,128)(2,1)}, bf16[128,512]{1,0:T(8,128)(2,1)S(1)}, u32[]{:S(2)}) copy-start(bf16[128,512]{1,0:T(8,128)(2,1)S(1)} %collective-permute-done.q_ref) | copy-start | bytes 393220
  50.4 7.8 %collective-permute-start.4 = (f32[136,256]{1,0:T(8,128)S(1)}, f32[136,256]{1,0:T(8,128)S(1)}, u32[]{:S(2)}, u32[]{:S(2)}) collective-permute-start(f32[136,256]{1,0:T(8,128)S(1)} %get-tuple-element.45), channel_id=1, source_target_pairs={{8,0},{16,8},{24,16},{32,24},{40,32},{48,40},{56,48},{64,56},{72,6... | collective-permute-start | bytes 417800 | tf_op jit(solution)/shard_map/ppermute | solution.py:22
  53.1 6.4 %collective-permute-start.3 = (f32[136,256]{1,0:T(8,128)S(1)}, f32[136,256]{1,0:T(8,128)S(1)}, u32[]{:S(2)}, u32[]{:S(2)}) collective-permute-start(f32[136,256]{1,0:T(8,128)S(1)} %get-tuple-element.46), channel_id=1, source_target_pairs={{8,0},{16,8},{24,16},{32,24},{40,32},{48,40},{56,48},{64,56},{72,6... | collective-permute-start | bytes 417800 | tf_op jit(solution)/shard_map/ppermute | solution.py:22
  60.6 11.4 %collective-permute-start.6 = (f32[136,256]{1,0:T(8,128)S(1)}, f32[136,256]{1,0:T(8,128)S(1)}, u32[]{:S(2)}, u32[]{:S(2)}) collective-permute-start(f32[136,256]{1,0:T(8,128)S(1)} %get-tuple-element.43), channel_id=1, source_target_pairs={{8,0},{16,8},{24,16},{32,24},{40,32},{48,40},{56,48},{64,56},{72,6... | collective-permute-start | bytes 417800 | tf_op jit(solution)/shard_map/ppermute | solution.py:22
  66.9 5.8 %collective-permute-start.5 = (f32[136,256]{1,0:T(8,128)S(1)}, f32[136,256]{1,0:T(8,128)S(1)}, u32[]{:S(2)}, u32[]{:S(2)}) collective-permute-start(f32[136,256]{1,0:T(8,128)S(1)} %get-tuple-element.44), channel_id=1, source_target_pairs={{8,0},{16,8},{24,16},{32,24},{40,32},{48,40},{56,48},{64,56},{72,6... | collective-permute-start | bytes 417800 | tf_op jit(solution)/shard_map/ppermute | solution.py:22
  72.0 14.5 %copy-start.2 = (f32[136,512]{1,0:T(8,128)S(1)}, f32[136,512]{1,0:T(8,128)}, u32[]{:S(2)}) copy-start(f32[136,512]{1,0:T(8,128)} %shard_map.73) | copy-start | bytes 835588
  73.8 9.0 %collective-permute-start.8 = (f32[136,256]{1,0:T(8,128)S(1)}, f32[136,256]{1,0:T(8,128)S(1)}, u32[]{:S(2)}, u32[]{:S(2)}) collective-permute-start(f32[136,256]{1,0:T(8,128)S(1)} %get-tuple-element.41), channel_id=1, source_target_pairs={{8,0},{16,8},{24,16},{32,24},{40,32},{48,40},{56,48},{64,56},{72,6... | collective-permute-start | bytes 417800 | tf_op jit(solution)/shard_map/ppermute | solution.py:22
  80.7 5.8 %collective-permute-start.7 = (f32[136,256]{1,0:T(8,128)S(1)}, f32[136,256]{1,0:T(8,128)S(1)}, u32[]{:S(2)}, u32[]{:S(2)}) collective-permute-start(f32[136,256]{1,0:T(8,128)S(1)} %get-tuple-element.42), channel_id=1, source_target_pairs={{8,0},{16,8},{24,16},{32,24},{40,32},{48,40},{56,48},{64,56},{72,6... | collective-permute-start | bytes 417800 | tf_op jit(solution)/shard_map/ppermute | solution.py:22

commit v9 on v6

--- a/solution.py
+++ b/solution.py
@@ -175,19 +175,19 @@
     count = jnp.broadcast_to(jnp.sum(wanted.astype(jnp.int32), axis=1, keepdims=True), (SPAN, slots_dev))
     meta = jnp.stack([order, order_limit, count], axis=1).astype(jnp.int32)
 
-    received = [shifted(q_own, "pool", offset) for offset in range(1, SPAN)]
-    part_own = attend(0, meta, q_own, cached_key_pages, cached_value_pages, k_new, v_new)
-    *received, part_own = lax.optimization_barrier((*received, part_own))
-    received = [q_own] + received
+    received = [q_own]
+    for offset in range(1, SPAN):
+        received.append(shifted(received[-1], "pool", 1))
+    received = list(lax.optimization_barrier(tuple(received)))
 
     def part(offset):
-        return attend(offset, meta, received[offset], cached_key_pages, cached_value_pages)
+        own = (k_new, v_new) if offset == 0 else ()
+        return attend(offset, meta, received[offset], cached_key_pages, cached_value_pages, *own)
 
     total = part(SPAN - 1)
     for offset in range(SPAN - 2, -1, -1):
         moved = shifted(total, "pool", -1)
-        here = part(offset) if offset > 0 else part_own
-        moved, here = lax.optimization_barrier((moved, here))
+        moved, here = lax.optimization_barrier((moved, part(offset)))
         total = here + moved
     heads = q_width // HEAD_SIZE
     numerator = total[:rows].reshape(rows, heads, HEAD_SIZE)

time: 94.5 us -> 98.9 us (1.047)
  waiting for transfers between devices: 21.9 us -> 31.7 us
  Pallas kernels: 16.1 us -> 12.1 us
  blocking collectives: 15 us -> 13.9 us
  starting transfers between devices: 31.2 us -> 30.2 us
    ppermute x6, waiting for transfers between devices: 18.3 us -> 27.1 us  [shifted(): return lax.ppermute(block, axis, route)]
    pallas_call x4, Pallas kernels: 16.1 us -> 12.1 us  [attend(): pl.pallas_call(functools.partial(_attend_kernel, dist, with_own), out_sha...]
    all_to_all x1, blocking collectives: 15 us -> 13.9 us  [on_device(): lax.all_to_all(attended, 'tensor', split_axis=0, concat_axis=1, tiled=True)]
    all_to_all x1, waiting for transfers between devices: 3.52 us -> 4.64 us  [on_device(): lax.all_to_all(packed, 'tensor', split_axis=1, concat_axis=0, tiled=True)]
    ppermute x6, starting transfers between devices: 21 us -> 20 us  [shifted(): return lax.ppermute(block, axis, route)]
  transfers between devices with their start and end apart: 7 -> 7, of which waited for: 5 -> 6; matrix products, arithmetic and copies ran while one was open for 4% -> 4% of each run, Pallas kernels for 13% -> 9%
where the time goes in v9:
time: 98.9 us; the launch traced here: 98.2 us
  waiting for transfers between devices  31.7 us (32%)
  starting transfers between devices  30.2 us (31%)
  blocking collectives  13.9 us (14%)
  Pallas kernels  12.1 us (12%)
  other arithmetic  5.41 us (5%)
  local copies, waits for them, and re-layouts  4.6 us (5%)
    ppermute x6, waiting for transfers between devices, shifted(): return lax.ppermute(block, axis, route)  27.1 us
    ppermute x6, starting transfers between devices, shifted(): return lax.ppermute(block, axis, route)  20 us
    all_to_all x1, blocking collectives, on_device(): lax.all_to_all(attended, 'tensor', split_axis=0, concat_axis=1, tiled=True)  13.9 us
    pallas_call x4, Pallas kernels, attend(): pl.pallas_call(functools.partial(_attend_kernel, dist, with_own), out_sha...  12.1 us
    all_to_all x1, starting transfers between devices, on_device(): lax.all_to_all(packed, 'tensor', split_axis=1, concat_axis=0, tiled=True)  10.2 us
    all_to_all x1, waiting for transfers between devices, on_device(): lax.all_to_all(packed, 'tensor', split_axis=1, concat_axis=0, tiled=True)  4.64 us
    add x3, other arithmetic, on_device(): total = here + moved  2.98 us
  transfers between devices with their start and end apart: 7, of which 6 were waited for; matrix products, arithmetic and copies ran while one was open for 4% of the time, Pallas kernels for 9%

profile of v9, /device:TPU:1, one launch (start us, length us, event | category | flops | bytes accessed | tf_op | source)
XLA Modules:
  0.0 98.2 jit_solution(1927912642570816769)
XLA Ops:
  0.0 1.0 copy.37
  1.0 0.7 pad_maximum_fusion
  1.7 10.2 %all-to-all-start = ((bf16[16,8,1024]{2,0,1:T(8,128)(2,1)}), bf16[16,8,1024]{2,0,1:T(8,128)(2,1)S(1)}, u32[]{:S(2)}, u32[]{:S(2)}) async-start(bf16[16,8,1024]{2,0,1:T(8,128)(2,1)} %pad_maximum_fusion), calls=%async_computation | async-start | bytes 524288 | tf_op jit(solution)/shard_map/all_to_all | solution.py:146
  12.0 0.6 gather_fusion
  12.6 0.2 compare_reduce_fusion
  13.0 0.6 gather_fusion.1
  13.8 4.6 %all-to-all-done = bf16[16,8,1024]{2,0,1:T(8,128)(2,1)S(1)} async-done(((bf16[16,8,1024]{2,0,1:T(8,128)(2,1)}), bf16[16,8,1024]{2,0,1:T(8,128)(2,1)S(1)}, u32[]{:S(2)}, u32[]{:S(2)}) %all-to-all-start) | async-done | bytes 262176 | tf_op jit(solution)/shard_map/all_to_all | solution.py:146
  18.5 1.9 %collective-permute-start = (bf16[128,512]{1,0:T(8,128)(2,1)S(1)}, bf16[128,512]{1,0:T(8,128)(2,1)S(1)}, u32[]{:S(2)}, u32[]{:S(2)}) collective-permute-start(bf16[128,512]{1,0:T(8,128)(2,1)S(1)} %slice.24.q_ref), channel_id=1, source_target_pairs={{504,0},{0,8},{8,16},{16,24},{24,32},{32,40},{40,48},{48,56},{56,6... | collective-permute-start | bytes 393224 | tf_op jit(solution)/shard_map/ppermute | solution.py:22
  20.4 0.2 reduce_window_sum.11
  20.6 9.8 %collective-permute-done.q_ref = bf16[128,512]{1,0:T(8,128)(2,1)S(1)} collective-permute-done((bf16[128,512]{1,0:T(8,128)(2,1)S(1)}, bf16[128,512]{1,0:T(8,128)(2,1)S(1)}, u32[]{:S(2)}, u32[]{:S(2)}) %collective-permute-start) | collective-permute-done | bytes 131104 | tf_op jit(solution)/shard_map/ppermute | solution.py:22
  30.4 1.9 %collective-permute-start.1 = (bf16[128,512]{1,0:T(8,128)(2,1)S(1)}, bf16[128,512]{1,0:T(8,128)(2,1)S(1)}, u32[]{:S(2)}, u32[]{:S(2)}) collective-permute-start(bf16[128,512]{1,0:T(8,128)(2,1)S(1)} %collective-permute-done.q_ref), channel_id=1, source_target_pairs={{504,0},{0,8},{8,16},{16,24},{24,32},{32,40},{40,48},{48,56},{56,6... | collective-permute-start | bytes 393224 | tf_op jit(solution)/shard_map/ppermute | solution.py:22
  32.5 7.0 %collective-permute-done.1.q_ref = bf16[128,512]{1,0:T(8,128)(2,1)S(1)} collective-permute-done((bf16[128,512]{1,0:T(8,128)(2,1)S(1)}, bf16[128,512]{1,0:T(8,128)(2,1)S(1)}, u32[]{:S(2)}, u32[]{:S(2)}) %collective-permute-start.1) | collective-permute-done | bytes 131104 | tf_op jit(solution)/shard_map/ppermute | solution.py:22
  39.5 1.9 %collective-permute-start.2 = (bf16[128,512]{1,0:T(8,128)(2,1)S(1)}, bf16[128,512]{1,0:T(8,128)(2,1)S(1)}, u32[]{:S(2)}, u32[]{:S(2)}) collective-permute-start(bf16[128,512]{1,0:T(8,128)(2,1)S(1)} %collective-permute-done.1.q_ref), channel_id=1, source_target_pairs={{504,0},{0,8},{8,16},{16,24},{24,32},{32,40},{40,48},{48,56},{56,6... | collective-permute-start | bytes 393224 | tf_op jit(solution)/shard_map/ppermute | solution.py:22
  41.6 0.6 pad_add_fusion.meta_ref
  42.2 6.3 %collective-permute-done.2.q_ref = bf16[128,512]{1,0:T(8,128)(2,1)S(1)} collective-permute-done((bf16[128,512]{1,0:T(8,128)(2,1)S(1)}, bf16[128,512]{1,0:T(8,128)(2,1)S(1)}, u32[]{:S(2)}, u32[]{:S(2)}) %collective-permute-start.2) | collective-permute-done | bytes 131104 | tf_op jit(solution)/shard_map/ppermute | solution.py:22
  48.5 0.7 copy-done.5
  49.1 3.1 %shard_map.73 = f32[136,512]{1,0:T(8,128)} custom-call(s32[4,3,16]{2,1,0:T(4,128)} %pad_add_fusion.meta_ref, bf16[128,512]{1,0:T(8,128)(2,1)} %copy-done.5, bf16[16,128,256]{2,1,0:T(8,128)(2,1)} %kp_hbm.7, bf16[16,128,256]{2,1,0:T(8,128)(2,1)} %vp_hbm.7), custom_call_target="tpu_custom_call" | custom-call | flops 134217728 | bytes 933888 | tf_op jit(solution)/shard_map/pallas_call | solution.py:110
  52.3 1.9 %collective-permute-start.3 = (f32[136,512]{1,0:T(8,128)}, f32[136,512]{1,0:T(8,128)S(1)}, u32[]{:S(2)}, u32[]{:S(2)}) collective-permute-start(f32[136,512]{1,0:T(8,128)} %shard_map.73), channel_id=1, source_target_pairs={{8,0},{16,8},{24,16},{32,24},{40,32},{48,40},{56,48},{64,56},{72,6... | collective-permute-start | bytes 835592 | tf_op jit(solution)/shard_map/ppermute | solution.py:22
  54.2 1.9 %shard_map.74 = f32[136,512]{1,0:T(8,128)} custom-call(s32[4,3,16]{2,1,0:T(4,128)} %pad_add_fusion.meta_ref, bf16[128,512]{1,0:T(8,128)(2,1)} %copy-done.4, bf16[16,128,256]{2,1,0:T(8,128)(2,1)} %kp_hbm.7, bf16[16,128,256]{2,1,0:T(8,128)(2,1)} %vp_hbm.7), custom_call_target="tpu_custom_call" | custom-call | flops 134217728 | bytes 933888 | tf_op jit(solution)/shard_map/pallas_call | solution.py:110
  56.2 3.6 %collective-permute-done.3 = f32[136,512]{1,0:T(8,128)S(1)} collective-permute-done((f32[136,512]{1,0:T(8,128)}, f32[136,512]{1,0:T(8,128)S(1)}, u32[]{:S(2)}, u32[]{:S(2)}) %collective-permute-start.3) | collective-permute-done | bytes 278560 | tf_op jit(solution)/shard_map/ppermute | solution.py:22
  59.8 1.0 %add.70 = f32[136,512]{1,0:T(8,128)S(1)} add(f32[136,512]{1,0:T(8,128)} %shard_map.74, f32[136,512]{1,0:T(8,128)S(1)} %collective-permute-done.3) | non-fusion elementwise | flops 69632 | bytes 835584 | tf_op jit(solution)/shard_map/add | solution.py:191
  60.8 5.2 %collective-permute-start.4 = (f32[136,512]{1,0:T(8,128)S(1)}, f32[136,512]{1,0:T(8,128)S(1)}, u32[]{:S(2)}, u32[]{:S(2)}) collective-permute-start(f32[136,512]{1,0:T(8,128)S(1)} %add.70), channel_id=1, source_target_pairs={{8,0},{16,8},{24,16},{32,24},{40,32},{48,40},{56,48},{64,56},{72,6... | collective-permute-start | bytes 835592 | tf_op jit(solution)/shard_map/ppermute | solution.py:22
  66.0 3.1 %shard_map.75 = f32[136,512]{1,0:T(8,128)} custom-call(s32[4,3,16]{2,1,0:T(4,128)} %pad_add_fusion.meta_ref, bf16[128,512]{1,0:T(8,128)(2,1)} %copy-done.3, bf16[16,128,256]{2,1,0:T(8,128)(2,1)} %kp_hbm.7, bf16[16,128,256]{2,1,0:T(8,128)(2,1)} %vp_hbm.7), custom_call_target="tpu_custom_call" | custom-call | flops 134217728 | bytes 933888 | tf_op jit(solution)/shard_map/pallas_call | solution.py:110
  69.2 0.3 collective-permute-done.4
  69.5 1.0 %add.71 = f32[136,512]{1,0:T(8,128)S(1)} add(f32[136,512]{1,0:T(8,128)} %shard_map.75, f32[136,512]{1,0:T(8,128)S(1)} %collective-permute-done.4) | non-fusion elementwise | flops 69632 | bytes 835584 | tf_op jit(solution)/shard_map/add | solution.py:191
  70.5 7.1 %collective-permute-start.5 = (f32[136,512]{1,0:T(8,128)S(1)}, f32[136,512]{1,0:T(8,128)S(1)}, u32[]{:S(2)}, u32[]{:S(2)}) collective-permute-start(f32[136,512]{1,0:T(8,128)S(1)} %add.71), channel_id=1, source_target_pairs={{8,0},{16,8},{24,16},{32,24},{40,32},{48,40},{56,48},{64,56},{72,6... | collective-permute-start | bytes 835592 | tf_op jit(solution)/shard_map/ppermute | solution.py:22
  77.7 0.7 fusion.9
  78.3 3.9 %shard_map.76 = f32[136,512]{1,0:T(8,128)} custom-call(s32[4,3,16]{2,1,0:T(4,128)} %pad_add_fusion.meta_ref, bf16[128,512]{1,0:T(8,128)(2,1)} %copy-done.2, bf16[16,128,256]{2,1,0:T(8,128)(2,1)} %kp_hbm.7, bf16[16,128,256]{2,1,0:T(8,128)(2,1)} %vp_hbm.7, bf16[128,256]{1,0:T(8,128)(2,1)} %get-tuple-element.34.refs_0_, bf16[128,256]{1,0:T(8,128)(2,1)} %get-tuple-element.33.refs_1_), custom_call_target="tpu_custom_call" | custom-call | flops 167772160 | bytes 1064960 | tf_op jit(solution)/shard_map/pallas_call | solution.py:110
  82.2 1.0 %add.72 = f32[136,512]{1,0:T(8,128)S(1)} add(f32[136,512]{1,0:T(8,128)} %shard_map.76, f32[136,512]{1,0:T(8,128)S(1)} %collective-permute-done.5) | non-fusion elementwise | flops 69632 | bytes 835584 | tf_op jit(solution)/shard_map/add | solution.py:191
  83.3 0.2 div.11
  83.6 13.9 %all_to_all.34 = bf16[8,16,512]{2,1,0:T(8,128)(2,1)S(1)} all-to-all(bf16[8,16,512]{2,1,0:T(8,128)(2,1)S(1)} %bitcast.36), channel_id=1, replica_groups=mesh['pool'=64,'tensor'=8] {'tensor'}, dimensions={0} | all-to-all | bytes 262144 | tf_op jit(solution)/shard_map/all_to_all | solution.py:197
  97.5 0.7 copy.32
  (36 shorter events, 1.0 us)
Async XLA Ops:
  0.0 12.0 %copy-start = (s32[64,64]{1,0:T(8,128)S(1)}, s32[64,64]{1,0:T(8,128)}, u32[]{:S(2)}) copy-start(s32[64,64]{1,0:T(8,128)} %param.12) | copy-start | bytes 49156
  0.0 1.0 copy-start.6
  0.0 1.0 copy-start.7
  1.7 16.7 %all-to-all-start = ((bf16[16,8,1024]{2,0,1:T(8,128)(2,1)}), bf16[16,8,1024]{2,0,1:T(8,128)(2,1)S(1)}, u32[]{:S(2)}, u32[]{:S(2)}) async-start(bf16[16,8,1024]{2,0,1:T(8,128)(2,1)} %pad_maximum_fusion), calls=%async_computation | async-start | bytes 524288 | tf_op jit(solution)/shard_map/all_to_all | solution.py:146
  12.0 1.0 %copy-start.1 = (s32[64]{0:T(128)S(1)}, s32[64]{0:T(128)}, u32[]{:S(2)}) copy-start(s32[64]{0:T(128)} %param.13) | copy-start | bytes 772
  18.4 33.8 %copy-start.2 = (bf16[128,512]{1,0:T(8,128)(2,1)}, bf16[128,512]{1,0:T(8,128)(2,1)S(1)}, u32[]{:S(2)}) copy-start(bf16[128,512]{1,0:T(8,128)(2,1)S(1)} %slice.24.q_ref) | copy-start | bytes 393220
  18.5 12.0 %collective-permute-start = (bf16[128,512]{1,0:T(8,128)(2,1)S(1)}, bf16[128,512]{1,0:T(8,128)(2,1)S(1)}, u32[]{:S(2)}, u32[]{:S(2)}) collective-permute-start(bf16[128,512]{1,0:T(8,128)(2,1)S(1)} %slice.24.q_ref), channel_id=1, source_target_pairs={{504,0},{0,8},{8,16},{16,24},{24,32},{32,40},{40,48},{48,56},{56,6... | collective-permute-start | bytes 393224 | tf_op jit(solution)/shard_map/ppermute | solution.py:22
  30.4 21.9 %copy-start.3 = (bf16[128,512]{1,0:T(8,128)(2,1)}, bf16[128,512]{1,0:T(8,128)(2,1)S(1)}, u32[]{:S(2)}) copy-start(bf16[128,512]{1,0:T(8,128)(2,1)S(1)} %collective-permute-done.q_ref) | copy-start | bytes 393220
  30.4 9.0 %collective-permute-start.1 = (bf16[128,512]{1,0:T(8,128)(2,1)S(1)}, bf16[128,512]{1,0:T(8,128)(2,1)S(1)}, u32[]{:S(2)}, u32[]{:S(2)}) collective-permute-start(bf16[128,512]{1,0:T(8,128)(2,1)S(1)} %collective-permute-done.q_ref), channel_id=1, source_target_pairs={{504,0},{0,8},{8,16},{16,24},{24,32},{32,40},{40,48},{48,56},{56,6... | collective-permute-start | bytes 393224 | tf_op jit(solution)/shard_map/ppermute | solution.py:22
  39.4 12.8 %copy-start.4 = (bf16[128,512]{1,0:T(8,128)(2,1)}, bf16[128,512]{1,0:T(8,128)(2,1)S(1)}, u32[]{:S(2)}) copy-start(bf16[128,512]{1,0:T(8,128)(2,1)S(1)} %collective-permute-done.1.q_ref) | copy-start | bytes 393220
  39.5 9.0 %collective-permute-start.2 = (bf16[128,512]{1,0:T(8,128)(2,1)S(1)}, bf16[128,512]{1,0:T(8,128)(2,1)S(1)}, u32[]{:S(2)}, u32[]{:S(2)}) collective-permute-start(bf16[128,512]{1,0:T(8,128)(2,1)S(1)} %collective-permute-done.1.q_ref), channel_id=1, source_target_pairs={{504,0},{0,8},{8,16},{16,24},{24,32},{32,40},{40,48},{48,56},{56,6... | collective-permute-start | bytes 393224 | tf_op jit(solution)/shard_map/ppermute | solution.py:22
  48.5 0.7 copy-start.5
  52.3 7.5 %collective-permute-start.3 = (f32[136,512]{1,0:T(8,128)}, f32[136,512]{1,0:T(8,128)S(1)}, u32[]{:S(2)}, u32[]{:S(2)}) collective-permute-start(f32[136,512]{1,0:T(8,128)} %shard_map.73), channel_id=1, source_target_pairs={{8,0},{16,8},{24,16},{32,24},{40,32},{48,40},{56,48},{64,56},{72,6... | collective-permute-start | bytes 835592 | tf_op jit(solution)/shard_map/ppermute | solution.py:22
  60.8 8.7 %collective-permute-start.4 = (f32[136,512]{1,0:T(8,128)S(1)}, f32[136,512]{1,0:T(8,128)S(1)}, u32[]{:S(2)}, u32[]{:S(2)}) collective-permute-start(f32[136,512]{1,0:T(8,128)S(1)} %add.70), channel_id=1, source_target_pairs={{8,0},{16,8},{24,16},{32,24},{40,32},{48,40},{56,48},{64,56},{72,6... | collective-permute-start | bytes 835592 | tf_op jit(solution)/shard_map/ppermute | solution.py:22
  70.5 11.7 %collective-permute-start.5 = (f32[136,512]{1,0:T(8,128)S(1)}, f32[136,512]{1,0:T(8,128)S(1)}, u32[]{:S(2)}, u32[]{:S(2)}) collective-permute-start(f32[136,512]{1,0:T(8,128)S(1)} %add.71), channel_id=1, source_target_pairs={{8,0},{16,8},{24,16},{32,24},{40,32},{48,40},{56,48},{64,56},{72,6... | collective-permute-start | bytes 835592 | tf_op jit(solution)/shard_map/ppermute | solution.py:22

commit v10 on v9

--- a/solution.py
+++ b/solution.py
@@ -175,20 +175,22 @@
     count = jnp.broadcast_to(jnp.sum(wanted.astype(jnp.int32), axis=1, keepdims=True), (SPAN, slots_dev))
     meta = jnp.stack([order, order_limit, count], axis=1).astype(jnp.int32)
 
-    received = [q_own]
-    for offset in range(1, SPAN):
-        received.append(shifted(received[-1], "pool", 1))
-    received = list(lax.optimization_barrier(tuple(received)))
-
-    def part(offset):
+    def part(offset, queries):
         own = (k_new, v_new) if offset == 0 else ()
-        return attend(offset, meta, received[offset], cached_key_pages, cached_value_pages, *own)
-
-    total = part(SPAN - 1)
-    for offset in range(SPAN - 2, -1, -1):
-        moved = shifted(total, "pool", -1)
-        moved, here = lax.optimization_barrier((moved, part(offset)))
-        total = here + moved
+        return attend(offset, meta, queries, cached_key_pages, cached_value_pages, *own)
+
+    held = q_own
+    total = None
+    for offset in range(SPAN):
+        here = part(offset, held)
+        if offset < SPAN - 1:
+            nxt = shifted(held, "pool", 1)
+            if offset < SPAN - 3:
+                nxt, here = lax.optimization_barrier((nxt, here))
+        back = here if offset == 0 else shifted(here, "pool", -offset)
+        total = back if total is None else total + back
+        if offset < SPAN - 1:
+            held = nxt
     heads = q_width // HEAD_SIZE
     numerator = total[:rows].reshape(rows, heads, HEAD_SIZE)
     totals = total[rows, : heads * rows].reshape(heads, rows)

time: 98.9 us -> 97 us (0.981)
  other arithmetic: 5.41 us -> 2.55 us
  blocking collectives: 13.9 us -> 16 us
  starting transfers between devices: 30.2 us -> 28.5 us
    add x3 -> x1, other arithmetic: 2.98 us -> 0.1 us  [on_device(): total = back if total is None else total + back]
    all_to_all x1, blocking collectives: 13.9 us -> 16 us  [on_device(): lax.all_to_all(attended, 'tensor', split_axis=0, concat_axis=1, tiled=True)]
    ppermute x6, starting transfers between devices: 20 us -> 18.3 us  [shifted(): return lax.ppermute(block, axis, route)]
    ppermute x6, waiting for transfers between devices: 27.1 us -> 28.6 us  [shifted(): return lax.ppermute(block, axis, route)]
    all_to_all x1, waiting for transfers between devices: 4.64 us -> 3.51 us  [on_device(): lax.all_to_all(packed, 'tensor', split_axis=1, concat_axis=0, tiled=True)]
  transfers between devices with their start and end apart: 7 -> 7, of which waited for: 6 -> 5; matrix products, arithmetic and copies ran while one was open for 4% -> 4% of each run, Pallas kernels for 9% -> 12%
where the time goes in v10:
time: 97 us; the launch traced here: 95.4 us
  waiting for transfers between devices  32.1 us (33%)
  starting transfers between devices  28.5 us (29%)
  blocking collectives  16 us (16%)
  Pallas kernels  11.4 us (12%)
  local copies, waits for them, and re-layouts  4.59 us (5%)
  other arithmetic  2.55 us (3%)
    ppermute x6, waiting for transfers between devices, shifted(): return lax.ppermute(block, axis, route)  28.6 us
    ppermute x6, starting transfers between devices, shifted(): return lax.ppermute(block, axis, route)  18.3 us
    all_to_all x1, blocking collectives, on_device(): lax.all_to_all(attended, 'tensor', split_axis=0, concat_axis=1, tiled=True)  16 us
    pallas_call x4, Pallas kernels, attend(): pl.pallas_call(functools.partial(_attend_kernel, dist, with_own), out_sha...  11.4 us
    all_to_all x1, starting transfers between devices, on_device(): lax.all_to_all(packed, 'tensor', split_axis=1, concat_axis=0, tiled=True)  10.2 us
    all_to_all x1, waiting for transfers between devices, on_device(): lax.all_to_all(packed, 'tensor', split_axis=1, concat_axis=0, tiled=True)  3.51 us
  transfers between devices with their start and end apart: 7, of which 5 were waited for; matrix products, arithmetic and copies ran while one was open for 4% of the time, Pallas kernels for 12%

profile of v10, /device:TPU:1, one launch (start us, length us, event | category | flops | bytes accessed | tf_op | source)
XLA Modules:
  0.0 95.4 jit_solution(5689398034772897436)
XLA Ops:
  0.0 1.0 copy.37
  1.0 0.7 pad_maximum_fusion
  1.7 10.2 %all-to-all-start = ((bf16[16,8,1024]{2,0,1:T(8,128)(2,1)}), bf16[16,8,1024]{2,0,1:T(8,128)(2,1)S(1)}, u32[]{:S(2)}, u32[]{:S(2)}) async-start(bf16[16,8,1024]{2,0,1:T(8,128)(2,1)} %pad_maximum_fusion), calls=%async_computation | async-start | bytes 524288 | tf_op jit(solution)/shard_map/all_to_all | solution.py:146
  12.0 0.6 gather_fusion
  12.6 0.2 fusion.1
  12.8 0.2 compare_reduce_fusion
  13.0 0.6 gather_fusion.1
  13.8 0.2 reduce_window_sum.11
  14.0 0.1 convert_reduce_fusion
  14.1 0.1 select_reduce_fusion.1
  14.3 0.6 pad_add_fusion.meta_ref
  14.9 3.5 %all-to-all-done = bf16[16,8,1024]{2,0,1:T(8,128)(2,1)S(1)} async-done(((bf16[16,8,1024]{2,0,1:T(8,128)(2,1)}), bf16[16,8,1024]{2,0,1:T(8,128)(2,1)S(1)}, u32[]{:S(2)}, u32[]{:S(2)}) %all-to-all-start) | async-done | bytes 262176 | tf_op jit(solution)/shard_map/all_to_all | solution.py:146
  18.5 1.9 %collective-permute-start = (bf16[128,512]{1,0:T(8,128)(2,1)S(1)}, bf16[128,512]{1,0:T(8,128)(2,1)S(1)}, u32[]{:S(2)}, u32[]{:S(2)}) collective-permute-start(bf16[128,512]{1,0:T(8,128)(2,1)S(1)} %slice.24.q_ref), channel_id=1, source_target_pairs={{504,0},{0,8},{8,16},{16,24},{24,32},{32,40},{40,48},{48,56},{56,6... | collective-permute-start | bytes 393224 | tf_op jit(solution)/shard_map/ppermute | solution.py:22
  20.4 0.7 fusion.9
  21.1 3.2 %shard_map.73 = f32[136,512]{1,0:T(8,128)} custom-call(s32[4,3,16]{2,1,0:T(4,128)} %pad_add_fusion.meta_ref, bf16[128,512]{1,0:T(8,128)(2,1)} %copy-done.3, bf16[16,128,256]{2,1,0:T(8,128)(2,1)} %kp_hbm.7, bf16[16,128,256]{2,1,0:T(8,128)(2,1)} %vp_hbm.7, bf16[128,256]{1,0:T(8,128)(2,1)} %get-tuple-element.18.refs_0_, bf16[128,256]{1,0:T(8,128)(2,1)} %get-tuple-element.17.refs_1_), custom_call_target="tpu_custom_call" | custom-call | flops 167772160 | bytes 1064960 | tf_op jit(solution)/shard_map/pallas_call | solution.py:110
  24.2 6.2 %collective-permute-done.q_ref = bf16[128,512]{1,0:T(8,128)(2,1)S(1)} collective-permute-done((bf16[128,512]{1,0:T(8,128)(2,1)S(1)}, bf16[128,512]{1,0:T(8,128)(2,1)S(1)}, u32[]{:S(2)}, u32[]{:S(2)}) %collective-permute-start) | collective-permute-done | bytes 131104 | tf_op jit(solution)/shard_map/ppermute | solution.py:22
  30.4 1.9 %collective-permute-start.2 = (bf16[128,512]{1,0:T(8,128)(2,1)S(1)}, bf16[128,512]{1,0:T(8,128)(2,1)S(1)}, u32[]{:S(2)}, u32[]{:S(2)}) collective-permute-start(bf16[128,512]{1,0:T(8,128)(2,1)S(1)} %collective-permute-done.q_ref), channel_id=1, source_target_pairs={{504,0},{0,8},{8,16},{16,24},{24,32},{32,40},{40,48},{48,56},{56,6... | collective-permute-start | bytes 393224 | tf_op jit(solution)/shard_map/ppermute | solution.py:22
  32.3 7.1 %collective-permute-done.2.q_ref = bf16[128,512]{1,0:T(8,128)(2,1)S(1)} collective-permute-done((bf16[128,512]{1,0:T(8,128)(2,1)S(1)}, bf16[128,512]{1,0:T(8,128)(2,1)S(1)}, u32[]{:S(2)}, u32[]{:S(2)}) %collective-permute-start.2) | collective-permute-done | bytes 131104 | tf_op jit(solution)/shard_map/ppermute | solution.py:22
  39.5 1.9 %collective-permute-start.4 = (bf16[128,512]{1,0:T(8,128)(2,1)S(1)}, bf16[128,512]{1,0:T(8,128)(2,1)S(1)}, u32[]{:S(2)}, u32[]{:S(2)}) collective-permute-start(bf16[128,512]{1,0:T(8,128)(2,1)S(1)} %collective-permute-done.2.q_ref), channel_id=1, source_target_pairs={{504,0},{0,8},{8,16},{16,24},{24,32},{32,40},{40,48},{48,56},{56,6... | collective-permute-start | bytes 393224 | tf_op jit(solution)/shard_map/ppermute | solution.py:22
  41.4 1.9 %shard_map.74 = f32[136,512]{1,0:T(8,128)} custom-call(s32[4,3,16]{2,1,0:T(4,128)} %pad_add_fusion.meta_ref, bf16[128,512]{1,0:T(8,128)(2,1)} %copy-done.4, bf16[16,128,256]{2,1,0:T(8,128)(2,1)} %kp_hbm.7, bf16[16,128,256]{2,1,0:T(8,128)(2,1)} %vp_hbm.7), custom_call_target="tpu_custom_call" | custom-call | flops 134217728 | bytes 933888 | tf_op jit(solution)/shard_map/pallas_call | solution.py:110
  43.3 8.2 %collective-permute-start.1 = (f32[136,512]{1,0:T(8,128)}, f32[136,512]{1,0:T(8,128)S(1)}, u32[]{:S(2)}, u32[]{:S(2)}) collective-permute-start(f32[136,512]{1,0:T(8,128)} %shard_map.74), channel_id=1, source_target_pairs={{8,0},{16,8},{24,16},{32,24},{40,32},{48,40},{56,48},{64,56},{72,6... | collective-permute-start | bytes 835592 | tf_op jit(solution)/shard_map/ppermute | solution.py:22
  51.6 3.1 %shard_map.75 = f32[136,512]{1,0:T(8,128)} custom-call(s32[4,3,16]{2,1,0:T(4,128)} %pad_add_fusion.meta_ref, bf16[128,512]{1,0:T(8,128)(2,1)} %copy-done.5, bf16[16,128,256]{2,1,0:T(8,128)(2,1)} %kp_hbm.7, bf16[16,128,256]{2,1,0:T(8,128)(2,1)} %vp_hbm.7), custom_call_target="tpu_custom_call" | custom-call | flops 134217728 | bytes 933888 | tf_op jit(solution)/shard_map/pallas_call | solution.py:110
  54.7 2.1 %collective-permute-start.3 = (f32[136,512]{1,0:T(8,128)}, f32[136,512]{1,0:T(8,128)S(1)}, u32[]{:S(2)}, u32[]{:S(2)}) collective-permute-start(f32[136,512]{1,0:T(8,128)} %shard_map.75), channel_id=1, source_target_pairs={{16,0},{24,8},{32,16},{40,24},{48,32},{56,40},{64,48},{72,56},{80,... | collective-permute-start | bytes 835592 | tf_op jit(solution)/shard_map/ppermute | solution.py:22
  56.8 0.6 copy-done.6
  57.4 3.1 %shard_map.76 = f32[136,512]{1,0:T(8,128)} custom-call(s32[4,3,16]{2,1,0:T(4,128)} %pad_add_fusion.meta_ref, bf16[128,512]{1,0:T(8,128)(2,1)} %copy-done.6, bf16[16,128,256]{2,1,0:T(8,128)(2,1)} %kp_hbm.7, bf16[16,128,256]{2,1,0:T(8,128)(2,1)} %vp_hbm.7), custom_call_target="tpu_custom_call" | custom-call | flops 134217728 | bytes 933888 | tf_op jit(solution)/shard_map/pallas_call | solution.py:110
  60.6 2.3 %collective-permute-start.5 = (f32[136,512]{1,0:T(8,128)}, f32[136,512]{1,0:T(8,128)S(1)}, u32[]{:S(2)}, u32[]{:S(2)}) collective-permute-start(f32[136,512]{1,0:T(8,128)} %shard_map.76), channel_id=1, source_target_pairs={{24,0},{32,8},{40,16},{48,24},{56,32},{64,40},{72,48},{80,56},{88,... | collective-permute-start | bytes 835592 | tf_op jit(solution)/shard_map/ppermute | solution.py:22
  62.9 3.9 %collective-permute-done.3 = f32[136,512]{1,0:T(8,128)S(1)} collective-permute-done((f32[136,512]{1,0:T(8,128)}, f32[136,512]{1,0:T(8,128)S(1)}, u32[]{:S(2)}, u32[]{:S(2)}) %collective-permute-start.3) | collective-permute-done | bytes 278560 | tf_op jit(solution)/shard_map/ppermute | solution.py:22
  66.8 11.4 %collective-permute-done.5 = f32[136,512]{1,0:T(8,128)S(1)} collective-permute-done((f32[136,512]{1,0:T(8,128)}, f32[136,512]{1,0:T(8,128)S(1)}, u32[]{:S(2)}, u32[]{:S(2)}) %collective-permute-start.5) | collective-permute-done | bytes 278560 | tf_op jit(solution)/shard_map/ppermute | solution.py:22
  78.3 0.1 copy.27
  78.4 0.2 div.11
  78.7 16.0 %all_to_all.34 = bf16[8,16,512]{2,1,0:T(8,128)(2,1)S(1)} all-to-all(bf16[8,16,512]{2,1,0:T(8,128)(2,1)S(1)} %bitcast.36), channel_id=1, replica_groups=mesh['pool'=64,'tensor'=8] {'tensor'}, dimensions={0} | all-to-all | bytes 262144 | tf_op jit(solution)/shard_map/all_to_all | solution.py:199
  94.7 0.7 copy.32
  (36 shorter events, 0.5 us)
Async XLA Ops:
  0.0 12.0 %copy-start = (s32[64,64]{1,0:T(8,128)S(1)}, s32[64,64]{1,0:T(8,128)}, u32[]{:S(2)}) copy-start(s32[64,64]{1,0:T(8,128)} %param.12) | copy-start | bytes 49156
  0.0 1.0 %copy-start.7 = (bf16[16,2048]{1,0:T(8,128)(2,1)S(1)}, bf16[16,2048]{1,0:T(8,128)(2,1)}, u32[]{:S(2)}) copy-start(bf16[16,2048]{1,0:T(8,128)(2,1)} %param.9) | copy-start | bytes 196612
  0.0 1.0 %copy-start.8 = (bf16[16,2048]{1,0:T(8,128)(2,1)S(1)}, bf16[16,2048]{1,0:T(8,128)(2,1)}, u32[]{:S(2)}) copy-start(bf16[16,2048]{1,0:T(8,128)(2,1)} %param.8) | copy-start | bytes 196612
  1.7 16.7 %all-to-all-start = ((bf16[16,8,1024]{2,0,1:T(8,128)(2,1)}), bf16[16,8,1024]{2,0,1:T(8,128)(2,1)S(1)}, u32[]{:S(2)}, u32[]{:S(2)}) async-start(bf16[16,8,1024]{2,0,1:T(8,128)(2,1)} %pad_maximum_fusion), calls=%async_computation | async-start | bytes 524288 | tf_op jit(solution)/shard_map/all_to_all | solution.py:146
  12.0 1.0 %copy-start.1 = (s32[64]{0:T(128)S(1)}, s32[64]{0:T(128)}, u32[]{:S(2)}) copy-start(s32[64]{0:T(128)} %param.13) | copy-start | bytes 772
  18.4 2.6 %copy-start.3 = (bf16[128,512]{1,0:T(8,128)(2,1)}, bf16[128,512]{1,0:T(8,128)(2,1)S(1)}, u32[]{:S(2)}) copy-start(bf16[128,512]{1,0:T(8,128)(2,1)S(1)} %slice.24.q_ref) | copy-start | bytes 393220
  18.5 12.0 %collective-permute-start = (bf16[128,512]{1,0:T(8,128)(2,1)S(1)}, bf16[128,512]{1,0:T(8,128)(2,1)S(1)}, u32[]{:S(2)}, u32[]{:S(2)}) collective-permute-start(bf16[128,512]{1,0:T(8,128)(2,1)S(1)} %slice.24.q_ref), channel_id=1, source_target_pairs={{504,0},{0,8},{8,16},{16,24},{24,32},{32,40},{40,48},{48,56},{56,6... | collective-permute-start | bytes 393224 | tf_op jit(solution)/shard_map/ppermute | solution.py:22
  30.4 10.9 %copy-start.4 = (bf16[128,512]{1,0:T(8,128)(2,1)}, bf16[128,512]{1,0:T(8,128)(2,1)S(1)}, u32[]{:S(2)}) copy-start(bf16[128,512]{1,0:T(8,128)(2,1)S(1)} %collective-permute-done.q_ref) | copy-start | bytes 393220
  30.4 9.0 %collective-permute-start.2 = (bf16[128,512]{1,0:T(8,128)(2,1)S(1)}, bf16[128,512]{1,0:T(8,128)(2,1)S(1)}, u32[]{:S(2)}, u32[]{:S(2)}) collective-permute-start(bf16[128,512]{1,0:T(8,128)(2,1)S(1)} %collective-permute-done.q_ref), channel_id=1, source_target_pairs={{504,0},{0,8},{8,16},{16,24},{24,32},{32,40},{40,48},{48,56},{56,6... | collective-permute-start | bytes 393224 | tf_op jit(solution)/shard_map/ppermute | solution.py:22
  39.4 3.9 %copy-start.5 = (bf16[128,512]{1,0:T(8,128)(2,1)}, bf16[128,512]{1,0:T(8,128)(2,1)S(1)}, u32[]{:S(2)}) copy-start(bf16[128,512]{1,0:T(8,128)(2,1)S(1)} %collective-permute-done.2.q_ref) | copy-start | bytes 393220
  39.5 17.3 %collective-permute-start.4 = (bf16[128,512]{1,0:T(8,128)(2,1)S(1)}, bf16[128,512]{1,0:T(8,128)(2,1)S(1)}, u32[]{:S(2)}, u32[]{:S(2)}) collective-permute-start(bf16[128,512]{1,0:T(8,128)(2,1)S(1)} %collective-permute-done.2.q_ref), channel_id=1, source_target_pairs={{504,0},{0,8},{8,16},{16,24},{24,32},{32,40},{40,48},{48,56},{56,6... | collective-permute-start | bytes 393224 | tf_op jit(solution)/shard_map/ppermute | solution.py:22
  43.3 19.6 %collective-permute-start.1 = (f32[136,512]{1,0:T(8,128)}, f32[136,512]{1,0:T(8,128)S(1)}, u32[]{:S(2)}, u32[]{:S(2)}) collective-permute-start(f32[136,512]{1,0:T(8,128)} %shard_map.74), channel_id=1, source_target_pairs={{8,0},{16,8},{24,16},{32,24},{40,32},{48,40},{56,48},{64,56},{72,6... | collective-permute-start | bytes 835592 | tf_op jit(solution)/shard_map/ppermute | solution.py:22
  54.7 23.5 %copy-start.2 = (f32[136,512]{1,0:T(8,128)S(1)}, f32[136,512]{1,0:T(8,128)}, u32[]{:S(2)}) copy-start(f32[136,512]{1,0:T(8,128)} %shard_map.73) | copy-start | bytes 835588
  54.7 12.0 %collective-permute-start.3 = (f32[136,512]{1,0:T(8,128)}, f32[136,512]{1,0:T(8,128)S(1)}, u32[]{:S(2)}, u32[]{:S(2)}) collective-permute-start(f32[136,512]{1,0:T(8,128)} %shard_map.75), channel_id=1, source_target_pairs={{16,0},{24,8},{32,16},{40,24},{48,32},{56,40},{64,48},{72,56},{80,... | collective-permute-start | bytes 835592 | tf_op jit(solution)/shard_map/ppermute | solution.py:22
  56.8 0.7 copy-start.6
  60.6 17.6 %collective-permute-start.5 = (f32[136,512]{1,0:T(8,128)}, f32[136,512]{1,0:T(8,128)S(1)}, u32[]{:S(2)}, u32[]{:S(2)}) collective-permute-start(f32[136,512]{1,0:T(8,128)} %shard_map.76), channel_id=1, source_target_pairs={{24,0},{32,8},{40,16},{48,24},{56,32},{64,40},{72,48},{80,56},{88,... | collective-permute-start | bytes 835592 | tf_op jit(solution)/shard_map/ppermute | solution.py:22

commit v11 on v10

--- a/solution.py
+++ b/solution.py
@@ -179,18 +179,19 @@
         own = (k_new, v_new) if offset == 0 else ()
         return attend(offset, meta, queries, cached_key_pages, cached_value_pages, *own)
 
-    held = q_own
-    total = None
-    for offset in range(SPAN):
-        here = part(offset, held)
-        if offset < SPAN - 1:
-            nxt = shifted(held, "pool", 1)
-            if offset < SPAN - 3:
-                nxt, here = lax.optimization_barrier((nxt, here))
-        back = here if offset == 0 else shifted(here, "pool", -offset)
-        total = back if total is None else total + back
-        if offset < SPAN - 1:
-            held = nxt
+    near = shifted(q_own, "pool", 1)
+    mid = shifted(q_own, "pool", 2)
+    part_own = part(0, q_own)
+    near, mid, part_own = lax.optimization_barrier((near, mid, part_own))
+    far = shifted(mid, "pool", 1)
+    part_near = part(1, near)
+    part_mid = part(2, mid)
+    far, part_near, part_mid = lax.optimization_barrier((far, part_near, part_mid))
+    parts = [part_own, part_near, part_mid, part(3, far)]
+
+    total = parts[SPAN - 1]
+    for offset in range(SPAN - 2, -1, -1):
+        total = parts[offset] + shifted(total, "pool", -1)
     heads = q_width // HEAD_SIZE
     numerator = total[:rows].reshape(rows, heads, HEAD_SIZE)
     totals = total[rows, : heads * rows].reshape(heads, rows)

time: 97 us -> 98 us (1.010)
  starting transfers between devices: 28.5 us -> 36.8 us
  waiting for transfers between devices: 32.1 us -> 25.4 us
  Pallas kernels: 11.4 us -> 16.1 us
  blocking collectives: 16 us -> 11.6 us
    ppermute x6, starting transfers between devices: 18.3 us -> 26.6 us  [shifted(): return lax.ppermute(block, axis, route)]
    ppermute x6, waiting for transfers between devices: 28.6 us -> 21.9 us  [shifted(): return lax.ppermute(block, axis, route)]
    pallas_call x4, Pallas kernels: 11.4 us -> 16.1 us  [attend(): pl.pallas_call(functools.partial(_attend_kernel, dist, with_own), out_sha...]
    all_to_all x1, blocking collectives: 16 us -> 11.6 us  [on_device(): lax.all_to_all(attended, 'tensor', split_axis=0, concat_axis=1, tiled=True)]
  transfers between devices with their start and end apart: 7 -> 7, of which waited for: 5 -> 6; matrix products, arithmetic and copies ran while one was open for 4% -> 4% of each run, Pallas kernels for 12% -> 12%
where the time goes in v11:
time: 98 us; the launch traced here: 97.3 us
  starting transfers between devices  36.8 us (38%)
  waiting for transfers between devices  25.4 us (26%)
  Pallas kernels  16.1 us (16%)
  blocking collectives  11.6 us (12%)
  local copies, waits for them, and re-layouts  4.61 us (5%)
  other arithmetic  2.55 us (3%)
    ppermute x6, starting transfers between devices, shifted(): return lax.ppermute(block, axis, route)  26.6 us
    ppermute x6, waiting for transfers between devices, shifted(): return lax.ppermute(block, axis, route)  21.9 us
    pallas_call x4, Pallas kernels, attend(): pl.pallas_call(functools.partial(_attend_kernel, dist, with_own), out_sha...  16.1 us
    all_to_all x1, blocking collectives, on_device(): lax.all_to_all(attended, 'tensor', split_axis=0, concat_axis=1, tiled=True)  11.6 us
    all_to_all x1, starting transfers between devices, on_device(): lax.all_to_all(packed, 'tensor', split_axis=1, concat_axis=0, tiled=True)  10.2 us
    all_to_all x1, waiting for transfers between devices, on_device(): lax.all_to_all(packed, 'tensor', split_axis=1, concat_axis=0, tiled=True)  3.53 us
  transfers between devices with their start and end apart: 7, of which 6 were waited for; matrix products, arithmetic and copies ran while one was open for 4% of the time, Pallas kernels for 12%

profile of v11, /device:TPU:1, one launch (start us, length us, event | category | flops | bytes accessed | tf_op | source)
XLA Modules:
  0.0 97.3 jit_solution(4832838605826571907)
XLA Ops:
  0.0 1.0 copy.37
  1.0 0.7 pad_maximum_fusion
  1.7 10.2 %all-to-all-start = ((bf16[16,8,1024]{2,0,1:T(8,128)(2,1)}), bf16[16,8,1024]{2,0,1:T(8,128)(2,1)S(1)}, u32[]{:S(2)}, u32[]{:S(2)}) async-start(bf16[16,8,1024]{2,0,1:T(8,128)(2,1)} %pad_maximum_fusion), calls=%async_computation | async-start | bytes 524288 | tf_op jit(solution)/shard_map/all_to_all | solution.py:146
  12.0 0.6 gather_fusion
  12.6 0.2 fusion.1
  12.8 0.2 compare_reduce_fusion
  13.0 0.6 gather_fusion.1
  13.8 0.2 reduce_window_sum.11
  14.0 0.1 convert_reduce_fusion
  14.3 0.6 pad_add_fusion.meta_ref
  14.9 3.5 %all-to-all-done = bf16[16,8,1024]{2,0,1:T(8,128)(2,1)S(1)} async-done(((bf16[16,8,1024]{2,0,1:T(8,128)(2,1)}), bf16[16,8,1024]{2,0,1:T(8,128)(2,1)S(1)}, u32[]{:S(2)}, u32[]{:S(2)}) %all-to-all-start) | async-done | bytes 262176 | tf_op jit(solution)/shard_map/all_to_all | solution.py:146
  18.5 1.9 %collective-permute-start.1 = (bf16[128,512]{1,0:T(8,128)(2,1)S(1)}, bf16[128,512]{1,0:T(8,128)(2,1)S(1)}, u32[]{:S(2)}, u32[]{:S(2)}) collective-permute-start(bf16[128,512]{1,0:T(8,128)(2,1)S(1)} %slice.24.q_ref), channel_id=1, source_target_pairs={{496,0},{504,8},{0,16},{8,24},{16,32},{24,40},{32,48},{40,56},{48,... | collective-permute-start | bytes 393224 | tf_op jit(solution)/shard_map/ppermute | solution.py:22
  20.4 2.1 %collective-permute-start = (bf16[128,512]{1,0:T(8,128)(2,1)S(1)}, bf16[128,512]{1,0:T(8,128)(2,1)S(1)}, u32[]{:S(2)}, u32[]{:S(2)}) collective-permute-start(bf16[128,512]{1,0:T(8,128)(2,1)S(1)} %slice.24.q_ref), channel_id=1, source_target_pairs={{504,0},{0,8},{8,16},{16,24},{24,32},{32,40},{40,48},{48,56},{56,6... | collective-permute-start | bytes 393224 | tf_op jit(solution)/shard_map/ppermute | solution.py:22
  22.5 0.7 fusion.9
  23.2 3.9 %shard_map.73 = f32[136,512]{1,0:T(8,128)} custom-call(s32[4,3,16]{2,1,0:T(4,128)} %pad_add_fusion.meta_ref, bf16[128,512]{1,0:T(8,128)(2,1)} %copy-done.5, bf16[16,128,256]{2,1,0:T(8,128)(2,1)} %kp_hbm.7, bf16[16,128,256]{2,1,0:T(8,128)(2,1)} %vp_hbm.7, bf16[128,256]{1,0:T(8,128)(2,1)} %get-tuple-element.26.refs_0_, bf16[128,256]{1,0:T(8,128)(2,1)} %get-tuple-element.25.refs_1_), custom_call_target="tpu_custom_call" | custom-call | flops 167772160 | bytes 1064960 | tf_op jit(solution)/shard_map/pallas_call | solution.py:110
  27.1 3.9 %collective-permute-done.1.q_ref = bf16[128,512]{1,0:T(8,128)(2,1)S(1)} collective-permute-done((bf16[128,512]{1,0:T(8,128)(2,1)S(1)}, bf16[128,512]{1,0:T(8,128)(2,1)S(1)}, u32[]{:S(2)}, u32[]{:S(2)}) %collective-permute-start.1) | collective-permute-done | bytes 131104 | tf_op jit(solution)/shard_map/ppermute | solution.py:22
  31.0 5.8 %collective-permute-done.q_ref = bf16[128,512]{1,0:T(8,128)(2,1)S(1)} collective-permute-done((bf16[128,512]{1,0:T(8,128)(2,1)S(1)}, bf16[128,512]{1,0:T(8,128)(2,1)S(1)}, u32[]{:S(2)}, u32[]{:S(2)}) %collective-permute-start) | collective-permute-done | bytes 131104 | tf_op jit(solution)/shard_map/ppermute | solution.py:22
  36.7 1.9 %collective-permute-start.2 = (bf16[128,512]{1,0:T(8,128)(2,1)S(1)}, bf16[128,512]{1,0:T(8,128)(2,1)S(1)}, u32[]{:S(2)}, u32[]{:S(2)}) collective-permute-start(bf16[128,512]{1,0:T(8,128)(2,1)S(1)} %collective-permute-done.1.q_ref), channel_id=1, source_target_pairs={{504,0},{0,8},{8,16},{16,24},{24,32},{32,40},{40,48},{48,56},{56,6... | collective-permute-start | bytes 393224 | tf_op jit(solution)/shard_map/ppermute | solution.py:22
  38.6 3.8 %shard_map.75 = f32[136,512]{1,0:T(8,128)} custom-call(s32[4,3,16]{2,1,0:T(4,128)} %pad_add_fusion.meta_ref, bf16[128,512]{1,0:T(8,128)(2,1)} %copy-done.6, bf16[16,128,256]{2,1,0:T(8,128)(2,1)} %kp_hbm.7, bf16[16,128,256]{2,1,0:T(8,128)(2,1)} %vp_hbm.7), custom_call_target="tpu_custom_call" | custom-call | flops 134217728 | bytes 933888 | tf_op jit(solution)/shard_map/pallas_call | solution.py:110
  42.5 4.2 %shard_map.74 = f32[136,512]{1,0:T(8,128)} custom-call(s32[4,3,16]{2,1,0:T(4,128)} %pad_add_fusion.meta_ref, bf16[128,512]{1,0:T(8,128)(2,1)} %copy-done.7, bf16[16,128,256]{2,1,0:T(8,128)(2,1)} %kp_hbm.7, bf16[16,128,256]{2,1,0:T(8,128)(2,1)} %vp_hbm.7), custom_call_target="tpu_custom_call" | custom-call | flops 134217728 | bytes 933888 | tf_op jit(solution)/shard_map/pallas_call | solution.py:110
  46.8 0.6 copy-done.8
  47.4 4.2 %shard_map.76 = f32[136,512]{1,0:T(8,128)} custom-call(s32[4,3,16]{2,1,0:T(4,128)} %pad_add_fusion.meta_ref, bf16[128,512]{1,0:T(8,128)(2,1)} %copy-done.8, bf16[16,128,256]{2,1,0:T(8,128)(2,1)} %kp_hbm.7, bf16[16,128,256]{2,1,0:T(8,128)(2,1)} %vp_hbm.7), custom_call_target="tpu_custom_call" | custom-call | flops 134217728 | bytes 933888 | tf_op jit(solution)/shard_map/pallas_call | solution.py:110
  51.6 5.7 %collective-permute-start.3 = (f32[136,512]{1,0:T(8,128)}, f32[136,512]{1,0:T(8,128)S(1)}, u32[]{:S(2)}, u32[]{:S(2)}) collective-permute-start(f32[136,512]{1,0:T(8,128)} %shard_map.76), channel_id=1, source_target_pairs={{8,0},{16,8},{24,16},{32,24},{40,32},{48,40},{56,48},{64,56},{72,6... | collective-permute-start | bytes 835592 | tf_op jit(solution)/shard_map/ppermute | solution.py:22
  57.4 5.0 %collective-permute-done.3 = f32[136,512]{1,0:T(8,128)S(1)} collective-permute-done((f32[136,512]{1,0:T(8,128)}, f32[136,512]{1,0:T(8,128)S(1)}, u32[]{:S(2)}, u32[]{:S(2)}) %collective-permute-start.3) | collective-permute-done | bytes 278560 | tf_op jit(solution)/shard_map/ppermute | solution.py:22
  62.4 7.5 %collective-permute-start.4 = (f32[136,512]{1,0:T(8,128)S(1)}, f32[136,512]{1,0:T(8,128)S(1)}, u32[]{:S(2)}, u32[]{:S(2)}) collective-permute-start(f32[136,512]{1,0:T(8,128)S(1)} %add.70), channel_id=1, source_target_pairs={{8,0},{16,8},{24,16},{32,24},{40,32},{48,40},{56,48},{64,56},{72,6... | collective-permute-start | bytes 835592 | tf_op jit(solution)/shard_map/ppermute | solution.py:22
  69.9 3.8 %collective-permute-done.4 = f32[136,512]{1,0:T(8,128)S(1)} collective-permute-done((f32[136,512]{1,0:T(8,128)S(1)}, f32[136,512]{1,0:T(8,128)S(1)}, u32[]{:S(2)}, u32[]{:S(2)}) %collective-permute-start.4) | collective-permute-done | bytes 278560 | tf_op jit(solution)/shard_map/ppermute | solution.py:22
  73.7 7.4 %collective-permute-start.5 = (f32[136,512]{1,0:T(8,128)S(1)}, f32[136,512]{1,0:T(8,128)S(1)}, u32[]{:S(2)}, u32[]{:S(2)}) collective-permute-start(f32[136,512]{1,0:T(8,128)S(1)} %add.71), channel_id=1, source_target_pairs={{8,0},{16,8},{24,16},{32,24},{40,32},{48,40},{56,48},{64,56},{72,6... | collective-permute-start | bytes 835592 | tf_op jit(solution)/shard_map/ppermute | solution.py:22
  81.1 3.5 %collective-permute-done.5 = f32[136,512]{1,0:T(8,128)S(1)} collective-permute-done((f32[136,512]{1,0:T(8,128)S(1)}, f32[136,512]{1,0:T(8,128)S(1)}, u32[]{:S(2)}, u32[]{:S(2)}) %collective-permute-start.5) | collective-permute-done | bytes 278560 | tf_op jit(solution)/shard_map/ppermute | solution.py:22
  84.7 0.1 copy.27
  84.8 0.2 div.11
  85.1 11.6 %all_to_all.34 = bf16[8,16,512]{2,1,0:T(8,128)(2,1)S(1)} all-to-all(bf16[8,16,512]{2,1,0:T(8,128)(2,1)S(1)} %bitcast.36), channel_id=1, replica_groups=mesh['pool'=64,'tensor'=8] {'tensor'}, dimensions={0} | all-to-all | bytes 262144 | tf_op jit(solution)/shard_map/all_to_all | solution.py:200
  96.7 0.7 copy.32
  (42 shorter events, 0.7 us)
Async XLA Ops:
  0.0 12.0 %copy-start = (s32[64,64]{1,0:T(8,128)S(1)}, s32[64,64]{1,0:T(8,128)}, u32[]{:S(2)}) copy-start(s32[64,64]{1,0:T(8,128)} %param.12) | copy-start | bytes 49156
  0.0 1.0 copy-start.9
  0.0 1.0 copy-start.10
  1.7 16.7 %all-to-all-start = ((bf16[16,8,1024]{2,0,1:T(8,128)(2,1)}), bf16[16,8,1024]{2,0,1:T(8,128)(2,1)S(1)}, u32[]{:S(2)}, u32[]{:S(2)}) async-start(bf16[16,8,1024]{2,0,1:T(8,128)(2,1)} %pad_maximum_fusion), calls=%async_computation | async-start | bytes 524288 | tf_op jit(solution)/shard_map/all_to_all | solution.py:146
  12.0 1.0 %copy-start.1 = (s32[64]{0:T(128)S(1)}, s32[64]{0:T(128)}, u32[]{:S(2)}) copy-start(s32[64]{0:T(128)} %param.13) | copy-start | bytes 772
  18.4 4.8 %copy-start.5 = (bf16[128,512]{1,0:T(8,128)(2,1)}, bf16[128,512]{1,0:T(8,128)(2,1)S(1)}, u32[]{:S(2)}) copy-start(bf16[128,512]{1,0:T(8,128)(2,1)S(1)} %slice.24.q_ref) | copy-start | bytes 393220
  18.5 12.5 %collective-permute-start.1 = (bf16[128,512]{1,0:T(8,128)(2,1)S(1)}, bf16[128,512]{1,0:T(8,128)(2,1)S(1)}, u32[]{:S(2)}, u32[]{:S(2)}) collective-permute-start(bf16[128,512]{1,0:T(8,128)(2,1)S(1)} %slice.24.q_ref), channel_id=1, source_target_pairs={{496,0},{504,8},{0,16},{8,24},{16,32},{24,40},{32,48},{40,56},{48,... | collective-permute-start | bytes 393224 | tf_op jit(solution)/shard_map/ppermute | solution.py:22
  20.4 16.3 %collective-permute-start = (bf16[128,512]{1,0:T(8,128)(2,1)S(1)}, bf16[128,512]{1,0:T(8,128)(2,1)S(1)}, u32[]{:S(2)}, u32[]{:S(2)}) collective-permute-start(bf16[128,512]{1,0:T(8,128)(2,1)S(1)} %slice.24.q_ref), channel_id=1, source_target_pairs={{504,0},{0,8},{8,16},{16,24},{24,32},{32,40},{40,48},{48,56},{56,6... | collective-permute-start | bytes 393224 | tf_op jit(solution)/shard_map/ppermute | solution.py:22
  31.0 7.7 %copy-start.6 = (bf16[128,512]{1,0:T(8,128)(2,1)}, bf16[128,512]{1,0:T(8,128)(2,1)S(1)}, u32[]{:S(2)}) copy-start(bf16[128,512]{1,0:T(8,128)(2,1)S(1)} %collective-permute-done.1.q_ref) | copy-start | bytes 393220
  36.7 5.8 %copy-start.7 = (bf16[128,512]{1,0:T(8,128)(2,1)}, bf16[128,512]{1,0:T(8,128)(2,1)S(1)}, u32[]{:S(2)}) copy-start(bf16[128,512]{1,0:T(8,128)(2,1)S(1)} %collective-permute-done.q_ref) | copy-start | bytes 393220
  36.7 10.0 %collective-permute-start.2 = (bf16[128,512]{1,0:T(8,128)(2,1)S(1)}, bf16[128,512]{1,0:T(8,128)(2,1)S(1)}, u32[]{:S(2)}, u32[]{:S(2)}) collective-permute-start(bf16[128,512]{1,0:T(8,128)(2,1)S(1)} %collective-permute-done.1.q_ref), channel_id=1, source_target_pairs={{504,0},{0,8},{8,16},{16,24},{24,32},{32,40},{40,48},{48,56},{56,6... | collective-permute-start | bytes 393224 | tf_op jit(solution)/shard_map/ppermute | solution.py:22
  46.7 15.7 %copy-start.4 = (f32[136,512]{1,0:T(8,128)S(1)}, f32[136,512]{1,0:T(8,128)}, u32[]{:S(2)}) copy-start(f32[136,512]{1,0:T(8,128)} %shard_map.75) | copy-start | bytes 835588
  46.7 0.7 copy-start.8
  51.6 22.1 %copy-start.3 = (f32[136,512]{1,0:T(8,128)S(1)}, f32[136,512]{1,0:T(8,128)}, u32[]{:S(2)}) copy-start(f32[136,512]{1,0:T(8,128)} %shard_map.74) | copy-start | bytes 835588
  51.6 10.8 %collective-permute-start.3 = (f32[136,512]{1,0:T(8,128)}, f32[136,512]{1,0:T(8,128)S(1)}, u32[]{:S(2)}, u32[]{:S(2)}) collective-permute-start(f32[136,512]{1,0:T(8,128)} %shard_map.76), channel_id=1, source_target_pairs={{8,0},{16,8},{24,16},{32,24},{40,32},{48,40},{56,48},{64,56},{72,6... | collective-permute-start | bytes 835592 | tf_op jit(solution)/shard_map/ppermute | solution.py:22
  62.4 22.2 %copy-start.2 = (f32[136,512]{1,0:T(8,128)S(1)}, f32[136,512]{1,0:T(8,128)}, u32[]{:S(2)}) copy-start(f32[136,512]{1,0:T(8,128)} %shard_map.73) | copy-start | bytes 835588
  62.4 11.2 %collective-permute-start.4 = (f32[136,512]{1,0:T(8,128)S(1)}, f32[136,512]{1,0:T(8,128)S(1)}, u32[]{:S(2)}, u32[]{:S(2)}) collective-permute-start(f32[136,512]{1,0:T(8,128)S(1)} %add.70), channel_id=1, source_target_pairs={{8,0},{16,8},{24,16},{32,24},{40,32},{48,40},{56,48},{64,56},{72,6... | collective-permute-start | bytes 835592 | tf_op jit(solution)/shard_map/ppermute | solution.py:22
  73.7 10.9 %collective-permute-start.5 = (f32[136,512]{1,0:T(8,128)S(1)}, f32[136,512]{1,0:T(8,128)S(1)}, u32[]{:S(2)}, u32[]{:S(2)}) collective-permute-start(f32[136,512]{1,0:T(8,128)S(1)} %add.71), channel_id=1, source_target_pairs={{8,0},{16,8},{24,16},{32,24},{40,32},{48,40},{56,48},{64,56},{72,6... | collective-permute-start | bytes 835592 | tf_op jit(solution)/shard_map/ppermute | solution.py:22

commit v12 on v6

--- a/solution.py
+++ b/solution.py
@@ -137,14 +137,14 @@
     kv_width = incoming_keys.shape[1] // tensor_size
     packed = jnp.concatenate(
         [
-            queries.reshape(n_tok, tensor_size, q_width),
-            incoming_keys.reshape(n_tok, tensor_size, kv_width),
-            incoming_values.reshape(n_tok, tensor_size, kv_width),
+            jnp.swapaxes(queries.reshape(n_tok, tensor_size, q_width), 0, 1),
+            jnp.swapaxes(incoming_keys.reshape(n_tok, tensor_size, kv_width), 0, 1),
+            jnp.swapaxes(incoming_values.reshape(n_tok, tensor_size, kv_width), 0, 1),
         ],
         axis=2,
     )
-    mixed = lax.all_to_all(packed, "tensor", split_axis=1, concat_axis=0, tiled=True)
-    rows = mixed.shape[0]
+    mixed = lax.all_to_all(packed, "tensor", split_axis=0, concat_axis=0, tiled=True)
+    rows = tensor_size * n_tok
     mixed = mixed.reshape(rows, q_width + 2 * kv_width)
     q_own = mixed[:, :q_width]
     k_new = mixed[:, q_width:q_width + kv_width]
@@ -193,8 +193,9 @@
     numerator = total[:rows].reshape(rows, heads, HEAD_SIZE)
     totals = total[rows, : heads * rows].reshape(heads, rows)
     attended = numerator / jnp.transpose(totals)[:, :, None]
-    attended = attended.reshape(rows, q_width).astype(jnp.bfloat16)
-    return lax.all_to_all(attended, "tensor", split_axis=0, concat_axis=1, tiled=True)
+    attended = attended.reshape(tensor_size, n_tok, q_width).astype(jnp.bfloat16)
+    sent = lax.all_to_all(attended, "tensor", split_axis=0, concat_axis=0, tiled=True)
+    return jnp.swapaxes(sent, 0, 1).reshape(n_tok, tensor_size * q_width)
 
 
 def solution(mesh):

time: 94.5 us -> 101 us (1.069)
  starting transfers between devices: 31.2 us -> 38.5 us
  blocking collectives: 15 us -> 17.5 us
  waiting for transfers between devices: 21.9 us -> 19.5 us
  Pallas kernels: 16.1 us -> 14 us
  local copies, waits for them, and re-layouts: 4.6 us -> 6.18 us
    ppermute x6, starting transfers between devices: 21 us -> 28.3 us  [shifted(): return lax.ppermute(block, axis, route)]
    all_to_all x1, blocking collectives: 15 us -> 17.5 us  [on_device(): lax.all_to_all(attended, 'tensor', split_axis=0, concat_axis=0, tiled=True)]
    ppermute x6, waiting for transfers between devices: 18.3 us -> 16 us  [shifted(): return lax.ppermute(block, axis, route)]
    pallas_call x4, Pallas kernels: 16.1 us -> 14 us  [attend(): pl.pallas_call(functools.partial(_attend_kernel, dist, with_own), out_sha...]
  transfers between devices with their start and end apart: 7 -> 7, of which waited for: 5 -> 5; matrix products, arithmetic and copies ran while one was open for 4% -> 4% of each run, Pallas kernels for 13% -> 11%
where the time goes in v12:
time: 101 us; the launch traced here: 100 us
  starting transfers between devices  38.5 us (38%)
  waiting for transfers between devices  19.5 us (19%)
  blocking collectives  17.5 us (17%)
  Pallas kernels  14 us (14%)
  local copies, waits for them, and re-layouts  6.18 us (6%)
  other arithmetic  4.5 us (4%)
    ppermute x6, starting transfers between devices, shifted(): return lax.ppermute(block, axis, route)  28.3 us
    all_to_all x1, blocking collectives, on_device(): lax.all_to_all(attended, 'tensor', split_axis=0, concat_axis=0, tiled=True)  17.5 us
    ppermute x6, waiting for transfers between devices, shifted(): return lax.ppermute(block, axis, route)  16 us
    pallas_call x4, Pallas kernels, attend(): pl.pallas_call(functools.partial(_attend_kernel, dist, with_own), out_sha...  14 us
    all_to_all x1, starting transfers between devices, on_device(): lax.all_to_all(packed, 'tensor', split_axis=0, concat_axis=0, tiled=True)  10.2 us
    all_to_all x1, waiting for transfers between devices, on_device(): lax.all_to_all(packed, 'tensor', split_axis=0, concat_axis=0, tiled=True)  3.51 us
    add x3, other arithmetic, on_device(): total = here + moved  2.07 us
  transfers between devices with their start and end apart: 7, of which 5 were waited for; matrix products, arithmetic and copies ran while one was open for 4% of the time, Pallas kernels for 11%

profile of v12, /device:TPU:1, one launch (start us, length us, event | category | flops | bytes accessed | tf_op | source)
XLA Modules:
  0.0 100.5 jit_solution(10959814026016294197)
XLA Ops:
  0.0 1.0 copy.36
  1.0 0.7 pad_maximum_fusion
  1.7 10.2 %all-to-all-start = ((bf16[8,16,1024]{2,1,0:T(8,128)(2,1)}), bf16[8,16,1024]{2,1,0:T(8,128)(2,1)S(1)}, u32[]{:S(2)}, u32[]{:S(2)}) async-start(bf16[8,16,1024]{2,1,0:T(8,128)(2,1)} %pad_maximum_fusion), calls=%async_computation | async-start | bytes 524288 | tf_op jit(solution)/shard_map/all_to_all | solution.py:146
  12.0 0.6 gather_fusion
  12.6 0.2 compare_reduce_fusion
  13.0 0.6 gather_fusion.1
  14.3 0.6 pad_add_fusion.meta_ref
  14.9 3.5 %all-to-all-done = bf16[8,16,1024]{2,1,0:T(8,128)(2,1)S(1)} async-done(((bf16[8,16,1024]{2,1,0:T(8,128)(2,1)}), bf16[8,16,1024]{2,1,0:T(8,128)(2,1)S(1)}, u32[]{:S(2)}, u32[]{:S(2)}) %all-to-all-start) | async-done | bytes 262176 | tf_op jit(solution)/shard_map/all_to_all | solution.py:146
  18.5 1.9 %collective-permute-start = (bf16[128,512]{1,0:T(8,128)(2,1)S(1)}, bf16[128,512]{1,0:T(8,128)(2,1)S(1)}, u32[]{:S(2)}, u32[]{:S(2)}) collective-permute-start(bf16[128,512]{1,0:T(8,128)(2,1)S(1)} %slice.24.q_ref), channel_id=1, source_target_pairs={{504,0},{0,8},{8,16},{16,24},{24,32},{32,40},{40,48},{48,56},{56,6... | collective-permute-start | bytes 393224 | tf_op jit(solution)/shard_map/ppermute | solution.py:22
  20.4 2.1 %collective-permute-start.1 = (bf16[128,512]{1,0:T(8,128)(2,1)S(1)}, bf16[128,512]{1,0:T(8,128)(2,1)S(1)}, u32[]{:S(2)}, u32[]{:S(2)}) collective-permute-start(bf16[128,512]{1,0:T(8,128)(2,1)S(1)} %slice.24.q_ref), channel_id=1, source_target_pairs={{496,0},{504,8},{0,16},{8,24},{16,32},{24,40},{32,48},{40,56},{48,... | collective-permute-start | bytes 393224 | tf_op jit(solution)/shard_map/ppermute | solution.py:22
  22.5 7.5 %collective-permute-start.2 = (bf16[128,512]{1,0:T(8,128)(2,1)S(1)}, bf16[128,512]{1,0:T(8,128)(2,1)S(1)}, u32[]{:S(2)}, u32[]{:S(2)}) collective-permute-start(bf16[128,512]{1,0:T(8,128)(2,1)S(1)} %slice.24.q_ref), channel_id=1, source_target_pairs={{488,0},{496,8},{504,16},{0,24},{8,32},{16,40},{24,48},{32,56},{40... | collective-permute-start | bytes 393224 | tf_op jit(solution)/shard_map/ppermute | solution.py:22
  30.0 0.7 fusion.8
  30.6 3.2 %shard_map.73 = f32[136,512]{1,0:T(8,128)} custom-call(s32[4,3,16]{2,1,0:T(4,128)} %pad_add_fusion.meta_ref, bf16[128,512]{1,0:T(8,128)(2,1)} %copy-done.4, bf16[16,128,256]{2,1,0:T(8,128)(2,1)} %kp_hbm.7, bf16[16,128,256]{2,1,0:T(8,128)(2,1)} %vp_hbm.7, bf16[128,256]{1,0:T(8,128)(2,1)} %get-tuple-element.34.refs_0_, bf16[128,256]{1,0:T(8,128)(2,1)} %get-tuple-element.33.refs_1_), custom_call_target="tpu_custom_call" | custom-call | flops 167772160 | bytes 1064960 | tf_op jit(solution)/shard_map/pallas_call | solution.py:110
  33.8 1.6 %collective-permute-done.1.q_ref = bf16[128,512]{1,0:T(8,128)(2,1)S(1)} collective-permute-done((bf16[128,512]{1,0:T(8,128)(2,1)S(1)}, bf16[128,512]{1,0:T(8,128)(2,1)S(1)}, u32[]{:S(2)}, u32[]{:S(2)}) %collective-permute-start.1) | collective-permute-done | bytes 131104 | tf_op jit(solution)/shard_map/ppermute | solution.py:22
  35.4 9.0 %collective-permute-done.2.q_ref = bf16[128,512]{1,0:T(8,128)(2,1)S(1)} collective-permute-done((bf16[128,512]{1,0:T(8,128)(2,1)S(1)}, bf16[128,512]{1,0:T(8,128)(2,1)S(1)}, u32[]{:S(2)}, u32[]{:S(2)}) %collective-permute-start.2) | collective-permute-done | bytes 131104 | tf_op jit(solution)/shard_map/ppermute | solution.py:22
  44.4 0.6 copy-done.7
  45.1 3.1 %shard_map.74 = f32[136,512]{1,0:T(8,128)} custom-call(s32[4,3,16]{2,1,0:T(4,128)} %pad_add_fusion.meta_ref, bf16[128,512]{1,0:T(8,128)(2,1)} %copy-done.7, bf16[16,128,256]{2,1,0:T(8,128)(2,1)} %kp_hbm.7, bf16[16,128,256]{2,1,0:T(8,128)(2,1)} %vp_hbm.7), custom_call_target="tpu_custom_call" | custom-call | flops 134217728 | bytes 933888 | tf_op jit(solution)/shard_map/pallas_call | solution.py:110
  48.2 5.2 %collective-permute-start.3 = (f32[136,512]{1,0:T(8,128)}, f32[136,512]{1,0:T(8,128)S(1)}, u32[]{:S(2)}, u32[]{:S(2)}) collective-permute-start(f32[136,512]{1,0:T(8,128)} %shard_map.74), channel_id=1, source_target_pairs={{8,0},{16,8},{24,16},{32,24},{40,32},{48,40},{56,48},{64,56},{72,6... | collective-permute-start | bytes 835592 | tf_op jit(solution)/shard_map/ppermute | solution.py:22
  53.4 3.9 %shard_map.75 = f32[136,512]{1,0:T(8,128)} custom-call(s32[4,3,16]{2,1,0:T(4,128)} %pad_add_fusion.meta_ref, bf16[128,512]{1,0:T(8,128)(2,1)} %copy-done.6, bf16[16,128,256]{2,1,0:T(8,128)(2,1)} %kp_hbm.7, bf16[16,128,256]{2,1,0:T(8,128)(2,1)} %vp_hbm.7), custom_call_target="tpu_custom_call" | custom-call | flops 134217728 | bytes 933888 | tf_op jit(solution)/shard_map/pallas_call | solution.py:110
  57.3 2.0 %collective-permute-done.3 = f32[136,512]{1,0:T(8,128)S(1)} collective-permute-done((f32[136,512]{1,0:T(8,128)}, f32[136,512]{1,0:T(8,128)S(1)}, u32[]{:S(2)}, u32[]{:S(2)}) %collective-permute-start.3) | collective-permute-done | bytes 278560 | tf_op jit(solution)/shard_map/ppermute | solution.py:22
  59.2 1.0 add.70
  60.2 5.0 %collective-permute-start.4 = (f32[136,512]{1,0:T(8,128)S(1)}, f32[136,512]{1,0:T(8,128)S(1)}, u32[]{:S(2)}, u32[]{:S(2)}) collective-permute-start(f32[136,512]{1,0:T(8,128)S(1)} %add.70), channel_id=1, source_target_pairs={{8,0},{16,8},{24,16},{32,24},{40,32},{48,40},{56,48},{64,56},{72,6... | collective-permute-start | bytes 835592 | tf_op jit(solution)/shard_map/ppermute | solution.py:22
  65.2 3.8 %shard_map.76 = f32[136,512]{1,0:T(8,128)} custom-call(s32[4,3,16]{2,1,0:T(4,128)} %pad_add_fusion.meta_ref, bf16[128,512]{1,0:T(8,128)(2,1)} %copy-done.5, bf16[16,128,256]{2,1,0:T(8,128)(2,1)} %kp_hbm.7, bf16[16,128,256]{2,1,0:T(8,128)(2,1)} %vp_hbm.7), custom_call_target="tpu_custom_call" | custom-call | flops 134217728 | bytes 933888 | tf_op jit(solution)/shard_map/pallas_call | solution.py:110
  69.1 1.0 %add.71 = f32[136,512]{1,0:T(8,128)S(1)} add(f32[136,512]{1,0:T(8,128)} %shard_map.76, f32[136,512]{1,0:T(8,128)S(1)} %collective-permute-done.4) | non-fusion elementwise | flops 69632 | bytes 835584 | tf_op jit(solution)/shard_map/add | solution.py:191
  70.1 6.7 %collective-permute-start.5 = (f32[136,512]{1,0:T(8,128)S(1)}, f32[136,512]{1,0:T(8,128)S(1)}, u32[]{:S(2)}, u32[]{:S(2)}) collective-permute-start(f32[136,512]{1,0:T(8,128)S(1)} %add.71), channel_id=1, source_target_pairs={{8,0},{16,8},{24,16},{32,24},{40,32},{48,40},{56,48},{64,56},{72,6... | collective-permute-start | bytes 835592 | tf_op jit(solution)/shard_map/ppermute | solution.py:22
  76.8 3.5 %collective-permute-done.5 = f32[136,512]{1,0:T(8,128)S(1)} collective-permute-done((f32[136,512]{1,0:T(8,128)S(1)}, f32[136,512]{1,0:T(8,128)S(1)}, u32[]{:S(2)}, u32[]{:S(2)}) %collective-permute-start.5) | collective-permute-done | bytes 278560 | tf_op jit(solution)/shard_map/ppermute | solution.py:22
  80.4 0.7 copy-done.3
  81.1 0.2 div.11
  81.4 0.2 div.12
  81.6 0.7 slice-done
  82.3 17.5 %all_to_all.10 = bf16[8,16,512]{2,1,0:T(8,128)(2,1)S(1)} all-to-all(bf16[8,16,512]{2,1,0:T(8,128)(2,1)S(1)} %divide_convert_fusion), channel_id=1, replica_groups=mesh['pool'=64,'tensor'=8] {'tensor'}, dimensions={0} | all-to-all | bytes 262144 | tf_op jit(solution)/shard_map/all_to_all | solution.py:197
  99.8 0.7 copy.32
  (42 shorter events, 1.2 us)
Async XLA Ops:
  0.0 12.0 %copy-start = (s32[64,64]{1,0:T(8,128)S(1)}, s32[64,64]{1,0:T(8,128)}, u32[]{:S(2)}) copy-start(s32[64,64]{1,0:T(8,128)} %param.12) | copy-start | bytes 49156
  0.0 1.0 copy-start.8
  0.0 1.0 copy-start.9
  1.7 16.7 %all-to-all-start = ((bf16[8,16,1024]{2,1,0:T(8,128)(2,1)}), bf16[8,16,1024]{2,1,0:T(8,128)(2,1)S(1)}, u32[]{:S(2)}, u32[]{:S(2)}) async-start(bf16[8,16,1024]{2,1,0:T(8,128)(2,1)} %pad_maximum_fusion), calls=%async_computation | async-start | bytes 524288 | tf_op jit(solution)/shard_map/all_to_all | solution.py:146
  12.0 1.0 %copy-start.1 = (s32[64]{0:T(128)S(1)}, s32[64]{0:T(128)}, u32[]{:S(2)}) copy-start(s32[64]{0:T(128)} %param.13) | copy-start | bytes 772
  18.4 12.2 %copy-start.4 = (bf16[128,512]{1,0:T(8,128)(2,1)}, bf16[128,512]{1,0:T(8,128)(2,1)S(1)}, u32[]{:S(2)}) copy-start(bf16[128,512]{1,0:T(8,128)(2,1)S(1)} %slice.24.q_ref) | copy-start | bytes 393220
  18.5 15.4 %collective-permute-start = (bf16[128,512]{1,0:T(8,128)(2,1)S(1)}, bf16[128,512]{1,0:T(8,128)(2,1)S(1)}, u32[]{:S(2)}, u32[]{:S(2)}) collective-permute-start(bf16[128,512]{1,0:T(8,128)(2,1)S(1)} %slice.24.q_ref), channel_id=1, source_target_pairs={{504,0},{0,8},{8,16},{16,24},{24,32},{32,40},{40,48},{48,56},{56,6... | collective-permute-start | bytes 393224 | tf_op jit(solution)/shard_map/ppermute | solution.py:22
  20.4 15.1 %collective-permute-start.1 = (bf16[128,512]{1,0:T(8,128)(2,1)S(1)}, bf16[128,512]{1,0:T(8,128)(2,1)S(1)}, u32[]{:S(2)}, u32[]{:S(2)}) collective-permute-start(bf16[128,512]{1,0:T(8,128)(2,1)S(1)} %slice.24.q_ref), channel_id=1, source_target_pairs={{496,0},{504,8},{0,16},{8,24},{16,32},{24,40},{32,48},{40,56},{48,... | collective-permute-start | bytes 393224 | tf_op jit(solution)/shard_map/ppermute | solution.py:22
  22.5 21.9 %collective-permute-start.2 = (bf16[128,512]{1,0:T(8,128)(2,1)S(1)}, bf16[128,512]{1,0:T(8,128)(2,1)S(1)}, u32[]{:S(2)}, u32[]{:S(2)}) collective-permute-start(bf16[128,512]{1,0:T(8,128)(2,1)S(1)} %slice.24.q_ref), channel_id=1, source_target_pairs={{488,0},{496,8},{504,16},{0,24},{8,32},{16,40},{24,48},{32,56},{40... | collective-permute-start | bytes 393224 | tf_op jit(solution)/shard_map/ppermute | solution.py:22
  33.8 14.4 %copy-start.5 = (bf16[128,512]{1,0:T(8,128)(2,1)}, bf16[128,512]{1,0:T(8,128)(2,1)S(1)}, u32[]{:S(2)}) copy-start(bf16[128,512]{1,0:T(8,128)(2,1)S(1)} %collective-permute-done.q_ref) | copy-start | bytes 393220
  35.4 12.8 %copy-start.6 = (bf16[128,512]{1,0:T(8,128)(2,1)}, bf16[128,512]{1,0:T(8,128)(2,1)S(1)}, u32[]{:S(2)}) copy-start(bf16[128,512]{1,0:T(8,128)(2,1)S(1)} %collective-permute-done.1.q_ref) | copy-start | bytes 393220
  44.4 0.6 copy-start.7
  48.2 11.0 %collective-permute-start.3 = (f32[136,512]{1,0:T(8,128)}, f32[136,512]{1,0:T(8,128)S(1)}, u32[]{:S(2)}, u32[]{:S(2)}) collective-permute-start(f32[136,512]{1,0:T(8,128)} %shard_map.74), channel_id=1, source_target_pairs={{8,0},{16,8},{24,16},{32,24},{40,32},{48,40},{56,48},{64,56},{72,6... | collective-permute-start | bytes 835592 | tf_op jit(solution)/shard_map/ppermute | solution.py:22
  60.2 8.8 %collective-permute-start.4 = (f32[136,512]{1,0:T(8,128)S(1)}, f32[136,512]{1,0:T(8,128)S(1)}, u32[]{:S(2)}, u32[]{:S(2)}) collective-permute-start(f32[136,512]{1,0:T(8,128)S(1)} %add.70), channel_id=1, source_target_pairs={{8,0},{16,8},{24,16},{32,24},{40,32},{48,40},{56,48},{64,56},{72,6... | collective-permute-start | bytes 835592 | tf_op jit(solution)/shard_map/ppermute | solution.py:22
  69.1 11.2 %copy-start.2 = (f32[136,512]{1,0:T(8,128)S(1)}, f32[136,512]{1,0:T(8,128)}, u32[]{:S(2)}) copy-start(f32[136,512]{1,0:T(8,128)} %shard_map.73) | copy-start | bytes 835588
  70.1 10.2 %collective-permute-start.5 = (f32[136,512]{1,0:T(8,128)S(1)}, f32[136,512]{1,0:T(8,128)S(1)}, u32[]{:S(2)}, u32[]{:S(2)}) collective-permute-start(f32[136,512]{1,0:T(8,128)S(1)} %add.71), channel_id=1, source_target_pairs={{8,0},{16,8},{24,16},{32,24},{40,32},{48,40},{56,48},{64,56},{72,6... | collective-permute-start | bytes 835592 | tf_op jit(solution)/shard_map/ppermute | solution.py:22
  80.3 0.7 copy-start.3
  81.3 1.0 slice-start

commit v13 on v6

--- a/solution.py
+++ b/solution.py
@@ -184,16 +184,17 @@
         return attend(offset, meta, received[offset], cached_key_pages, cached_value_pages)
 
     total = part(SPAN - 1)
-    for offset in range(SPAN - 2, -1, -1):
+    for offset in range(SPAN - 2, 0, -1):
         moved = shifted(total, "pool", -1)
-        here = part(offset) if offset > 0 else part_own
-        moved, here = lax.optimization_barrier((moved, here))
+        moved, here = lax.optimization_barrier((moved, part(offset)))
         total = here + moved
+    total = total + shifted(part_own, "pool", 1)
     heads = q_width // HEAD_SIZE
     numerator = total[:rows].reshape(rows, heads, HEAD_SIZE)
     totals = total[rows, : heads * rows].reshape(heads, rows)
     attended = numerator / jnp.transpose(totals)[:, :, None]
     attended = attended.reshape(rows, q_width).astype(jnp.bfloat16)
+    attended = shifted(attended, "pool", -1)
     return lax.all_to_all(attended, "tensor", split_axis=0, concat_axis=1, tiled=True)
 
 

time: 94.5 us -> 98.9 us (1.047)
  blocking collectives: 15 us -> 17.4 us
  waiting for transfers between devices: 21.9 us -> 24.1 us
    all_to_all x1, blocking collectives: 15 us -> 17.4 us  [on_device(): lax.all_to_all(attended, 'tensor', split_axis=0, concat_axis=1, tiled=True)]
    ppermute x6 -> x7, waiting for transfers between devices: 18.3 us -> 20.5 us  [shifted(): return lax.ppermute(block, axis, route)]
    add x3 -> x1, other arithmetic: 2.02 us -> 0.99 us  [on_device(): total = here + moved]
    add x0 -> x1, other arithmetic: none -> 1.01 us  [on_device(): total = total + shifted(part_own, 'pool', 1)]
    ppermute x6 -> x7, starting transfers between devices: 21 us -> 21 us  [shifted(): return lax.ppermute(block, axis, route)]
  transfers between devices with their start and end apart: 7 -> 8, of which waited for: 5 -> 6; matrix products, arithmetic and copies ran while one was open for 4% -> 4% of each run, Pallas kernels for 13% -> 13%
where the time goes in v13:
time: 98.9 us; the launch traced here: 98.1 us
  starting transfers between devices  31.2 us (32%)
  waiting for transfers between devices  24.1 us (24%)
  blocking collectives  17.4 us (18%)
  Pallas kernels  16.1 us (16%)
  local copies, waits for them, and re-layouts  4.59 us (5%)
  other arithmetic  4.44 us (4%)
    ppermute x7, starting transfers between devices, shifted(): return lax.ppermute(block, axis, route)  21 us
    ppermute x7, waiting for transfers between devices, shifted(): return lax.ppermute(block, axis, route)  20.5 us
    all_to_all x1, blocking collectives, on_device(): lax.all_to_all(attended, 'tensor', split_axis=0, concat_axis=1, tiled=True)  17.4 us
    pallas_call x4, Pallas kernels, attend(): pl.pallas_call(functools.partial(_attend_kernel, dist, with_own), out_sha...  16.1 us
    all_to_all x1, starting transfers between devices, on_device(): lax.all_to_all(packed, 'tensor', split_axis=1, concat_axis=0, tiled=True)  10.2 us
    all_to_all x1, waiting for transfers between devices, on_device(): lax.all_to_all(packed, 'tensor', split_axis=1, concat_axis=0, tiled=True)  3.53 us
  transfers between devices with their start and end apart: 8, of which 6 were waited for; matrix products, arithmetic and copies ran while one was open for 4% of the time, Pallas kernels for 13%

profile of v13, /device:TPU:1, one launch (start us, length us, event | category | flops | bytes accessed | tf_op | source)
XLA Modules:
  0.0 98.1 jit_solution(7656600394047735149)
XLA Ops:
  0.0 1.0 copy.37
  1.0 0.7 pad_maximum_fusion
  1.7 10.2 %all-to-all-start = ((bf16[16,8,1024]{2,0,1:T(8,128)(2,1)}), bf16[16,8,1024]{2,0,1:T(8,128)(2,1)S(1)}, u32[]{:S(2)}, u32[]{:S(2)}) async-start(bf16[16,8,1024]{2,0,1:T(8,128)(2,1)} %pad_maximum_fusion), calls=%async_computation | async-start | bytes 524288 | tf_op jit(solution)/shard_map/all_to_all | solution.py:146
  12.0 0.6 gather_fusion
  12.6 0.2 compare_reduce_fusion
  12.8 0.2 fusion.1
  13.0 0.6 gather_fusion.1
  13.8 0.2 reduce_window_sum.11
  14.3 0.6 pad_add_fusion.meta_ref
  14.9 3.5 %all-to-all-done = bf16[16,8,1024]{2,0,1:T(8,128)(2,1)S(1)} async-done(((bf16[16,8,1024]{2,0,1:T(8,128)(2,1)}), bf16[16,8,1024]{2,0,1:T(8,128)(2,1)S(1)}, u32[]{:S(2)}, u32[]{:S(2)}) %all-to-all-start) | async-done | bytes 262176 | tf_op jit(solution)/shard_map/all_to_all | solution.py:146
  18.5 1.9 %collective-permute-start = (bf16[128,512]{1,0:T(8,128)(2,1)S(1)}, bf16[128,512]{1,0:T(8,128)(2,1)S(1)}, u32[]{:S(2)}, u32[]{:S(2)}) collective-permute-start(bf16[128,512]{1,0:T(8,128)(2,1)S(1)} %slice.24.q_ref), channel_id=1, source_target_pairs={{504,0},{0,8},{8,16},{16,24},{24,32},{32,40},{40,48},{48,56},{56,6... | collective-permute-start | bytes 393224 | tf_op jit(solution)/shard_map/ppermute | solution.py:22
  20.4 2.1 %collective-permute-start.1 = (bf16[128,512]{1,0:T(8,128)(2,1)S(1)}, bf16[128,512]{1,0:T(8,128)(2,1)S(1)}, u32[]{:S(2)}, u32[]{:S(2)}) collective-permute-start(bf16[128,512]{1,0:T(8,128)(2,1)S(1)} %slice.24.q_ref), channel_id=1, source_target_pairs={{496,0},{504,8},{0,16},{8,24},{16,32},{24,40},{32,48},{40,56},{48,... | collective-permute-start | bytes 393224 | tf_op jit(solution)/shard_map/ppermute | solution.py:22
  22.5 7.5 %collective-permute-start.2 = (bf16[128,512]{1,0:T(8,128)(2,1)S(1)}, bf16[128,512]{1,0:T(8,128)(2,1)S(1)}, u32[]{:S(2)}, u32[]{:S(2)}) collective-permute-start(bf16[128,512]{1,0:T(8,128)(2,1)S(1)} %slice.24.q_ref), channel_id=1, source_target_pairs={{488,0},{496,8},{504,16},{0,24},{8,32},{16,40},{24,48},{32,56},{40... | collective-permute-start | bytes 393224 | tf_op jit(solution)/shard_map/ppermute | solution.py:22
  30.0 0.7 fusion.9
  30.7 4.6 %shard_map.73 = f32[136,512]{1,0:T(8,128)} custom-call(s32[4,3,16]{2,1,0:T(4,128)} %pad_add_fusion.meta_ref, bf16[128,512]{1,0:T(8,128)(2,1)} %copy-done.2, bf16[16,128,256]{2,1,0:T(8,128)(2,1)} %kp_hbm.7, bf16[16,128,256]{2,1,0:T(8,128)(2,1)} %vp_hbm.7, bf16[128,256]{1,0:T(8,128)(2,1)} %get-tuple-element.30.refs_0_, bf16[128,256]{1,0:T(8,128)(2,1)} %get-tuple-element.29.refs_1_), custom_call_target="tpu_custom_call" | custom-call | flops 167772160 | bytes 1064960 | tf_op jit(solution)/shard_map/pallas_call | solution.py:110
  35.4 9.0 %collective-permute-done.2.q_ref = bf16[128,512]{1,0:T(8,128)(2,1)S(1)} collective-permute-done((bf16[128,512]{1,0:T(8,128)(2,1)S(1)}, bf16[128,512]{1,0:T(8,128)(2,1)S(1)}, u32[]{:S(2)}, u32[]{:S(2)}) %collective-permute-start.2) | collective-permute-done | bytes 131104 | tf_op jit(solution)/shard_map/ppermute | solution.py:22
  44.4 0.6 copy-done.6
  45.1 3.1 %shard_map.74 = f32[136,512]{1,0:T(8,128)} custom-call(s32[4,3,16]{2,1,0:T(4,128)} %pad_add_fusion.meta_ref, bf16[128,512]{1,0:T(8,128)(2,1)} %copy-done.6, bf16[16,128,256]{2,1,0:T(8,128)(2,1)} %kp_hbm.7, bf16[16,128,256]{2,1,0:T(8,128)(2,1)} %vp_hbm.7), custom_call_target="tpu_custom_call" | custom-call | flops 134217728 | bytes 933888 | tf_op jit(solution)/shard_map/pallas_call | solution.py:110
  48.2 1.9 %collective-permute-start.3 = (f32[136,512]{1,0:T(8,128)}, f32[136,512]{1,0:T(8,128)S(1)}, u32[]{:S(2)}, u32[]{:S(2)}) collective-permute-start(f32[136,512]{1,0:T(8,128)} %shard_map.74), channel_id=1, source_target_pairs={{8,0},{16,8},{24,16},{32,24},{40,32},{48,40},{56,48},{64,56},{72,6... | collective-permute-start | bytes 835592 | tf_op jit(solution)/shard_map/ppermute | solution.py:22
  50.2 4.9 %shard_map.75 = f32[136,512]{1,0:T(8,128)} custom-call(s32[4,3,16]{2,1,0:T(4,128)} %pad_add_fusion.meta_ref, bf16[128,512]{1,0:T(8,128)(2,1)} %copy-done.5, bf16[16,128,256]{2,1,0:T(8,128)(2,1)} %kp_hbm.7, bf16[16,128,256]{2,1,0:T(8,128)(2,1)} %vp_hbm.7), custom_call_target="tpu_custom_call" | custom-call | flops 134217728 | bytes 933888 | tf_op jit(solution)/shard_map/pallas_call | solution.py:110
  55.1 2.2 %collective-permute-done.3 = f32[136,512]{1,0:T(8,128)S(1)} collective-permute-done((f32[136,512]{1,0:T(8,128)}, f32[136,512]{1,0:T(8,128)S(1)}, u32[]{:S(2)}, u32[]{:S(2)}) %collective-permute-start.3) | collective-permute-done | bytes 278560 | tf_op jit(solution)/shard_map/ppermute | solution.py:22
  57.3 1.0 %add.70 = f32[136,512]{1,0:T(8,128)S(1)} add(f32[136,512]{1,0:T(8,128)} %shard_map.75, f32[136,512]{1,0:T(8,128)S(1)} %collective-permute-done.3) | non-fusion elementwise | flops 69632 | bytes 835584 | tf_op jit(solution)/shard_map/add | solution.py:190
  58.3 3.7 %collective-permute-start.4 = (f32[136,512]{1,0:T(8,128)S(1)}, f32[136,512]{1,0:T(8,128)S(1)}, u32[]{:S(2)}, u32[]{:S(2)}) collective-permute-start(f32[136,512]{1,0:T(8,128)S(1)} %add.70), channel_id=1, source_target_pairs={{8,0},{16,8},{24,16},{32,24},{40,32},{48,40},{56,48},{64,56},{72,6... | collective-permute-start | bytes 835592 | tf_op jit(solution)/shard_map/ppermute | solution.py:22
  62.0 1.9 %collective-permute-start.5 = (f32[136,512]{1,0:T(8,128)S(1)}, f32[136,512]{1,0:T(8,128)S(1)}, u32[]{:S(2)}, u32[]{:S(2)}) collective-permute-start(f32[136,512]{1,0:T(8,128)S(1)} %copy-done.3), channel_id=1, source_target_pairs={{504,0},{0,8},{8,16},{16,24},{24,32},{32,40},{40,48},{48,56},{56,6... | collective-permute-start | bytes 835592 | tf_op jit(solution)/shard_map/ppermute | solution.py:22
  63.9 3.5 %shard_map.76 = f32[136,512]{1,0:T(8,128)} custom-call(s32[4,3,16]{2,1,0:T(4,128)} %pad_add_fusion.meta_ref, bf16[128,512]{1,0:T(8,128)(2,1)} %copy-done.4, bf16[16,128,256]{2,1,0:T(8,128)(2,1)} %kp_hbm.7, bf16[16,128,256]{2,1,0:T(8,128)(2,1)} %vp_hbm.7), custom_call_target="tpu_custom_call" | custom-call | flops 134217728 | bytes 933888 | tf_op jit(solution)/shard_map/pallas_call | solution.py:110
  67.4 5.2 %collective-permute-done.5 = f32[136,512]{1,0:T(8,128)S(1)} collective-permute-done((f32[136,512]{1,0:T(8,128)S(1)}, f32[136,512]{1,0:T(8,128)S(1)}, u32[]{:S(2)}, u32[]{:S(2)}) %collective-permute-start.5) | collective-permute-done | bytes 278560 | tf_op jit(solution)/shard_map/ppermute | solution.py:22
  72.6 1.0 %add_add_fusion = f32[136,512]{1,0:T(8,128)S(1)} fusion(f32[136,512]{1,0:T(8,128)S(1)} %collective-permute-done.5, f32[136,512]{1,0:T(8,128)} %shard_map.76, f32[136,512]{1,0:T(8,128)S(1)} %collective-permute-done.4), kind=kLoop, calls=%fused_computation.2 | loop fusion | flops 139264 | bytes 1114112 | tf_op jit(solution)/shard_map/add | solution.py:191
  73.7 0.2 div.11
  74.0 2.0 %collective-permute-start.6 = (bf16[128,512]{1,0:T(8,128)(2,1)S(1)}, bf16[128,512]{1,0:T(8,128)(2,1)S(1)}, u32[]{:S(2)}, u32[]{:S(2)}) collective-permute-start(bf16[128,512]{1,0:T(8,128)(2,1)S(1)} %fusion), channel_id=1, source_target_pairs={{8,0},{16,8},{24,16},{32,24},{40,32},{48,40},{56,48},{64,56},{72,6... | collective-permute-start | bytes 393224 | tf_op jit(solution)/shard_map/ppermute | solution.py:22
  76.0 4.0 %collective-permute-done.6 = bf16[128,512]{1,0:T(8,128)(2,1)S(1)} collective-permute-done((bf16[128,512]{1,0:T(8,128)(2,1)S(1)}, bf16[128,512]{1,0:T(8,128)(2,1)S(1)}, u32[]{:S(2)}, u32[]{:S(2)}) %collective-permute-start.6) | collective-permute-done | bytes 131104 | tf_op jit(solution)/shard_map/ppermute | solution.py:22
  80.0 17.4 %all_to_all.34 = bf16[8,16,512]{2,1,0:T(8,128)(2,1)S(1)} all-to-all(bf16[8,16,512]{2,1,0:T(8,128)(2,1)S(1)} %bitcast.39), channel_id=1, replica_groups=mesh['pool'=64,'tensor'=8] {'tensor'}, dimensions={0} | all-to-all | bytes 262144 | tf_op jit(solution)/shard_map/all_to_all | solution.py:198
  97.5 0.7 copy.32
  (39 shorter events, 0.9 us)
Async XLA Ops:
  0.0 12.0 %copy-start = (s32[64,64]{1,0:T(8,128)S(1)}, s32[64,64]{1,0:T(8,128)}, u32[]{:S(2)}) copy-start(s32[64,64]{1,0:T(8,128)} %param.12) | copy-start | bytes 49156
  0.0 1.0 copy-start.7
  0.0 1.0 copy-start.8
  1.7 16.7 %all-to-all-start = ((bf16[16,8,1024]{2,0,1:T(8,128)(2,1)}), bf16[16,8,1024]{2,0,1:T(8,128)(2,1)S(1)}, u32[]{:S(2)}, u32[]{:S(2)}) async-start(bf16[16,8,1024]{2,0,1:T(8,128)(2,1)} %pad_maximum_fusion), calls=%async_computation | async-start | bytes 524288 | tf_op jit(solution)/shard_map/all_to_all | solution.py:146
  12.0 1.0 %copy-start.1 = (s32[64]{0:T(128)S(1)}, s32[64]{0:T(128)}, u32[]{:S(2)}) copy-start(s32[64]{0:T(128)} %param.13) | copy-start | bytes 772
  18.4 12.2 %copy-start.2 = (bf16[128,512]{1,0:T(8,128)(2,1)}, bf16[128,512]{1,0:T(8,128)(2,1)S(1)}, u32[]{:S(2)}) copy-start(bf16[128,512]{1,0:T(8,128)(2,1)S(1)} %slice.24.q_ref) | copy-start | bytes 393220
  18.5 16.8 %collective-permute-start = (bf16[128,512]{1,0:T(8,128)(2,1)S(1)}, bf16[128,512]{1,0:T(8,128)(2,1)S(1)}, u32[]{:S(2)}, u32[]{:S(2)}) collective-permute-start(bf16[128,512]{1,0:T(8,128)(2,1)S(1)} %slice.24.q_ref), channel_id=1, source_target_pairs={{504,0},{0,8},{8,16},{16,24},{24,32},{32,40},{40,48},{48,56},{56,6... | collective-permute-start | bytes 393224 | tf_op jit(solution)/shard_map/ppermute | solution.py:22
  20.4 15.1 %collective-permute-start.1 = (bf16[128,512]{1,0:T(8,128)(2,1)S(1)}, bf16[128,512]{1,0:T(8,128)(2,1)S(1)}, u32[]{:S(2)}, u32[]{:S(2)}) collective-permute-start(bf16[128,512]{1,0:T(8,128)(2,1)S(1)} %slice.24.q_ref), channel_id=1, source_target_pairs={{496,0},{504,8},{0,16},{8,24},{16,32},{24,40},{32,48},{40,56},{48,... | collective-permute-start | bytes 393224 | tf_op jit(solution)/shard_map/ppermute | solution.py:22
  22.5 21.9 %collective-permute-start.2 = (bf16[128,512]{1,0:T(8,128)(2,1)S(1)}, bf16[128,512]{1,0:T(8,128)(2,1)S(1)}, u32[]{:S(2)}, u32[]{:S(2)}) collective-permute-start(bf16[128,512]{1,0:T(8,128)(2,1)S(1)} %slice.24.q_ref), channel_id=1, source_target_pairs={{488,0},{496,8},{504,16},{0,24},{8,32},{16,40},{24,48},{32,56},{40... | collective-permute-start | bytes 393224 | tf_op jit(solution)/shard_map/ppermute | solution.py:22
  35.3 12.9 %copy-start.4 = (bf16[128,512]{1,0:T(8,128)(2,1)}, bf16[128,512]{1,0:T(8,128)(2,1)S(1)}, u32[]{:S(2)}) copy-start(bf16[128,512]{1,0:T(8,128)(2,1)S(1)} %collective-permute-done.q_ref) | copy-start | bytes 393220
  35.4 12.8 %copy-start.5 = (bf16[128,512]{1,0:T(8,128)(2,1)}, bf16[128,512]{1,0:T(8,128)(2,1)S(1)}, u32[]{:S(2)}) copy-start(bf16[128,512]{1,0:T(8,128)(2,1)S(1)} %collective-permute-done.1.q_ref) | copy-start | bytes 393220
  44.4 0.6 copy-start.6
  48.2 9.0 %collective-permute-start.3 = (f32[136,512]{1,0:T(8,128)}, f32[136,512]{1,0:T(8,128)S(1)}, u32[]{:S(2)}, u32[]{:S(2)}) collective-permute-start(f32[136,512]{1,0:T(8,128)} %shard_map.74), channel_id=1, source_target_pairs={{8,0},{16,8},{24,16},{32,24},{40,32},{48,40},{56,48},{64,56},{72,6... | collective-permute-start | bytes 835592 | tf_op jit(solution)/shard_map/ppermute | solution.py:22
  55.1 6.9 %copy-start.3 = (f32[136,512]{1,0:T(8,128)S(1)}, f32[136,512]{1,0:T(8,128)}, u32[]{:S(2)}) copy-start(f32[136,512]{1,0:T(8,128)} %shard_map.73) | copy-start | bytes 835588
  58.3 9.2 %collective-permute-start.4 = (f32[136,512]{1,0:T(8,128)S(1)}, f32[136,512]{1,0:T(8,128)S(1)}, u32[]{:S(2)}, u32[]{:S(2)}) collective-permute-start(f32[136,512]{1,0:T(8,128)S(1)} %add.70), channel_id=1, source_target_pairs={{8,0},{16,8},{24,16},{32,24},{40,32},{48,40},{56,48},{64,56},{72,6... | collective-permute-start | bytes 835592 | tf_op jit(solution)/shard_map/ppermute | solution.py:22
  62.0 10.6 %collective-permute-start.5 = (f32[136,512]{1,0:T(8,128)S(1)}, f32[136,512]{1,0:T(8,128)S(1)}, u32[]{:S(2)}, u32[]{:S(2)}) collective-permute-start(f32[136,512]{1,0:T(8,128)S(1)} %copy-done.3), channel_id=1, source_target_pairs={{504,0},{0,8},{8,16},{16,24},{24,32},{32,40},{40,48},{48,56},{56,6... | collective-permute-start | bytes 835592 | tf_op jit(solution)/shard_map/ppermute | solution.py:22
  74.0 6.0 %collective-permute-start.6 = (bf16[128,512]{1,0:T(8,128)(2,1)S(1)}, bf16[128,512]{1,0:T(8,128)(2,1)S(1)}, u32[]{:S(2)}, u32[]{:S(2)}) collective-permute-start(bf16[128,512]{1,0:T(8,128)(2,1)S(1)} %fusion), channel_id=1, source_target_pairs={{8,0},{16,8},{24,16},{32,24},{40,32},{48,40},{56,48},{64,56},{72,6... | collective-permute-start | bytes 393224 | tf_op jit(solution)/shard_map/ppermute | solution.py:22

commit v14 on v6

--- a/solution.py
+++ b/solution.py
@@ -183,12 +183,16 @@
     def part(offset):
         return attend(offset, meta, received[offset], cached_key_pages, cached_value_pages)
 
-    total = part(SPAN - 1)
-    for offset in range(SPAN - 2, -1, -1):
-        moved = shifted(total, "pool", -1)
-        here = part(offset) if offset > 0 else part_own
-        moved, here = lax.optimization_barrier((moved, here))
-        total = here + moved
+    stacked = jnp.stack([part_own] + [part(offset) for offset in range(1, SPAN)])
+    sums = []
+    for start in range(SPAN):
+        groups = [
+            [(SPAN * k + start + j) % pool_size for j in range(SPAN)]
+            for k in range(pool_size // SPAN)
+        ]
+        mine = lax.dynamic_index_in_dim(stacked, (holder - start) % SPAN, axis=0, keepdims=False)
+        sums.append(lax.psum(mine, "pool", axis_index_groups=groups))
+    total = lax.dynamic_index_in_dim(jnp.stack(sums), holder % SPAN, axis=0, keepdims=False)
     heads = q_width // HEAD_SIZE
     numerator = total[:rows].reshape(rows, heads, HEAD_SIZE)
     totals = total[rows, : heads * rows].reshape(heads, rows)

time: 94.5 us -> 336 us (3.56)
  waiting for transfers between devices: 21.9 us -> 264 us
  between operations: 0.28 us -> 13.4 us
  starting transfers between devices: 31.2 us -> 21.8 us
  Pallas kernels: 16.1 us -> 12.1 us
    psum x0 -> x4, waiting for transfers between devices: none -> 248 us  [on_device(): sums.append(lax.psum(mine, 'pool', axis_index_groups=groups))]
    ppermute x6 -> x3, starting transfers between devices: 21 us -> 11.5 us  [shifted(): return lax.ppermute(block, axis, route)]
    ppermute x6 -> x3, waiting for transfers between devices: 18.3 us -> 10.6 us  [shifted(): return lax.ppermute(block, axis, route)]
    pallas_call x4, Pallas kernels: 16.1 us -> 12.1 us  [attend(): pl.pallas_call(functools.partial(_attend_kernel, dist, with_own), out_sha...]
  transfers between devices with their start and end apart: 7 -> 8, of which waited for: 5 -> 7; matrix products, arithmetic and copies ran while one was open for 4% -> 1% of each run, Pallas kernels for 13% -> 1%
where the time goes in v14:
time: 336 us; the launch traced here: 335 us
  waiting for transfers between devices  264 us (79%)
  starting transfers between devices  21.8 us (6%)
  between operations  13.4 us (4%)
  blocking collectives  12.3 us (4%)
  Pallas kernels  12.1 us (4%)
  local copies, waits for them, and re-layouts  6.72 us (2%)
  other arithmetic  4.54 us (1%)
    psum x4, waiting for transfers between devices, on_device(): sums.append(lax.psum(mine, 'pool', axis_index_groups=groups))  248 us
    all_to_all x1, blocking collectives, on_device(): lax.all_to_all(attended, 'tensor', split_axis=0, concat_axis=1, tiled=True)  12.3 us
    pallas_call x4, Pallas kernels, attend(): pl.pallas_call(functools.partial(_attend_kernel, dist, with_own), out_sha...  12.1 us
    ppermute x3, starting transfers between devices, shifted(): return lax.ppermute(block, axis, route)  11.5 us
    ppermute x3, waiting for transfers between devices, shifted(): return lax.ppermute(block, axis, route)  10.6 us
    all_to_all x1, starting transfers between devices, on_device(): lax.all_to_all(packed, 'tensor', split_axis=1, concat_axis=0, tiled=True)  10.2 us
  transfers between devices with their start and end apart: 8, of which 7 were waited for; matrix products, arithmetic and copies ran while one was open for 1% of the time, Pallas kernels for 1%

profile of v14, /device:TPU:1, one launch (start us, length us, event | category | flops | bytes accessed | tf_op | source)
XLA Modules:
  0.0 335.0 jit_solution(15548857838391863625)
XLA Ops:
  6.5 0.9 copy.35
  7.5 0.9 copy_bitcast_fusion.1
  8.3 0.7 pad_maximum_fusion.1
  9.1 10.2 %all-to-all-start = ((bf16[16,8,1024]{2,0,1:T(8,128)(2,1)}), bf16[16,8,1024]{2,0,1:T(8,128)(2,1)S(1)}, u32[]{:S(2)}, u32[]{:S(2)}) async-start(bf16[16,8,1024]{2,0,1:T(8,128)(2,1)} %pad_maximum_fusion.1), calls=%async_computation | async-start | bytes 524288 | tf_op jit(solution)/shard_map/all_to_all | solution.py:146
  19.3 0.6 gather_fusion
  20.2 0.2 compare_reduce_fusion
  20.4 0.6 gather_fusion.1
  21.6 0.6 pad_add_fusion.meta_ref
  22.3 3.5 %all-to-all-done = bf16[16,8,1024]{2,0,1:T(8,128)(2,1)S(1)} async-done(((bf16[16,8,1024]{2,0,1:T(8,128)(2,1)}), bf16[16,8,1024]{2,0,1:T(8,128)(2,1)S(1)}, u32[]{:S(2)}, u32[]{:S(2)}) %all-to-all-start) | async-done | bytes 262176 | tf_op jit(solution)/shard_map/all_to_all | solution.py:146
  25.8 1.9 collective-permute-start.2
  27.7 6.0 %collective-permute-start.1 = (bf16[128,512]{1,0:T(8,128)(2,1)S(1)}, bf16[128,512]{1,0:T(8,128)(2,1)S(1)}, u32[]{:S(2)}, u32[]{:S(2)}) collective-permute-start(bf16[128,512]{1,0:T(8,128)(2,1)S(1)} %slice.25.q_ref), channel_id=1, source_target_pairs={{496,0},{504,8},{0,16},{8,24},{16,32},{24,40},{32,48},{40,56},{48,... | collective-permute-start | bytes 393224 | tf_op jit(solution)/shard_map/ppermute | solution.py:22
  33.8 3.5 %collective-permute-start = (bf16[128,512]{1,0:T(8,128)(2,1)S(1)}, bf16[128,512]{1,0:T(8,128)(2,1)S(1)}, u32[]{:S(2)}, u32[]{:S(2)}) collective-permute-start(bf16[128,512]{1,0:T(8,128)(2,1)S(1)} %slice.25.q_ref), channel_id=1, source_target_pairs={{504,0},{0,8},{8,16},{16,24},{24,32},{32,40},{40,48},{48,56},{56,6... | collective-permute-start | bytes 393224 | tf_op jit(solution)/shard_map/ppermute | solution.py:22
  37.3 0.7 fusion.11
  38.0 3.9 %shard_map.73 = f32[136,512]{1,0:T(8,128)} custom-call(s32[4,3,16]{2,1,0:T(4,128)} %pad_add_fusion.meta_ref, bf16[128,512]{1,0:T(8,128)(2,1)} %copy-done.5, bf16[16,128,256]{2,1,0:T(8,128)(2,1)} %kp_hbm.7, bf16[16,128,256]{2,1,0:T(8,128)(2,1)} %vp_hbm.7, bf16[128,256]{1,0:T(8,128)(2,1)} %get-tuple-element.26.refs_0_, bf16[128,256]{1,0:T(8,128)(2,1)} %get-tuple-element.25.refs_1_), custom_call_target="tpu_custom_call" | custom-call | flops 167772160 | bytes 1064960 | tf_op jit(solution)/shard_map/pallas_call | solution.py:110
  41.9 7.9 %collective-permute-done.1.q_ref = bf16[128,512]{1,0:T(8,128)(2,1)S(1)} collective-permute-done((bf16[128,512]{1,0:T(8,128)(2,1)S(1)}, bf16[128,512]{1,0:T(8,128)(2,1)S(1)}, u32[]{:S(2)}, u32[]{:S(2)}) %collective-permute-start.1) | collective-permute-done | bytes 131104 | tf_op jit(solution)/shard_map/ppermute | solution.py:22
  49.8 2.7 collective-permute-done.q_ref
  52.5 0.6 copy-done.8
  53.1 3.1 shard_map.74
  56.3 1.9 shard_map.75
  58.3 3.2 shard_map.76
  61.5 1.0 pad_maximum_fusion
  62.6 1.1 constant_dynamic-slice_fusion
  63.7 0.7 all-reduce.9.cloned.1.call-update
  64.4 0.7 all-reduce.7.cloned.1.call-update
  65.2 0.5 all-reduce.5.cloned.1.call-update
  65.7 62.4 %all-reduce.11.cloned.1.call-done = f32[1,136,512]{2,1,0:T(8,128)} async-done(((f32[1,136,512]{2,1,0:T(8,128)}), f32[1,136,512]{2,1,0:T(8,128)}) %all-reduce.11.cloned.1.call-update) | async-done | bytes 278544 | tf_op jit(solution)/shard_map/psum | solution.py:194
  128.2 62.0 %all-reduce.9.cloned.1.call-done = f32[1,136,512]{2,1,0:T(8,128)} async-done(((f32[1,136,512]{2,1,0:T(8,128)}), f32[1,136,512]{2,1,0:T(8,128)}) %all-reduce.9.cloned.1.call-update) | async-done | bytes 278544 | tf_op jit(solution)/shard_map/psum | solution.py:194
  190.1 68.3 %all-reduce.7.cloned.1.call-done = f32[1,136,512]{2,1,0:T(8,128)} async-done(((f32[1,136,512]{2,1,0:T(8,128)}), f32[1,136,512]{2,1,0:T(8,128)}) %all-reduce.7.cloned.1.call-update) | async-done | bytes 278544 | tf_op jit(solution)/shard_map/psum | solution.py:194
  258.4 55.4 %all-reduce.5.cloned.1.call-done = f32[1,136,512]{2,1,0:T(8,128)} async-done(((f32[1,136,512]{2,1,0:T(8,128)}), f32[1,136,512]{2,1,0:T(8,128)}) %all-reduce.5.cloned.1.call-update) | async-done | bytes 278544 | tf_op jit(solution)/shard_map/psum | solution.py:194
  313.8 1.1 fusion.2
  315.5 12.3 %all_to_all.31 = bf16[8,16,512]{2,1,0:T(8,128)(2,1)S(1)} all-to-all(bf16[8,16,512]{2,1,0:T(8,128)(2,1)S(1)} %divide_convert_fusion), channel_id=1, replica_groups=mesh['pool'=64,'tensor'=8] {'tensor'}, dimensions={0} | all-to-all | bytes 262144 | tf_op jit(solution)/shard_map/all_to_all | solution.py:201
  327.8 0.7 copy.31
  (45 shorter events, 1.7 us)
Async XLA Ops:
  6.5 12.8 %copy-start = (s32[64,64]{1,0:T(8,128)S(1)}, s32[64,64]{1,0:T(8,128)}, u32[]{:S(2)}) copy-start(s32[64,64]{1,0:T(8,128)} %param.12) | copy-start | bytes 49156
  6.5 13.8 %copy-start.1 = (s32[64]{0:T(128)S(1)}, s32[64]{0:T(128)}, u32[]{:S(2)}) copy-start(s32[64]{0:T(128)} %param.13) | copy-start | bytes 772
  9.1 16.7 %all-to-all-start = ((bf16[16,8,1024]{2,0,1:T(8,128)(2,1)}), bf16[16,8,1024]{2,0,1:T(8,128)(2,1)S(1)}, u32[]{:S(2)}, u32[]{:S(2)}) async-start(bf16[16,8,1024]{2,0,1:T(8,128)(2,1)} %pad_maximum_fusion.1), calls=%async_computation | async-start | bytes 524288 | tf_op jit(solution)/shard_map/all_to_all | solution.py:146
  19.3 108.9 %all-reduce.11.cloned.1.call-start = ((), (), s32[]{:S(2)}) async-start(), calls=%async_computation.5 | async-start | bytes 557056 | tf_op jit(solution)/shard_map/psum | solution.py:194
  25.8 12.2 %copy-start.5 = (bf16[128,512]{1,0:T(8,128)(2,1)}, bf16[128,512]{1,0:T(8,128)(2,1)S(1)}, u32[]{:S(2)}) copy-start(bf16[128,512]{1,0:T(8,128)(2,1)S(1)} %slice.25.q_ref) | copy-start | bytes 393220
  25.8 16.1 %collective-permute-start.2 = (bf16[128,512]{1,0:T(8,128)(2,1)S(1)}, bf16[128,512]{1,0:T(8,128)(2,1)S(1)}, u32[]{:S(2)}, u32[]{:S(2)}) collective-permute-start(bf16[128,512]{1,0:T(8,128)(2,1)S(1)} %slice.25.q_ref), channel_id=1, source_target_pairs={{488,0},{496,8},{504,16},{0,24},{8,32},{16,40},{24,48},{32,56},{40... | collective-permute-start | bytes 393224 | tf_op jit(solution)/shard_map/ppermute | solution.py:22
  27.7 22.1 %collective-permute-start.1 = (bf16[128,512]{1,0:T(8,128)(2,1)S(1)}, bf16[128,512]{1,0:T(8,128)(2,1)S(1)}, u32[]{:S(2)}, u32[]{:S(2)}) collective-permute-start(bf16[128,512]{1,0:T(8,128)(2,1)S(1)} %slice.25.q_ref), channel_id=1, source_target_pairs={{496,0},{504,8},{0,16},{8,24},{16,32},{24,40},{32,48},{40,56},{48,... | collective-permute-start | bytes 393224 | tf_op jit(solution)/shard_map/ppermute | solution.py:22
  33.8 18.7 %collective-permute-start = (bf16[128,512]{1,0:T(8,128)(2,1)S(1)}, bf16[128,512]{1,0:T(8,128)(2,1)S(1)}, u32[]{:S(2)}, u32[]{:S(2)}) collective-permute-start(bf16[128,512]{1,0:T(8,128)(2,1)S(1)} %slice.25.q_ref), channel_id=1, source_target_pairs={{504,0},{0,8},{8,16},{16,24},{24,32},{32,40},{40,48},{48,56},{56,6... | collective-permute-start | bytes 393224 | tf_op jit(solution)/shard_map/ppermute | solution.py:22
  41.9 14.4 %copy-start.6 = (bf16[128,512]{1,0:T(8,128)(2,1)}, bf16[128,512]{1,0:T(8,128)(2,1)S(1)}, u32[]{:S(2)}) copy-start(bf16[128,512]{1,0:T(8,128)(2,1)S(1)} %collective-permute-done.2.q_ref) | copy-start | bytes 393220
  49.8 6.5 %copy-start.7 = (bf16[128,512]{1,0:T(8,128)(2,1)}, bf16[128,512]{1,0:T(8,128)(2,1)S(1)}, u32[]{:S(2)}) copy-start(bf16[128,512]{1,0:T(8,128)(2,1)S(1)} %collective-permute-done.1.q_ref) | copy-start | bytes 393220
  52.5 0.7 copy-start.8
  58.2 3.2 copy-start.2
  58.3 3.2 copy-start.3
  58.3 3.2 copy-start.4
  63.6 126.5 %all-reduce.9.cloned.1.call-start = ((), (), s32[]{:S(2)}) async-start(), calls=%async_computation.4 | async-start | bytes 557056 | tf_op jit(solution)/shard_map/psum | solution.py:194
  64.4 194.0 %all-reduce.7.cloned.1.call-start = ((), (), s32[]{:S(2)}) async-start(), calls=%async_computation.3 | async-start | bytes 557056 | tf_op jit(solution)/shard_map/psum | solution.py:194
  65.1 248.7 %all-reduce.5.cloned.1.call-start = ((), (), s32[]{:S(2)}) async-start(), calls=%async_computation.2 | async-start | bytes 557056 | tf_op jit(solution)/shard_map/psum | solution.py:194
Sparse Core Ops, SparseCore 0:
  63.8 64.3 all-reduce.10
  131.1 58.9 all-reduce.8
  193.1 65.2 all-reduce.6
  261.2 52.5 all-reduce.4

commit v15 on v6

--- a/solution.py
+++ b/solution.py
@@ -175,10 +175,11 @@
     count = jnp.broadcast_to(jnp.sum(wanted.astype(jnp.int32), axis=1, keepdims=True), (SPAN, slots_dev))
     meta = jnp.stack([order, order_limit, count], axis=1).astype(jnp.int32)
 
-    received = [shifted(q_own, "pool", offset) for offset in range(1, SPAN)]
+    received = {offset: shifted(q_own, "pool", offset) for offset in range(SPAN - 1, 0, -1)}
     part_own = attend(0, meta, q_own, cached_key_pages, cached_value_pages, k_new, v_new)
-    *received, part_own = lax.optimization_barrier((*received, part_own))
-    received = [q_own] + received
+    nearer = tuple(received[offset] for offset in range(1, SPAN - 1))
+    *nearer, part_own = lax.optimization_barrier((*nearer, part_own))
+    received = [q_own] + list(nearer) + [received[SPAN - 1]]
 
     def part(offset):
         return attend(offset, meta, received[offset], cached_key_pages, cached_value_pages)

time: 94.5 us -> 97.7 us (1.034)
  starting transfers between devices: 31.2 us -> 34.4 us
  Pallas kernels: 16.1 us -> 14 us
    ppermute x6, starting transfers between devices: 21 us -> 24.2 us  [shifted(): return lax.ppermute(block, axis, route)]
    pallas_call x4, Pallas kernels: 16.1 us -> 14 us  [attend(): pl.pallas_call(functools.partial(_attend_kernel, dist, with_own), out_sha...]
  transfers between devices with their start and end apart: 7 -> 7, of which waited for: 5 -> 5; matrix products, arithmetic and copies ran while one was open for 4% -> 4% of each run, Pallas kernels for 13% -> 11%
where the time goes in v15:
time: 97.7 us; the launch traced here: 97 us
  starting transfers between devices  34.4 us (35%)
  waiting for transfers between devices  22.7 us (23%)
  blocking collectives  15.9 us (16%)
  Pallas kernels  14 us (14%)
  local copies, waits for them, and re-layouts  5.22 us (5%)
  other arithmetic  4.46 us (5%)
    ppermute x6, starting transfers between devices, shifted(): return lax.ppermute(block, axis, route)  24.2 us
    ppermute x6, waiting for transfers between devices, shifted(): return lax.ppermute(block, axis, route)  18.4 us
    all_to_all x1, blocking collectives, on_device(): lax.all_to_all(attended, 'tensor', split_axis=0, concat_axis=1, tiled=True)  15.9 us
    pallas_call x4, Pallas kernels, attend(): pl.pallas_call(functools.partial(_attend_kernel, dist, with_own), out_sha...  14 us
    all_to_all x1, starting transfers between devices, on_device(): lax.all_to_all(packed, 'tensor', split_axis=1, concat_axis=0, tiled=True)  10.2 us
    all_to_all x1, waiting for transfers between devices, on_device(): lax.all_to_all(packed, 'tensor', split_axis=1, concat_axis=0, tiled=True)  4.32 us
    add x3, other arithmetic, on_device(): total = here + moved  2.03 us
  transfers between devices with their start and end apart: 7, of which 5 were waited for; matrix products, arithmetic and copies ran while one was open for 4% of the time, Pallas kernels for 11%

profile of v15, /device:TPU:1, one launch (start us, length us, event | category | flops | bytes accessed | tf_op | source)
XLA Modules:
  0.0 97.0 jit_solution(16910794390456503964)
XLA Ops:
  0.0 1.0 copy.37
  1.0 0.7 pad_maximum_fusion
  1.7 10.2 %all-to-all-start = ((bf16[16,8,1024]{2,0,1:T(8,128)(2,1)}), bf16[16,8,1024]{2,0,1:T(8,128)(2,1)S(1)}, u32[]{:S(2)}, u32[]{:S(2)}) async-start(bf16[16,8,1024]{2,0,1:T(8,128)(2,1)} %pad_maximum_fusion), calls=%async_computation | async-start | bytes 524288 | tf_op jit(solution)/shard_map/all_to_all | solution.py:146
  12.0 0.6 gather_fusion
  12.6 0.2 compare_reduce_fusion
  12.8 0.2 fusion.1
  13.0 0.6 gather_fusion.1
  13.8 0.2 reduce_window_sum.11
  14.1 4.3 %all-to-all-done = bf16[16,8,1024]{2,0,1:T(8,128)(2,1)S(1)} async-done(((bf16[16,8,1024]{2,0,1:T(8,128)(2,1)}), bf16[16,8,1024]{2,0,1:T(8,128)(2,1)S(1)}, u32[]{:S(2)}, u32[]{:S(2)}) %all-to-all-start) | async-done | bytes 262176 | tf_op jit(solution)/shard_map/all_to_all | solution.py:146
  18.5 1.9 %collective-permute-start = (bf16[128,512]{1,0:T(8,128)(2,1)S(1)}, bf16[128,512]{1,0:T(8,128)(2,1)S(1)}, u32[]{:S(2)}, u32[]{:S(2)}) collective-permute-start(bf16[128,512]{1,0:T(8,128)(2,1)S(1)} %slice.24.q_ref), channel_id=1, source_target_pairs={{488,0},{496,8},{504,16},{0,24},{8,32},{16,40},{24,48},{32,56},{40... | collective-permute-start | bytes 393224 | tf_op jit(solution)/shard_map/ppermute | solution.py:22
  20.6 0.6 pad_add_fusion.meta_ref
  21.2 10.3 %collective-permute-done.q_ref = bf16[128,512]{1,0:T(8,128)(2,1)S(1)} collective-permute-done((bf16[128,512]{1,0:T(8,128)(2,1)S(1)}, bf16[128,512]{1,0:T(8,128)(2,1)S(1)}, u32[]{:S(2)}, u32[]{:S(2)}) %collective-permute-start) | collective-permute-done | bytes 131104 | tf_op jit(solution)/shard_map/ppermute | solution.py:22
  31.4 0.6 copy-done.6
  32.1 3.5 %shard_map.73 = f32[136,512]{1,0:T(8,128)} custom-call(s32[4,3,16]{2,1,0:T(4,128)} %pad_add_fusion.meta_ref, bf16[128,512]{1,0:T(8,128)(2,1)} %copy-done.6, bf16[16,128,256]{2,1,0:T(8,128)(2,1)} %kp_hbm.7, bf16[16,128,256]{2,1,0:T(8,128)(2,1)} %vp_hbm.7), custom_call_target="tpu_custom_call" | custom-call | flops 134217728 | bytes 933888 | tf_op jit(solution)/shard_map/pallas_call | solution.py:110
  35.6 4.6 %collective-permute-start.1 = (f32[136,512]{1,0:T(8,128)}, f32[136,512]{1,0:T(8,128)S(1)}, u32[]{:S(2)}, u32[]{:S(2)}) collective-permute-start(f32[136,512]{1,0:T(8,128)} %shard_map.73), channel_id=1, source_target_pairs={{8,0},{16,8},{24,16},{32,24},{40,32},{48,40},{56,48},{64,56},{72,6... | collective-permute-start | bytes 835592 | tf_op jit(solution)/shard_map/ppermute | solution.py:22
  40.1 5.1 %collective-permute-start.2 = (bf16[128,512]{1,0:T(8,128)(2,1)S(1)}, bf16[128,512]{1,0:T(8,128)(2,1)S(1)}, u32[]{:S(2)}, u32[]{:S(2)}) collective-permute-start(bf16[128,512]{1,0:T(8,128)(2,1)S(1)} %slice.24.q_ref), channel_id=1, source_target_pairs={{504,0},{0,8},{8,16},{16,24},{24,32},{32,40},{40,48},{48,56},{56,6... | collective-permute-start | bytes 393224 | tf_op jit(solution)/shard_map/ppermute | solution.py:22
  45.3 3.1 %collective-permute-start.3 = (bf16[128,512]{1,0:T(8,128)(2,1)S(1)}, bf16[128,512]{1,0:T(8,128)(2,1)S(1)}, u32[]{:S(2)}, u32[]{:S(2)}) collective-permute-start(bf16[128,512]{1,0:T(8,128)(2,1)S(1)} %slice.24.q_ref), channel_id=1, source_target_pairs={{496,0},{504,8},{0,16},{8,24},{16,32},{24,40},{32,48},{40,56},{48,... | collective-permute-start | bytes 393224 | tf_op jit(solution)/shard_map/ppermute | solution.py:22
  48.4 0.7 fusion.9
  49.0 3.9 %shard_map.74 = f32[136,512]{1,0:T(8,128)} custom-call(s32[4,3,16]{2,1,0:T(4,128)} %pad_add_fusion.meta_ref, bf16[128,512]{1,0:T(8,128)(2,1)} %copy-done.3, bf16[16,128,256]{2,1,0:T(8,128)(2,1)} %kp_hbm.7, bf16[16,128,256]{2,1,0:T(8,128)(2,1)} %vp_hbm.7, bf16[128,256]{1,0:T(8,128)(2,1)} %get-tuple-element.32.refs_0_, bf16[128,256]{1,0:T(8,128)(2,1)} %get-tuple-element.31.refs_1_), custom_call_target="tpu_custom_call" | custom-call | flops 167772160 | bytes 1064960 | tf_op jit(solution)/shard_map/pallas_call | solution.py:110
  53.0 3.6 %collective-permute-done.3.q_ref = bf16[128,512]{1,0:T(8,128)(2,1)S(1)} collective-permute-done((bf16[128,512]{1,0:T(8,128)(2,1)S(1)}, bf16[128,512]{1,0:T(8,128)(2,1)S(1)}, u32[]{:S(2)}, u32[]{:S(2)}) %collective-permute-start.3) | collective-permute-done | bytes 131104 | tf_op jit(solution)/shard_map/ppermute | solution.py:22
  56.5 0.6 copy-done.5
  57.2 3.1 %shard_map.75 = f32[136,512]{1,0:T(8,128)} custom-call(s32[4,3,16]{2,1,0:T(4,128)} %pad_add_fusion.meta_ref, bf16[128,512]{1,0:T(8,128)(2,1)} %copy-done.5, bf16[16,128,256]{2,1,0:T(8,128)(2,1)} %kp_hbm.7, bf16[16,128,256]{2,1,0:T(8,128)(2,1)} %vp_hbm.7), custom_call_target="tpu_custom_call" | custom-call | flops 134217728 | bytes 933888 | tf_op jit(solution)/shard_map/pallas_call | solution.py:110
  60.4 1.0 %add.70 = f32[136,512]{1,0:T(8,128)S(1)} add(f32[136,512]{1,0:T(8,128)} %shard_map.75, f32[136,512]{1,0:T(8,128)S(1)} %collective-permute-done.1) | non-fusion elementwise | flops 69632 | bytes 835584 | tf_op jit(solution)/shard_map/add | solution.py:192
  61.4 3.5 %collective-permute-start.4 = (f32[136,512]{1,0:T(8,128)S(1)}, f32[136,512]{1,0:T(8,128)S(1)}, u32[]{:S(2)}, u32[]{:S(2)}) collective-permute-start(f32[136,512]{1,0:T(8,128)S(1)} %add.70), channel_id=1, source_target_pairs={{8,0},{16,8},{24,16},{32,24},{40,32},{48,40},{56,48},{64,56},{72,6... | collective-permute-start | bytes 835592 | tf_op jit(solution)/shard_map/ppermute | solution.py:22
  64.8 3.5 %shard_map.76 = f32[136,512]{1,0:T(8,128)} custom-call(s32[4,3,16]{2,1,0:T(4,128)} %pad_add_fusion.meta_ref, bf16[128,512]{1,0:T(8,128)(2,1)} %copy-done.4, bf16[16,128,256]{2,1,0:T(8,128)(2,1)} %kp_hbm.7, bf16[16,128,256]{2,1,0:T(8,128)(2,1)} %vp_hbm.7), custom_call_target="tpu_custom_call" | custom-call | flops 134217728 | bytes 933888 | tf_op jit(solution)/shard_map/pallas_call | solution.py:110
  68.3 1.1 %collective-permute-done.4 = f32[136,512]{1,0:T(8,128)S(1)} collective-permute-done((f32[136,512]{1,0:T(8,128)S(1)}, f32[136,512]{1,0:T(8,128)S(1)}, u32[]{:S(2)}, u32[]{:S(2)}) %collective-permute-start.4) | collective-permute-done | bytes 278560 | tf_op jit(solution)/shard_map/ppermute | solution.py:22
  69.4 1.0 %add.71 = f32[136,512]{1,0:T(8,128)S(1)} add(f32[136,512]{1,0:T(8,128)} %shard_map.76, f32[136,512]{1,0:T(8,128)S(1)} %collective-permute-done.4) | non-fusion elementwise | flops 69632 | bytes 835584 | tf_op jit(solution)/shard_map/add | solution.py:192
  70.4 6.0 %collective-permute-start.5 = (f32[136,512]{1,0:T(8,128)S(1)}, f32[136,512]{1,0:T(8,128)S(1)}, u32[]{:S(2)}, u32[]{:S(2)}) collective-permute-start(f32[136,512]{1,0:T(8,128)S(1)} %add.71), channel_id=1, source_target_pairs={{8,0},{16,8},{24,16},{32,24},{40,32},{48,40},{56,48},{64,56},{72,6... | collective-permute-start | bytes 835592 | tf_op jit(solution)/shard_map/ppermute | solution.py:22
  76.5 3.5 %collective-permute-done.5 = f32[136,512]{1,0:T(8,128)S(1)} collective-permute-done((f32[136,512]{1,0:T(8,128)S(1)}, f32[136,512]{1,0:T(8,128)S(1)}, u32[]{:S(2)}, u32[]{:S(2)}) %collective-permute-start.5) | collective-permute-done | bytes 278560 | tf_op jit(solution)/shard_map/ppermute | solution.py:22
  80.1 0.2 div.11
  80.4 15.9 %all_to_all.34 = bf16[8,16,512]{2,1,0:T(8,128)(2,1)S(1)} all-to-all(bf16[8,16,512]{2,1,0:T(8,128)(2,1)S(1)} %bitcast.36), channel_id=1, replica_groups=mesh['pool'=64,'tensor'=8] {'tensor'}, dimensions={0} | all-to-all | bytes 262144 | tf_op jit(solution)/shard_map/all_to_all | solution.py:198
  96.3 0.7 copy.32
  (38 shorter events, 0.8 us)
Async XLA Ops:
  0.0 12.0 %copy-start = (s32[64,64]{1,0:T(8,128)S(1)}, s32[64,64]{1,0:T(8,128)}, u32[]{:S(2)}) copy-start(s32[64,64]{1,0:T(8,128)} %param.12) | copy-start | bytes 49156
  0.0 1.0 copy-start.7
  0.0 1.0 %copy-start.8 = (bf16[16,2048]{1,0:T(8,128)(2,1)S(1)}, bf16[16,2048]{1,0:T(8,128)(2,1)}, u32[]{:S(2)}) copy-start(bf16[16,2048]{1,0:T(8,128)(2,1)} %param.8) | copy-start | bytes 196612
  1.7 16.7 %all-to-all-start = ((bf16[16,8,1024]{2,0,1:T(8,128)(2,1)}), bf16[16,8,1024]{2,0,1:T(8,128)(2,1)S(1)}, u32[]{:S(2)}, u32[]{:S(2)}) async-start(bf16[16,8,1024]{2,0,1:T(8,128)(2,1)} %pad_maximum_fusion), calls=%async_computation | async-start | bytes 524288 | tf_op jit(solution)/shard_map/all_to_all | solution.py:146
  12.0 1.0 %copy-start.1 = (s32[64]{0:T(128)S(1)}, s32[64]{0:T(128)}, u32[]{:S(2)}) copy-start(s32[64]{0:T(128)} %param.13) | copy-start | bytes 772
  18.4 26.8 %copy-start.3 = (bf16[128,512]{1,0:T(8,128)(2,1)}, bf16[128,512]{1,0:T(8,128)(2,1)S(1)}, u32[]{:S(2)}) copy-start(bf16[128,512]{1,0:T(8,128)(2,1)S(1)} %slice.24.q_ref) | copy-start | bytes 393220
  18.5 13.0 %collective-permute-start = (bf16[128,512]{1,0:T(8,128)(2,1)S(1)}, bf16[128,512]{1,0:T(8,128)(2,1)S(1)}, u32[]{:S(2)}, u32[]{:S(2)}) collective-permute-start(bf16[128,512]{1,0:T(8,128)(2,1)S(1)} %slice.24.q_ref), channel_id=1, source_target_pairs={{488,0},{496,8},{504,16},{0,24},{8,32},{16,40},{24,48},{32,56},{40... | collective-permute-start | bytes 393224 | tf_op jit(solution)/shard_map/ppermute | solution.py:22
  31.4 0.6 copy-start.6
  35.6 24.8 %collective-permute-start.1 = (f32[136,512]{1,0:T(8,128)}, f32[136,512]{1,0:T(8,128)S(1)}, u32[]{:S(2)}, u32[]{:S(2)}) collective-permute-start(f32[136,512]{1,0:T(8,128)} %shard_map.73), channel_id=1, source_target_pairs={{8,0},{16,8},{24,16},{32,24},{40,32},{48,40},{56,48},{64,56},{72,6... | collective-permute-start | bytes 835592 | tf_op jit(solution)/shard_map/ppermute | solution.py:22
  40.1 12.8 %collective-permute-start.2 = (bf16[128,512]{1,0:T(8,128)(2,1)S(1)}, bf16[128,512]{1,0:T(8,128)(2,1)S(1)}, u32[]{:S(2)}, u32[]{:S(2)}) collective-permute-start(bf16[128,512]{1,0:T(8,128)(2,1)S(1)} %slice.24.q_ref), channel_id=1, source_target_pairs={{504,0},{0,8},{8,16},{16,24},{24,32},{32,40},{40,48},{48,56},{56,6... | collective-permute-start | bytes 393224 | tf_op jit(solution)/shard_map/ppermute | solution.py:22
  45.3 11.3 %collective-permute-start.3 = (bf16[128,512]{1,0:T(8,128)(2,1)S(1)}, bf16[128,512]{1,0:T(8,128)(2,1)S(1)}, u32[]{:S(2)}, u32[]{:S(2)}) collective-permute-start(bf16[128,512]{1,0:T(8,128)(2,1)S(1)} %slice.24.q_ref), channel_id=1, source_target_pairs={{496,0},{504,8},{0,16},{8,24},{16,32},{24,40},{32,48},{40,56},{48,... | collective-permute-start | bytes 393224 | tf_op jit(solution)/shard_map/ppermute | solution.py:22
  52.9 7.4 %copy-start.4 = (bf16[128,512]{1,0:T(8,128)(2,1)}, bf16[128,512]{1,0:T(8,128)(2,1)S(1)}, u32[]{:S(2)}) copy-start(bf16[128,512]{1,0:T(8,128)(2,1)S(1)} %collective-permute-done.2.q_ref) | copy-start | bytes 393220
  56.5 0.6 copy-start.5
  61.4 8.1 %collective-permute-start.4 = (f32[136,512]{1,0:T(8,128)S(1)}, f32[136,512]{1,0:T(8,128)S(1)}, u32[]{:S(2)}, u32[]{:S(2)}) collective-permute-start(f32[136,512]{1,0:T(8,128)S(1)} %add.70), channel_id=1, source_target_pairs={{8,0},{16,8},{24,16},{32,24},{40,32},{48,40},{56,48},{64,56},{72,6... | collective-permute-start | bytes 835592 | tf_op jit(solution)/shard_map/ppermute | solution.py:22
  68.3 11.6 %copy-start.2 = (f32[136,512]{1,0:T(8,128)S(1)}, f32[136,512]{1,0:T(8,128)}, u32[]{:S(2)}) copy-start(f32[136,512]{1,0:T(8,128)} %shard_map.74) | copy-start | bytes 835588
  70.4 9.5 %collective-permute-start.5 = (f32[136,512]{1,0:T(8,128)S(1)}, f32[136,512]{1,0:T(8,128)S(1)}, u32[]{:S(2)}, u32[]{:S(2)}) collective-permute-start(f32[136,512]{1,0:T(8,128)S(1)} %add.71), channel_id=1, source_target_pairs={{8,0},{16,8},{24,16},{32,24},{40,32},{48,40},{56,48},{64,56},{72,6... | collective-permute-start | bytes 835592 | tf_op jit(solution)/shard_map/ppermute | solution.py:22

commit v16 on v6

--- a/solution.py
+++ b/solution.py
@@ -185,10 +185,9 @@
 
     total = part(SPAN - 1)
     for offset in range(SPAN - 2, -1, -1):
-        moved = shifted(total, "pool", -1)
         here = part(offset) if offset > 0 else part_own
-        moved, here = lax.optimization_barrier((moved, here))
-        total = here + moved
+        total, here = lax.optimization_barrier((total, here))
+        total = here + shifted(total, "pool", -1)
     heads = q_width // HEAD_SIZE
     numerator = total[:rows].reshape(rows, heads, HEAD_SIZE)
     totals = total[rows, : heads * rows].reshape(heads, rows)

time: 94.5 us -> 95.6 us (1.012)
  waiting for transfers between devices: 21.9 us -> 26.2 us
  other arithmetic: 4.46 us -> 2.56 us
  Pallas kernels: 16.1 us -> 14.4 us
    ppermute x6, waiting for transfers between devices: 18.3 us -> 22.7 us  [shifted(): return lax.ppermute(block, axis, route)]
    add x3, other arithmetic: 2.02 us -> 0.12 us  [on_device(): total = here + shifted(total, 'pool', -1)]
    pallas_call x4, Pallas kernels: 16.1 us -> 14.4 us  [attend(): pl.pallas_call(functools.partial(_attend_kernel, dist, with_own), out_sha...]
  transfers between devices with their start and end apart: 7 -> 7, of which waited for: 5 -> 6; matrix products, arithmetic and copies ran while one was open for 4% -> 4% of each run, Pallas kernels for 13% -> 9%
where the time goes in v16:
time: 95.6 us; the launch traced here: 94.9 us
  starting transfers between devices  31.5 us (33%)
  waiting for transfers between devices  26.2 us (27%)
  blocking collectives  15.4 us (16%)
  Pallas kernels  14.4 us (15%)
  local copies, waits for them, and re-layouts  4.61 us (5%)
  other arithmetic  2.56 us (3%)
    ppermute x6, waiting for transfers between devices, shifted(): return lax.ppermute(block, axis, route)  22.7 us
    ppermute x6, starting transfers between devices, shifted(): return lax.ppermute(block, axis, route)  21.3 us
    all_to_all x1, blocking collectives, on_device(): lax.all_to_all(attended, 'tensor', split_axis=0, concat_axis=1, tiled=True)  15.4 us
    pallas_call x4, Pallas kernels, attend(): pl.pallas_call(functools.partial(_attend_kernel, dist, with_own), out_sha...  14.4 us
    all_to_all x1, starting transfers between devices, on_device(): lax.all_to_all(packed, 'tensor', split_axis=1, concat_axis=0, tiled=True)  10.2 us
    all_to_all x1, waiting for transfers between devices, on_device(): lax.all_to_all(packed, 'tensor', split_axis=1, concat_axis=0, tiled=True)  3.51 us
  transfers between devices with their start and end apart: 7, of which 6 were waited for; matrix products, arithmetic and copies ran while one was open for 4% of the time, Pallas kernels for 9%

profile of v16, /device:TPU:1, one launch (start us, length us, event | category | flops | bytes accessed | tf_op | source)
XLA Modules:
  0.0 94.9 jit_solution(15199314791264487965)
XLA Ops:
  0.0 1.0 %copy.37 = bf16[2,8,8,512]{3,2,0,1:T(8,128)(2,1)S(1)} copy(bf16[2,8,8,512]{3,2,1,0:T(8,128)(2,1)} %bitcast.39) | data formatting | bytes 262144 | tf_op jit(solution)/shard_map/reshape | solution.py:140
  1.0 0.7 pad_maximum_fusion
  1.7 10.2 %all-to-all-start = ((bf16[16,8,1024]{2,0,1:T(8,128)(2,1)}), bf16[16,8,1024]{2,0,1:T(8,128)(2,1)S(1)}, u32[]{:S(2)}, u32[]{:S(2)}) async-start(bf16[16,8,1024]{2,0,1:T(8,128)(2,1)} %pad_maximum_fusion), calls=%async_computation | async-start | bytes 524288 | tf_op jit(solution)/shard_map/all_to_all | solution.py:146
  12.0 0.6 gather_fusion
  12.6 0.2 compare_reduce_fusion
  12.8 0.2 fusion.1
  13.0 0.6 gather_fusion.1
  13.8 0.1 convert_reduce_fusion
  13.9 0.2 reduce_window_sum.11
  14.3 0.6 pad_add_fusion.meta_ref
  14.9 3.5 %all-to-all-done = bf16[16,8,1024]{2,0,1:T(8,128)(2,1)S(1)} async-done(((bf16[16,8,1024]{2,0,1:T(8,128)(2,1)}), bf16[16,8,1024]{2,0,1:T(8,128)(2,1)S(1)}, u32[]{:S(2)}, u32[]{:S(2)}) %all-to-all-start) | async-done | bytes 262176 | tf_op jit(solution)/shard_map/all_to_all | solution.py:146
  18.5 1.9 %collective-permute-start = (bf16[128,512]{1,0:T(8,128)(2,1)S(1)}, bf16[128,512]{1,0:T(8,128)(2,1)S(1)}, u32[]{:S(2)}, u32[]{:S(2)}) collective-permute-start(bf16[128,512]{1,0:T(8,128)(2,1)S(1)} %slice.24.q_ref), channel_id=1, source_target_pairs={{504,0},{0,8},{8,16},{16,24},{24,32},{32,40},{40,48},{48,56},{56,6... | collective-permute-start | bytes 393224 | tf_op jit(solution)/shard_map/ppermute | solution.py:22
  20.4 2.1 %collective-permute-start.1 = (bf16[128,512]{1,0:T(8,128)(2,1)S(1)}, bf16[128,512]{1,0:T(8,128)(2,1)S(1)}, u32[]{:S(2)}, u32[]{:S(2)}) collective-permute-start(bf16[128,512]{1,0:T(8,128)(2,1)S(1)} %slice.24.q_ref), channel_id=1, source_target_pairs={{496,0},{504,8},{0,16},{8,24},{16,32},{24,40},{32,48},{40,56},{48,... | collective-permute-start | bytes 393224 | tf_op jit(solution)/shard_map/ppermute | solution.py:22
  22.5 7.5 %collective-permute-start.2 = (bf16[128,512]{1,0:T(8,128)(2,1)S(1)}, bf16[128,512]{1,0:T(8,128)(2,1)S(1)}, u32[]{:S(2)}, u32[]{:S(2)}) collective-permute-start(bf16[128,512]{1,0:T(8,128)(2,1)S(1)} %slice.24.q_ref), channel_id=1, source_target_pairs={{488,0},{496,8},{504,16},{0,24},{8,32},{16,40},{24,48},{32,56},{40... | collective-permute-start | bytes 393224 | tf_op jit(solution)/shard_map/ppermute | solution.py:22
  30.0 0.7 fusion.9
  30.6 4.2 %shard_map.73 = f32[136,512]{1,0:T(8,128)} custom-call(s32[4,3,16]{2,1,0:T(4,128)} %pad_add_fusion.meta_ref, bf16[128,512]{1,0:T(8,128)(2,1)} %copy-done.5, bf16[16,128,256]{2,1,0:T(8,128)(2,1)} %kp_hbm.7, bf16[16,128,256]{2,1,0:T(8,128)(2,1)} %vp_hbm.7, bf16[128,256]{1,0:T(8,128)(2,1)} %get-tuple-element.34.refs_0_, bf16[128,256]{1,0:T(8,128)(2,1)} %get-tuple-element.33.refs_1_), custom_call_target="tpu_custom_call" | custom-call | flops 167772160 | bytes 1064960 | tf_op jit(solution)/shard_map/pallas_call | solution.py:110
  34.9 0.5 collective-permute-done.1.q_ref
  35.4 9.0 %collective-permute-done.2.q_ref = bf16[128,512]{1,0:T(8,128)(2,1)S(1)} collective-permute-done((bf16[128,512]{1,0:T(8,128)(2,1)S(1)}, bf16[128,512]{1,0:T(8,128)(2,1)S(1)}, u32[]{:S(2)}, u32[]{:S(2)}) %collective-permute-start.2) | collective-permute-done | bytes 131104 | tf_op jit(solution)/shard_map/ppermute | solution.py:22
  44.4 0.7 copy-done.9
  45.1 3.1 %shard_map.74 = f32[136,512]{1,0:T(8,128)} custom-call(s32[4,3,16]{2,1,0:T(4,128)} %pad_add_fusion.meta_ref, bf16[128,512]{1,0:T(8,128)(2,1)} %copy-done.9, bf16[16,128,256]{2,1,0:T(8,128)(2,1)} %kp_hbm.7, bf16[16,128,256]{2,1,0:T(8,128)(2,1)} %vp_hbm.7), custom_call_target="tpu_custom_call" | custom-call | flops 134217728 | bytes 933888 | tf_op jit(solution)/shard_map/pallas_call | solution.py:110
  48.2 3.2 %shard_map.75 = f32[136,512]{1,0:T(8,128)} custom-call(s32[4,3,16]{2,1,0:T(4,128)} %pad_add_fusion.meta_ref, bf16[128,512]{1,0:T(8,128)(2,1)} %copy-done.8, bf16[16,128,256]{2,1,0:T(8,128)(2,1)} %kp_hbm.7, bf16[16,128,256]{2,1,0:T(8,128)(2,1)} %vp_hbm.7), custom_call_target="tpu_custom_call" | custom-call | flops 134217728 | bytes 933888 | tf_op jit(solution)/shard_map/pallas_call | solution.py:110
  51.5 2.1 %collective-permute-start.3 = (f32[136,512]{1,0:T(8,128)S(1)}, f32[136,512]{1,0:T(8,128)S(1)}, u32[]{:S(2)}, u32[]{:S(2)}) collective-permute-start(f32[136,512]{1,0:T(8,128)S(1)} %copy-done.6), channel_id=1, source_target_pairs={{8,0},{16,8},{24,16},{32,24},{40,32},{48,40},{56,48},{64,56},{72,6... | collective-permute-start | bytes 835592 | tf_op jit(solution)/shard_map/ppermute | solution.py:22
  53.5 3.9 %shard_map.76 = f32[136,512]{1,0:T(8,128)} custom-call(s32[4,3,16]{2,1,0:T(4,128)} %pad_add_fusion.meta_ref, bf16[128,512]{1,0:T(8,128)(2,1)} %copy-done.7, bf16[16,128,256]{2,1,0:T(8,128)(2,1)} %kp_hbm.7, bf16[16,128,256]{2,1,0:T(8,128)(2,1)} %vp_hbm.7), custom_call_target="tpu_custom_call" | custom-call | flops 134217728 | bytes 933888 | tf_op jit(solution)/shard_map/pallas_call | solution.py:110
  57.4 4.3 %collective-permute-done.3 = f32[136,512]{1,0:T(8,128)S(1)} collective-permute-done((f32[136,512]{1,0:T(8,128)S(1)}, f32[136,512]{1,0:T(8,128)S(1)}, u32[]{:S(2)}, u32[]{:S(2)}) %collective-permute-start.3) | collective-permute-done | bytes 278560 | tf_op jit(solution)/shard_map/ppermute | solution.py:22
  61.7 2.6 %collective-permute-start.4 = (f32[136,512]{1,0:T(8,128)S(1)}, f32[136,512]{1,0:T(8,128)S(1)}, u32[]{:S(2)}, u32[]{:S(2)}) collective-permute-start(f32[136,512]{1,0:T(8,128)S(1)} %add.70), channel_id=1, source_target_pairs={{8,0},{16,8},{24,16},{32,24},{40,32},{48,40},{56,48},{64,56},{72,6... | collective-permute-start | bytes 835592 | tf_op jit(solution)/shard_map/ppermute | solution.py:22
  64.3 5.4 %collective-permute-done.4 = f32[136,512]{1,0:T(8,128)S(1)} collective-permute-done((f32[136,512]{1,0:T(8,128)S(1)}, f32[136,512]{1,0:T(8,128)S(1)}, u32[]{:S(2)}, u32[]{:S(2)}) %collective-permute-start.4) | collective-permute-done | bytes 278560 | tf_op jit(solution)/shard_map/ppermute | solution.py:22
  69.8 5.2 %collective-permute-start.5 = (f32[136,512]{1,0:T(8,128)S(1)}, f32[136,512]{1,0:T(8,128)S(1)}, u32[]{:S(2)}, u32[]{:S(2)}) collective-permute-start(f32[136,512]{1,0:T(8,128)S(1)} %add.71), channel_id=1, source_target_pairs={{8,0},{16,8},{24,16},{32,24},{40,32},{48,40},{56,48},{64,56},{72,6... | collective-permute-start | bytes 835592 | tf_op jit(solution)/shard_map/ppermute | solution.py:22
  75.0 3.5 %collective-permute-done.5 = f32[136,512]{1,0:T(8,128)S(1)} collective-permute-done((f32[136,512]{1,0:T(8,128)S(1)}, f32[136,512]{1,0:T(8,128)S(1)}, u32[]{:S(2)}, u32[]{:S(2)}) %collective-permute-start.5) | collective-permute-done | bytes 278560 | tf_op jit(solution)/shard_map/ppermute | solution.py:22
  78.5 0.1 copy.27
  78.6 0.2 div.11
  78.9 15.4 %all_to_all.34 = bf16[8,16,512]{2,1,0:T(8,128)(2,1)S(1)} all-to-all(bf16[8,16,512]{2,1,0:T(8,128)(2,1)S(1)} %bitcast.36), channel_id=1, replica_groups=mesh['pool'=64,'tensor'=8] {'tensor'}, dimensions={0} | all-to-all | bytes 262144 | tf_op jit(solution)/shard_map/all_to_all | solution.py:196
  94.3 0.7 copy.32
  (44 shorter events, 0.7 us)
Async XLA Ops:
  0.0 12.0 %copy-start = (s32[64,64]{1,0:T(8,128)S(1)}, s32[64,64]{1,0:T(8,128)}, u32[]{:S(2)}) copy-start(s32[64,64]{1,0:T(8,128)} %param.12) | copy-start | bytes 49156
  0.0 1.0 %copy-start.10 = (bf16[16,2048]{1,0:T(8,128)(2,1)S(1)}, bf16[16,2048]{1,0:T(8,128)(2,1)}, u32[]{:S(2)}) copy-start(bf16[16,2048]{1,0:T(8,128)(2,1)} %param.9) | copy-start | bytes 196612
  0.0 1.0 %copy-start.11 = (bf16[16,2048]{1,0:T(8,128)(2,1)S(1)}, bf16[16,2048]{1,0:T(8,128)(2,1)}, u32[]{:S(2)}) copy-start(bf16[16,2048]{1,0:T(8,128)(2,1)} %param.8) | copy-start | bytes 196612
  1.7 16.7 %all-to-all-start = ((bf16[16,8,1024]{2,0,1:T(8,128)(2,1)}), bf16[16,8,1024]{2,0,1:T(8,128)(2,1)S(1)}, u32[]{:S(2)}, u32[]{:S(2)}) async-start(bf16[16,8,1024]{2,0,1:T(8,128)(2,1)} %pad_maximum_fusion), calls=%async_computation | async-start | bytes 524288 | tf_op jit(solution)/shard_map/all_to_all | solution.py:146
  12.0 1.0 %copy-start.1 = (s32[64]{0:T(128)S(1)}, s32[64]{0:T(128)}, u32[]{:S(2)}) copy-start(s32[64]{0:T(128)} %param.13) | copy-start | bytes 772
  18.4 12.2 %copy-start.5 = (bf16[128,512]{1,0:T(8,128)(2,1)}, bf16[128,512]{1,0:T(8,128)(2,1)S(1)}, u32[]{:S(2)}) copy-start(bf16[128,512]{1,0:T(8,128)(2,1)S(1)} %slice.24.q_ref) | copy-start | bytes 393220
  18.5 16.4 %collective-permute-start = (bf16[128,512]{1,0:T(8,128)(2,1)S(1)}, bf16[128,512]{1,0:T(8,128)(2,1)S(1)}, u32[]{:S(2)}, u32[]{:S(2)}) collective-permute-start(bf16[128,512]{1,0:T(8,128)(2,1)S(1)} %slice.24.q_ref), channel_id=1, source_target_pairs={{504,0},{0,8},{8,16},{16,24},{24,32},{32,40},{40,48},{48,56},{56,6... | collective-permute-start | bytes 393224 | tf_op jit(solution)/shard_map/ppermute | solution.py:22
  20.4 15.1 %collective-permute-start.1 = (bf16[128,512]{1,0:T(8,128)(2,1)S(1)}, bf16[128,512]{1,0:T(8,128)(2,1)S(1)}, u32[]{:S(2)}, u32[]{:S(2)}) collective-permute-start(bf16[128,512]{1,0:T(8,128)(2,1)S(1)} %slice.24.q_ref), channel_id=1, source_target_pairs={{496,0},{504,8},{0,16},{8,24},{16,32},{24,40},{32,48},{40,56},{48,... | collective-permute-start | bytes 393224 | tf_op jit(solution)/shard_map/ppermute | solution.py:22
  22.5 21.9 %collective-permute-start.2 = (bf16[128,512]{1,0:T(8,128)(2,1)S(1)}, bf16[128,512]{1,0:T(8,128)(2,1)S(1)}, u32[]{:S(2)}, u32[]{:S(2)}) collective-permute-start(bf16[128,512]{1,0:T(8,128)(2,1)S(1)} %slice.24.q_ref), channel_id=1, source_target_pairs={{488,0},{496,8},{504,16},{0,24},{8,32},{16,40},{24,48},{32,56},{40... | collective-permute-start | bytes 393224 | tf_op jit(solution)/shard_map/ppermute | solution.py:22
  34.9 13.3 %copy-start.7 = (bf16[128,512]{1,0:T(8,128)(2,1)}, bf16[128,512]{1,0:T(8,128)(2,1)S(1)}, u32[]{:S(2)}) copy-start(bf16[128,512]{1,0:T(8,128)(2,1)S(1)} %collective-permute-done.q_ref) | copy-start | bytes 393220
  35.4 12.8 %copy-start.8 = (bf16[128,512]{1,0:T(8,128)(2,1)}, bf16[128,512]{1,0:T(8,128)(2,1)S(1)}, u32[]{:S(2)}) copy-start(bf16[128,512]{1,0:T(8,128)(2,1)S(1)} %collective-permute-done.1.q_ref) | copy-start | bytes 393220
  44.4 0.7 copy-start.9
  48.2 3.2 %copy-start.6 = (f32[136,512]{1,0:T(8,128)S(1)}, f32[136,512]{1,0:T(8,128)}, u32[]{:S(2)}) copy-start(f32[136,512]{1,0:T(8,128)} %shard_map.74) | copy-start | bytes 835588
  51.4 10.2 %copy-start.4 = (f32[136,512]{1,0:T(8,128)S(1)}, f32[136,512]{1,0:T(8,128)}, u32[]{:S(2)}) copy-start(f32[136,512]{1,0:T(8,128)} %shard_map.75) | copy-start | bytes 835588
  51.5 10.2 %collective-permute-start.3 = (f32[136,512]{1,0:T(8,128)S(1)}, f32[136,512]{1,0:T(8,128)S(1)}, u32[]{:S(2)}, u32[]{:S(2)}) collective-permute-start(f32[136,512]{1,0:T(8,128)S(1)} %copy-done.6), channel_id=1, source_target_pairs={{8,0},{16,8},{24,16},{32,24},{40,32},{48,40},{56,48},{64,56},{72,6... | collective-permute-start | bytes 835592 | tf_op jit(solution)/shard_map/ppermute | solution.py:22
  57.4 12.4 %copy-start.3 = (f32[136,512]{1,0:T(8,128)S(1)}, f32[136,512]{1,0:T(8,128)}, u32[]{:S(2)}) copy-start(f32[136,512]{1,0:T(8,128)} %shard_map.76) | copy-start | bytes 835588
  61.7 16.7 %copy-start.2 = (f32[136,512]{1,0:T(8,128)S(1)}, f32[136,512]{1,0:T(8,128)}, u32[]{:S(2)}) copy-start(f32[136,512]{1,0:T(8,128)} %shard_map.73) | copy-start | bytes 835588
  61.7 8.0 %collective-permute-start.4 = (f32[136,512]{1,0:T(8,128)S(1)}, f32[136,512]{1,0:T(8,128)S(1)}, u32[]{:S(2)}, u32[]{:S(2)}) collective-permute-start(f32[136,512]{1,0:T(8,128)S(1)} %add.70), channel_id=1, source_target_pairs={{8,0},{16,8},{24,16},{32,24},{40,32},{48,40},{56,48},{64,56},{72,6... | collective-permute-start | bytes 835592 | tf_op jit(solution)/shard_map/ppermute | solution.py:22
  69.8 8.6 %collective-permute-start.5 = (f32[136,512]{1,0:T(8,128)S(1)}, f32[136,512]{1,0:T(8,128)S(1)}, u32[]{:S(2)}, u32[]{:S(2)}) collective-permute-start(f32[136,512]{1,0:T(8,128)S(1)} %add.71), channel_id=1, source_target_pairs={{8,0},{16,8},{24,16},{32,24},{40,32},{48,40},{56,48},{64,56},{72,6... | collective-permute-start | bytes 835592 | tf_op jit(solution)/shard_map/ppermute | solution.py:22

commit v17 on v6

--- a/solution.py
+++ b/solution.py
@@ -175,10 +175,10 @@
     count = jnp.broadcast_to(jnp.sum(wanted.astype(jnp.int32), axis=1, keepdims=True), (SPAN, slots_dev))
     meta = jnp.stack([order, order_limit, count], axis=1).astype(jnp.int32)
 
-    received = [shifted(q_own, "pool", offset) for offset in range(1, SPAN)]
+    received = [shifted(q_own, "pool", offset) for offset in range(SPAN - 1, 0, -1)]
     part_own = attend(0, meta, q_own, cached_key_pages, cached_value_pages, k_new, v_new)
     *received, part_own = lax.optimization_barrier((*received, part_own))
-    received = [q_own] + received
+    received = [q_own] + received[::-1]
 
     def part(offset):
         return attend(offset, meta, received[offset], cached_key_pages, cached_value_pages)

time: 94.5 us -> 94.1 us (level)
  starting transfers between devices: 31.2 us -> 36.4 us
  blocking collectives: 15 us -> 11.3 us
  waiting for transfers between devices: 21.9 us -> 20.5 us
    ppermute x6, starting transfers between devices: 21 us -> 26.2 us  [shifted(): return lax.ppermute(block, axis, route)]
    all_to_all x1, blocking collectives: 15 us -> 11.3 us  [on_device(): lax.all_to_all(attended, 'tensor', split_axis=0, concat_axis=1, tiled=True)]
    ppermute x6, waiting for transfers between devices: 18.3 us -> 17 us  [shifted(): return lax.ppermute(block, axis, route)]
  transfers between devices with their start and end apart: 7 -> 7, of which waited for: 5 -> 6; matrix products, arithmetic and copies ran while one was open for 4% -> 4% of each run, Pallas kernels for 13% -> 13%
where the time goes in v17:
time: 94.1 us; the launch traced here: 93.7 us
  starting transfers between devices  36.4 us (39%)
  waiting for transfers between devices  20.5 us (22%)
  Pallas kernels  16.9 us (18%)
  blocking collectives  11.3 us (12%)
  other arithmetic  4.46 us (5%)
  local copies, waits for them, and re-layouts  3.95 us (4%)
    ppermute x6, starting transfers between devices, shifted(): return lax.ppermute(block, axis, route)  26.2 us
    ppermute x6, waiting for transfers between devices, shifted(): return lax.ppermute(block, axis, route)  17 us
    pallas_call x4, Pallas kernels, attend(): pl.pallas_call(functools.partial(_attend_kernel, dist, with_own), out_sha...  16.9 us
    all_to_all x1, blocking collectives, on_device(): lax.all_to_all(attended, 'tensor', split_axis=0, concat_axis=1, tiled=True)  11.3 us
    all_to_all x1, starting transfers between devices, on_device(): lax.all_to_all(packed, 'tensor', split_axis=1, concat_axis=0, tiled=True)  10.2 us
    all_to_all x1, waiting for transfers between devices, on_device(): lax.all_to_all(packed, 'tensor', split_axis=1, concat_axis=0, tiled=True)  3.52 us
    add x3, other arithmetic, on_device(): total = here + moved  2.02 us
  transfers between devices with their start and end apart: 7, of which 6 were waited for; matrix products, arithmetic and copies ran while one was open for 4% of the time, Pallas kernels for 13%

profile of v17, /device:TPU:1, one launch (start us, length us, event | category | flops | bytes accessed | tf_op | source)
XLA Modules:
  0.0 93.7 jit_solution(6106583348195482748)
XLA Ops:
  0.0 1.0 %copy.37 = bf16[2,8,8,512]{3,2,0,1:T(8,128)(2,1)S(1)} copy(bf16[2,8,8,512]{3,2,1,0:T(8,128)(2,1)} %bitcast.39) | data formatting | bytes 262144 | tf_op jit(solution)/shard_map/reshape | solution.py:140
  1.0 0.7 pad_maximum_fusion
  1.7 10.2 %all-to-all-start = ((bf16[16,8,1024]{2,0,1:T(8,128)(2,1)}), bf16[16,8,1024]{2,0,1:T(8,128)(2,1)S(1)}, u32[]{:S(2)}, u32[]{:S(2)}) async-start(bf16[16,8,1024]{2,0,1:T(8,128)(2,1)} %pad_maximum_fusion), calls=%async_computation | async-start | bytes 524288 | tf_op jit(solution)/shard_map/all_to_all | solution.py:146
  12.0 0.6 gather_fusion
  12.6 0.2 compare_reduce_fusion
  12.8 0.2 fusion.1
  13.0 0.6 gather_fusion.1
  13.8 0.2 reduce_window_sum.11
  14.0 0.1 convert_reduce_fusion
  14.3 0.6 pad_add_fusion.meta_ref
  14.9 3.5 %all-to-all-done = bf16[16,8,1024]{2,0,1:T(8,128)(2,1)S(1)} async-done(((bf16[16,8,1024]{2,0,1:T(8,128)(2,1)}), bf16[16,8,1024]{2,0,1:T(8,128)(2,1)S(1)}, u32[]{:S(2)}, u32[]{:S(2)}) %all-to-all-start) | async-done | bytes 262176 | tf_op jit(solution)/shard_map/all_to_all | solution.py:146
  18.5 1.9 %collective-permute-start = (bf16[128,512]{1,0:T(8,128)(2,1)S(1)}, bf16[128,512]{1,0:T(8,128)(2,1)S(1)}, u32[]{:S(2)}, u32[]{:S(2)}) collective-permute-start(bf16[128,512]{1,0:T(8,128)(2,1)S(1)} %slice.24.q_ref), channel_id=1, source_target_pairs={{488,0},{496,8},{504,16},{0,24},{8,32},{16,40},{24,48},{32,56},{40... | collective-permute-start | bytes 393224 | tf_op jit(solution)/shard_map/ppermute | solution.py:22
  20.4 6.0 %collective-permute-start.1 = (bf16[128,512]{1,0:T(8,128)(2,1)S(1)}, bf16[128,512]{1,0:T(8,128)(2,1)S(1)}, u32[]{:S(2)}, u32[]{:S(2)}) collective-permute-start(bf16[128,512]{1,0:T(8,128)(2,1)S(1)} %slice.24.q_ref), channel_id=1, source_target_pairs={{496,0},{504,8},{0,16},{8,24},{16,32},{24,40},{32,48},{40,56},{48,... | collective-permute-start | bytes 393224 | tf_op jit(solution)/shard_map/ppermute | solution.py:22
  26.4 3.5 %collective-permute-start.2 = (bf16[128,512]{1,0:T(8,128)(2,1)S(1)}, bf16[128,512]{1,0:T(8,128)(2,1)S(1)}, u32[]{:S(2)}, u32[]{:S(2)}) collective-permute-start(bf16[128,512]{1,0:T(8,128)(2,1)S(1)} %slice.24.q_ref), channel_id=1, source_target_pairs={{504,0},{0,8},{8,16},{16,24},{24,32},{32,40},{40,48},{48,56},{56,6... | collective-permute-start | bytes 393224 | tf_op jit(solution)/shard_map/ppermute | solution.py:22
  30.0 0.7 fusion.9
  30.7 4.9 %shard_map.73 = f32[136,512]{1,0:T(8,128)} custom-call(s32[4,3,16]{2,1,0:T(4,128)} %pad_add_fusion.meta_ref, bf16[128,512]{1,0:T(8,128)(2,1)} %copy-done.3, bf16[16,128,256]{2,1,0:T(8,128)(2,1)} %kp_hbm.7, bf16[16,128,256]{2,1,0:T(8,128)(2,1)} %vp_hbm.7, bf16[128,256]{1,0:T(8,128)(2,1)} %get-tuple-element.34.refs_0_, bf16[128,256]{1,0:T(8,128)(2,1)} %get-tuple-element.33.refs_1_), custom_call_target="tpu_custom_call" | custom-call | flops 167772160 | bytes 1064960 | tf_op jit(solution)/shard_map/pallas_call | solution.py:110
  35.6 6.8 %collective-permute-done.1.q_ref = bf16[128,512]{1,0:T(8,128)(2,1)S(1)} collective-permute-done((bf16[128,512]{1,0:T(8,128)(2,1)S(1)}, bf16[128,512]{1,0:T(8,128)(2,1)S(1)}, u32[]{:S(2)}, u32[]{:S(2)}) %collective-permute-start.1) | collective-permute-done | bytes 131104 | tf_op jit(solution)/shard_map/ppermute | solution.py:22
  42.5 2.7 %collective-permute-done.2.q_ref = bf16[128,512]{1,0:T(8,128)(2,1)S(1)} collective-permute-done((bf16[128,512]{1,0:T(8,128)(2,1)S(1)}, bf16[128,512]{1,0:T(8,128)(2,1)S(1)}, u32[]{:S(2)}, u32[]{:S(2)}) %collective-permute-start.2) | collective-permute-done | bytes 131104 | tf_op jit(solution)/shard_map/ppermute | solution.py:22
  45.2 4.6 %shard_map.74 = f32[136,512]{1,0:T(8,128)} custom-call(s32[4,3,16]{2,1,0:T(4,128)} %pad_add_fusion.meta_ref, bf16[128,512]{1,0:T(8,128)(2,1)} %copy-done.6, bf16[16,128,256]{2,1,0:T(8,128)(2,1)} %kp_hbm.7, bf16[16,128,256]{2,1,0:T(8,128)(2,1)} %vp_hbm.7), custom_call_target="tpu_custom_call" | custom-call | flops 134217728 | bytes 933888 | tf_op jit(solution)/shard_map/pallas_call | solution.py:110
  49.8 2.0 %collective-permute-start.3 = (f32[136,512]{1,0:T(8,128)}, f32[136,512]{1,0:T(8,128)S(1)}, u32[]{:S(2)}, u32[]{:S(2)}) collective-permute-start(f32[136,512]{1,0:T(8,128)} %shard_map.74), channel_id=1, source_target_pairs={{8,0},{16,8},{24,16},{32,24},{40,32},{48,40},{56,48},{64,56},{72,6... | collective-permute-start | bytes 835592 | tf_op jit(solution)/shard_map/ppermute | solution.py:22
  51.8 3.8 %shard_map.75 = f32[136,512]{1,0:T(8,128)} custom-call(s32[4,3,16]{2,1,0:T(4,128)} %pad_add_fusion.meta_ref, bf16[128,512]{1,0:T(8,128)(2,1)} %copy-done.5, bf16[16,128,256]{2,1,0:T(8,128)(2,1)} %kp_hbm.7, bf16[16,128,256]{2,1,0:T(8,128)(2,1)} %vp_hbm.7), custom_call_target="tpu_custom_call" | custom-call | flops 134217728 | bytes 933888 | tf_op jit(solution)/shard_map/pallas_call | solution.py:110
  55.6 3.5 %collective-permute-done.3 = f32[136,512]{1,0:T(8,128)S(1)} collective-permute-done((f32[136,512]{1,0:T(8,128)}, f32[136,512]{1,0:T(8,128)S(1)}, u32[]{:S(2)}, u32[]{:S(2)}) %collective-permute-start.3) | collective-permute-done | bytes 278560 | tf_op jit(solution)/shard_map/ppermute | solution.py:22
  59.1 1.0 %add.70 = f32[136,512]{1,0:T(8,128)S(1)} add(f32[136,512]{1,0:T(8,128)} %shard_map.75, f32[136,512]{1,0:T(8,128)S(1)} %collective-permute-done.3) | non-fusion elementwise | flops 69632 | bytes 835584 | tf_op jit(solution)/shard_map/add | solution.py:191
  60.1 5.3 %collective-permute-start.4 = (f32[136,512]{1,0:T(8,128)S(1)}, f32[136,512]{1,0:T(8,128)S(1)}, u32[]{:S(2)}, u32[]{:S(2)}) collective-permute-start(f32[136,512]{1,0:T(8,128)S(1)} %add.70), channel_id=1, source_target_pairs={{8,0},{16,8},{24,16},{32,24},{40,32},{48,40},{56,48},{64,56},{72,6... | collective-permute-start | bytes 835592 | tf_op jit(solution)/shard_map/ppermute | solution.py:22
  65.4 3.5 %shard_map.76 = f32[136,512]{1,0:T(8,128)} custom-call(s32[4,3,16]{2,1,0:T(4,128)} %pad_add_fusion.meta_ref, bf16[128,512]{1,0:T(8,128)(2,1)} %copy-done.4, bf16[16,128,256]{2,1,0:T(8,128)(2,1)} %kp_hbm.7, bf16[16,128,256]{2,1,0:T(8,128)(2,1)} %vp_hbm.7), custom_call_target="tpu_custom_call" | custom-call | flops 134217728 | bytes 933888 | tf_op jit(solution)/shard_map/pallas_call | solution.py:110
  68.9 0.6 collective-permute-done.4
  69.4 1.0 %add.71 = f32[136,512]{1,0:T(8,128)S(1)} add(f32[136,512]{1,0:T(8,128)} %shard_map.76, f32[136,512]{1,0:T(8,128)S(1)} %collective-permute-done.4) | non-fusion elementwise | flops 69632 | bytes 835584 | tf_op jit(solution)/shard_map/add | solution.py:191
  70.4 7.4 %collective-permute-start.5 = (f32[136,512]{1,0:T(8,128)S(1)}, f32[136,512]{1,0:T(8,128)S(1)}, u32[]{:S(2)}, u32[]{:S(2)}) collective-permute-start(f32[136,512]{1,0:T(8,128)S(1)} %add.71), channel_id=1, source_target_pairs={{8,0},{16,8},{24,16},{32,24},{40,32},{48,40},{56,48},{64,56},{72,6... | collective-permute-start | bytes 835592 | tf_op jit(solution)/shard_map/ppermute | solution.py:22
  77.9 3.5 %collective-permute-done.5 = f32[136,512]{1,0:T(8,128)S(1)} collective-permute-done((f32[136,512]{1,0:T(8,128)S(1)}, f32[136,512]{1,0:T(8,128)S(1)}, u32[]{:S(2)}, u32[]{:S(2)}) %collective-permute-start.5) | collective-permute-done | bytes 278560 | tf_op jit(solution)/shard_map/ppermute | solution.py:22
  81.5 0.2 div.11
  81.8 11.3 %all_to_all.34 = bf16[8,16,512]{2,1,0:T(8,128)(2,1)S(1)} all-to-all(bf16[8,16,512]{2,1,0:T(8,128)(2,1)S(1)} %bitcast.36), channel_id=1, replica_groups=mesh['pool'=64,'tensor'=8] {'tensor'}, dimensions={0} | all-to-all | bytes 262144 | tf_op jit(solution)/shard_map/all_to_all | solution.py:197
  93.1 0.7 copy.32
  (38 shorter events, 0.7 us)
Async XLA Ops:
  0.0 12.0 %copy-start = (s32[64,64]{1,0:T(8,128)S(1)}, s32[64,64]{1,0:T(8,128)}, u32[]{:S(2)}) copy-start(s32[64,64]{1,0:T(8,128)} %param.12) | copy-start | bytes 49156
  0.0 1.0 %copy-start.7 = (bf16[16,2048]{1,0:T(8,128)(2,1)S(1)}, bf16[16,2048]{1,0:T(8,128)(2,1)}, u32[]{:S(2)}) copy-start(bf16[16,2048]{1,0:T(8,128)(2,1)} %param.9) | copy-start | bytes 196612
  0.0 1.0 %copy-start.8 = (bf16[16,2048]{1,0:T(8,128)(2,1)S(1)}, bf16[16,2048]{1,0:T(8,128)(2,1)}, u32[]{:S(2)}) copy-start(bf16[16,2048]{1,0:T(8,128)(2,1)} %param.8) | copy-start | bytes 196612
  1.7 16.7 %all-to-all-start = ((bf16[16,8,1024]{2,0,1:T(8,128)(2,1)}), bf16[16,8,1024]{2,0,1:T(8,128)(2,1)S(1)}, u32[]{:S(2)}, u32[]{:S(2)}) async-start(bf16[16,8,1024]{2,0,1:T(8,128)(2,1)} %pad_maximum_fusion), calls=%async_computation | async-start | bytes 524288 | tf_op jit(solution)/shard_map/all_to_all | solution.py:146
  12.0 1.0 %copy-start.1 = (s32[64]{0:T(128)S(1)}, s32[64]{0:T(128)}, u32[]{:S(2)}) copy-start(s32[64]{0:T(128)} %param.13) | copy-start | bytes 772
  18.4 12.2 %copy-start.3 = (bf16[128,512]{1,0:T(8,128)(2,1)}, bf16[128,512]{1,0:T(8,128)(2,1)S(1)}, u32[]{:S(2)}) copy-start(bf16[128,512]{1,0:T(8,128)(2,1)S(1)} %slice.24.q_ref) | copy-start | bytes 393220
  18.5 17.2 %collective-permute-start = (bf16[128,512]{1,0:T(8,128)(2,1)S(1)}, bf16[128,512]{1,0:T(8,128)(2,1)S(1)}, u32[]{:S(2)}, u32[]{:S(2)}) collective-permute-start(bf16[128,512]{1,0:T(8,128)(2,1)S(1)} %slice.24.q_ref), channel_id=1, source_target_pairs={{488,0},{496,8},{504,16},{0,24},{8,32},{16,40},{24,48},{32,56},{40... | collective-permute-start | bytes 393224 | tf_op jit(solution)/shard_map/ppermute | solution.py:22
  20.4 22.1 %collective-permute-start.1 = (bf16[128,512]{1,0:T(8,128)(2,1)S(1)}, bf16[128,512]{1,0:T(8,128)(2,1)S(1)}, u32[]{:S(2)}, u32[]{:S(2)}) collective-permute-start(bf16[128,512]{1,0:T(8,128)(2,1)S(1)} %slice.24.q_ref), channel_id=1, source_target_pairs={{496,0},{504,8},{0,16},{8,24},{16,32},{24,40},{32,48},{40,56},{48,... | collective-permute-start | bytes 393224 | tf_op jit(solution)/shard_map/ppermute | solution.py:22
  26.4 18.7 %collective-permute-start.2 = (bf16[128,512]{1,0:T(8,128)(2,1)S(1)}, bf16[128,512]{1,0:T(8,128)(2,1)S(1)}, u32[]{:S(2)}, u32[]{:S(2)}) collective-permute-start(bf16[128,512]{1,0:T(8,128)(2,1)S(1)} %slice.24.q_ref), channel_id=1, source_target_pairs={{504,0},{0,8},{8,16},{16,24},{24,32},{32,40},{40,48},{48,56},{56,6... | collective-permute-start | bytes 393224 | tf_op jit(solution)/shard_map/ppermute | solution.py:22
  35.6 9.5 %copy-start.6 = (bf16[128,512]{1,0:T(8,128)(2,1)}, bf16[128,512]{1,0:T(8,128)(2,1)S(1)}, u32[]{:S(2)}) copy-start(bf16[128,512]{1,0:T(8,128)(2,1)S(1)} %collective-permute-done.q_ref) | copy-start | bytes 393220
  42.5 7.3 %copy-start.5 = (bf16[128,512]{1,0:T(8,128)(2,1)}, bf16[128,512]{1,0:T(8,128)(2,1)S(1)}, u32[]{:S(2)}) copy-start(bf16[128,512]{1,0:T(8,128)(2,1)S(1)} %collective-permute-done.1.q_ref) | copy-start | bytes 393220
  45.2 4.6 %copy-start.4 = (bf16[128,512]{1,0:T(8,128)(2,1)}, bf16[128,512]{1,0:T(8,128)(2,1)S(1)}, u32[]{:S(2)}) copy-start(bf16[128,512]{1,0:T(8,128)(2,1)S(1)} %collective-permute-done.2.q_ref) | copy-start | bytes 393220
  49.8 9.3 %collective-permute-start.3 = (f32[136,512]{1,0:T(8,128)}, f32[136,512]{1,0:T(8,128)S(1)}, u32[]{:S(2)}, u32[]{:S(2)}) collective-permute-start(f32[136,512]{1,0:T(8,128)} %shard_map.74), channel_id=1, source_target_pairs={{8,0},{16,8},{24,16},{32,24},{40,32},{48,40},{56,48},{64,56},{72,6... | collective-permute-start | bytes 835592 | tf_op jit(solution)/shard_map/ppermute | solution.py:22
  60.1 9.4 %collective-permute-start.4 = (f32[136,512]{1,0:T(8,128)S(1)}, f32[136,512]{1,0:T(8,128)S(1)}, u32[]{:S(2)}, u32[]{:S(2)}) collective-permute-start(f32[136,512]{1,0:T(8,128)S(1)} %add.70), channel_id=1, source_target_pairs={{8,0},{16,8},{24,16},{32,24},{40,32},{48,40},{56,48},{64,56},{72,6... | collective-permute-start | bytes 835592 | tf_op jit(solution)/shard_map/ppermute | solution.py:22
  68.9 12.5 %copy-start.2 = (f32[136,512]{1,0:T(8,128)S(1)}, f32[136,512]{1,0:T(8,128)}, u32[]{:S(2)}) copy-start(f32[136,512]{1,0:T(8,128)} %shard_map.73) | copy-start | bytes 835588
  70.4 10.9 %collective-permute-start.5 = (f32[136,512]{1,0:T(8,128)S(1)}, f32[136,512]{1,0:T(8,128)S(1)}, u32[]{:S(2)}, u32[]{:S(2)}) collective-permute-start(f32[136,512]{1,0:T(8,128)S(1)} %add.71), channel_id=1, source_target_pairs={{8,0},{16,8},{24,16},{32,24},{40,32},{48,40},{56,48},{64,56},{72,6... | collective-permute-start | bytes 835592 | tf_op jit(solution)/shard_map/ppermute | solution.py:22

commit v18 on v16

--- a/solution.py
+++ b/solution.py
@@ -175,10 +175,10 @@
     count = jnp.broadcast_to(jnp.sum(wanted.astype(jnp.int32), axis=1, keepdims=True), (SPAN, slots_dev))
     meta = jnp.stack([order, order_limit, count], axis=1).astype(jnp.int32)
 
-    received = [shifted(q_own, "pool", offset) for offset in range(1, SPAN)]
+    received = [shifted(q_own, "pool", offset) for offset in range(SPAN - 1, 0, -1)]
     part_own = attend(0, meta, q_own, cached_key_pages, cached_value_pages, k_new, v_new)
     *received, part_own = lax.optimization_barrier((*received, part_own))
-    received = [q_own] + received
+    received = [q_own] + received[::-1]
 
     def part(offset):
         return attend(offset, meta, received[offset], cached_key_pages, cached_value_pages)

time: 95.6 us -> 96.5 us (level)
  starting transfers between devices: 31.5 us -> 41.3 us
  blocking collectives: 15.4 us -> 11.3 us
  waiting for transfers between devices: 26.2 us -> 22.4 us
    ppermute x6, starting transfers between devices: 21.3 us -> 31.1 us  [shifted(): return lax.ppermute(block, axis, route)]
    all_to_all x1, blocking collectives: 15.4 us -> 11.3 us  [on_device(): lax.all_to_all(attended, 'tensor', split_axis=0, concat_axis=1, tiled=True)]
    ppermute x6, waiting for transfers between devices: 22.7 us -> 18.9 us  [shifted(): return lax.ppermute(block, axis, route)]
  transfers between devices with their start and end apart: 7 -> 7, of which waited for: 6 -> 6; matrix products, arithmetic and copies ran while one was open for 4% -> 4% of each run, Pallas kernels for 9% -> 8%
where the time goes in v18:
time: 96.5 us; the launch traced here: 96.6 us
  starting transfers between devices  41.3 us (43%)
  waiting for transfers between devices  22.4 us (23%)
  Pallas kernels  14.8 us (15%)
  blocking collectives  11.3 us (12%)
  local copies, waits for them, and re-layouts  3.95 us (4%)
  other arithmetic  2.56 us (3%)
    ppermute x6, starting transfers between devices, shifted(): return lax.ppermute(block, axis, route)  31.1 us
    ppermute x6, waiting for transfers between devices, shifted(): return lax.ppermute(block, axis, route)  18.9 us
    pallas_call x4, Pallas kernels, attend(): pl.pallas_call(functools.partial(_attend_kernel, dist, with_own), out_sha...  14.8 us
    all_to_all x1, blocking collectives, on_device(): lax.all_to_all(attended, 'tensor', split_axis=0, concat_axis=1, tiled=True)  11.3 us
    all_to_all x1, starting transfers between devices, on_device(): lax.all_to_all(packed, 'tensor', split_axis=1, concat_axis=0, tiled=True)  10.2 us
    all_to_all x1, waiting for transfers between devices, on_device(): lax.all_to_all(packed, 'tensor', split_axis=1, concat_axis=0, tiled=True)  3.51 us
  transfers between devices with their start and end apart: 7, of which 6 were waited for; matrix products, arithmetic and copies ran while one was open for 4% of the time, Pallas kernels for 8%

profile of v18, /device:TPU:1, one launch (start us, length us, event | category | flops | bytes accessed | tf_op | source)
XLA Modules:
  0.0 96.6 jit_solution(8054210263168815173)
XLA Ops:
  0.0 1.0 copy.37
  1.0 0.7 pad_maximum_fusion
  1.7 10.2 %all-to-all-start = ((bf16[16,8,1024]{2,0,1:T(8,128)(2,1)}), bf16[16,8,1024]{2,0,1:T(8,128)(2,1)S(1)}, u32[]{:S(2)}, u32[]{:S(2)}) async-start(bf16[16,8,1024]{2,0,1:T(8,128)(2,1)} %pad_maximum_fusion), calls=%async_computation | async-start | bytes 524288 | tf_op jit(solution)/shard_map/all_to_all | solution.py:146
  12.0 0.6 gather_fusion
  12.6 0.2 compare_reduce_fusion
  12.8 0.2 fusion.1
  13.0 0.6 gather_fusion.1
  13.8 0.1 convert_reduce_fusion
  13.9 0.2 reduce_window_sum.11
  14.1 0.1 select_reduce_fusion.1
  14.3 0.6 pad_add_fusion.meta_ref
  14.9 3.5 %all-to-all-done = bf16[16,8,1024]{2,0,1:T(8,128)(2,1)S(1)} async-done(((bf16[16,8,1024]{2,0,1:T(8,128)(2,1)}), bf16[16,8,1024]{2,0,1:T(8,128)(2,1)S(1)}, u32[]{:S(2)}, u32[]{:S(2)}) %all-to-all-start) | async-done | bytes 262176 | tf_op jit(solution)/shard_map/all_to_all | solution.py:146
  18.5 1.9 %collective-permute-start = (bf16[128,512]{1,0:T(8,128)(2,1)S(1)}, bf16[128,512]{1,0:T(8,128)(2,1)S(1)}, u32[]{:S(2)}, u32[]{:S(2)}) collective-permute-start(bf16[128,512]{1,0:T(8,128)(2,1)S(1)} %slice.24.q_ref), channel_id=1, source_target_pairs={{488,0},{496,8},{504,16},{0,24},{8,32},{16,40},{24,48},{32,56},{40... | collective-permute-start | bytes 393224 | tf_op jit(solution)/shard_map/ppermute | solution.py:22
  20.4 6.0 %collective-permute-start.1 = (bf16[128,512]{1,0:T(8,128)(2,1)S(1)}, bf16[128,512]{1,0:T(8,128)(2,1)S(1)}, u32[]{:S(2)}, u32[]{:S(2)}) collective-permute-start(bf16[128,512]{1,0:T(8,128)(2,1)S(1)} %slice.24.q_ref), channel_id=1, source_target_pairs={{496,0},{504,8},{0,16},{8,24},{16,32},{24,40},{32,48},{40,56},{48,... | collective-permute-start | bytes 393224 | tf_op jit(solution)/shard_map/ppermute | solution.py:22
  26.4 3.5 %collective-permute-start.2 = (bf16[128,512]{1,0:T(8,128)(2,1)S(1)}, bf16[128,512]{1,0:T(8,128)(2,1)S(1)}, u32[]{:S(2)}, u32[]{:S(2)}) collective-permute-start(bf16[128,512]{1,0:T(8,128)(2,1)S(1)} %slice.24.q_ref), channel_id=1, source_target_pairs={{504,0},{0,8},{8,16},{16,24},{24,32},{32,40},{40,48},{48,56},{56,6... | collective-permute-start | bytes 393224 | tf_op jit(solution)/shard_map/ppermute | solution.py:22
  30.0 0.7 fusion.9
  30.6 3.9 %shard_map.73 = f32[136,512]{1,0:T(8,128)} custom-call(s32[4,3,16]{2,1,0:T(4,128)} %pad_add_fusion.meta_ref, bf16[128,512]{1,0:T(8,128)(2,1)} %copy-done.5, bf16[16,128,256]{2,1,0:T(8,128)(2,1)} %kp_hbm.7, bf16[16,128,256]{2,1,0:T(8,128)(2,1)} %vp_hbm.7, bf16[128,256]{1,0:T(8,128)(2,1)} %get-tuple-element.34.refs_0_, bf16[128,256]{1,0:T(8,128)(2,1)} %get-tuple-element.33.refs_1_), custom_call_target="tpu_custom_call" | custom-call | flops 167772160 | bytes 1064960 | tf_op jit(solution)/shard_map/pallas_call | solution.py:110
  34.5 7.9 %collective-permute-done.1.q_ref = bf16[128,512]{1,0:T(8,128)(2,1)S(1)} collective-permute-done((bf16[128,512]{1,0:T(8,128)(2,1)S(1)}, bf16[128,512]{1,0:T(8,128)(2,1)S(1)}, u32[]{:S(2)}, u32[]{:S(2)}) %collective-permute-start.1) | collective-permute-done | bytes 131104 | tf_op jit(solution)/shard_map/ppermute | solution.py:22
  42.4 2.7 %collective-permute-done.2.q_ref = bf16[128,512]{1,0:T(8,128)(2,1)S(1)} collective-permute-done((bf16[128,512]{1,0:T(8,128)(2,1)S(1)}, bf16[128,512]{1,0:T(8,128)(2,1)S(1)}, u32[]{:S(2)}, u32[]{:S(2)}) %collective-permute-start.2) | collective-permute-done | bytes 131104 | tf_op jit(solution)/shard_map/ppermute | solution.py:22
  45.1 3.2 %shard_map.74 = f32[136,512]{1,0:T(8,128)} custom-call(s32[4,3,16]{2,1,0:T(4,128)} %pad_add_fusion.meta_ref, bf16[128,512]{1,0:T(8,128)(2,1)} %copy-done.8, bf16[16,128,256]{2,1,0:T(8,128)(2,1)} %kp_hbm.7, bf16[16,128,256]{2,1,0:T(8,128)(2,1)} %vp_hbm.7), custom_call_target="tpu_custom_call" | custom-call | flops 134217728 | bytes 933888 | tf_op jit(solution)/shard_map/pallas_call | solution.py:110
  48.4 3.5 %shard_map.75 = f32[136,512]{1,0:T(8,128)} custom-call(s32[4,3,16]{2,1,0:T(4,128)} %pad_add_fusion.meta_ref, bf16[128,512]{1,0:T(8,128)(2,1)} %copy-done.9, bf16[16,128,256]{2,1,0:T(8,128)(2,1)} %kp_hbm.7, bf16[16,128,256]{2,1,0:T(8,128)(2,1)} %vp_hbm.7), custom_call_target="tpu_custom_call" | custom-call | flops 134217728 | bytes 933888 | tf_op jit(solution)/shard_map/pallas_call | solution.py:110
  51.9 4.6 %collective-permute-start.3 = (f32[136,512]{1,0:T(8,128)S(1)}, f32[136,512]{1,0:T(8,128)S(1)}, u32[]{:S(2)}, u32[]{:S(2)}) collective-permute-start(f32[136,512]{1,0:T(8,128)S(1)} %copy-done.6), channel_id=1, source_target_pairs={{8,0},{16,8},{24,16},{32,24},{40,32},{48,40},{56,48},{64,56},{72,6... | collective-permute-start | bytes 835592 | tf_op jit(solution)/shard_map/ppermute | solution.py:22
  56.5 4.2 %shard_map.76 = f32[136,512]{1,0:T(8,128)} custom-call(s32[4,3,16]{2,1,0:T(4,128)} %pad_add_fusion.meta_ref, bf16[128,512]{1,0:T(8,128)(2,1)} %copy-done.7, bf16[16,128,256]{2,1,0:T(8,128)(2,1)} %kp_hbm.7, bf16[16,128,256]{2,1,0:T(8,128)(2,1)} %vp_hbm.7), custom_call_target="tpu_custom_call" | custom-call | flops 134217728 | bytes 933888 | tf_op jit(solution)/shard_map/pallas_call | solution.py:110
  60.8 0.7 collective-permute-done.3
  61.6 7.6 %collective-permute-start.4 = (f32[136,512]{1,0:T(8,128)S(1)}, f32[136,512]{1,0:T(8,128)S(1)}, u32[]{:S(2)}, u32[]{:S(2)}) collective-permute-start(f32[136,512]{1,0:T(8,128)S(1)} %add.70), channel_id=1, source_target_pairs={{8,0},{16,8},{24,16},{32,24},{40,32},{48,40},{56,48},{64,56},{72,6... | collective-permute-start | bytes 835592 | tf_op jit(solution)/shard_map/ppermute | solution.py:22
  69.1 4.1 %collective-permute-done.4 = f32[136,512]{1,0:T(8,128)S(1)} collective-permute-done((f32[136,512]{1,0:T(8,128)S(1)}, f32[136,512]{1,0:T(8,128)S(1)}, u32[]{:S(2)}, u32[]{:S(2)}) %collective-permute-start.4) | collective-permute-done | bytes 278560 | tf_op jit(solution)/shard_map/ppermute | solution.py:22
  73.2 7.4 %collective-permute-start.5 = (f32[136,512]{1,0:T(8,128)S(1)}, f32[136,512]{1,0:T(8,128)S(1)}, u32[]{:S(2)}, u32[]{:S(2)}) collective-permute-start(f32[136,512]{1,0:T(8,128)S(1)} %add.71), channel_id=1, source_target_pairs={{8,0},{16,8},{24,16},{32,24},{40,32},{48,40},{56,48},{64,56},{72,6... | collective-permute-start | bytes 835592 | tf_op jit(solution)/shard_map/ppermute | solution.py:22
  80.7 3.5 %collective-permute-done.5 = f32[136,512]{1,0:T(8,128)S(1)} collective-permute-done((f32[136,512]{1,0:T(8,128)S(1)}, f32[136,512]{1,0:T(8,128)S(1)}, u32[]{:S(2)}, u32[]{:S(2)}) %collective-permute-start.5) | collective-permute-done | bytes 278560 | tf_op jit(solution)/shard_map/ppermute | solution.py:22
  84.2 0.1 copy.27
  84.3 0.2 div.11
  84.6 11.3 %all_to_all.34 = bf16[8,16,512]{2,1,0:T(8,128)(2,1)S(1)} all-to-all(bf16[8,16,512]{2,1,0:T(8,128)(2,1)S(1)} %bitcast.36), channel_id=1, replica_groups=mesh['pool'=64,'tensor'=8] {'tensor'}, dimensions={0} | all-to-all | bytes 262144 | tf_op jit(solution)/shard_map/all_to_all | solution.py:196
  95.9 0.7 copy.32
  (44 shorter events, 0.6 us)
Async XLA Ops:
  0.0 12.0 %copy-start = (s32[64,64]{1,0:T(8,128)S(1)}, s32[64,64]{1,0:T(8,128)}, u32[]{:S(2)}) copy-start(s32[64,64]{1,0:T(8,128)} %param.12) | copy-start | bytes 49156
  0.0 1.0 copy-start.10
  0.0 1.0 %copy-start.11 = (bf16[16,2048]{1,0:T(8,128)(2,1)S(1)}, bf16[16,2048]{1,0:T(8,128)(2,1)}, u32[]{:S(2)}) copy-start(bf16[16,2048]{1,0:T(8,128)(2,1)} %param.8) | copy-start | bytes 196612
  1.7 16.7 %all-to-all-start = ((bf16[16,8,1024]{2,0,1:T(8,128)(2,1)}), bf16[16,8,1024]{2,0,1:T(8,128)(2,1)S(1)}, u32[]{:S(2)}, u32[]{:S(2)}) async-start(bf16[16,8,1024]{2,0,1:T(8,128)(2,1)} %pad_maximum_fusion), calls=%async_computation | async-start | bytes 524288 | tf_op jit(solution)/shard_map/all_to_all | solution.py:146
  12.0 1.0 %copy-start.1 = (s32[64]{0:T(128)S(1)}, s32[64]{0:T(128)}, u32[]{:S(2)}) copy-start(s32[64]{0:T(128)} %param.13) | copy-start | bytes 772
  18.4 12.2 %copy-start.5 = (bf16[128,512]{1,0:T(8,128)(2,1)}, bf16[128,512]{1,0:T(8,128)(2,1)S(1)}, u32[]{:S(2)}) copy-start(bf16[128,512]{1,0:T(8,128)(2,1)S(1)} %slice.24.q_ref) | copy-start | bytes 393220
  18.5 16.1 %collective-permute-start = (bf16[128,512]{1,0:T(8,128)(2,1)S(1)}, bf16[128,512]{1,0:T(8,128)(2,1)S(1)}, u32[]{:S(2)}, u32[]{:S(2)}) collective-permute-start(bf16[128,512]{1,0:T(8,128)(2,1)S(1)} %slice.24.q_ref), channel_id=1, source_target_pairs={{488,0},{496,8},{504,16},{0,24},{8,32},{16,40},{24,48},{32,56},{40... | collective-permute-start | bytes 393224 | tf_op jit(solution)/shard_map/ppermute | solution.py:22
  20.4 22.1 %collective-permute-start.1 = (bf16[128,512]{1,0:T(8,128)(2,1)S(1)}, bf16[128,512]{1,0:T(8,128)(2,1)S(1)}, u32[]{:S(2)}, u32[]{:S(2)}) collective-permute-start(bf16[128,512]{1,0:T(8,128)(2,1)S(1)} %slice.24.q_ref), channel_id=1, source_target_pairs={{496,0},{504,8},{0,16},{8,24},{16,32},{24,40},{32,48},{40,56},{48,... | collective-permute-start | bytes 393224 | tf_op jit(solution)/shard_map/ppermute | solution.py:22
  26.4 18.7 %collective-permute-start.2 = (bf16[128,512]{1,0:T(8,128)(2,1)S(1)}, bf16[128,512]{1,0:T(8,128)(2,1)S(1)}, u32[]{:S(2)}, u32[]{:S(2)}) collective-permute-start(bf16[128,512]{1,0:T(8,128)(2,1)S(1)} %slice.24.q_ref), channel_id=1, source_target_pairs={{504,0},{0,8},{8,16},{16,24},{24,32},{32,40},{40,48},{48,56},{56,6... | collective-permute-start | bytes 393224 | tf_op jit(solution)/shard_map/ppermute | solution.py:22
  34.5 10.6 %copy-start.8 = (bf16[128,512]{1,0:T(8,128)(2,1)}, bf16[128,512]{1,0:T(8,128)(2,1)S(1)}, u32[]{:S(2)}) copy-start(bf16[128,512]{1,0:T(8,128)(2,1)S(1)} %collective-permute-done.q_ref) | copy-start | bytes 393220
  42.4 5.9 %copy-start.9 = (bf16[128,512]{1,0:T(8,128)(2,1)}, bf16[128,512]{1,0:T(8,128)(2,1)S(1)}, u32[]{:S(2)}) copy-start(bf16[128,512]{1,0:T(8,128)(2,1)S(1)} %collective-permute-done.1.q_ref) | copy-start | bytes 393220
  45.1 3.2 %copy-start.7 = (bf16[128,512]{1,0:T(8,128)(2,1)}, bf16[128,512]{1,0:T(8,128)(2,1)S(1)}, u32[]{:S(2)}) copy-start(bf16[128,512]{1,0:T(8,128)(2,1)S(1)} %collective-permute-done.2.q_ref) | copy-start | bytes 393220
  48.4 3.6 %copy-start.6 = (f32[136,512]{1,0:T(8,128)S(1)}, f32[136,512]{1,0:T(8,128)}, u32[]{:S(2)}) copy-start(f32[136,512]{1,0:T(8,128)} %shard_map.74) | copy-start | bytes 835588
  51.9 9.6 %copy-start.4 = (f32[136,512]{1,0:T(8,128)S(1)}, f32[136,512]{1,0:T(8,128)}, u32[]{:S(2)}) copy-start(f32[136,512]{1,0:T(8,128)} %shard_map.75) | copy-start | bytes 835588
  51.9 9.6 %collective-permute-start.3 = (f32[136,512]{1,0:T(8,128)S(1)}, f32[136,512]{1,0:T(8,128)S(1)}, u32[]{:S(2)}, u32[]{:S(2)}) collective-permute-start(f32[136,512]{1,0:T(8,128)S(1)} %copy-done.6), channel_id=1, source_target_pairs={{8,0},{16,8},{24,16},{32,24},{40,32},{48,40},{56,48},{64,56},{72,6... | collective-permute-start | bytes 835592 | tf_op jit(solution)/shard_map/ppermute | solution.py:22
  60.7 12.4 %copy-start.3 = (f32[136,512]{1,0:T(8,128)S(1)}, f32[136,512]{1,0:T(8,128)}, u32[]{:S(2)}) copy-start(f32[136,512]{1,0:T(8,128)} %shard_map.76) | copy-start | bytes 835588
  61.5 22.6 %copy-start.2 = (f32[136,512]{1,0:T(8,128)S(1)}, f32[136,512]{1,0:T(8,128)}, u32[]{:S(2)}) copy-start(f32[136,512]{1,0:T(8,128)} %shard_map.73) | copy-start | bytes 835588
  61.6 11.6 %collective-permute-start.4 = (f32[136,512]{1,0:T(8,128)S(1)}, f32[136,512]{1,0:T(8,128)S(1)}, u32[]{:S(2)}, u32[]{:S(2)}) collective-permute-start(f32[136,512]{1,0:T(8,128)S(1)} %add.70), channel_id=1, source_target_pairs={{8,0},{16,8},{24,16},{32,24},{40,32},{48,40},{56,48},{64,56},{72,6... | collective-permute-start | bytes 835592 | tf_op jit(solution)/shard_map/ppermute | solution.py:22
  73.2 10.9 %collective-permute-start.5 = (f32[136,512]{1,0:T(8,128)S(1)}, f32[136,512]{1,0:T(8,128)S(1)}, u32[]{:S(2)}, u32[]{:S(2)}) collective-permute-start(f32[136,512]{1,0:T(8,128)S(1)} %add.71), channel_id=1, source_target_pairs={{8,0},{16,8},{24,16},{32,24},{40,32},{48,40},{56,48},{64,56},{72,6... | collective-permute-start | bytes 835592 | tf_op jit(solution)/shard_map/ppermute | solution.py:22
